TPU v7x, 32 devices: a whole 2x2x4 slice. The times are simulated.
32 devices in a mesh: ctx: 8 (over y, x, core), uly: 4 (over z).
Axes of the slice: x: 2, y: 2, z: 4, core: 2. Of those that a mesh axis runs over, the one named last changes fastest.
Arguments:
- query_rows: bfloat16 [3072, 6144], P('ctx', 'uly'), may hold values from -150 to 150
- key_rows: bfloat16 [3072, 1024], P('ctx'), may hold values from -7 to 7
- value_rows: bfloat16 [3072, 1024], P('ctx'), may hold values from -6 to 6
- out_grad: bfloat16 [3072, 6144], P('ctx', 'uly'), may hold values from -96 to 96
- block_list: int32 [24, 8], replicated, may hold values from 0 to 23, as said below
Outputs:
- query_grad: bfloat16 [3072, 6144], P(('ctx', 'uly'))
- key_grad: bfloat16 [3072, 1024], P(('ctx', 'uly'))
- value_grad: bfloat16 [3072, 1024], P(('ctx', 'uly'))
Inputs may be any that keep to these rules, and one draw needn't show every extreme that they name: `block_list`: row i holds (i - 1) mod 24, i, (i + 1) mod 24 in columns 0 to 2 and 0, 1 in columns 3 and 4. Columns 5 to 7 hold blocks j whose index j // 3 is none of i // 3 and its two cyclic neighbours; the rows of one index name at most 2 blocks of any one other index there, and some index reaches 2.
All inputs are finite; a program needn't handle non-finite values.
Results may differ from a plain program's by a relative error of at most 0.015.
Values may be sent and summed in bfloat16 or wider, within the bound.
No kernel may reach another device: no remote copies, remote signals or barrier semaphores. Data moves between devices by JAX's collectives and lax.ppermute only.
A program may use at most 64 MiB of HBM per device.

v0:
```python
import functools
import math

import jax
import jax.numpy as jnp
from jax import lax
from jax.experimental import pallas as pl
from jax.experimental.pallas import tpu as pltpu
from jax.sharding import PartitionSpec as P

HD = 128
KVH = 8
BLK = 128
GROUP = 6
SLOTS = 8


def attention_kernel(
    blk_ref, dst_ref, kind_ref,
    q_ref, do_ref, k_ref, v_ref,
    dq_ref, loc_ref, far_ref,
    kc_ref, vc_ref, loc_acc, far_acc,
    *, hpk, kv_here, nb,
):
    g = pl.program_id(0)
    b = pl.program_id(1)
    scale = 1.0 / math.sqrt(HD)

    @pl.when((g == 0) & (b == 0))
    def _():
        loc_acc[...] = jnp.zeros_like(loc_acc)
        far_acc[...] = jnp.zeros_like(far_acc)

    for s in range(SLOTS):
        row = pl.multiple_of(blk_ref[b * SLOTS + s] * BLK, BLK)
        kc_ref[s * BLK:(s + 1) * BLK, :] = k_ref[pl.ds(row, BLK), :]
        vc_ref[s * BLK:(s + 1) * BLK, :] = v_ref[pl.ds(row, BLK), :]

    kc = kc_ref[...]
    vc = vc_ref[...]
    qs = jnp.concatenate([q_ref[:, h * HD:(h + 1) * HD] for h in range(hpk)], axis=0)
    dos = jnp.concatenate([do_ref[:, h * HD:(h + 1) * HD] for h in range(hpk)], axis=0)
    nt = (((1,), (1,)), ((), ()))
    tn = (((0,), (0,)), ((), ()))
    scores = lax.dot_general(qs, kc, nt, preferred_element_type=jnp.float32) * scale
    peak = jnp.max(scores, axis=1, keepdims=True)
    lifted = jnp.exp(scores - peak)
    probs = lifted / jnp.sum(lifted, axis=1, keepdims=True)
    probs_b = probs.astype(jnp.bfloat16)
    attended = jnp.dot(probs_b, vc, preferred_element_type=jnp.float32)
    delta = jnp.sum(dos.astype(jnp.float32) * attended, axis=1, keepdims=True)
    dprobs = lax.dot_general(dos, vc, nt, preferred_element_type=jnp.float32)
    dscores = (probs * (dprobs - delta) * scale).astype(jnp.bfloat16)
    dq = jnp.dot(dscores, kc, preferred_element_type=jnp.float32)
    for h in range(hpk):
        dq_ref[:, h * HD:(h + 1) * HD] = dq[h * BLK:(h + 1) * BLK].astype(jnp.bfloat16)
    kterm = lax.dot_general(dscores, qs, tn, preferred_element_type=jnp.float32)
    vterm = lax.dot_general(probs_b, dos, tn, preferred_element_type=jnp.float32)

    for s in range(SLOTS):
        kind = kind_ref[b * SLOTS + s]
        row = pl.multiple_of(dst_ref[b * SLOTS + s] * BLK, BLK)
        kt = kterm[s * BLK:(s + 1) * BLK]
        vt = vterm[s * BLK:(s + 1) * BLK]
        rounded = kind == 0
        kt = jnp.where(rounded, kt.astype(jnp.bfloat16).astype(jnp.float32), kt)
        vt = jnp.where(rounded, vt.astype(jnp.bfloat16).astype(jnp.float32), vt)

        @pl.when(kind == 2)
        def _():
            loc_acc[g, pl.ds(row, BLK), :] += kt
            loc_acc[kv_here + g, pl.ds(row, BLK), :] += vt

        @pl.when(kind != 2)
        def _():
            far_acc[g, pl.ds(row, BLK), :] += kt
            far_acc[kv_here + g, pl.ds(row, BLK), :] += vt

    @pl.when((g == kv_here - 1) & (b == nb - 1))
    def _():
        for j in range(2 * kv_here):
            loc_ref[:, j * HD:(j + 1) * HD] = loc_acc[j]
            far_ref[:, j * HD:(j + 1) * HD] = far_acc[j].astype(jnp.bfloat16)


def shards(query_rows, key_rows, value_rows, out_grad, block_list):
    shard_index = lax.axis_index("ctx")
    lane_index = lax.axis_index("uly")
    nb = key_rows.shape[0] // BLK
    seq = block_list.shape[0] * BLK
    heads_here = query_rows.shape[1] // HD
    kv_here = max(1, heads_here // GROUP)
    hpk = heads_here // kv_here
    width = 2 * kv_here * HD
    first_kv = lane_index * heads_here // GROUP
    key_own = lax.dynamic_slice_in_dim(key_rows, first_kv * HD, kv_here * HD, axis=1)
    value_own = lax.dynamic_slice_in_dim(value_rows, first_kv * HD, kv_here * HD, axis=1)
    kv_own = jnp.concatenate([key_own, value_own], axis=1)
    kv_all = lax.all_gather(kv_own, "ctx", axis=0, tiled=True)

    rows = lax.dynamic_slice_in_dim(block_list, shard_index * nb, nb, axis=0).astype(jnp.int32)
    owner = rows // nb
    cols = jnp.arange(SLOTS)[None, :]
    is_global = (cols == 3) | (cols == 4)
    local = owner == shard_index
    remote = jnp.logical_not(local) & jnp.logical_not(is_global)
    kind = jnp.where(local, 2, jnp.where(remote, 0, 1)).astype(jnp.int32).reshape(-1)
    dst = jnp.where(local, rows - shard_index * nb, rows).astype(jnp.int32).reshape(-1)
    blk = rows.reshape(-1)

    kernel = functools.partial(attention_kernel, hpk=hpk, kv_here=kv_here, nb=nb)
    grid_spec = pltpu.PrefetchScalarGridSpec(
        num_scalar_prefetch=3,
        grid=(kv_here, nb),
        in_specs=[
            pl.BlockSpec((BLK, hpk * HD), lambda g, b, *_: (b, g)),
            pl.BlockSpec((BLK, hpk * HD), lambda g, b, *_: (b, g)),
            pl.BlockSpec((seq, HD), lambda g, b, *_: (0, g)),
            pl.BlockSpec((seq, HD), lambda g, b, *_: (0, kv_here + g)),
        ],
        out_specs=[
            pl.BlockSpec((BLK, hpk * HD), lambda g, b, *_: (b, g)),
            pl.BlockSpec((nb * BLK, width), lambda g, b, *_: (0, 0)),
            pl.BlockSpec((seq, width), lambda g, b, *_: (0, 0)),
        ],
        scratch_shapes=[
            pltpu.VMEM((SLOTS * BLK, HD), jnp.bfloat16),
            pltpu.VMEM((SLOTS * BLK, HD), jnp.bfloat16),
            pltpu.VMEM((2 * kv_here, nb * BLK, HD), jnp.float32),
            pltpu.VMEM((2 * kv_here, seq, HD), jnp.float32),
        ],
    )
    dq, loc, far = pl.pallas_call(
        kernel,
        grid_spec=grid_spec,
        out_shape=[
            jax.ShapeDtypeStruct((nb * BLK, heads_here * HD), jnp.bfloat16),
            jax.ShapeDtypeStruct((nb * BLK, width), jnp.float32),
            jax.ShapeDtypeStruct((seq, width), jnp.bfloat16),
        ],
        compiler_params=pltpu.CompilerParams(dimension_semantics=("arbitrary", "arbitrary")),
    )(blk, dst, kind, query_rows, out_grad, kv_all, kv_all)

    got = lax.psum_scatter(far, "ctx", scatter_dimension=0, tiled=True)
    kv_grad = (got.astype(jnp.float32) + loc).astype(jnp.bfloat16)

    query_out = lax.all_to_all(dq, "uly", split_axis=0, concat_axis=1, tiled=True)
    kv_seq = lax.all_to_all(kv_grad, "uly", split_axis=0, concat_axis=1, tiled=True)
    rows_here = kv_seq.shape[0]
    lane_count = kv_seq.shape[1] // width
    spread = kv_seq.reshape(rows_here, lane_count, 2, kv_here * HD)

    def gather_heads(part):
        if heads_here >= GROUP:
            return part.reshape(rows_here, KVH * HD)
        lanes_per = GROUP // heads_here
        merged = part.astype(jnp.float32).reshape(rows_here, KVH, lanes_per, HD).sum(axis=2)
        return merged.reshape(rows_here, KVH * HD).astype(jnp.bfloat16)

    return (query_out, gather_heads(spread[:, :, 0]), gather_heads(spread[:, :, 1]))


def solution(mesh):
    return jax.shard_map(
        shards,
        mesh=mesh,
        in_specs=(P("ctx", "uly"), P("ctx", None), P("ctx", None), P("ctx", "uly"), P()),
        out_specs=(P(("ctx", "uly"), None), P(("ctx", "uly"), None), P(("ctx", "uly"), None)),
        check_vma=False,
    )
```

profile of v0, /device:TPU:0, one launch (start us, length us, event | category | flops | bytes accessed | tf_op | source)
XLA Modules:
  0.0 148.3 jit_solution(13454349176173901573)
XLA Ops:
  7.2 0.0 copy-start.1
  7.2 0.0 all-gather.2.cloned.1.call-start
  7.3 1.1 constant_dynamic-slice_fusion
  8.3 0.8 pad_maximum_fusion
  9.1 0.0 all-gather.2.cloned.1.call-update
  9.1 0.0 reduce-scatter.2.cloned.1.call-start
  9.2 0.0 copy-done.1
  9.2 0.1 select_select_fusion
  9.3 0.1 copy.10
  9.4 0.6 reshape.40.kind_ref
  10.0 0.1 copy.8
  10.1 0.6 reshape.38.blk_ref
  10.7 0.1 copy.9
  10.7 0.6 reshape.39.dst_ref
  11.3 34.2 %all-gather.2.cloned.1.call-done.k_ref.v_ref = bf16[3072,512]{1,0:T(8,128)(2,1)} async-done(((bf16[384,512]{1,0:T(8,128)(2,1)}), bf16[3072,512]{1,0:T(8,128)(2,1)}) %all-gather.2.cloned.1.call-update) | async-done | bytes 3145744 | tf_op jit(solution)/shard_map/all_gather | solution.py:99
  45.5 28.8 %shard_map.76 = (bf16[384,1536]{1,0:T(8,128)(2,1)}, f32[384,512]{1,0:T(8,128)}, bf16[3072,512]{1,0:T(8,128)(2,1)}) custom-call(s32[24]{0:T(128)} %reshape.38.blk_ref, s32[24]{0:T(128)} %reshape.39.dst_ref, s32[24]{0:T(128)} %reshape.40.kind_ref, bf16[384,1536]{1,0:T(8,128)(2,1)} %q_ref.1, bf16[384,1536]{1,0:T(8,128)(2,1)} %do_ref.1, ...), custom_call_target="tpu_custom_call" | custom-call | tf_op jit(solution)/shard_map/pallas_call | solution.py:133
  74.3 0.0 reduce-scatter.2.cloned.1.call-update
  74.3 0.0 copy-start
  74.3 4.7 %all-to-all-start = ((bf16[4,96,1536]{2,1,0:T(8,128)(2,1)}), bf16[4,96,1536]{2,1,0:T(8,128)(2,1)S(1)}, u32[]{:S(2)}, u32[]{:S(2)}) async-start(bf16[4,96,1536]{2,1,0:T(8,128)(2,1)} %bitcast), calls=%async_computation | async-start | bytes 2359296 | tf_op jit(solution)/shard_map/all_to_all | solution.py:147
  79.1 41.7 %reduce-scatter.2.cloned.1.call-done = bf16[384,512]{1,0:T(8,128)(2,1)} async-done(((bf16[3072,512]{1,0:T(8,128)(2,1)}), bf16[384,512]{1,0:T(8,128)(2,1)}) %reduce-scatter.2.cloned.1.call-update) | async-done | bytes 393232 | tf_op jit(solution)/shard_map/reduce_scatter | solution.py:144
  120.8 0.0 copy-done
  120.8 1.9 %add_convert_fusion = bf16[384,512]{1,0:T(8,128)(2,1)} fusion(f32[384,512]{1,0:T(8,128)S(1)} %copy-done, bf16[384,512]{1,0:T(8,128)(2,1)} %reduce-scatter.2.cloned.1.call-done), kind=kLoop, calls=%fused_computation | loop fusion | flops 589824 | bytes 1572864 | tf_op jit(solution)/shard_map/convert_element_type | solution.py:145
  122.6 0.0 all-to-all-done
  122.6 4.6 %all-to-all-start.1 = ((bf16[4,96,512]{2,1,0:T(8,128)(2,1)}), bf16[4,96,512]{2,1,0:T(8,128)(2,1)S(1)}, u32[]{:S(2)}, u32[]{:S(2)}) async-start(bf16[4,96,512]{2,1,0:T(8,128)(2,1)} %bitcast.2), calls=%async_computation.2 | async-start | bytes 786432 | tf_op jit(solution)/shard_map/all_to_all | solution.py:148
  127.2 1.1 copy.16
  128.4 10.5 %all-to-all-done.1 = bf16[4,96,512]{2,1,0:T(8,128)(2,1)S(1)} async-done(((bf16[4,96,512]{2,1,0:T(8,128)(2,1)}), bf16[4,96,512]{2,1,0:T(8,128)(2,1)S(1)}, u32[]{:S(2)}, u32[]{:S(2)}) %all-to-all-start.1) | async-done | bytes 393248 | tf_op jit(solution)/shard_map/all_to_all | solution.py:148
  138.9 0.1 reshape.41
  139.0 0.5 fusion.2
  139.6 0.3 copy.15
  139.8 0.7 copy.18
  140.5 0.3 copy.14
  140.8 0.7 copy.17
  (2 shorter events, 0.0 us)
Async XLA Ops:
  7.2 2.0 %copy-start.1 = (s32[24,8]{0,1:T(8,128)S(1)}, s32[24,8]{0,1:T(8,128)}, u32[]{:S(2)}) copy-start(s32[24,8]{0,1:T(8,128)} %param.9) | copy-start | bytes 2308
  7.2 38.3 %all-gather.2.cloned.1.call-start = ((), (), s32[]{:S(2)}) async-start(), calls=%async_computation.3 | async-start | bytes 3538944 | tf_op jit(solution)/shard_map/all_gather | solution.py:99
  9.1 111.7 %reduce-scatter.2.cloned.1.call-start = ((), (), s32[]{:S(2)}) async-start(), calls=%async_computation.4 | async-start | bytes 3538944 | tf_op jit(solution)/shard_map/reduce_scatter | solution.py:144
  74.3 46.4 %copy-start = (f32[384,512]{1,0:T(8,128)S(1)}, f32[384,512]{1,0:T(8,128)}, u32[]{:S(2)}) copy-start(f32[384,512]{1,0:T(8,128)} %get-tuple-element.8) | copy-start | bytes 2359300
  74.3 48.3 %all-to-all-start = ((bf16[4,96,1536]{2,1,0:T(8,128)(2,1)}), bf16[4,96,1536]{2,1,0:T(8,128)(2,1)S(1)}, u32[]{:S(2)}, u32[]{:S(2)}) async-start(bf16[4,96,1536]{2,1,0:T(8,128)(2,1)} %bitcast), calls=%async_computation | async-start | bytes 2359296 | tf_op jit(solution)/shard_map/all_to_all | solution.py:147
  122.6 16.3 %all-to-all-start.1 = ((bf16[4,96,512]{2,1,0:T(8,128)(2,1)}), bf16[4,96,512]{2,1,0:T(8,128)(2,1)S(1)}, u32[]{:S(2)}, u32[]{:S(2)}) async-start(bf16[4,96,512]{2,1,0:T(8,128)(2,1)} %bitcast.2), calls=%async_computation.2 | async-start | bytes 786432 | tf_op jit(solution)/shard_map/all_to_all | solution.py:148
Sparse Core Ops, SparseCore 0:
  10.5 35.0 all-gather.1
  74.5 46.2 reduce-scatter.1
where the time goes:
time: 149 us; the launch traced here: 148 us
  waiting for transfers between devices  86.5 us (58%)
  Pallas kernels  28.8 us (19%)
  between operations  14.1 us (9%)
  starting transfers between devices  9.41 us (6%)
  local copies, waits for them, and re-layouts  6.8 us (5%)
  other arithmetic  2.74 us (2%)
    reduce_scatter x1, waiting for transfers between devices, shards(): got = lax.psum_scatter(far, 'ctx', scatter_dimension=0, tiled=True)  41.7 us
    all_gather x1, waiting for transfers between devices, shards(): kv_all = lax.all_gather(kv_own, 'ctx', axis=0, tiled=True)  34.2 us
    pallas_call x1, Pallas kernels, shards(): pl.pallas_call(kernel, grid_spec=grid_spec, out_shape=[jax.ShapeDtypeStru...  28.8 us
    all_to_all x1, waiting for transfers between devices, shards(): lax.all_to_all(kv_grad, 'uly', split_axis=0, concat_axis=1, tiled=True)  10.5 us
    all_to_all x1, starting transfers between devices, shards(): lax.all_to_all(dq, 'uly', split_axis=0, concat_axis=1, tiled=True)  4.74 us
    all_to_all x1, starting transfers between devices, shards(): lax.all_to_all(kv_grad, 'uly', split_axis=0, concat_axis=1, tiled=True)  4.59 us
  transfers between devices with their start and end apart: 4, of which 3 were waited for; matrix products, arithmetic and copies ran while one was open for 3% of the time, Pallas kernels for 0%

commit v1 on v0

--- a/solution.py
+++ b/solution.py
@@ -15,11 +15,30 @@
 SLOTS = 8
 
 
+def remote_plan(block_list, shard_count, block_count):
+    listed = block_list.reshape(shard_count, block_count, SLOTS)
+    wanted = jnp.concatenate(
+        [
+            listed[:, 0, 0:1],
+            listed[:, block_count - 1, 2:3],
+            listed[:, :, 5:8].reshape(shard_count, 3 * block_count),
+        ],
+        axis=1,
+    )
+    owners = wanted // block_count
+    inside = wanted - owners * block_count
+    slot_count = wanted.shape[1]
+    same_owner = owners[:, :, None] == owners[:, None, :]
+    earlier = jnp.arange(slot_count)[None, :] < jnp.arange(slot_count)[:, None]
+    places = jnp.sum((same_owner & earlier[None]).astype(jnp.int32), axis=2)
+    return (owners, inside, places)
+
+
 def attention_kernel(
-    blk_ref, dst_ref, kind_ref,
-    q_ref, do_ref, k_ref, v_ref,
-    dq_ref, loc_ref, far_ref,
-    kc_ref, vc_ref, loc_acc, far_acc,
+    kind_ref, idx_ref,
+    q_ref, do_ref, ok_ref, ov_ref, fk_ref, fv_ref, gk_ref, gv_ref,
+    dq_ref, loc_ref, back_ref, gsum_ref,
+    kc_ref, vc_ref, loc_acc, back_acc, g_acc,
     *, hpk, kv_here, nb,
 ):
     g = pl.program_id(0)
@@ -29,12 +48,17 @@
     @pl.when((g == 0) & (b == 0))
     def _():
         loc_acc[...] = jnp.zeros_like(loc_acc)
-        far_acc[...] = jnp.zeros_like(far_acc)
+        back_acc[...] = jnp.zeros_like(back_acc)
+        g_acc[...] = jnp.zeros_like(g_acc)
 
     for s in range(SLOTS):
-        row = pl.multiple_of(blk_ref[b * SLOTS + s] * BLK, BLK)
-        kc_ref[s * BLK:(s + 1) * BLK, :] = k_ref[pl.ds(row, BLK), :]
-        vc_ref[s * BLK:(s + 1) * BLK, :] = v_ref[pl.ds(row, BLK), :]
+        kind = kind_ref[b * SLOTS + s]
+        row = pl.multiple_of(idx_ref[b * SLOTS + s] * BLK, BLK)
+        for code, tk, tv in ((2, ok_ref, ov_ref), (0, fk_ref, fv_ref), (1, gk_ref, gv_ref)):
+            @pl.when(kind == code)
+            def _():
+                kc_ref[s * BLK:(s + 1) * BLK, :] = tk[pl.ds(row, BLK), :]
+                vc_ref[s * BLK:(s + 1) * BLK, :] = tv[pl.ds(row, BLK), :]
 
     kc = kc_ref[...]
     vc = vc_ref[...]
@@ -59,90 +83,134 @@
 
     for s in range(SLOTS):
         kind = kind_ref[b * SLOTS + s]
-        row = pl.multiple_of(dst_ref[b * SLOTS + s] * BLK, BLK)
+        row = pl.multiple_of(idx_ref[b * SLOTS + s] * BLK, BLK)
         kt = kterm[s * BLK:(s + 1) * BLK]
         vt = vterm[s * BLK:(s + 1) * BLK]
-        rounded = kind == 0
-        kt = jnp.where(rounded, kt.astype(jnp.bfloat16).astype(jnp.float32), kt)
-        vt = jnp.where(rounded, vt.astype(jnp.bfloat16).astype(jnp.float32), vt)
 
         @pl.when(kind == 2)
         def _():
             loc_acc[g, pl.ds(row, BLK), :] += kt
             loc_acc[kv_here + g, pl.ds(row, BLK), :] += vt
 
-        @pl.when(kind != 2)
+        @pl.when(kind == 1)
         def _():
-            far_acc[g, pl.ds(row, BLK), :] += kt
-            far_acc[kv_here + g, pl.ds(row, BLK), :] += vt
+            g_acc[g, pl.ds(row, BLK), :] += kt
+            g_acc[kv_here + g, pl.ds(row, BLK), :] += vt
+
+        @pl.when(kind == 0)
+        def _():
+            back_acc[g, pl.ds(row, BLK), :] += kt.astype(jnp.bfloat16).astype(jnp.float32)
+            back_acc[kv_here + g, pl.ds(row, BLK), :] += vt.astype(jnp.bfloat16).astype(jnp.float32)
 
     @pl.when((g == kv_here - 1) & (b == nb - 1))
     def _():
         for j in range(2 * kv_here):
             loc_ref[:, j * HD:(j + 1) * HD] = loc_acc[j]
-            far_ref[:, j * HD:(j + 1) * HD] = far_acc[j].astype(jnp.bfloat16)
+            back_ref[:, j * HD:(j + 1) * HD] = back_acc[j].astype(jnp.bfloat16)
+            gsum_ref[:, j * HD:(j + 1) * HD] = g_acc[j].astype(jnp.bfloat16)
 
 
 def shards(query_rows, key_rows, value_rows, out_grad, block_list):
     shard_index = lax.axis_index("ctx")
     lane_index = lax.axis_index("uly")
+    shard_count = lax.axis_size("ctx")
     nb = key_rows.shape[0] // BLK
-    seq = block_list.shape[0] * BLK
     heads_here = query_rows.shape[1] // HD
     kv_here = max(1, heads_here // GROUP)
     hpk = heads_here // kv_here
     width = 2 * kv_here * HD
+    capacity = (3 * nb + shard_count - 4) // (shard_count - 3)
+    far_count = shard_count * capacity
     first_kv = lane_index * heads_here // GROUP
     key_own = lax.dynamic_slice_in_dim(key_rows, first_kv * HD, kv_here * HD, axis=1)
     value_own = lax.dynamic_slice_in_dim(value_rows, first_kv * HD, kv_here * HD, axis=1)
     kv_own = jnp.concatenate([key_own, value_own], axis=1)
-    kv_all = lax.all_gather(kv_own, "ctx", axis=0, tiled=True)
-
+
+    owners, inside, places = remote_plan(block_list, shard_count, nb)
+    from_here = owners == shard_index
+    send_pick = (
+        from_here[:, :, None] & (places[:, :, None] == jnp.arange(capacity)[None, None, :])
+    ).astype(jnp.bfloat16)
+    send_block = (inside[:, :, None] == jnp.arange(nb)[None, None, :]).astype(jnp.bfloat16)
+    selector = jnp.einsum(
+        "ric,rib->rcb", send_pick, send_block, preferred_element_type=jnp.float32
+    ).astype(jnp.bfloat16).reshape(far_count, nb)
+    send = jnp.einsum(
+        "kb,btx->ktx", selector, kv_own.reshape(nb, BLK, width),
+        preferred_element_type=jnp.float32,
+    ).astype(jnp.bfloat16).reshape(far_count * BLK, width)
+    got = lax.all_to_all(send, "ctx", split_axis=0, concat_axis=0, tiled=True)
+    is_root = shard_index == 0
+    heads = lax.psum(jnp.where(is_root, kv_own[0:2 * BLK], jnp.zeros_like(kv_own[0:2 * BLK])), "ctx")
+
+    my_owner = lax.dynamic_index_in_dim(owners, shard_index, 0, keepdims=False)
+    my_place = lax.dynamic_index_in_dim(places, shard_index, 0, keepdims=False)
+    target = my_owner * capacity + my_place
     rows = lax.dynamic_slice_in_dim(block_list, shard_index * nb, nb, axis=0).astype(jnp.int32)
-    owner = rows // nb
+    local = rows // nb == shard_index
     cols = jnp.arange(SLOTS)[None, :]
+    blocks = jnp.arange(nb)[:, None]
     is_global = (cols == 3) | (cols == 4)
-    local = owner == shard_index
-    remote = jnp.logical_not(local) & jnp.logical_not(is_global)
-    kind = jnp.where(local, 2, jnp.where(remote, 0, 1)).astype(jnp.int32).reshape(-1)
-    dst = jnp.where(local, rows - shard_index * nb, rows).astype(jnp.int32).reshape(-1)
-    blk = rows.reshape(-1)
+    wanted_at = jnp.where(cols == 0, 0, jnp.where(cols == 2, 1, 2 + 3 * blocks + cols - 5))
+    wanted_at = jnp.clip(wanted_at, 0, target.shape[0] - 1)
+    far_index = jnp.take(target, wanted_at)
+    kind = jnp.where(local, 2, jnp.where(is_global, 1, 0)).astype(jnp.int32)
+    index = jnp.where(local, rows - shard_index * nb, jnp.where(is_global, rows, far_index))
+    index = jnp.clip(index, 0, jnp.where(local, nb - 1, jnp.where(is_global, 1, far_count - 1)))
+    kind = kind.reshape(-1)
+    index = index.astype(jnp.int32).reshape(-1)
 
     kernel = functools.partial(attention_kernel, hpk=hpk, kv_here=kv_here, nb=nb)
+
+    def columns(count):
+        return [
+            pl.BlockSpec((count, HD), lambda g, b, *_: (0, g)),
+            pl.BlockSpec((count, HD), lambda g, b, *_: (0, kv_here + g)),
+        ]
+
     grid_spec = pltpu.PrefetchScalarGridSpec(
-        num_scalar_prefetch=3,
+        num_scalar_prefetch=2,
         grid=(kv_here, nb),
         in_specs=[
             pl.BlockSpec((BLK, hpk * HD), lambda g, b, *_: (b, g)),
             pl.BlockSpec((BLK, hpk * HD), lambda g, b, *_: (b, g)),
-            pl.BlockSpec((seq, HD), lambda g, b, *_: (0, g)),
-            pl.BlockSpec((seq, HD), lambda g, b, *_: (0, kv_here + g)),
-        ],
+        ] + columns(nb * BLK) + columns(far_count * BLK) + columns(2 * BLK),
         out_specs=[
             pl.BlockSpec((BLK, hpk * HD), lambda g, b, *_: (b, g)),
             pl.BlockSpec((nb * BLK, width), lambda g, b, *_: (0, 0)),
-            pl.BlockSpec((seq, width), lambda g, b, *_: (0, 0)),
+            pl.BlockSpec((far_count * BLK, width), lambda g, b, *_: (0, 0)),
+            pl.BlockSpec((2 * BLK, width), lambda g, b, *_: (0, 0)),
         ],
         scratch_shapes=[
             pltpu.VMEM((SLOTS * BLK, HD), jnp.bfloat16),
             pltpu.VMEM((SLOTS * BLK, HD), jnp.bfloat16),
             pltpu.VMEM((2 * kv_here, nb * BLK, HD), jnp.float32),
-            pltpu.VMEM((2 * kv_here, seq, HD), jnp.float32),
-        ],
-    )
-    dq, loc, far = pl.pallas_call(
+            pltpu.VMEM((2 * kv_here, far_count * BLK, HD), jnp.float32),
+            pltpu.VMEM((2 * kv_here, 2 * BLK, HD), jnp.float32),
+        ],
+    )
+    dq, loc, back, gsum = pl.pallas_call(
         kernel,
         grid_spec=grid_spec,
         out_shape=[
             jax.ShapeDtypeStruct((nb * BLK, heads_here * HD), jnp.bfloat16),
             jax.ShapeDtypeStruct((nb * BLK, width), jnp.float32),
-            jax.ShapeDtypeStruct((seq, width), jnp.bfloat16),
+            jax.ShapeDtypeStruct((far_count * BLK, width), jnp.bfloat16),
+            jax.ShapeDtypeStruct((2 * BLK, width), jnp.bfloat16),
         ],
         compiler_params=pltpu.CompilerParams(dimension_semantics=("arbitrary", "arbitrary")),
-    )(blk, dst, kind, query_rows, out_grad, kv_all, kv_all)
-
-    got = lax.psum_scatter(far, "ctx", scatter_dimension=0, tiled=True)
-    kv_grad = (got.astype(jnp.float32) + loc).astype(jnp.bfloat16)
+    )(kind, index, query_rows, out_grad, kv_own, kv_own, got, got, heads, heads)
+
+    ret = lax.all_to_all(back, "ctx", split_axis=0, concat_axis=0, tiled=True)
+    head_sum = lax.psum(gsum, "ctx")
+    added = jnp.einsum(
+        "kb,ktx->btx", selector, ret.reshape(far_count, BLK, width),
+        preferred_element_type=jnp.float32,
+    ).reshape(nb * BLK, width)
+    root_part = jnp.where(
+        is_root, jnp.pad(head_sum.astype(jnp.float32), ((0, (nb - 2) * BLK), (0, 0))), 0.0
+    )
+    kv_grad = (loc + added + root_part).astype(jnp.bfloat16)
 
     query_out = lax.all_to_all(dq, "uly", split_axis=0, concat_axis=1, tiled=True)
     kv_seq = lax.all_to_all(kv_grad, "uly", split_axis=0, concat_axis=1, tiled=True)

time: 149 us -> 232 us (1.56)
  waiting for transfers between devices: 86.5 us -> 126 us
  blocking collectives: 0 us -> 30.1 us
  local copies, waits for them, and re-layouts: 6.8 us -> 12.1 us
  starting transfers between devices: 9.41 us -> 14.4 us
    psum x0 -> x2, waiting for transfers between devices: none -> 116 us  [the longest x1 60.8 us: shards(): lax.psum(jnp.where(is_root, kv_own[0:2 * BLK], jnp.zeros_like(kv_own[0:2...]
    reduce_scatter x1 -> x0, waiting for transfers between devices: 41.7 us -> none  [shards(): got = lax.psum_scatter(far, 'ctx', scatter_dimension=0, tiled=True)]
    all_gather x1 -> x0, waiting for transfers between devices: 34.2 us -> none  [shards(): kv_all = lax.all_gather(kv_own, 'ctx', axis=0, tiled=True)]
    all_to_all x0 -> x1, blocking collectives: none -> 30.1 us  [shards(): ret = lax.all_to_all(back, 'ctx', split_axis=0, concat_axis=0, tiled=True)]
    all_to_all x0 -> x1, starting transfers between devices: none -> 5.17 us  [shards(): got = lax.all_to_all(send, 'ctx', split_axis=0, concat_axis=0, tiled=True)]
    convert_element_type x0 -> x1, local copies, waits for them, and re-layouts: none -> 2.49 us  [shards(): send = jnp.einsum('kb,btx->ktx', selector, kv_own.reshape(nb, BLK, width)...]
  transfers between devices with their start and end apart: 4 -> 5, of which waited for: 3 -> 3; matrix products, arithmetic and copies ran while one was open for 3% -> 3% of each run, Pallas kernels for 0% -> 0%
where the time goes in v1:
time: 232 us
  waiting for transfers between devices  126 us (54%)
  blocking collectives  30.1 us (13%)
  Pallas kernels  29.1 us (13%)
  starting transfers between devices  14.4 us (6%)
  between operations  14.2 us (6%)
  local copies, waits for them, and re-layouts  12.1 us (5%)
  other arithmetic  3.38 us (1%)
    psum x1, waiting for transfers between devices, shards(): lax.psum(jnp.where(is_root, kv_own[0:2 * BLK], jnp.zeros_like(kv_own[0:2...  60.8 us
    psum x1, waiting for transfers between devices, shards(): head_sum = lax.psum(gsum, 'ctx')  55 us
    all_to_all x1, blocking collectives, shards(): ret = lax.all_to_all(back, 'ctx', split_axis=0, concat_axis=0, tiled=True)  30.1 us
    pallas_call x1, Pallas kernels, shards(): pl.pallas_call(kernel, grid_spec=grid_spec, out_shape=[jax.ShapeDtypeStru...  29.1 us
    all_to_all x1, waiting for transfers between devices, shards(): lax.all_to_all(kv_grad, 'uly', split_axis=0, concat_axis=1, tiled=True)  9.73 us
    all_to_all x1, starting transfers between devices, shards(): got = lax.all_to_all(send, 'ctx', split_axis=0, concat_axis=0, tiled=True)  5.17 us
  transfers between devices with their start and end apart: 5, of which 3 were waited for; matrix products, arithmetic and copies ran while one was open for 3% of the time, Pallas kernels for 0%

profile of v1, /device:TPU:0, one launch (start us, length us, event | category | flops | bytes accessed | tf_op | source)
XLA Modules:
  0.0 231.6 jit_solution(6991933453747230533)
XLA Ops:
  7.2 0.8 copy.70
  8.2 0.1 broadcast_compare_fusion
  8.5 0.3 convert_reduce_fusion
  8.9 1.1 constant_dynamic-slice_fusion
  10.0 0.1 convolution_convert_fusion.1
  10.1 0.7 convolution_convert_fusion
  10.8 2.5 %copy.81 = bf16[16,128,512]{2,1,0:T(8,128)(2,1)} copy(bf16[16,128,512]{2,0,1:T(8,128)(2,1)S(1)} %convolution_convert_fusion) | data formatting | bytes 4194304 | tf_op jit(solution)/shard_map/convert_element_type | solution.py:141
  13.3 5.2 %all-to-all-start = ((bf16[8,256,512]{2,1,0:T(8,128)(2,1)}), bf16[8,256,512]{2,1,0:T(8,128)(2,1)S(1)}, u32[]{:S(2)}, u32[]{:S(2)}) async-start(bf16[8,256,512]{2,1,0:T(8,128)(2,1)} %bitcast.42), calls=%async_computation | async-start | bytes 4194304 | tf_op jit(solution)/shard_map/all_to_all | solution.py:142
  18.5 0.7 fusion.6
  19.5 0.7 gather_fusion
  20.3 0.1 maximum_minimum_fusion
  20.4 0.6 reshape.446.idx_ref
  21.0 0.6 reshape.443.kind_ref
  21.6 60.8 %all-reduce.4.cloned.1.call-done.gk_ref.gv_ref = bf16[256,512]{1,0:T(8,128)(2,1)} async-done(((bf16[256,512]{1,0:T(8,128)(2,1)}), bf16[256,512]{1,0:T(8,128)(2,1)}) %all-reduce.4.cloned.1.call-update) | async-done | bytes 262160 | tf_op jit(solution)/shard_map/psum | solution.py:144
  82.4 1.3 copy-done
  83.7 29.1 %shard_map.76 = (bf16[384,1536]{1,0:T(8,128)(2,1)}, f32[384,512]{1,0:T(8,128)}, bf16[2048,512]{1,0:T(8,128)(2,1)}, bf16[256,512]{1,0:T(8,128)(2,1)}) custom-call(s32[24]{0:T(128)} %reshape.443.kind_ref, s32[24]{0:T(128)} %reshape.446.idx_ref, bf16[384,1536]{1,0:T(8,128)(2,1)} %q_ref.1, bf16[384,1536]{1,0:T(8,128)(2,1)} %do_ref.1, ...), custom_call_target="tpu_custom_call" | custom-call | tf_op jit(solution)/shard_map/pallas_call | solution.py:192
  112.8 30.1 %all_to_all.55 = bf16[8,256,512]{2,1,0:T(8,128)(2,1)S(1)} all-to-all(bf16[8,256,512]{2,1,0:T(8,128)(2,1)} %bitcast.46), channel_id=1, replica_groups=mesh['ctx'=8,'uly'=4] {'ctx'}, dimensions={0} | all-to-all | bytes 4194304 | tf_op jit(solution)/shard_map/all_to_all | solution.py:204
  142.9 4.6 %all-to-all-start.1 = ((bf16[4,96,1536]{2,1,0:T(8,128)(2,1)}), bf16[4,96,1536]{2,1,0:T(8,128)(2,1)S(1)}, u32[]{:S(2)}, u32[]{:S(2)}) async-start(bf16[4,96,1536]{2,1,0:T(8,128)(2,1)} %bitcast.48), calls=%async_computation.1 | async-start | bytes 2359296 | tf_op jit(solution)/shard_map/all_to_all | solution.py:215
  147.5 0.7 all-reduce.6.cloned.1.call-update
  148.2 1.3 fusion
  149.5 0.3 copy.84
  149.8 55.0 %all-reduce.6.cloned.1.call-done = bf16[256,512]{1,0:T(8,128)(2,1)} async-done(((bf16[256,512]{1,0:T(8,128)(2,1)}), bf16[256,512]{1,0:T(8,128)(2,1)}) %all-reduce.6.cloned.1.call-update) | async-done | bytes 262160 | tf_op jit(solution)/shard_map/psum | solution.py:205
  204.8 1.9 fusion.3
  206.7 4.6 %all-to-all-start.3 = ((bf16[4,96,512]{2,1,0:T(8,128)(2,1)}), bf16[4,96,512]{2,1,0:T(8,128)(2,1)S(1)}, u32[]{:S(2)}, u32[]{:S(2)}) async-start(bf16[4,96,512]{2,1,0:T(8,128)(2,1)} %bitcast.13), calls=%async_computation.3 | async-start | bytes 786432 | tf_op jit(solution)/shard_map/all_to_all | solution.py:216
  211.3 1.1 copy.91
  212.4 9.7 %all-to-all-done.3 = bf16[4,96,512]{2,1,0:T(8,128)(2,1)S(1)} async-done(((bf16[4,96,512]{2,1,0:T(8,128)(2,1)}), bf16[4,96,512]{2,1,0:T(8,128)(2,1)S(1)}, u32[]{:S(2)}, u32[]{:S(2)}) %all-to-all-start.3) | async-done | bytes 393248 | tf_op jit(solution)/shard_map/all_to_all | solution.py:216
  222.2 0.1 reshape.451
  222.3 0.5 fusion.18
  222.8 0.3 copy.90
  223.1 0.7 copy.93
  223.8 0.3 copy.89
  224.0 0.7 copy.92
  (30 shorter events, 0.9 us)
Async XLA Ops:
  10.0 3.3 %copy-start.1 = (bf16[384,512]{1,0:T(8,128)(2,1)}, bf16[384,512]{1,0:T(8,128)(2,1)S(1)}, u32[]{:S(2)}) copy-start(bf16[384,512]{1,0:T(8,128)(2,1)S(1)} %pad_maximum_fusion.ok_ref.ov_ref) | copy-start | bytes 1179652
  13.3 69.1 %all-to-all-start = ((bf16[8,256,512]{2,1,0:T(8,128)(2,1)}), bf16[8,256,512]{2,1,0:T(8,128)(2,1)S(1)}, u32[]{:S(2)}, u32[]{:S(2)}) async-start(bf16[8,256,512]{2,1,0:T(8,128)(2,1)} %bitcast.42), calls=%async_computation | async-start | bytes 4194304 | tf_op jit(solution)/shard_map/all_to_all | solution.py:142
  18.5 63.9 %all-reduce.4.cloned.1.call-start = ((), (), s32[]{:S(2)}) async-start(), calls=%async_computation.4 | async-start | bytes 524288 | tf_op jit(solution)/shard_map/psum | solution.py:144
  82.4 1.3 copy-start
  142.9 63.8 %all-to-all-start.1 = ((bf16[4,96,1536]{2,1,0:T(8,128)(2,1)}), bf16[4,96,1536]{2,1,0:T(8,128)(2,1)S(1)}, u32[]{:S(2)}, u32[]{:S(2)}) async-start(bf16[4,96,1536]{2,1,0:T(8,128)(2,1)} %bitcast.48), calls=%async_computation.1 | async-start | bytes 2359296 | tf_op jit(solution)/shard_map/all_to_all | solution.py:215
  147.5 57.3 %all-reduce.6.cloned.1.call-start = ((), (), s32[]{:S(2)}) async-start(), calls=%async_computation.5 | async-start | bytes 524288 | tf_op jit(solution)/shard_map/psum | solution.py:205
  149.5 55.3 %copy-start.2 = (f32[384,512]{1,0:T(8,128)S(1)}, f32[384,512]{1,0:T(8,128)}, u32[]{:S(2)}) copy-start(f32[384,512]{1,0:T(8,128)} %get-tuple-element.8) | copy-start | bytes 2359300
  206.7 15.5 %all-to-all-start.3 = ((bf16[4,96,512]{2,1,0:T(8,128)(2,1)}), bf16[4,96,512]{2,1,0:T(8,128)(2,1)S(1)}, u32[]{:S(2)}, u32[]{:S(2)}) async-start(bf16[4,96,512]{2,1,0:T(8,128)(2,1)} %bitcast.13), calls=%async_computation.3 | async-start | bytes 786432 | tf_op jit(solution)/shard_map/all_to_all | solution.py:216
Sparse Core Ops, SparseCore 0:
  23.0 59.3 all-reduce.3
  151.7 53.0 all-reduce.5

commit v2 on v1

--- a/solution.py
+++ b/solution.py
@@ -107,7 +107,29 @@
         for j in range(2 * kv_here):
             loc_ref[:, j * HD:(j + 1) * HD] = loc_acc[j]
             back_ref[:, j * HD:(j + 1) * HD] = back_acc[j].astype(jnp.bfloat16)
-            gsum_ref[:, j * HD:(j + 1) * HD] = g_acc[j].astype(jnp.bfloat16)
+            gsum_ref[:, j * HD:(j + 1) * HD] = g_acc[j]
+
+
+def tree_broadcast(x, shard_index, shard_count):
+    step = 1
+    while step < shard_count:
+        pairs = [(i, i + step) for i in range(step) if i + step < shard_count]
+        got = lax.ppermute(x, "ctx", pairs)
+        x = jnp.where((shard_index >= step) & (shard_index < 2 * step), got, x)
+        step *= 2
+    return x
+
+
+def tree_reduce(x, shard_count):
+    steps = []
+    step = 1
+    while step < shard_count:
+        steps.append(step)
+        step *= 2
+    for step in reversed(steps):
+        pairs = [(i + step, i) for i in range(step) if i + step < shard_count]
+        x = x + lax.ppermute(x.astype(jnp.bfloat16), "ctx", pairs).astype(jnp.float32)
+    return x
 
 
 def shards(query_rows, key_rows, value_rows, out_grad, block_list):
@@ -120,7 +142,9 @@
     hpk = heads_here // kv_here
     width = 2 * kv_here * HD
     capacity = (3 * nb + shard_count - 4) // (shard_count - 3)
-    far_count = shard_count * capacity
+    shift_caps = [1] + [capacity] * (shard_count - 3) + [1]
+    shift_offsets = [sum(shift_caps[:i]) for i in range(shard_count - 1)]
+    far_count = sum(shift_caps)
     first_kv = lane_index * heads_here // GROUP
     key_own = lax.dynamic_slice_in_dim(key_rows, first_kv * HD, kv_here * HD, axis=1)
     value_own = lax.dynamic_slice_in_dim(value_rows, first_kv * HD, kv_here * HD, axis=1)
@@ -134,18 +158,30 @@
     send_block = (inside[:, :, None] == jnp.arange(nb)[None, None, :]).astype(jnp.bfloat16)
     selector = jnp.einsum(
         "ric,rib->rcb", send_pick, send_block, preferred_element_type=jnp.float32
-    ).astype(jnp.bfloat16).reshape(far_count, nb)
+    ).astype(jnp.bfloat16)
     send = jnp.einsum(
-        "kb,btx->ktx", selector, kv_own.reshape(nb, BLK, width),
+        "rcb,btx->rctx", selector, kv_own.reshape(nb, BLK, width),
         preferred_element_type=jnp.float32,
-    ).astype(jnp.bfloat16).reshape(far_count * BLK, width)
-    got = lax.all_to_all(send, "ctx", split_axis=0, concat_axis=0, tiled=True)
+    ).astype(jnp.bfloat16)
+    got_parts = []
+    sel_parts = []
+    for d in range(1, shard_count):
+        cap_d = shift_caps[d - 1]
+        peer = (shard_index + d) % shard_count
+        payload = lax.dynamic_index_in_dim(send, peer, 0, keepdims=False)[:cap_d]
+        pairs = [(i, (i + d) % shard_count) for i in range(shard_count)]
+        got_parts.append(lax.ppermute(payload, "ctx", pairs))
+        sel_parts.append(lax.dynamic_index_in_dim(selector, peer, 0, keepdims=False)[:cap_d])
+    got = jnp.concatenate(got_parts, axis=0).reshape(far_count * BLK, width)
+    back_sel = jnp.concatenate(sel_parts, axis=0)
     is_root = shard_index == 0
-    heads = lax.psum(jnp.where(is_root, kv_own[0:2 * BLK], jnp.zeros_like(kv_own[0:2 * BLK])), "ctx")
+    heads = tree_broadcast(kv_own[0:2 * BLK], shard_index, shard_count)
 
     my_owner = lax.dynamic_index_in_dim(owners, shard_index, 0, keepdims=False)
     my_place = lax.dynamic_index_in_dim(places, shard_index, 0, keepdims=False)
-    target = my_owner * capacity + my_place
+    shift = (shard_index - my_owner) % shard_count
+    offsets = jnp.asarray([0] + shift_offsets, jnp.int32)
+    target = jnp.take(offsets, jnp.clip(shift, 0, shard_count - 1)) + my_place
     rows = lax.dynamic_slice_in_dim(block_list, shard_index * nb, nb, axis=0).astype(jnp.int32)
     local = rows // nb == shard_index
     cols = jnp.arange(SLOTS)[None, :]
@@ -196,20 +232,23 @@
             jax.ShapeDtypeStruct((nb * BLK, heads_here * HD), jnp.bfloat16),
             jax.ShapeDtypeStruct((nb * BLK, width), jnp.float32),
             jax.ShapeDtypeStruct((far_count * BLK, width), jnp.bfloat16),
-            jax.ShapeDtypeStruct((2 * BLK, width), jnp.bfloat16),
+            jax.ShapeDtypeStruct((2 * BLK, width), jnp.float32),
         ],
         compiler_params=pltpu.CompilerParams(dimension_semantics=("arbitrary", "arbitrary")),
     )(kind, index, query_rows, out_grad, kv_own, kv_own, got, got, heads, heads)
 
-    ret = lax.all_to_all(back, "ctx", split_axis=0, concat_axis=0, tiled=True)
-    head_sum = lax.psum(gsum, "ctx")
+    back = back.reshape(far_count, BLK, width)
+    ret_parts = []
+    for d in range(1, shard_count):
+        lo = shift_offsets[d - 1]
+        pairs = [(i, (i - d) % shard_count) for i in range(shard_count)]
+        ret_parts.append(lax.ppermute(back[lo:lo + shift_caps[d - 1]], "ctx", pairs))
+    ret = jnp.concatenate(ret_parts, axis=0)
+    head_sum = tree_reduce(gsum, shard_count)
     added = jnp.einsum(
-        "kb,ktx->btx", selector, ret.reshape(far_count, BLK, width),
-        preferred_element_type=jnp.float32,
+        "kb,ktx->btx", back_sel, ret, preferred_element_type=jnp.float32,
     ).reshape(nb * BLK, width)
-    root_part = jnp.where(
-        is_root, jnp.pad(head_sum.astype(jnp.float32), ((0, (nb - 2) * BLK), (0, 0))), 0.0
-    )
+    root_part = jnp.where(is_root, jnp.pad(head_sum, ((0, (nb - 2) * BLK), (0, 0))), 0.0)
     kv_grad = (loc + added + root_part).astype(jnp.bfloat16)
 
     query_out = lax.all_to_all(dq, "uly", split_axis=0, concat_axis=1, tiled=True)

time: 232 us -> 189 us (0.81)
  waiting for transfers between devices: 126 us -> 48.2 us
  local copies, waits for them, and re-layouts: 12.1 us -> 48 us
  starting transfers between devices: 14.4 us -> 38.5 us
  blocking collectives: 30.1 us -> 16.1 us
  between operations: 14.2 us -> 1.21 us
    psum x2 -> x0, waiting for transfers between devices: 116 us -> none  [the longest x1 60.8 us: shards(): lax.psum(jnp.where(is_root, kv_own[0:2 * BLK], jnp.zeros_like(kv_own[0:2...]
    ppermute x0 -> x20, starting transfers between devices: none -> 34.9 us  [the longest x7 17.3 us: shards(): lax.ppermute(back[lo:lo + shift_caps[d - 1]], 'ctx', pairs)]
    all_to_all x1, waiting for transfers between devices: 0.01 us -> 25.7 us  [shards(): lax.all_to_all(dq, 'uly', split_axis=0, concat_axis=1, tiled=True)]
    ppermute x0 -> x20, waiting for transfers between devices: none -> 22.5 us  [the longest x7 10.4 us: shards(): lax.ppermute(back[lo:lo + shift_caps[d - 1]], 'ctx', pairs)]
    concatenate x0 -> x3, local copies, waits for them, and re-layouts: none -> 21 us  [the longest x1 20.9 us: shards(): ret = jnp.concatenate(ret_parts, axis=0)]
    all_to_all x1, blocking collectives: 30.1 us -> 16.1 us  [shards(): lax.all_to_all(kv_grad, 'uly', split_axis=0, concat_axis=1, tiled=True)]
    all_to_all x2 -> x0, starting transfers between devices: 9.77 us -> none  [the longest x1 5.17 us: shards(): got = lax.all_to_all(send, 'ctx', split_axis=0, concat_axis=0, tiled=True)]
    all_to_all x2 -> x0, waiting for transfers between devices: 9.73 us -> none  [the longest x1 9.73 us: shards(): lax.all_to_all(kv_grad, 'uly', split_axis=0, concat_axis=1, tiled=True)]
  transfers between devices with their start and end apart: 5 -> 21, of which waited for: 3 -> 8; matrix products, arithmetic and copies ran while one was open for 3% -> 22% of each run, Pallas kernels for 0% -> 0%
where the time goes in v2:
time: 189 us; the launch traced here: 187 us
  waiting for transfers between devices  48.2 us (26%)
  local copies, waits for them, and re-layouts  48 us (25%)
  starting transfers between devices  38.5 us (20%)
  Pallas kernels  28.8 us (15%)
  blocking collectives  16.1 us (9%)
  other arithmetic  4.66 us (2%)
    pallas_call x1, Pallas kernels, shards(): pl.pallas_call(kernel, grid_spec=grid_spec, out_shape=[jax.ShapeDtypeStru...  28.8 us
    all_to_all x1, waiting for transfers between devices, shards(): lax.all_to_all(dq, 'uly', split_axis=0, concat_axis=1, tiled=True)  25.7 us
    concatenate x1, local copies, waits for them, and re-layouts, shards(): ret = jnp.concatenate(ret_parts, axis=0)  20.9 us
    ppermute x7, starting transfers between devices, shards(): lax.ppermute(back[lo:lo + shift_caps[d - 1]], 'ctx', pairs)  17.3 us
    all_to_all x1, blocking collectives, shards(): lax.all_to_all(kv_grad, 'uly', split_axis=0, concat_axis=1, tiled=True)  16.1 us
    ppermute x7, waiting for transfers between devices, shards(): lax.ppermute(back[lo:lo + shift_caps[d - 1]], 'ctx', pairs)  10.4 us
    unnamed x46, local copies, waits for them, and re-layouts  10 us
    ppermute x3, waiting for transfers between devices, tree_broadcast(): got = lax.ppermute(x, 'ctx', pairs)  9.5 us
  transfers between devices with their start and end apart: 21, of which 8 were waited for; matrix products, arithmetic and copies ran while one was open for 22% of the time, Pallas kernels for 0%

profile of v2, /device:TPU:0, one launch (start us, length us, event | category | flops | bytes accessed | tf_op | source)
XLA Modules:
  0.0 186.7 jit_solution(13747800264213368057)
XLA Ops:
  3.0 1.1 constant_dynamic-slice_fusion.14
  5.5 3.8 %constant_dynamic-slice_fusion.8 = (bf16[1,2,128,512]{3,0,2,1:T(2,128)(2,1)S(1)}, bf16[1,2,128,512]{3,0,2,1:T(2,128)(2,1)S(1)}, bf16[1,2,128,512]{3,0,2,1:T(2,12...) fusion(bf16[8,2,128,512]{3,0,2,1:T(8,128)(2,1)S(1)} %convolution_convert_fusion, s32[]{:T(128)S(6)} %select_n.280, ...), kind=kLoop, calls=%fused_computation.56 | loop fusion | bytes 2621460 | tf_op jit(solution)/shard_map/jit(dynamic_index_in_dim)/dynamic_slice | solution.py:171
  10.0 2.9 %collective-permute-start.1 = (bf16[2,128,512]{2,1,0:T(8,128)(2,1)}, bf16[2,128,512]{2,1,0:T(8,128)(2,1)}, u32[]{:S(2)}, u32[]{:S(2)}) collective-permute-start(bf16[2,128,512]{2,1,0:T(8,128)(2,1)} %bitcast.83), channel_id=1, source_target_pairs={{0,8},{4,12},{8,16},{12,20},{16,24},{20,28},{24,0},{28,4},{1,9},{5... | collective-permute-start | bytes 786440 | tf_op jit(solution)/shard_map/ppermute | solution.py:173
  13.0 1.3 constant_dynamic-slice_fusion.7
  15.1 2.7 %collective-permute-start.2 = (bf16[2,128,512]{2,1,0:T(8,128)(2,1)}, bf16[2,128,512]{2,1,0:T(8,128)(2,1)}, u32[]{:S(2)}, u32[]{:S(2)}) collective-permute-start(bf16[2,128,512]{2,1,0:T(8,128)(2,1)} %bitcast.82), channel_id=1, source_target_pairs={{0,12},{4,16},{8,20},{12,24},{16,28},{20,0},{24,4},{28,8},{1,13},{... | collective-permute-start | bytes 786440 | tf_op jit(solution)/shard_map/ppermute | solution.py:173
  18.4 2.0 %collective-permute-start.7 = (bf16[256,512]{1,0:T(8,128)(2,1)S(1)}, bf16[256,512]{1,0:T(8,128)(2,1)}, u32[]{:S(2)}, u32[]{:S(2)}) collective-permute-start(bf16[256,512]{1,0:T(8,128)(2,1)S(1)} %fusion.5), channel_id=1, source_target_pairs={{0,4},{1,5},{2,6},{3,7}} | collective-permute-start | bytes 786440 | tf_op jit(solution)/shard_map/ppermute | solution.py:117
  26.7 3.3 %collective-permute-start.8 = (bf16[256,512]{1,0:T(8,128)(2,1)S(1)}, bf16[256,512]{1,0:T(8,128)(2,1)S(1)}, u32[]{:S(2)}, u32[]{:S(2)}) collective-permute-start(bf16[256,512]{1,0:T(8,128)(2,1)S(1)} %broadcast_select_fusion), channel_id=1, source_target_pairs={{0,8},{4,12},{1,9},{5,13},{2,10},{6,14},{3,11},{7,15}} | collective-permute-start | bytes 786440 | tf_op jit(solution)/shard_map/ppermute | solution.py:117
  30.1 1.0 constant_dynamic-update-slice_fusion.5
  33.1 6.0 %collective-permute-done.8 = bf16[256,512]{1,0:T(8,128)(2,1)S(1)} collective-permute-done((bf16[256,512]{1,0:T(8,128)(2,1)S(1)}, bf16[256,512]{1,0:T(8,128)(2,1)S(1)}, u32[]{:S(2)}, u32[]{:S(2)}) %collective-permute-start.8) | collective-permute-done | bytes 262176 | tf_op jit(solution)/shard_map/ppermute | solution.py:117
  39.1 1.3 collective-permute-start.9
  40.5 1.2 collective-permute-done.6
  41.7 3.5 %collective-permute-done.9 = bf16[256,512]{1,0:T(8,128)(2,1)S(1)} collective-permute-done((bf16[256,512]{1,0:T(8,128)(2,1)S(1)}, bf16[256,512]{1,0:T(8,128)(2,1)S(1)}, u32[]{:S(2)}, u32[]{:S(2)}) %collective-permute-start.9) | collective-permute-done | bytes 262176 | tf_op jit(solution)/shard_map/ppermute | solution.py:117
  46.0 28.8 %shard_map.85 = (bf16[384,1536]{1,0:T(8,128)(2,1)}, f32[384,512]{1,0:T(8,128)}, bf16[1536,512]{1,0:T(8,128)(2,1)}, f32[256,512]{1,0:T(8,128)}) custom-call(s32[24]{0:T(128)} %reshape.507.kind_ref, s32[24]{0:T(128)} %reshape.510.idx_ref, bf16[384,1536]{1,0:T(8,128)(2,1)} %q_ref.1, bf16[384,1536]{1,0:T(8,128)(2,1)} %do_ref.1, bf16[384,512]{1,0:T(8,128)(2,1)} %copy-done.2, ...), custom_call_target="tpu_custom_call" | custom-call | tf_op jit(solution)/shard_map/pallas_call | solution.py:228
  74.8 1.1 convert_element_type.37
  75.8 1.5 collective-permute-start.17
  77.3 1.4 fusion.30
  79.0 4.9 %collective-permute-start.11 = (bf16[2,128,512]{2,0,1:T(2,128)(2,1)S(1)}, bf16[2,128,512]{2,0,1:T(2,128)(2,1)S(1)}, u32[]{:S(2)}, u32[]{:S(2)}) collective-permute-start(bf16[2,128,512]{2,0,1:T(2,128)(2,1)S(1)} %copy.163), channel_id=1, source_target_pairs={{0,24},{4,28},{8,0},{12,4},{16,8},{20,12},{24,16},{28,20},{1,25},{... | collective-permute-start | bytes 786440 | tf_op jit(solution)/shard_map/ppermute | solution.py:245
  83.9 1.0 slice_bitcast_fusion
  85.9 2.5 %collective-permute-start.13 = (bf16[2,128,512]{2,0,1:T(2,128)(2,1)S(1)}, bf16[2,128,512]{2,0,1:T(2,128)(2,1)}, u32[]{:S(2)}, u32[]{:S(2)}) collective-permute-start(bf16[2,128,512]{2,0,1:T(2,128)(2,1)S(1)} %copy.165), channel_id=1, source_target_pairs={{0,16},{4,20},{8,24},{12,28},{16,0},{20,4},{24,8},{28,12},{1,17},{... | collective-permute-start | bytes 786440 | tf_op jit(solution)/shard_map/ppermute | solution.py:245
  90.2 2.8 %collective-permute-done.10 = bf16[1,128,512]{2,1,0:T(8,128)(2,1)S(1)} collective-permute-done((bf16[1,128,512]{2,1,0:T(8,128)(2,1)S(1)}, bf16[1,128,512]{2,1,0:T(8,128)(2,1)S(1)}, u32[]{:S(2)}, u32[]{:S(2)}) %collective-permute-start.10) | collective-permute-done | bytes 131104 | tf_op jit(solution)/shard_map/ppermute | solution.py:245
  93.1 7.3 %collective-permute-start.14 = (bf16[2,128,512]{2,0,1:T(2,128)(2,1)S(1)}, bf16[2,128,512]{2,0,1:T(2,128)(2,1)}, u32[]{:S(2)}, u32[]{:S(2)}) collective-permute-start(bf16[2,128,512]{2,0,1:T(2,128)(2,1)S(1)} %copy.166), channel_id=1, source_target_pairs={{0,12},{4,16},{8,20},{12,24},{16,28},{20,0},{24,4},{28,8},{1,13},{... | collective-permute-start | bytes 786440 | tf_op jit(solution)/shard_map/ppermute | solution.py:245
  100.4 1.3 collective-permute-done.16
  101.7 1.6 collective-permute-start.15
  103.2 1.3 collective-permute-start.18
  106.5 6.3 %collective-permute-done.14 = bf16[2,128,512]{2,0,1:T(2,128)(2,1)} collective-permute-done((bf16[2,128,512]{2,0,1:T(2,128)(2,1)S(1)}, bf16[2,128,512]{2,0,1:T(2,128)(2,1)}, u32[]{:S(2)}, u32[]{:S(2)}) %collective-permute-start.14) | collective-permute-done | bytes 262176 | tf_op jit(solution)/shard_map/ppermute | solution.py:245
  112.9 20.9 %concatenate.56 = bf16[12,128,512]{2,0,1:T(8,128)(2,1)S(1)} concatenate(bf16[1,128,512]{2,0,1:T(2,128)(2,1)S(1)} %copy.168, bf16[2,128,512]{2,0,1:T(2,128)(2,1)} %copy-done.12, bf16[2,128,512]{2,0,1:T(2,128)(2,1)} %collective-permute-done.12, bf16[2,128,512]{2,0,1:T(2,128)(2,1)} %collective-permute-done.13, bf16[2,128,512]{2,0,1:T(2,128)(2,1)} %collective-permute-done.14, ...), dimensions={0} | concatenate | bytes 3145728 | tf_op jit(solution)/shard_map/concatenate | solution.py:246
  133.8 1.3 collective-permute-start.19
  135.8 1.4 collective-permute-done.19
  137.7 16.1 %all_to_all.35 = bf16[4,96,512]{2,1,0:T(8,128)(2,1)S(1)} all-to-all(bf16[4,96,512]{2,1,0:T(8,128)(2,1)S(1)} %bitcast.91), channel_id=1, replica_groups=mesh['ctx'=8,'uly'=4] {'uly'}, dimensions={0} | all-to-all | bytes 786432 | tf_op jit(solution)/shard_map/all_to_all | solution.py:255
  153.7 3.5 %all-to-all-start = ((bf16[4,96,1536]{2,1,0:T(8,128)(2,1)}), bf16[4,96,1536]{2,1,0:T(8,128)(2,1)S(1)}, u32[]{:S(2)}, u32[]{:S(2)}) async-start(bf16[4,96,1536]{2,1,0:T(8,128)(2,1)} %bitcast.9), calls=%async_computation | async-start | bytes 2359296 | tf_op jit(solution)/shard_map/all_to_all | solution.py:254
  159.9 25.7 %all-to-all-done = bf16[4,96,1536]{2,1,0:T(8,128)(2,1)S(1)} async-done(((bf16[4,96,1536]{2,1,0:T(8,128)(2,1)}), bf16[4,96,1536]{2,1,0:T(8,128)(2,1)S(1)}, u32[]{:S(2)}, u32[]{:S(2)}) %all-to-all-start) | async-done | bytes 1179680 | tf_op jit(solution)/shard_map/all_to_all | solution.py:254
  185.6 1.1 copy.186
  (128 shorter events, 23.8 us)
Async XLA Ops:
  4.1 5.2 %copy-start.2 = (bf16[384,512]{1,0:T(8,128)(2,1)}, bf16[384,512]{1,0:T(8,128)(2,1)S(1)}, u32[]{:S(2)}) copy-start(bf16[384,512]{1,0:T(8,128)(2,1)S(1)} %pad_maximum_fusion.ok_ref.ov_ref) | copy-start | bytes 1179652
  10.0 8.3 %copy-start.7 = (bf16[384,256]{1,0:T(8,128)(2,1)S(1)}, bf16[384,256]{1,0:T(8,128)(2,1)}, u32[]{:S(2)}) copy-start(bf16[384,256]{1,0:T(8,128)(2,1)} %copy-done.6) | copy-start | bytes 589828
  10.0 8.3 %copy-start.9 = (bf16[384,256]{1,0:T(8,128)(2,1)S(1)}, bf16[384,256]{1,0:T(8,128)(2,1)}, u32[]{:S(2)}) copy-start(bf16[384,256]{1,0:T(8,128)(2,1)} %copy-done.8) | copy-start | bytes 589828
  10.0 16.7 %collective-permute-start.1 = (bf16[2,128,512]{2,1,0:T(8,128)(2,1)}, bf16[2,128,512]{2,1,0:T(8,128)(2,1)}, u32[]{:S(2)}, u32[]{:S(2)}) collective-permute-start(bf16[2,128,512]{2,1,0:T(8,128)(2,1)} %bitcast.83), channel_id=1, source_target_pairs={{0,8},{4,12},{8,16},{12,20},{16,24},{20,28},{24,0},{28,4},{1,9},{5... | collective-permute-start | bytes 786440 | tf_op jit(solution)/shard_map/ppermute | solution.py:173
  13.0 1.4 copy-start.5
  13.0 4.8 %copy-start.4 = (bf16[1,2,128,512]{3,0,2,1:T(2,128)(2,1)S(1)}, bf16[1,2,128,512]{3,0,2,1:T(2,128)(2,1)}, u32[]{:S(2)}) copy-start(bf16[1,2,128,512]{3,0,2,1:T(2,128)(2,1)} %get-tuple-element.19) | copy-start | bytes 786436
  14.2 10.9 %collective-permute-start = (bf16[1,128,512]{2,1,0:T(8,128)(2,1)S(1)}, bf16[1,128,512]{2,1,0:T(8,128)(2,1)}, u32[]{:S(2)}, u32[]{:S(2)}) collective-permute-start(bf16[1,128,512]{2,1,0:T(8,128)(2,1)S(1)} %bitcast.105), channel_id=1, source_target_pairs={{0,4},{4,8},{8,12},{12,16},{16,20},{20,24},{24,28},{28,0},{1,5},{5... | collective-permute-start | bytes 393224 | tf_op jit(solution)/shard_map/ppermute | solution.py:173
  15.1 6.4 %copy-start.10 = (bf16[1,1,128,512]{3,0,2,1:T(2,128)(2,1)S(1)}, bf16[1,1,128,512]{3,0,2,1:T(2,128)(2,1)}, u32[]{:S(2)}) copy-start(bf16[1,1,128,512]{3,0,2,1:T(2,128)(2,1)} %get-tuple-element.15) | copy-start | bytes 393220
  15.1 16.0 %collective-permute-start.2 = (bf16[2,128,512]{2,1,0:T(8,128)(2,1)}, bf16[2,128,512]{2,1,0:T(8,128)(2,1)}, u32[]{:S(2)}, u32[]{:S(2)}) collective-permute-start(bf16[2,128,512]{2,1,0:T(8,128)(2,1)} %bitcast.82), channel_id=1, source_target_pairs={{0,12},{4,16},{8,20},{12,24},{16,28},{20,0},{24,4},{28,8},{1,13},{... | collective-permute-start | bytes 786440 | tf_op jit(solution)/shard_map/ppermute | solution.py:173
  17.7 3.9 %copy-start = (s32[8]{0:T(128)S(1)}, s32[8]{0:T(128)}, u32[]{:S(2)}) copy-start(s32[8]{0:T(128)} %constant.178.clone) | copy-start | bytes 100
  17.8 14.3 %collective-permute-start.3 = (bf16[2,128,512]{2,1,0:T(8,128)(2,1)S(1)}, bf16[2,128,512]{2,1,0:T(8,128)(2,1)}, u32[]{:S(2)}, u32[]{:S(2)}) collective-permute-start(bf16[2,128,512]{2,1,0:T(8,128)(2,1)S(1)} %bitcast.100), channel_id=1, source_target_pairs={{0,16},{4,20},{8,24},{12,28},{16,0},{20,4},{24,8},{28,12},{1,17},{... | collective-permute-start | bytes 786440 | tf_op jit(solution)/shard_map/ppermute | solution.py:173
  18.4 7.7 %collective-permute-start.7 = (bf16[256,512]{1,0:T(8,128)(2,1)S(1)}, bf16[256,512]{1,0:T(8,128)(2,1)}, u32[]{:S(2)}, u32[]{:S(2)}) collective-permute-start(bf16[256,512]{1,0:T(8,128)(2,1)S(1)} %fusion.5), channel_id=1, source_target_pairs={{0,4},{1,5},{2,6},{3,7}} | collective-permute-start | bytes 786440 | tf_op jit(solution)/shard_map/ppermute | solution.py:117
  25.1 15.3 %collective-permute-start.4 = (bf16[2,128,512]{2,1,0:T(8,128)(2,1)}, bf16[2,128,512]{2,1,0:T(8,128)(2,1)S(1)}, u32[]{:S(2)}, u32[]{:S(2)}) collective-permute-start(bf16[2,128,512]{2,1,0:T(8,128)(2,1)} %bitcast.80), channel_id=1, source_target_pairs={{0,20},{4,24},{8,28},{12,0},{16,4},{20,8},{24,12},{28,16},{1,21},{... | collective-permute-start | bytes 786440 | tf_op jit(solution)/shard_map/ppermute | solution.py:173
  26.1 14.4 %collective-permute-start.5 = (bf16[2,128,512]{2,1,0:T(8,128)(2,1)S(1)}, bf16[2,128,512]{2,1,0:T(8,128)(2,1)S(1)}, u32[]{:S(2)}, u32[]{:S(2)}) collective-permute-start(bf16[2,128,512]{2,1,0:T(8,128)(2,1)S(1)} %bitcast.101), channel_id=1, source_target_pairs={{0,24},{4,28},{8,0},{12,4},{16,8},{20,12},{24,16},{28,20},{1,25},{... | collective-permute-start | bytes 786440 | tf_op jit(solution)/shard_map/ppermute | solution.py:173
  26.7 12.3 %collective-permute-start.8 = (bf16[256,512]{1,0:T(8,128)(2,1)S(1)}, bf16[256,512]{1,0:T(8,128)(2,1)S(1)}, u32[]{:S(2)}, u32[]{:S(2)}) collective-permute-start(bf16[256,512]{1,0:T(8,128)(2,1)S(1)} %broadcast_select_fusion), channel_id=1, source_target_pairs={{0,8},{4,12},{1,9},{5,13},{2,10},{6,14},{3,11},{7,15}} | collective-permute-start | bytes 786440 | tf_op jit(solution)/shard_map/ppermute | solution.py:117
  31.1 10.6 %collective-permute-start.6 = (bf16[1,128,512]{2,1,0:T(8,128)(2,1)S(1)}, bf16[1,128,512]{2,1,0:T(8,128)(2,1)S(1)}, u32[]{:S(2)}, u32[]{:S(2)}) collective-permute-start(bf16[1,128,512]{2,1,0:T(8,128)(2,1)S(1)} %bitcast.104), channel_id=1, source_target_pairs={{0,28},{4,0},{8,4},{12,8},{16,12},{20,16},{24,20},{28,24},{1,29},{... | collective-permute-start | bytes 393224 | tf_op jit(solution)/shard_map/ppermute | solution.py:173
  39.1 6.1 %collective-permute-start.9 = (bf16[256,512]{1,0:T(8,128)(2,1)S(1)}, bf16[256,512]{1,0:T(8,128)(2,1)S(1)}, u32[]{:S(2)}, u32[]{:S(2)}) collective-permute-start(bf16[256,512]{1,0:T(8,128)(2,1)S(1)} %broadcast_select_fusion.1), channel_id=1, source_target_pairs={{0,16},{4,20},{8,24},{12,28},{1,17},{5,21},{9,25},{13,29},{2,18},{... | collective-permute-start | bytes 786440 | tf_op jit(solution)/shard_map/ppermute | solution.py:117
  41.7 4.3 %copy-start.3 = (bf16[12,128,512]{2,1,0:T(8,128)(2,1)}, bf16[12,128,512]{2,1,0:T(8,128)(2,1)S(1)}, u32[]{:S(2)}) copy-start(bf16[12,128,512]{2,1,0:T(8,128)(2,1)S(1)} %constant_dynamic-update-slice_fusion) | copy-start | bytes 4718596
  75.8 13.2 %collective-permute-start.17 = (bf16[256,512]{1,0:T(8,128)(2,1)S(1)}, bf16[256,512]{1,0:T(8,128)(2,1)S(1)}, u32[]{:S(2)}, u32[]{:S(2)}) collective-permute-start(bf16[256,512]{1,0:T(8,128)(2,1)S(1)} %convert_element_type.37), channel_id=1, source_target_pairs={{16,0},{20,4},{24,8},{28,12},{17,1},{21,5},{25,9},{29,13},{18,2},{... | collective-permute-start | bytes 786440 | tf_op jit(solution)/shard_map/ppermute | solution.py:131
  78.7 10.8 %copy-start.1 = (f32[256,512]{1,0:T(8,128)S(1)}, f32[256,512]{1,0:T(8,128)}, u32[]{:S(2)}) copy-start(f32[256,512]{1,0:T(8,128)} %get-tuple-element.10) | copy-start | bytes 1572868
  79.0 24.2 %collective-permute-start.11 = (bf16[2,128,512]{2,0,1:T(2,128)(2,1)S(1)}, bf16[2,128,512]{2,0,1:T(2,128)(2,1)S(1)}, u32[]{:S(2)}, u32[]{:S(2)}) collective-permute-start(bf16[2,128,512]{2,0,1:T(2,128)(2,1)S(1)} %copy.163), channel_id=1, source_target_pairs={{0,24},{4,28},{8,0},{12,4},{16,8},{20,12},{24,16},{28,20},{1,25},{... | collective-permute-start | bytes 786440 | tf_op jit(solution)/shard_map/ppermute | solution.py:245
  85.1 21.4 %collective-permute-start.12 = (bf16[2,128,512]{2,0,1:T(2,128)(2,1)S(1)}, bf16[2,128,512]{2,0,1:T(2,128)(2,1)}, u32[]{:S(2)}, u32[]{:S(2)}) collective-permute-start(bf16[2,128,512]{2,0,1:T(2,128)(2,1)S(1)} %copy.164), channel_id=1, source_target_pairs={{0,20},{4,24},{8,28},{12,0},{16,4},{20,8},{24,12},{28,16},{1,21},{... | collective-permute-start | bytes 786440 | tf_op jit(solution)/shard_map/ppermute | solution.py:245
  85.9 20.7 %collective-permute-start.13 = (bf16[2,128,512]{2,0,1:T(2,128)(2,1)S(1)}, bf16[2,128,512]{2,0,1:T(2,128)(2,1)}, u32[]{:S(2)}, u32[]{:S(2)}) collective-permute-start(bf16[2,128,512]{2,0,1:T(2,128)(2,1)S(1)} %copy.165), channel_id=1, source_target_pairs={{0,16},{4,20},{8,24},{12,28},{16,0},{20,4},{24,8},{28,12},{1,17},{... | collective-permute-start | bytes 786440 | tf_op jit(solution)/shard_map/ppermute | solution.py:245
  88.9 4.2 %collective-permute-start.10 = (bf16[1,128,512]{2,1,0:T(8,128)(2,1)S(1)}, bf16[1,128,512]{2,1,0:T(8,128)(2,1)S(1)}, u32[]{:S(2)}, u32[]{:S(2)}) collective-permute-start(bf16[1,128,512]{2,1,0:T(8,128)(2,1)S(1)} %get-tuple-element.23), channel_id=1, source_target_pairs={{0,28},{4,0},{8,4},{12,8},{16,12},{20,16},{24,20},{28,24},{1,29},{... | collective-permute-start | bytes 393224 | tf_op jit(solution)/shard_map/ppermute | solution.py:245
  89.1 12.6 %collective-permute-start.16 = (bf16[1,128,512]{2,1,0:T(8,128)(2,1)S(1)}, bf16[1,128,512]{2,1,0:T(8,128)(2,1)S(1)}, u32[]{:S(2)}, u32[]{:S(2)}) collective-permute-start(bf16[1,128,512]{2,1,0:T(8,128)(2,1)S(1)} %get-tuple-element.22), channel_id=1, source_target_pairs={{0,4},{4,8},{8,12},{12,16},{16,20},{20,24},{24,28},{28,0},{1,5},{5... | collective-permute-start | bytes 393224 | tf_op jit(solution)/shard_map/ppermute | solution.py:245
  93.1 19.8 %collective-permute-start.14 = (bf16[2,128,512]{2,0,1:T(2,128)(2,1)S(1)}, bf16[2,128,512]{2,0,1:T(2,128)(2,1)}, u32[]{:S(2)}, u32[]{:S(2)}) collective-permute-start(bf16[2,128,512]{2,0,1:T(2,128)(2,1)S(1)} %copy.166), channel_id=1, source_target_pairs={{0,12},{4,16},{8,20},{12,24},{16,28},{20,0},{24,4},{28,8},{1,13},{... | collective-permute-start | bytes 786440 | tf_op jit(solution)/shard_map/ppermute | solution.py:245
  101.7 11.2 %collective-permute-start.15 = (bf16[2,128,512]{2,0,1:T(2,128)(2,1)S(1)}, bf16[2,128,512]{2,0,1:T(2,128)(2,1)}, u32[]{:S(2)}, u32[]{:S(2)}) collective-permute-start(bf16[2,128,512]{2,0,1:T(2,128)(2,1)S(1)} %copy.167), channel_id=1, source_target_pairs={{0,8},{4,12},{8,16},{12,20},{16,24},{20,28},{24,0},{28,4},{1,9},{5... | collective-permute-start | bytes 786440 | tf_op jit(solution)/shard_map/ppermute | solution.py:245
  103.2 9.6 %copy-start.12 = (bf16[2,128,512]{2,0,1:T(2,128)(2,1)}, bf16[2,128,512]{2,0,1:T(2,128)(2,1)S(1)}, u32[]{:S(2)}) copy-start(bf16[2,128,512]{2,0,1:T(2,128)(2,1)S(1)} %collective-permute-done.11) | copy-start | bytes 786436
  103.2 30.5 %collective-permute-start.18 = (bf16[256,512]{1,0:T(8,128)(2,1)}, bf16[256,512]{1,0:T(8,128)(2,1)S(1)}, u32[]{:S(2)}, u32[]{:S(2)}) collective-permute-start(bf16[256,512]{1,0:T(8,128)(2,1)} %fusion.4), channel_id=1, source_target_pairs={{8,0},{12,4},{9,1},{13,5},{10,2},{14,6},{11,3},{15,7}} | collective-permute-start | bytes 786440 | tf_op jit(solution)/shard_map/ppermute | solution.py:131
  133.8 3.4 %collective-permute-start.19 = (bf16[256,512]{1,0:T(8,128)(2,1)S(1)}, bf16[256,512]{1,0:T(8,128)(2,1)S(1)}, u32[]{:S(2)}, u32[]{:S(2)}) collective-permute-start(bf16[256,512]{1,0:T(8,128)(2,1)S(1)} %fusion.6), channel_id=1, source_target_pairs={{4,0},{5,1},{6,2},{7,3}} | collective-permute-start | bytes 786440 | tf_op jit(solution)/shard_map/ppermute | solution.py:131
  135.6 1.8 copy-start.11
  153.7 31.8 %all-to-all-start = ((bf16[4,96,1536]{2,1,0:T(8,128)(2,1)}), bf16[4,96,1536]{2,1,0:T(8,128)(2,1)S(1)}, u32[]{:S(2)}, u32[]{:S(2)}) async-start(bf16[4,96,1536]{2,1,0:T(8,128)(2,1)} %bitcast.9), calls=%async_computation | async-start | bytes 2359296 | tf_op jit(solution)/shard_map/all_to_all | solution.py:254
  (3 other events, 2.0 us)

commit v3 on v2

--- a/solution.py
+++ b/solution.py
@@ -132,10 +132,49 @@
     return x
 
 
+def combine_kernel(tb_ref, *refs, caps, far_count):
+    parts = refs[:len(caps)]
+    loc_ref, hs_ref, out_ref, acc = refs[len(caps):]
+    acc[...] = loc_ref[...]
+
+    @pl.when(tb_ref[far_count] == 1)
+    def _():
+        acc[0:hs_ref.shape[0], :] += hs_ref[...]
+
+    k = 0
+    for part, cap in zip(parts, caps):
+        for p in range(cap):
+            t = tb_ref[k]
+
+            @pl.when(t >= 0)
+            def _():
+                row = pl.multiple_of(t * BLK, BLK)
+                acc[pl.ds(row, BLK), :] += part[p * BLK:(p + 1) * BLK, :].astype(jnp.float32)
+
+            k += 1
+    out_ref[...] = acc[...].astype(out_ref.dtype)
+
+
+def lane_transpose(x, lane, lanes):
+    rows = x.shape[0] // lanes
+    cols = x.shape[1]
+    chunks = x.reshape(lanes, rows, cols)
+    out = jnp.zeros((rows, lanes * cols), x.dtype)
+    own = lax.dynamic_index_in_dim(chunks, lane, 0, keepdims=False)
+    out = lax.dynamic_update_slice(out, own, (0, lane * cols))
+    for e in range(1, lanes):
+        send = lax.dynamic_index_in_dim(chunks, (lane + e) % lanes, 0, keepdims=False)
+        pairs = [(i, (i + e) % lanes) for i in range(lanes)]
+        got = lax.ppermute(send, "uly", pairs)
+        out = lax.dynamic_update_slice(out, got, (0, ((lane - e) % lanes) * cols))
+    return out
+
+
 def shards(query_rows, key_rows, value_rows, out_grad, block_list):
     shard_index = lax.axis_index("ctx")
     lane_index = lax.axis_index("uly")
     shard_count = lax.axis_size("ctx")
+    lane_count_all = lax.axis_size("uly")
     nb = key_rows.shape[0] // BLK
     heads_here = query_rows.shape[1] // HD
     kv_here = max(1, heads_here // GROUP)
@@ -151,29 +190,24 @@
     kv_own = jnp.concatenate([key_own, value_own], axis=1)
 
     owners, inside, places = remote_plan(block_list, shard_count, nb)
-    from_here = owners == shard_index
-    send_pick = (
-        from_here[:, :, None] & (places[:, :, None] == jnp.arange(capacity)[None, None, :])
-    ).astype(jnp.bfloat16)
-    send_block = (inside[:, :, None] == jnp.arange(nb)[None, None, :]).astype(jnp.bfloat16)
-    selector = jnp.einsum(
-        "ric,rib->rcb", send_pick, send_block, preferred_element_type=jnp.float32
-    ).astype(jnp.bfloat16)
-    send = jnp.einsum(
-        "rcb,btx->rctx", selector, kv_own.reshape(nb, BLK, width),
-        preferred_element_type=jnp.float32,
-    ).astype(jnp.bfloat16)
+    match = (owners == shard_index)[:, :, None] & (
+        places[:, :, None] == jnp.arange(capacity)[None, None, :]
+    )
+    pick = jnp.sum(jnp.where(match, inside[:, :, None], 0), axis=1)
+    valid = jnp.any(match, axis=1)
+    kv_blocks = kv_own.reshape(nb, BLK, width)
     got_parts = []
-    sel_parts = []
+    back_targets = []
     for d in range(1, shard_count):
         cap_d = shift_caps[d - 1]
         peer = (shard_index + d) % shard_count
-        payload = lax.dynamic_index_in_dim(send, peer, 0, keepdims=False)[:cap_d]
+        pick_d = lax.dynamic_index_in_dim(pick, peer, 0, keepdims=False)[:cap_d]
+        valid_d = lax.dynamic_index_in_dim(valid, peer, 0, keepdims=False)[:cap_d]
+        payload = jnp.take(kv_blocks, pick_d, axis=0, mode="clip")
         pairs = [(i, (i + d) % shard_count) for i in range(shard_count)]
         got_parts.append(lax.ppermute(payload, "ctx", pairs))
-        sel_parts.append(lax.dynamic_index_in_dim(selector, peer, 0, keepdims=False)[:cap_d])
+        back_targets.append(jnp.where(valid_d, pick_d, -1))
     got = jnp.concatenate(got_parts, axis=0).reshape(far_count * BLK, width)
-    back_sel = jnp.concatenate(sel_parts, axis=0)
     is_root = shard_index == 0
     heads = tree_broadcast(kv_own[0:2 * BLK], shard_index, shard_count)
 
@@ -237,22 +271,25 @@
         compiler_params=pltpu.CompilerParams(dimension_semantics=("arbitrary", "arbitrary")),
     )(kind, index, query_rows, out_grad, kv_own, kv_own, got, got, heads, heads)
 
-    back = back.reshape(far_count, BLK, width)
     ret_parts = []
     for d in range(1, shard_count):
-        lo = shift_offsets[d - 1]
+        lo = shift_offsets[d - 1] * BLK
         pairs = [(i, (i - d) % shard_count) for i in range(shard_count)]
-        ret_parts.append(lax.ppermute(back[lo:lo + shift_caps[d - 1]], "ctx", pairs))
-    ret = jnp.concatenate(ret_parts, axis=0)
+        ret_parts.append(lax.ppermute(back[lo:lo + shift_caps[d - 1] * BLK], "ctx", pairs))
     head_sum = tree_reduce(gsum, shard_count)
-    added = jnp.einsum(
-        "kb,ktx->btx", back_sel, ret, preferred_element_type=jnp.float32,
-    ).reshape(nb * BLK, width)
-    root_part = jnp.where(is_root, jnp.pad(head_sum, ((0, (nb - 2) * BLK), (0, 0))), 0.0)
-    kv_grad = (loc + added + root_part).astype(jnp.bfloat16)
-
-    query_out = lax.all_to_all(dq, "uly", split_axis=0, concat_axis=1, tiled=True)
-    kv_seq = lax.all_to_all(kv_grad, "uly", split_axis=0, concat_axis=1, tiled=True)
+    targets = jnp.concatenate(back_targets + [is_root.astype(jnp.int32)[None]]).astype(jnp.int32)
+    part_count = len(ret_parts)
+    kv_grad = pl.pallas_call(
+        functools.partial(combine_kernel, caps=tuple(shift_caps), far_count=far_count),
+        out_shape=jax.ShapeDtypeStruct((nb * BLK, width), jnp.bfloat16),
+        in_specs=[pl.BlockSpec(memory_space=pltpu.SMEM)]
+        + [pl.BlockSpec(memory_space=pltpu.VMEM)] * (part_count + 2),
+        out_specs=pl.BlockSpec(memory_space=pltpu.VMEM),
+        scratch_shapes=[pltpu.VMEM((nb * BLK, width), jnp.float32)],
+    )(targets, *ret_parts, loc, head_sum)
+
+    query_out = lane_transpose(dq, lane_index, lane_count_all)
+    kv_seq = lane_transpose(kv_grad, lane_index, lane_count_all)
     rows_here = kv_seq.shape[0]
     lane_count = kv_seq.shape[1] // width
     spread = kv_seq.reshape(rows_here, lane_count, 2, kv_here * HD)

time: 189 us -> 157 us (0.83); the launches traced: 187 us -> 157 us
  local copies, waits for them, and re-layouts: 48 us -> 22.8 us
  blocking collectives: 16.1 us -> 0 us
  waiting for transfers between devices: 48.2 us -> 59.4 us
  starting transfers between devices: 38.5 us -> 35.4 us
  Pallas kernels: 28.8 us -> 31.7 us
    ppermute x7 -> x13, waiting for transfers between devices: 10.4 us -> 43.3 us  [the longest x6 23.5 us: lane_transpose(): got = lax.ppermute(send, 'uly', pairs)]
    all_to_all x1 -> x0, waiting for transfers between devices: 25.7 us -> none  [shards(): lax.all_to_all(dq, 'uly', split_axis=0, concat_axis=1, tiled=True)]
    concatenate x2 -> x1, local copies, waits for them, and re-layouts: 21 us -> 0.65 us  [shards(): jnp.concatenate(back_targets + [is_root.astype(jnp.int32)[None]])]
    all_to_all x1 -> x0, blocking collectives: 16.1 us -> none  [shards(): lax.all_to_all(kv_grad, 'uly', split_axis=0, concat_axis=1, tiled=True)]
    unnamed x46 -> x35, local copies, waits for them, and re-layouts: 10 us -> 4.98 us
    gather x0 -> x6, local copies, waits for them, and re-layouts: none -> 4.84 us  [shards(): payload = jnp.take(kv_blocks, pick_d, axis=0, mode='clip')]
    dynamic_slice x2 -> x1, local copies, waits for them, and re-layouts: 3.82 us -> 0.07 us  [shards(): valid_d = lax.dynamic_index_in_dim(valid, peer, 0, keepdims=False)[:cap_d]]
    ppermute x3, waiting for transfers between devices: 1.43 us -> 5.18 us  [tree_reduce(): lax.ppermute(x.astype(jnp.bfloat16), 'ctx', pairs).astype(jnp.float32)]
  transfers between devices with their start and end apart: 21 -> 26, of which waited for: 8 -> 13; matrix products, arithmetic and copies ran while one was open for 22% -> 9% of each run, Pallas kernels for 0% -> 0%
where the time goes in v3:
time: 157 us
  waiting for transfers between devices  59.4 us (38%)
  starting transfers between devices  35.4 us (23%)
  Pallas kernels  31.7 us (20%)
  local copies, waits for them, and re-layouts  22.8 us (15%)
  other arithmetic  4.48 us (3%)
  between operations  2.88 us (2%)
    pallas_call x1, Pallas kernels, shards(): pl.pallas_call(kernel, grid_spec=grid_spec, out_shape=[jax.ShapeDtypeStru...  28.8 us
    ppermute x6, waiting for transfers between devices, lane_transpose(): got = lax.ppermute(send, 'uly', pairs)  23.5 us
    ppermute x7, waiting for transfers between devices, shards(): lax.ppermute(back[lo:lo + shift_caps[d - 1] * BLK], 'ctx', pairs)  19.8 us
    ppermute x6, starting transfers between devices, lane_transpose(): got = lax.ppermute(send, 'uly', pairs)  10.9 us
    ppermute x3, waiting for transfers between devices, tree_broadcast(): got = lax.ppermute(x, 'ctx', pairs)  9.43 us
    ppermute x7, starting transfers between devices, shards(): lax.ppermute(back[lo:lo + shift_caps[d - 1] * BLK], 'ctx', pairs)  7.25 us
    ppermute x7, starting transfers between devices, shards(): got_parts.append(lax.ppermute(payload, 'ctx', pairs))  7.01 us
    ppermute x3, starting transfers between devices, tree_broadcast(): got = lax.ppermute(x, 'ctx', pairs)  6.37 us
  transfers between devices with their start and end apart: 26, of which 13 were waited for; matrix products, arithmetic and copies ran while one was open for 9% of the time, Pallas kernels for 0%

profile of v3, /device:TPU:0, one launch (start us, length us, event | category | flops | bytes accessed | tf_op | source)
XLA Modules:
  0.0 156.7 jit_solution(15826687517122206697)
XLA Ops:
  5.3 2.0 %constant_dynamic-slice_fusion = (bf16[1,128,512]{2,1,0:T(8,128)(2,1)}, bf16[1,128,512]{2,1,0:T(8,128)(2,1)S(1)}) fusion(bf16[3,128,512]{2,1,0:T(8,128)(2,1)S(1)} %bitcast.41, s32[]{:T(128)} %bitcast.7, s32[]{:T(128)} %bitcast.6), kind=kLoop, calls=%fused_computation.37 | loop fusion | bytes 524296 | tf_op jit(solution)/shard_map/jit(_take)/gather | solution.py:206
  8.3 2.5 %collective-permute-start.1 = (bf16[2,128,512]{2,1,0:T(8,128)(2,1)S(1)}, bf16[2,128,512]{2,1,0:T(8,128)(2,1)}, u32[]{:S(2)}, u32[]{:S(2)}) collective-permute-start(bf16[2,128,512]{2,1,0:T(8,128)(2,1)S(1)} %gather_fusion.2), channel_id=1, source_target_pairs={{0,8},{4,12},{8,16},{12,20},{16,24},{20,28},{24,0},{28,4},{1,9},{5... | collective-permute-start | bytes 786440 | tf_op jit(solution)/shard_map/ppermute | solution.py:208
  11.5 2.5 %collective-permute-start.2 = (bf16[2,128,512]{2,1,0:T(8,128)(2,1)S(1)}, bf16[2,128,512]{2,1,0:T(8,128)(2,1)S(1)}, u32[]{:S(2)}, u32[]{:S(2)}) collective-permute-start(bf16[2,128,512]{2,1,0:T(8,128)(2,1)S(1)} %gather_fusion.3), channel_id=1, source_target_pairs={{0,12},{4,16},{8,20},{12,24},{16,28},{20,0},{24,4},{28,8},{1,13},{... | collective-permute-start | bytes 786440 | tf_op jit(solution)/shard_map/ppermute | solution.py:208
  15.1 2.0 %collective-permute-start.7 = (bf16[256,512]{1,0:T(8,128)(2,1)S(1)}, bf16[256,512]{1,0:T(8,128)(2,1)}, u32[]{:S(2)}, u32[]{:S(2)}) collective-permute-start(bf16[256,512]{1,0:T(8,128)(2,1)S(1)} %fusion.1), channel_id=1, source_target_pairs={{0,4},{1,5},{2,6},{3,7}} | collective-permute-start | bytes 786440 | tf_op jit(solution)/shard_map/ppermute | solution.py:117
  24.8 3.1 %collective-permute-start.8 = (bf16[256,512]{1,0:T(8,128)(2,1)S(1)}, bf16[256,512]{1,0:T(8,128)(2,1)S(1)}, u32[]{:S(2)}, u32[]{:S(2)}) collective-permute-start(bf16[256,512]{1,0:T(8,128)(2,1)S(1)} %broadcast_select_fusion), channel_id=1, source_target_pairs={{0,8},{4,12},{1,9},{5,13},{2,10},{6,14},{3,11},{7,15}} | collective-permute-start | bytes 786440 | tf_op jit(solution)/shard_map/ppermute | solution.py:117
  29.9 7.2 %collective-permute-done.8 = bf16[256,512]{1,0:T(8,128)(2,1)S(1)} collective-permute-done((bf16[256,512]{1,0:T(8,128)(2,1)S(1)}, bf16[256,512]{1,0:T(8,128)(2,1)S(1)}, u32[]{:S(2)}, u32[]{:S(2)}) %collective-permute-start.8) | collective-permute-done | bytes 262176 | tf_op jit(solution)/shard_map/ppermute | solution.py:117
  37.1 1.3 collective-permute-start.9
  38.5 1.5 collective-permute-done.6
  40.0 2.3 %collective-permute-done.9 = bf16[256,512]{1,0:T(8,128)(2,1)S(1)} collective-permute-done((bf16[256,512]{1,0:T(8,128)(2,1)S(1)}, bf16[256,512]{1,0:T(8,128)(2,1)S(1)}, u32[]{:S(2)}, u32[]{:S(2)}) %collective-permute-start.9) | collective-permute-done | bytes 262176 | tf_op jit(solution)/shard_map/ppermute | solution.py:117
  43.0 28.8 %shard_map.85 = (bf16[384,1536]{1,0:T(8,128)(2,1)}, f32[384,512]{1,0:T(8,128)}, bf16[1536,512]{1,0:T(8,128)(2,1)}, f32[256,512]{1,0:T(8,128)}) custom-call(s32[24]{0:T(128)} %reshape.516.kind_ref, s32[24]{0:T(128)} %reshape.519.idx_ref, bf16[384,1536]{1,0:T(8,128)(2,1)} %q_ref.1, bf16[384,1536]{1,0:T(8,128)(2,1)} %do_ref.1, bf16[384,512]{1,0:T(8,128)(2,1)} %copy-done.1, ...), custom_call_target="tpu_custom_call" | custom-call | tf_op jit(solution)/shard_map/pallas_call | solution.py:262
  71.8 1.1 convert_element_type.23
  72.9 1.3 collective-permute-start.20
  74.2 1.4 fusion.33
  76.7 4.9 %collective-permute-start.14 = (bf16[256,512]{1,0:T(8,128)(2,1)S(1)}, bf16[256,512]{1,0:T(8,128)(2,1)S(1)}, u32[]{:S(2)}, u32[]{:S(2)}) collective-permute-start(bf16[256,512]{1,0:T(8,128)(2,1)S(1)} %get-tuple-element.55), channel_id=1, source_target_pairs={{0,24},{4,28},{8,0},{12,4},{16,8},{20,12},{24,16},{28,20},{1,25},{... | collective-permute-start | bytes 786440 | tf_op jit(solution)/shard_map/ppermute | solution.py:278
  81.6 1.4 collective-permute-start.15
  83.8 1.6 %collective-permute-start.10 = (bf16[96,1536]{1,0:T(8,128)(2,1)S(1)}, bf16[96,1536]{1,0:T(8,128)(2,1)S(1)}, u32[]{:S(2)}, u32[]{:S(2)}) collective-permute-start(bf16[96,1536]{1,0:T(8,128)(2,1)S(1)} %get-tuple-element.58), channel_id=1, source_target_pairs={{0,1},{1,2},{2,3},{3,0},{4,5},{5,6},{6,7},{7,4},{8,9},{9,10},{10,1... | collective-permute-start | bytes 884744 | tf_op jit(solution)/shard_map/ppermute | solution.py:168
  85.5 1.3 collective-permute-start.21
  86.9 7.7 %collective-permute-done.10 = bf16[96,1536]{1,0:T(8,128)(2,1)S(1)} collective-permute-done((bf16[96,1536]{1,0:T(8,128)(2,1)S(1)}, bf16[96,1536]{1,0:T(8,128)(2,1)S(1)}, u32[]{:S(2)}, u32[]{:S(2)}) %collective-permute-start.10) | collective-permute-done | bytes 294944 | tf_op jit(solution)/shard_map/ppermute | solution.py:168
  95.3 5.2 %collective-permute-done.21 = bf16[256,512]{1,0:T(8,128)(2,1)S(1)} collective-permute-done((bf16[256,512]{1,0:T(8,128)(2,1)S(1)}, bf16[256,512]{1,0:T(8,128)(2,1)S(1)}, u32[]{:S(2)}, u32[]{:S(2)}) %collective-permute-start.21) | collective-permute-done | bytes 262176 | tf_op jit(solution)/shard_map/ppermute | solution.py:131
  100.5 3.0 %collective-permute-start.12 = (bf16[96,1536]{1,0:T(8,128)(2,1)S(1)}, bf16[96,1536]{1,0:T(8,128)(2,1)S(1)}, u32[]{:S(2)}, u32[]{:S(2)}) collective-permute-start(bf16[96,1536]{1,0:T(8,128)(2,1)S(1)} %get-tuple-element.56), channel_id=1, source_target_pairs={{0,3},{1,0},{2,1},{3,2},{4,7},{5,4},{6,5},{7,6},{8,11},{9,8},{10,9... | collective-permute-start | bytes 884744 | tf_op jit(solution)/shard_map/ppermute | solution.py:168
  103.6 5.5 %collective-permute-done.11 = bf16[96,1536]{1,0:T(8,128)(2,1)S(1)} collective-permute-done((bf16[96,1536]{1,0:T(8,128)(2,1)S(1)}, bf16[96,1536]{1,0:T(8,128)(2,1)S(1)}, u32[]{:S(2)}, u32[]{:S(2)}) %collective-permute-start.11) | collective-permute-done | bytes 294944 | tf_op jit(solution)/shard_map/ppermute | solution.py:168
  109.2 1.3 collective-permute-start.22
  110.5 4.8 %collective-permute-done.12 = bf16[96,1536]{1,0:T(8,128)(2,1)S(1)} collective-permute-done((bf16[96,1536]{1,0:T(8,128)(2,1)S(1)}, bf16[96,1536]{1,0:T(8,128)(2,1)S(1)}, u32[]{:S(2)}, u32[]{:S(2)}) %collective-permute-start.12) | collective-permute-done | bytes 294944 | tf_op jit(solution)/shard_map/ppermute | solution.py:168
  115.5 5.1 %collective-permute-done.19.refs_6_ = bf16[128,512]{1,0:T(8,128)(2,1)S(1)} collective-permute-done((bf16[128,512]{1,0:T(8,128)(2,1)S(1)}, bf16[128,512]{1,0:T(8,128)(2,1)S(1)}, u32[]{:S(2)}, u32[]{:S(2)}) %collective-permute-start.19) | collective-permute-done | bytes 131104 | tf_op jit(solution)/shard_map/ppermute | solution.py:278
  121.7 12.8 %collective-permute-done.16.refs_3_ = bf16[256,512]{1,0:T(8,128)(2,1)S(1)} collective-permute-done((bf16[256,512]{1,0:T(8,128)(2,1)S(1)}, bf16[256,512]{1,0:T(8,128)(2,1)S(1)}, u32[]{:S(2)}, u32[]{:S(2)}) %collective-permute-start.16) | collective-permute-done | bytes 262176 | tf_op jit(solution)/shard_map/ppermute | solution.py:278
  134.5 1.8 %collective-permute-done.17.refs_4_ = bf16[256,512]{1,0:T(8,128)(2,1)S(1)} collective-permute-done((bf16[256,512]{1,0:T(8,128)(2,1)S(1)}, bf16[256,512]{1,0:T(8,128)(2,1)S(1)}, u32[]{:S(2)}, u32[]{:S(2)}) %collective-permute-start.17) | collective-permute-done | bytes 262176 | tf_op jit(solution)/shard_map/ppermute | solution.py:278
  137.1 3.0 %shard_map.86 = bf16[384,512]{1,0:T(8,128)(2,1)} custom-call(s32[13]{0:T(128)} %concatenate.52.tb_ref, bf16[128,512]{1,0:T(8,128)(2,1)} %copy-done.11, bf16[256,512]{1,0:T(8,128)(2,1)} %copy-done.6, bf16[256,512]{1,0:T(8,128)(2,1)} %copy-done.7, bf16[256,512]{1,0:T(8,128)(2,1)} %copy-done.8, bf16[256,512]{1,0:T(8,128)(2,1)} %copy-done.9, ...), custom_call_target="tpu_custom_call" | custom-call | tf_op jit(solution)/shard_map/pallas_call | solution.py:282
  141.1 2.2 %collective-permute-start.23 = (bf16[96,512]{1,0:T(8,128)(2,1)S(1)}, bf16[96,512]{1,0:T(8,128)(2,1)S(1)}, u32[]{:S(2)}, u32[]{:S(2)}) collective-permute-start(bf16[96,512]{1,0:T(8,128)(2,1)S(1)} %get-tuple-element.61), channel_id=1, source_target_pairs={{0,1},{1,2},{2,3},{3,0},{4,5},{5,6},{6,7},{7,4},{8,9},{9,10},{10,1... | collective-permute-start | bytes 294920 | tf_op jit(solution)/shard_map/ppermute | solution.py:168
  143.4 3.4 %collective-permute-start.24 = (bf16[96,512]{1,0:T(8,128)(2,1)S(1)}, bf16[96,512]{1,0:T(8,128)(2,1)S(1)}, u32[]{:S(2)}, u32[]{:S(2)}) collective-permute-start(bf16[96,512]{1,0:T(8,128)(2,1)S(1)} %get-tuple-element.60), channel_id=1, source_target_pairs={{0,2},{1,3},{2,0},{3,1},{4,6},{5,7},{6,4},{7,5},{8,10},{9,11},{10,... | collective-permute-start | bytes 294920 | tf_op jit(solution)/shard_map/ppermute | solution.py:168
  147.7 2.3 %collective-permute-done.23 = bf16[96,512]{1,0:T(8,128)(2,1)S(1)} collective-permute-done((bf16[96,512]{1,0:T(8,128)(2,1)S(1)}, bf16[96,512]{1,0:T(8,128)(2,1)S(1)}, u32[]{:S(2)}, u32[]{:S(2)}) %collective-permute-start.23) | collective-permute-done | bytes 98336 | tf_op jit(solution)/shard_map/ppermute | solution.py:168
  150.0 2.9 %collective-permute-done.24 = bf16[96,512]{1,0:T(8,128)(2,1)S(1)} collective-permute-done((bf16[96,512]{1,0:T(8,128)(2,1)S(1)}, bf16[96,512]{1,0:T(8,128)(2,1)S(1)}, u32[]{:S(2)}, u32[]{:S(2)}) %collective-permute-start.24) | collective-permute-done | bytes 98336 | tf_op jit(solution)/shard_map/ppermute | solution.py:168
  153.5 1.8 %slice_reduce_fusion = (bf16[96,4,256]{2,1,0:T(4,128)(2,1)S(1)}, bf16[96,4,256]{2,1,0:T(4,128)(2,1)S(1)}) fusion(bf16[96,4,2,256]{3,2,1,0:T(2,128)(2,1)S(1)} %reshape.524), kind=kLoop, calls=%fused_computation.13 | loop fusion | bytes 786432 | tf_op jit(solution)/shard_map/slice | solution.py:304
  (131 shorter events, 25.0 us)
Async XLA Ops:
  5.3 14.6 %copy-start.1 = (bf16[384,512]{1,0:T(8,128)(2,1)}, bf16[384,512]{1,0:T(8,128)(2,1)S(1)}, u32[]{:S(2)}) copy-start(bf16[384,512]{1,0:T(8,128)(2,1)S(1)} %pad_maximum_fusion.ok_ref.ov_ref) | copy-start | bytes 1179652
  7.3 16.5 %collective-permute-start = (bf16[1,128,512]{2,1,0:T(8,128)(2,1)S(1)}, bf16[1,128,512]{2,1,0:T(8,128)(2,1)S(1)}, u32[]{:S(2)}, u32[]{:S(2)}) collective-permute-start(bf16[1,128,512]{2,1,0:T(8,128)(2,1)S(1)} %get-tuple-element.63), channel_id=1, source_target_pairs={{0,4},{4,8},{8,12},{12,16},{16,20},{20,24},{24,28},{28,0},{1,5},{5... | collective-permute-start | bytes 393224 | tf_op jit(solution)/shard_map/ppermute | solution.py:208
  8.3 16.4 %collective-permute-start.1 = (bf16[2,128,512]{2,1,0:T(8,128)(2,1)S(1)}, bf16[2,128,512]{2,1,0:T(8,128)(2,1)}, u32[]{:S(2)}, u32[]{:S(2)}) collective-permute-start(bf16[2,128,512]{2,1,0:T(8,128)(2,1)S(1)} %gather_fusion.2), channel_id=1, source_target_pairs={{0,8},{4,12},{8,16},{12,20},{16,24},{20,28},{24,0},{28,4},{1,9},{5... | collective-permute-start | bytes 786440 | tf_op jit(solution)/shard_map/ppermute | solution.py:208
  11.5 17.4 %collective-permute-start.2 = (bf16[2,128,512]{2,1,0:T(8,128)(2,1)S(1)}, bf16[2,128,512]{2,1,0:T(8,128)(2,1)S(1)}, u32[]{:S(2)}, u32[]{:S(2)}) collective-permute-start(bf16[2,128,512]{2,1,0:T(8,128)(2,1)S(1)} %gather_fusion.3), channel_id=1, source_target_pairs={{0,12},{4,16},{8,20},{12,24},{16,28},{20,0},{24,4},{28,8},{1,13},{... | collective-permute-start | bytes 786440 | tf_op jit(solution)/shard_map/ppermute | solution.py:208
  14.5 14.4 %collective-permute-start.3 = (bf16[2,128,512]{2,1,0:T(8,128)(2,1)S(1)}, bf16[2,128,512]{2,1,0:T(8,128)(2,1)}, u32[]{:S(2)}, u32[]{:S(2)}) collective-permute-start(bf16[2,128,512]{2,1,0:T(8,128)(2,1)S(1)} %gather_fusion.4), channel_id=1, source_target_pairs={{0,16},{4,20},{8,24},{12,28},{16,0},{20,4},{24,8},{28,12},{1,17},{... | collective-permute-start | bytes 786440 | tf_op jit(solution)/shard_map/ppermute | solution.py:208
  15.1 8.7 %collective-permute-start.7 = (bf16[256,512]{1,0:T(8,128)(2,1)S(1)}, bf16[256,512]{1,0:T(8,128)(2,1)}, u32[]{:S(2)}, u32[]{:S(2)}) collective-permute-start(bf16[256,512]{1,0:T(8,128)(2,1)S(1)} %fusion.1), channel_id=1, source_target_pairs={{0,4},{1,5},{2,6},{3,7}} | collective-permute-start | bytes 786440 | tf_op jit(solution)/shard_map/ppermute | solution.py:117
  23.8 14.6 %collective-permute-start.4 = (bf16[2,128,512]{2,1,0:T(8,128)(2,1)S(1)}, bf16[2,128,512]{2,1,0:T(8,128)(2,1)S(1)}, u32[]{:S(2)}, u32[]{:S(2)}) collective-permute-start(bf16[2,128,512]{2,1,0:T(8,128)(2,1)S(1)} %gather_fusion.5), channel_id=1, source_target_pairs={{0,20},{4,24},{8,28},{12,0},{16,4},{20,8},{24,12},{28,16},{1,21},{... | collective-permute-start | bytes 786440 | tf_op jit(solution)/shard_map/ppermute | solution.py:208
  23.8 14.7 %collective-permute-start.5 = (bf16[2,128,512]{2,1,0:T(8,128)(2,1)S(1)}, bf16[2,128,512]{2,1,0:T(8,128)(2,1)S(1)}, u32[]{:S(2)}, u32[]{:S(2)}) collective-permute-start(bf16[2,128,512]{2,1,0:T(8,128)(2,1)S(1)} %gather_fusion.6), channel_id=1, source_target_pairs={{0,24},{4,28},{8,0},{12,4},{16,8},{20,12},{24,16},{28,20},{1,25},{... | collective-permute-start | bytes 786440 | tf_op jit(solution)/shard_map/ppermute | solution.py:208
  24.8 12.3 %collective-permute-start.8 = (bf16[256,512]{1,0:T(8,128)(2,1)S(1)}, bf16[256,512]{1,0:T(8,128)(2,1)S(1)}, u32[]{:S(2)}, u32[]{:S(2)}) collective-permute-start(bf16[256,512]{1,0:T(8,128)(2,1)S(1)} %broadcast_select_fusion), channel_id=1, source_target_pairs={{0,8},{4,12},{1,9},{5,13},{2,10},{6,14},{3,11},{7,15}} | collective-permute-start | bytes 786440 | tf_op jit(solution)/shard_map/ppermute | solution.py:117
  28.9 11.1 %collective-permute-start.6 = (bf16[1,128,512]{2,1,0:T(8,128)(2,1)}, bf16[1,128,512]{2,1,0:T(8,128)(2,1)S(1)}, u32[]{:S(2)}, u32[]{:S(2)}) collective-permute-start(bf16[1,128,512]{2,1,0:T(8,128)(2,1)} %get-tuple-element.62), channel_id=1, source_target_pairs={{0,28},{4,0},{8,4},{12,8},{16,12},{20,16},{24,20},{28,24},{1,29},{... | collective-permute-start | bytes 393224 | tf_op jit(solution)/shard_map/ppermute | solution.py:208
  37.1 5.2 %collective-permute-start.9 = (bf16[256,512]{1,0:T(8,128)(2,1)S(1)}, bf16[256,512]{1,0:T(8,128)(2,1)S(1)}, u32[]{:S(2)}, u32[]{:S(2)}) collective-permute-start(bf16[256,512]{1,0:T(8,128)(2,1)S(1)} %broadcast_select_fusion.1), channel_id=1, source_target_pairs={{0,16},{4,20},{8,24},{12,28},{1,17},{5,21},{9,25},{13,29},{2,18},{... | collective-permute-start | bytes 786440 | tf_op jit(solution)/shard_map/ppermute | solution.py:117
  72.9 12.5 %collective-permute-start.20 = (bf16[256,512]{1,0:T(8,128)(2,1)S(1)}, bf16[256,512]{1,0:T(8,128)(2,1)S(1)}, u32[]{:S(2)}, u32[]{:S(2)}) collective-permute-start(bf16[256,512]{1,0:T(8,128)(2,1)S(1)} %convert_element_type.23), channel_id=1, source_target_pairs={{16,0},{20,4},{24,8},{28,12},{17,1},{21,5},{25,9},{29,13},{18,2},{... | collective-permute-start | bytes 786440 | tf_op jit(solution)/shard_map/ppermute | solution.py:131
  76.7 44.9 %collective-permute-start.14 = (bf16[256,512]{1,0:T(8,128)(2,1)S(1)}, bf16[256,512]{1,0:T(8,128)(2,1)S(1)}, u32[]{:S(2)}, u32[]{:S(2)}) collective-permute-start(bf16[256,512]{1,0:T(8,128)(2,1)S(1)} %get-tuple-element.55), channel_id=1, source_target_pairs={{0,24},{4,28},{8,0},{12,4},{16,8},{20,12},{24,16},{28,20},{1,25},{... | collective-permute-start | bytes 786440 | tf_op jit(solution)/shard_map/ppermute | solution.py:278
  81.6 40.1 %collective-permute-start.15 = (bf16[256,512]{1,0:T(8,128)(2,1)S(1)}, bf16[256,512]{1,0:T(8,128)(2,1)S(1)}, u32[]{:S(2)}, u32[]{:S(2)}) collective-permute-start(bf16[256,512]{1,0:T(8,128)(2,1)S(1)} %get-tuple-element.54), channel_id=1, source_target_pairs={{0,20},{4,24},{8,28},{12,0},{16,4},{20,8},{24,12},{28,16},{1,21},{... | collective-permute-start | bytes 786440 | tf_op jit(solution)/shard_map/ppermute | solution.py:278
  82.9 32.5 %collective-permute-start.13 = (bf16[128,512]{1,0:T(8,128)(2,1)S(1)}, bf16[128,512]{1,0:T(8,128)(2,1)S(1)}, u32[]{:S(2)}, u32[]{:S(2)}) collective-permute-start(bf16[128,512]{1,0:T(8,128)(2,1)S(1)} %get-tuple-element.50), channel_id=1, source_target_pairs={{0,28},{4,0},{8,4},{12,8},{16,12},{20,16},{24,20},{28,24},{1,29},{... | collective-permute-start | bytes 393224 | tf_op jit(solution)/shard_map/ppermute | solution.py:278
  83.8 10.8 %collective-permute-start.10 = (bf16[96,1536]{1,0:T(8,128)(2,1)S(1)}, bf16[96,1536]{1,0:T(8,128)(2,1)S(1)}, u32[]{:S(2)}, u32[]{:S(2)}) collective-permute-start(bf16[96,1536]{1,0:T(8,128)(2,1)S(1)} %get-tuple-element.58), channel_id=1, source_target_pairs={{0,1},{1,2},{2,3},{3,0},{4,5},{5,6},{6,7},{7,4},{8,9},{9,10},{10,1... | collective-permute-start | bytes 884744 | tf_op jit(solution)/shard_map/ppermute | solution.py:168
  85.5 15.1 %collective-permute-start.21 = (bf16[256,512]{1,0:T(8,128)(2,1)S(1)}, bf16[256,512]{1,0:T(8,128)(2,1)S(1)}, u32[]{:S(2)}, u32[]{:S(2)}) collective-permute-start(bf16[256,512]{1,0:T(8,128)(2,1)S(1)} %fusion), channel_id=1, source_target_pairs={{8,0},{12,4},{9,1},{13,5},{10,2},{14,6},{11,3},{15,7}} | collective-permute-start | bytes 786440 | tf_op jit(solution)/shard_map/ppermute | solution.py:131
  94.6 14.6 %collective-permute-start.11 = (bf16[96,1536]{1,0:T(8,128)(2,1)S(1)}, bf16[96,1536]{1,0:T(8,128)(2,1)S(1)}, u32[]{:S(2)}, u32[]{:S(2)}) collective-permute-start(bf16[96,1536]{1,0:T(8,128)(2,1)S(1)} %get-tuple-element.57), channel_id=1, source_target_pairs={{0,2},{1,3},{2,0},{3,1},{4,6},{5,7},{6,4},{7,5},{8,10},{9,11},{10,... | collective-permute-start | bytes 884744 | tf_op jit(solution)/shard_map/ppermute | solution.py:168
  100.5 14.7 %collective-permute-start.12 = (bf16[96,1536]{1,0:T(8,128)(2,1)S(1)}, bf16[96,1536]{1,0:T(8,128)(2,1)S(1)}, u32[]{:S(2)}, u32[]{:S(2)}) collective-permute-start(bf16[96,1536]{1,0:T(8,128)(2,1)S(1)} %get-tuple-element.56), channel_id=1, source_target_pairs={{0,3},{1,0},{2,1},{3,2},{4,7},{5,4},{6,5},{7,6},{8,11},{9,8},{10,9... | collective-permute-start | bytes 884744 | tf_op jit(solution)/shard_map/ppermute | solution.py:168
  109.2 11.5 %collective-permute-start.22 = (bf16[256,512]{1,0:T(8,128)(2,1)S(1)}, bf16[256,512]{1,0:T(8,128)(2,1)S(1)}, u32[]{:S(2)}, u32[]{:S(2)}) collective-permute-start(bf16[256,512]{1,0:T(8,128)(2,1)S(1)} %fusion.2), channel_id=1, source_target_pairs={{4,0},{5,1},{6,2},{7,3}} | collective-permute-start | bytes 786440 | tf_op jit(solution)/shard_map/ppermute | solution.py:131
  115.2 5.4 %collective-permute-start.19 = (bf16[128,512]{1,0:T(8,128)(2,1)S(1)}, bf16[128,512]{1,0:T(8,128)(2,1)S(1)}, u32[]{:S(2)}, u32[]{:S(2)}) collective-permute-start(bf16[128,512]{1,0:T(8,128)(2,1)S(1)} %get-tuple-element.49), channel_id=1, source_target_pairs={{0,4},{4,8},{8,12},{12,16},{16,20},{20,24},{24,28},{28,0},{1,5},{5... | collective-permute-start | bytes 393224 | tf_op jit(solution)/shard_map/ppermute | solution.py:278
  115.4 24.7 %copy-start.5 = (bf16[96,6144]{1,0:T(8,128)(2,1)}, bf16[96,6144]{1,0:T(8,128)(2,1)S(1)}, u32[]{:S(2)}) copy-start(bf16[96,6144]{1,0:T(8,128)(2,1)S(1)} %constant_dynamic-update-slice_fusion.10) | copy-start | bytes 3538948
  115.4 20.9 %copy-start.11 = (bf16[128,512]{1,0:T(8,128)(2,1)}, bf16[128,512]{1,0:T(8,128)(2,1)S(1)}, u32[]{:S(2)}) copy-start(bf16[128,512]{1,0:T(8,128)(2,1)S(1)} %collective-permute-done.13.refs_0_) | copy-start | bytes 393220
  115.4 19.1 %collective-permute-start.16 = (bf16[256,512]{1,0:T(8,128)(2,1)S(1)}, bf16[256,512]{1,0:T(8,128)(2,1)S(1)}, u32[]{:S(2)}, u32[]{:S(2)}) collective-permute-start(bf16[256,512]{1,0:T(8,128)(2,1)S(1)} %get-tuple-element.53), channel_id=1, source_target_pairs={{0,16},{4,20},{8,24},{12,28},{16,0},{20,4},{24,8},{28,12},{1,17},{... | collective-permute-start | bytes 786440 | tf_op jit(solution)/shard_map/ppermute | solution.py:278
  120.6 15.7 %copy-start.12 = (bf16[128,512]{1,0:T(8,128)(2,1)}, bf16[128,512]{1,0:T(8,128)(2,1)S(1)}, u32[]{:S(2)}) copy-start(bf16[128,512]{1,0:T(8,128)(2,1)S(1)} %collective-permute-done.19.refs_6_) | copy-start | bytes 393220
  120.6 15.7 %collective-permute-start.17 = (bf16[256,512]{1,0:T(8,128)(2,1)S(1)}, bf16[256,512]{1,0:T(8,128)(2,1)S(1)}, u32[]{:S(2)}, u32[]{:S(2)}) collective-permute-start(bf16[256,512]{1,0:T(8,128)(2,1)S(1)} %get-tuple-element.52), channel_id=1, source_target_pairs={{0,12},{4,16},{8,20},{12,24},{16,28},{20,0},{24,4},{28,8},{1,13},{... | collective-permute-start | bytes 786440 | tf_op jit(solution)/shard_map/ppermute | solution.py:278
  120.7 15.7 %collective-permute-start.18 = (bf16[256,512]{1,0:T(8,128)(2,1)S(1)}, bf16[256,512]{1,0:T(8,128)(2,1)S(1)}, u32[]{:S(2)}, u32[]{:S(2)}) collective-permute-start(bf16[256,512]{1,0:T(8,128)(2,1)S(1)} %get-tuple-element.51), channel_id=1, source_target_pairs={{0,8},{4,12},{8,16},{12,20},{16,24},{20,28},{24,0},{28,4},{1,9},{5... | collective-permute-start | bytes 786440 | tf_op jit(solution)/shard_map/ppermute | solution.py:278
  121.6 14.7 %copy-start.6 = (bf16[256,512]{1,0:T(8,128)(2,1)}, bf16[256,512]{1,0:T(8,128)(2,1)S(1)}, u32[]{:S(2)}) copy-start(bf16[256,512]{1,0:T(8,128)(2,1)S(1)} %collective-permute-done.14.refs_1_) | copy-start | bytes 786436
  121.6 14.7 %copy-start.7 = (bf16[256,512]{1,0:T(8,128)(2,1)}, bf16[256,512]{1,0:T(8,128)(2,1)S(1)}, u32[]{:S(2)}) copy-start(bf16[256,512]{1,0:T(8,128)(2,1)S(1)} %collective-permute-done.15.refs_2_) | copy-start | bytes 786436
  141.1 8.9 %collective-permute-start.23 = (bf16[96,512]{1,0:T(8,128)(2,1)S(1)}, bf16[96,512]{1,0:T(8,128)(2,1)S(1)}, u32[]{:S(2)}, u32[]{:S(2)}) collective-permute-start(bf16[96,512]{1,0:T(8,128)(2,1)S(1)} %get-tuple-element.61), channel_id=1, source_target_pairs={{0,1},{1,2},{2,3},{3,0},{4,5},{5,6},{6,7},{7,4},{8,9},{9,10},{10,1... | collective-permute-start | bytes 294920 | tf_op jit(solution)/shard_map/ppermute | solution.py:168
  143.4 9.6 %collective-permute-start.24 = (bf16[96,512]{1,0:T(8,128)(2,1)S(1)}, bf16[96,512]{1,0:T(8,128)(2,1)S(1)}, u32[]{:S(2)}, u32[]{:S(2)}) collective-permute-start(bf16[96,512]{1,0:T(8,128)(2,1)S(1)} %get-tuple-element.60), channel_id=1, source_target_pairs={{0,2},{1,3},{2,0},{3,1},{4,6},{5,7},{6,4},{7,5},{8,10},{9,11},{10,... | collective-permute-start | bytes 294920 | tf_op jit(solution)/shard_map/ppermute | solution.py:168
  146.8 6.5 %collective-permute-start.25 = (bf16[96,512]{1,0:T(8,128)(2,1)S(1)}, bf16[96,512]{1,0:T(8,128)(2,1)S(1)}, u32[]{:S(2)}, u32[]{:S(2)}) collective-permute-start(bf16[96,512]{1,0:T(8,128)(2,1)S(1)} %get-tuple-element.59), channel_id=1, source_target_pairs={{0,3},{1,0},{2,1},{3,2},{4,7},{5,4},{6,5},{7,6},{8,11},{9,8},{10,9... | collective-permute-start | bytes 294920 | tf_op jit(solution)/shard_map/ppermute | solution.py:168
  (7 other events, 38.0 us)

commit v4 on v0

--- a/solution.py
+++ b/solution.py
@@ -17,16 +17,15 @@
 
 def attention_kernel(
     blk_ref, dst_ref, kind_ref,
-    q_ref, do_ref, k_ref, v_ref,
+    q_ref, do_ref, k_ref, v_ref, dq_in,
     dq_ref, loc_ref, far_ref,
     kc_ref, vc_ref, loc_acc, far_acc,
-    *, hpk, kv_here, nb,
+    *, hpk, nb,
 ):
-    g = pl.program_id(0)
-    b = pl.program_id(1)
+    b = pl.program_id(0)
     scale = 1.0 / math.sqrt(HD)
 
-    @pl.when((g == 0) & (b == 0))
+    @pl.when(b == 0)
     def _():
         loc_acc[...] = jnp.zeros_like(loc_acc)
         far_acc[...] = jnp.zeros_like(far_acc)
@@ -45,7 +44,7 @@
     scores = lax.dot_general(qs, kc, nt, preferred_element_type=jnp.float32) * scale
     peak = jnp.max(scores, axis=1, keepdims=True)
     lifted = jnp.exp(scores - peak)
-    probs = lifted / jnp.sum(lifted, axis=1, keepdims=True)
+    probs = lifted * (1.0 / jnp.sum(lifted, axis=1, keepdims=True))
     probs_b = probs.astype(jnp.bfloat16)
     attended = jnp.dot(probs_b, vc, preferred_element_type=jnp.float32)
     delta = jnp.sum(dos.astype(jnp.float32) * attended, axis=1, keepdims=True)
@@ -68,17 +67,17 @@
 
         @pl.when(kind == 2)
         def _():
-            loc_acc[g, pl.ds(row, BLK), :] += kt
-            loc_acc[kv_here + g, pl.ds(row, BLK), :] += vt
+            loc_acc[0, pl.ds(row, BLK), :] += kt
+            loc_acc[1, pl.ds(row, BLK), :] += vt
 
         @pl.when(kind != 2)
         def _():
-            far_acc[g, pl.ds(row, BLK), :] += kt
-            far_acc[kv_here + g, pl.ds(row, BLK), :] += vt
+            far_acc[0, pl.ds(row, BLK), :] += kt
+            far_acc[1, pl.ds(row, BLK), :] += vt
 
-    @pl.when((g == kv_here - 1) & (b == nb - 1))
+    @pl.when(b == nb - 1)
     def _():
-        for j in range(2 * kv_here):
+        for j in range(2):
             loc_ref[:, j * HD:(j + 1) * HD] = loc_acc[j]
             far_ref[:, j * HD:(j + 1) * HD] = far_acc[j].astype(jnp.bfloat16)
 
@@ -91,12 +90,7 @@
     heads_here = query_rows.shape[1] // HD
     kv_here = max(1, heads_here // GROUP)
     hpk = heads_here // kv_here
-    width = 2 * kv_here * HD
     first_kv = lane_index * heads_here // GROUP
-    key_own = lax.dynamic_slice_in_dim(key_rows, first_kv * HD, kv_here * HD, axis=1)
-    value_own = lax.dynamic_slice_in_dim(value_rows, first_kv * HD, kv_here * HD, axis=1)
-    kv_own = jnp.concatenate([key_own, value_own], axis=1)
-    kv_all = lax.all_gather(kv_own, "ctx", axis=0, tiled=True)
 
     rows = lax.dynamic_slice_in_dim(block_list, shard_index * nb, nb, axis=0).astype(jnp.int32)
     owner = rows // nb
@@ -108,41 +102,59 @@
     dst = jnp.where(local, rows - shard_index * nb, rows).astype(jnp.int32).reshape(-1)
     blk = rows.reshape(-1)
 
-    kernel = functools.partial(attention_kernel, hpk=hpk, kv_here=kv_here, nb=nb)
-    grid_spec = pltpu.PrefetchScalarGridSpec(
-        num_scalar_prefetch=3,
-        grid=(kv_here, nb),
-        in_specs=[
-            pl.BlockSpec((BLK, hpk * HD), lambda g, b, *_: (b, g)),
-            pl.BlockSpec((BLK, hpk * HD), lambda g, b, *_: (b, g)),
-            pl.BlockSpec((seq, HD), lambda g, b, *_: (0, g)),
-            pl.BlockSpec((seq, HD), lambda g, b, *_: (0, kv_here + g)),
-        ],
-        out_specs=[
-            pl.BlockSpec((BLK, hpk * HD), lambda g, b, *_: (b, g)),
-            pl.BlockSpec((nb * BLK, width), lambda g, b, *_: (0, 0)),
-            pl.BlockSpec((seq, width), lambda g, b, *_: (0, 0)),
-        ],
-        scratch_shapes=[
-            pltpu.VMEM((SLOTS * BLK, HD), jnp.bfloat16),
-            pltpu.VMEM((SLOTS * BLK, HD), jnp.bfloat16),
-            pltpu.VMEM((2 * kv_here, nb * BLK, HD), jnp.float32),
-            pltpu.VMEM((2 * kv_here, seq, HD), jnp.float32),
-        ],
-    )
-    dq, loc, far = pl.pallas_call(
-        kernel,
-        grid_spec=grid_spec,
-        out_shape=[
-            jax.ShapeDtypeStruct((nb * BLK, heads_here * HD), jnp.bfloat16),
-            jax.ShapeDtypeStruct((nb * BLK, width), jnp.float32),
-            jax.ShapeDtypeStruct((seq, width), jnp.bfloat16),
-        ],
-        compiler_params=pltpu.CompilerParams(dimension_semantics=("arbitrary", "arbitrary")),
-    )(blk, dst, kind, query_rows, out_grad, kv_all, kv_all)
-
-    got = lax.psum_scatter(far, "ctx", scatter_dimension=0, tiled=True)
-    kv_grad = (got.astype(jnp.float32) + loc).astype(jnp.bfloat16)
+    kernel = functools.partial(attention_kernel, hpk=hpk, nb=nb)
+    dq = jnp.zeros((nb * BLK, heads_here * HD), jnp.bfloat16)
+    key_parts = []
+    value_parts = []
+    for g in range(kv_here):
+        col = (first_kv + g) * HD
+        kv_own = jnp.concatenate(
+            [
+                lax.dynamic_slice_in_dim(key_rows, col, HD, axis=1),
+                lax.dynamic_slice_in_dim(value_rows, col, HD, axis=1),
+            ],
+            axis=1,
+        )
+        kv_all = lax.all_gather(kv_own, "ctx", axis=0, tiled=True)
+        grid_spec = pltpu.PrefetchScalarGridSpec(
+            num_scalar_prefetch=3,
+            grid=(nb,),
+            in_specs=[
+                pl.BlockSpec((BLK, hpk * HD), lambda b, *_, g=g: (b, g)),
+                pl.BlockSpec((BLK, hpk * HD), lambda b, *_, g=g: (b, g)),
+                pl.BlockSpec((seq, HD), lambda b, *_: (0, 0)),
+                pl.BlockSpec((seq, HD), lambda b, *_: (0, 1)),
+                pl.BlockSpec(memory_space=pl.ANY),
+            ],
+            out_specs=[
+                pl.BlockSpec((BLK, hpk * HD), lambda b, *_, g=g: (b, g)),
+                pl.BlockSpec((nb * BLK, 2 * HD), lambda b, *_: (0, 0)),
+                pl.BlockSpec((seq, 2 * HD), lambda b, *_: (0, 0)),
+            ],
+            scratch_shapes=[
+                pltpu.VMEM((SLOTS * BLK, HD), jnp.bfloat16),
+                pltpu.VMEM((SLOTS * BLK, HD), jnp.bfloat16),
+                pltpu.VMEM((2, nb * BLK, HD), jnp.float32),
+                pltpu.VMEM((2, seq, HD), jnp.float32),
+            ],
+        )
+        dq, loc, far = pl.pallas_call(
+            kernel,
+            grid_spec=grid_spec,
+            out_shape=[
+                jax.ShapeDtypeStruct((nb * BLK, heads_here * HD), jnp.bfloat16),
+                jax.ShapeDtypeStruct((nb * BLK, 2 * HD), jnp.float32),
+                jax.ShapeDtypeStruct((seq, 2 * HD), jnp.bfloat16),
+            ],
+            input_output_aliases={7: 0},
+            compiler_params=pltpu.CompilerParams(dimension_semantics=("arbitrary",)),
+        )(blk, dst, kind, query_rows, out_grad, kv_all, kv_all, dq)
+        got = lax.psum_scatter(far, "ctx", scatter_dimension=0, tiled=True)
+        part = (got.astype(jnp.float32) + loc).astype(jnp.bfloat16)
+        key_parts.append(part[:, :HD])
+        value_parts.append(part[:, HD:])
+    kv_grad = jnp.concatenate(key_parts + value_parts, axis=1)
+    width = 2 * kv_here * HD
 
     query_out = lax.all_to_all(dq, "uly", split_axis=0, concat_axis=1, tiled=True)
     kv_seq = lax.all_to_all(kv_grad, "uly", split_axis=0, concat_axis=1, tiled=True)

time: 149 us -> 178 us (1.19)
  waiting for transfers between devices: 86.5 us -> 111 us
  Pallas kernels: 28.8 us -> 31.3 us
    reduce_scatter x1 -> x2, waiting for transfers between devices: 41.7 us -> 62 us  [shards(): got = lax.psum_scatter(far, 'ctx', scatter_dimension=0, tiled=True)]
    all_gather x1 -> x2, waiting for transfers between devices: 34.2 us -> 38.1 us  [shards(): kv_all = lax.all_gather(kv_own, 'ctx', axis=0, tiled=True)]
    pallas_call x1 -> x2, Pallas kernels: 28.8 us -> 31.3 us  [shards(): pl.pallas_call(kernel, grid_spec=grid_spec, out_shape=[jax.ShapeDtypeStru...]
  transfers between devices with their start and end apart: 4 -> 6, of which waited for: 3 -> 5; matrix products, arithmetic and copies ran while one was open for 3% -> 4% of each run, Pallas kernels for 0% -> 18%
where the time goes in v4:
time: 178 us
  waiting for transfers between devices  111 us (62%)
  Pallas kernels  31.3 us (18%)
  between operations  13.9 us (8%)
  starting transfers between devices  9.5 us (5%)
  local copies, waits for them, and re-layouts  8.03 us (5%)
  other arithmetic  4.26 us (2%)
    reduce_scatter x2, waiting for transfers between devices, shards(): got = lax.psum_scatter(far, 'ctx', scatter_dimension=0, tiled=True)  62 us
    all_gather x2, waiting for transfers between devices, shards(): kv_all = lax.all_gather(kv_own, 'ctx', axis=0, tiled=True)  38.1 us
    pallas_call x2, Pallas kernels, shards(): pl.pallas_call(kernel, grid_spec=grid_spec, out_shape=[jax.ShapeDtypeStru...  31.3 us
    all_to_all x1, waiting for transfers between devices, shards(): lax.all_to_all(kv_grad, 'uly', split_axis=0, concat_axis=1, tiled=True)  10.5 us
    all_to_all x1, starting transfers between devices, shards(): lax.all_to_all(dq, 'uly', split_axis=0, concat_axis=1, tiled=True)  4.74 us
    all_to_all x1, starting transfers between devices, shards(): lax.all_to_all(kv_grad, 'uly', split_axis=0, concat_axis=1, tiled=True)  4.6 us
  transfers between devices with their start and end apart: 6, of which 5 were waited for; matrix products, arithmetic and copies ran while one was open for 4% of the time, Pallas kernels for 18%

profile of v4, /device:TPU:0, one launch (start us, length us, event | category | flops | bytes accessed | tf_op | source)
XLA Modules:
  0.0 177.7 jit_solution(4943203983285717429)
XLA Ops:
  7.3 1.1 constant_dynamic-slice_fusion
  8.3 0.7 pad_maximum_fusion.2
  9.1 0.0 all-gather.3.cloned.1.call-start
  9.1 0.7 pad_maximum_fusion.1
  9.8 0.0 reduce-scatter.3.cloned.1.call-start
  9.9 0.1 select_select_fusion
  10.0 0.1 copy.10
  10.1 0.1 copy.11
  10.2 0.6 reshape.39.dst_ref
  10.8 0.6 reshape.38.blk_ref
  11.4 0.1 copy.12
  11.5 0.7 reshape.40.kind_ref
  12.2 26.7 %all-gather.5.cloned.1.call-done.k_ref.v_ref = bf16[3072,256]{1,0:T(8,128)(2,1)} async-done(((bf16[384,256]{1,0:T(8,128)(2,1)}), bf16[3072,256]{1,0:T(8,128)(2,1)}) %all-gather.5.cloned.1.call-update) | async-done | bytes 1572880 | tf_op jit(solution)/shard_map/all_gather | solution.py:118
  38.9 1.1 broadcast_in_dim.13.dq_in
  40.0 15.7 %shard_map.76 = (bf16[384,1536]{1,0:T(8,128)(2,1)}, f32[384,256]{1,0:T(8,128)}, bf16[3072,256]{1,0:T(8,128)(2,1)}) custom-call(s32[24]{0:T(128)} %reshape.38.blk_ref, s32[24]{0:T(128)} %reshape.39.dst_ref, s32[24]{0:T(128)} %reshape.40.kind_ref, bf16[384,1536]{1,0:T(8,128)(2,1)} %q_ref.3, bf16[384,1536]{1,0:T(8,128)(2,1)} %do_ref.3, ...), custom_call_target="tpu_custom_call", output_to_operand_aliasing={{0}: (7, {})} | custom-call | tf_op jit(solution)/shard_map/pallas_call | solution.py:141
  55.7 11.3 %all-gather.3.cloned.1.call-done.k_ref.v_ref = bf16[3072,256]{1,0:T(8,128)(2,1)} async-done(((bf16[384,256]{1,0:T(8,128)(2,1)}), bf16[3072,256]{1,0:T(8,128)(2,1)}) %all-gather.3.cloned.1.call-update) | async-done | bytes 1572880 | tf_op jit(solution)/shard_map/all_gather | solution.py:118
  67.1 15.7 %shard_map.77 = (bf16[384,1536]{1,0:T(8,128)(2,1)}, f32[384,256]{1,0:T(8,128)}, bf16[3072,256]{1,0:T(8,128)(2,1)}) custom-call(s32[24]{0:T(128)} %reshape.38.blk_ref, s32[24]{0:T(128)} %reshape.39.dst_ref, s32[24]{0:T(128)} %reshape.40.kind_ref, bf16[384,1536]{1,0:T(8,128)(2,1)} %q_ref.3, bf16[384,1536]{1,0:T(8,128)(2,1)} %do_ref.3, ...), custom_call_target="tpu_custom_call", output_to_operand_aliasing={{0}: (7, {})} | custom-call | tf_op jit(solution)/shard_map/pallas_call | solution.py:141
  82.8 4.7 %all-to-all-start = ((bf16[4,96,1536]{2,1,0:T(8,128)(2,1)}), bf16[4,96,1536]{2,1,0:T(8,128)(2,1)S(1)}, u32[]{:S(2)}, u32[]{:S(2)}) async-start(bf16[4,96,1536]{2,1,0:T(8,128)(2,1)} %bitcast), calls=%async_computation | async-start | bytes 2359296 | tf_op jit(solution)/shard_map/all_to_all | solution.py:159
  87.5 21.4 %reduce-scatter.3.cloned.1.call-done = bf16[384,256]{1,0:T(8,128)(2,1)} async-done(((bf16[3072,256]{1,0:T(8,128)(2,1)}), bf16[384,256]{1,0:T(8,128)(2,1)}) %reduce-scatter.3.cloned.1.call-update) | async-done | bytes 196624 | tf_op jit(solution)/shard_map/reduce_scatter | solution.py:152
  108.9 1.0 add_convert_fusion.1
  109.9 40.6 %reduce-scatter.5.cloned.1.call-done = bf16[384,256]{1,0:T(8,128)(2,1)} async-done(((bf16[3072,256]{1,0:T(8,128)(2,1)}), bf16[384,256]{1,0:T(8,128)(2,1)}) %reduce-scatter.5.cloned.1.call-update) | async-done | bytes 196624 | tf_op jit(solution)/shard_map/reduce_scatter | solution.py:152
  150.5 1.0 add_convert_fusion
  151.5 0.8 pad_maximum_fusion
  152.3 4.6 %all-to-all-start.1 = ((bf16[4,96,512]{2,1,0:T(8,128)(2,1)}), bf16[4,96,512]{2,1,0:T(8,128)(2,1)S(1)}, u32[]{:S(2)}, u32[]{:S(2)}) async-start(bf16[4,96,512]{2,1,0:T(8,128)(2,1)} %bitcast.2), calls=%async_computation.3 | async-start | bytes 786432 | tf_op jit(solution)/shard_map/all_to_all | solution.py:160
  156.9 1.1 copy.18
  158.1 10.5 %all-to-all-done.1 = bf16[4,96,512]{2,1,0:T(8,128)(2,1)S(1)} async-done(((bf16[4,96,512]{2,1,0:T(8,128)(2,1)}), bf16[4,96,512]{2,1,0:T(8,128)(2,1)S(1)}, u32[]{:S(2)}, u32[]{:S(2)}) %all-to-all-start.1) | async-done | bytes 393248 | tf_op jit(solution)/shard_map/all_to_all | solution.py:160
  168.6 0.1 reshape.41
  168.7 0.5 fusion.2
  169.2 0.3 copy.16
  169.5 0.7 copy.19
  170.2 0.3 copy.17
  170.5 0.7 copy.20
  (17 shorter events, 0.2 us)
Async XLA Ops:
  7.2 2.7 %copy-start.2 = (s32[24,8]{0,1:T(8,128)S(1)}, s32[24,8]{0,1:T(8,128)}, u32[]{:S(2)}) copy-start(s32[24,8]{0,1:T(8,128)} %param.9) | copy-start | bytes 2308
  7.2 31.7 %all-gather.5.cloned.1.call-start = ((), (), s32[]{:S(2)}) async-start(), calls=%async_computation.5 | async-start | bytes 1769472 | tf_op jit(solution)/shard_map/all_gather | solution.py:118
  9.1 58.0 %all-gather.3.cloned.1.call-start = ((), (), s32[]{:S(2)}) async-start(), calls=%async_computation.4 | async-start | bytes 1769472 | tf_op jit(solution)/shard_map/all_gather | solution.py:118
  9.8 99.0 %reduce-scatter.3.cloned.1.call-start = ((), (), s32[]{:S(2)}) async-start(), calls=%async_computation.6 | async-start | bytes 1769472 | tf_op jit(solution)/shard_map/reduce_scatter | solution.py:152
  55.7 94.8 %reduce-scatter.5.cloned.1.call-start = ((), (), s32[]{:S(2)}) async-start(), calls=%async_computation.7 | async-start | bytes 1769472 | tf_op jit(solution)/shard_map/reduce_scatter | solution.py:152
  82.8 26.1 %copy-start = (f32[384,256]{1,0:T(8,128)S(1)}, f32[384,256]{1,0:T(8,128)}, u32[]{:S(2)}) copy-start(f32[384,256]{1,0:T(8,128)} %get-tuple-element.12) | copy-start | bytes 1179652
  82.8 69.5 %all-to-all-start = ((bf16[4,96,1536]{2,1,0:T(8,128)(2,1)}), bf16[4,96,1536]{2,1,0:T(8,128)(2,1)S(1)}, u32[]{:S(2)}, u32[]{:S(2)}) async-start(bf16[4,96,1536]{2,1,0:T(8,128)(2,1)} %bitcast), calls=%async_computation | async-start | bytes 2359296 | tf_op jit(solution)/shard_map/all_to_all | solution.py:159
  87.5 63.0 %copy-start.1 = (f32[384,256]{1,0:T(8,128)S(1)}, f32[384,256]{1,0:T(8,128)}, u32[]{:S(2)}) copy-start(f32[384,256]{1,0:T(8,128)} %get-tuple-element.14) | copy-start | bytes 1179652
  152.3 16.3 %all-to-all-start.1 = ((bf16[4,96,512]{2,1,0:T(8,128)(2,1)}), bf16[4,96,512]{2,1,0:T(8,128)(2,1)S(1)}, u32[]{:S(2)}, u32[]{:S(2)}) async-start(bf16[4,96,512]{2,1,0:T(8,128)(2,1)} %bitcast.2), calls=%async_computation.3 | async-start | bytes 786432 | tf_op jit(solution)/shard_map/all_to_all | solution.py:160
Sparse Core Ops, SparseCore 0:
  10.5 28.3 all-gather.4
  41.3 25.6 all-gather.2
  70.4 38.4 reduce-scatter.2
  112.0 38.4 reduce-scatter.4

commit v5 on v0

--- a/solution.py
+++ b/solution.py
@@ -45,7 +45,7 @@
     scores = lax.dot_general(qs, kc, nt, preferred_element_type=jnp.float32) * scale
     peak = jnp.max(scores, axis=1, keepdims=True)
     lifted = jnp.exp(scores - peak)
-    probs = lifted / jnp.sum(lifted, axis=1, keepdims=True)
+    probs = lifted * (1.0 / jnp.sum(lifted, axis=1, keepdims=True))
     probs_b = probs.astype(jnp.bfloat16)
     attended = jnp.dot(probs_b, vc, preferred_element_type=jnp.float32)
     delta = jnp.sum(dos.astype(jnp.float32) * attended, axis=1, keepdims=True)
@@ -54,14 +54,14 @@
     dq = jnp.dot(dscores, kc, preferred_element_type=jnp.float32)
     for h in range(hpk):
         dq_ref[:, h * HD:(h + 1) * HD] = dq[h * BLK:(h + 1) * BLK].astype(jnp.bfloat16)
-    kterm = lax.dot_general(dscores, qs, tn, preferred_element_type=jnp.float32)
-    vterm = lax.dot_general(probs_b, dos, tn, preferred_element_type=jnp.float32)
+    kterm = lax.dot_general(qs, dscores, tn, preferred_element_type=jnp.float32)
+    vterm = lax.dot_general(dos, probs_b, tn, preferred_element_type=jnp.float32)
 
     for s in range(SLOTS):
         kind = kind_ref[b * SLOTS + s]
         row = pl.multiple_of(dst_ref[b * SLOTS + s] * BLK, BLK)
-        kt = kterm[s * BLK:(s + 1) * BLK]
-        vt = vterm[s * BLK:(s + 1) * BLK]
+        kt = kterm[:, s * BLK:(s + 1) * BLK]
+        vt = vterm[:, s * BLK:(s + 1) * BLK]
         rounded = kind == 0
         kt = jnp.where(rounded, kt.astype(jnp.bfloat16).astype(jnp.float32), kt)
         vt = jnp.where(rounded, vt.astype(jnp.bfloat16).astype(jnp.float32), vt)
@@ -142,7 +142,8 @@
     )(blk, dst, kind, query_rows, out_grad, kv_all, kv_all)
 
     got = lax.psum_scatter(far, "ctx", scatter_dimension=0, tiled=True)
-    kv_grad = (got.astype(jnp.float32) + loc).astype(jnp.bfloat16)
+    kv_sum = (got.astype(jnp.float32) + loc).reshape(nb, HD, 2 * kv_here, BLK)
+    kv_grad = jnp.transpose(kv_sum, (0, 3, 2, 1)).reshape(nb * BLK, width).astype(jnp.bfloat16)
 
     query_out = lax.all_to_all(dq, "uly", split_axis=0, concat_axis=1, tiled=True)
     kv_seq = lax.all_to_all(kv_grad, "uly", split_axis=0, concat_axis=1, tiled=True)

time: 149 us -> 146 us (0.980)
  Pallas kernels: 28.8 us -> 25.6 us
    pallas_call x1, Pallas kernels: 28.8 us -> 25.6 us  [shards(): pl.pallas_call(kernel, grid_spec=grid_spec, out_shape=[jax.ShapeDtypeStru...]
  transfers between devices with their start and end apart: 4 -> 4, of which waited for: 3 -> 3; matrix products, arithmetic and copies ran while one was open for 3% -> 4% of each run, Pallas kernels for 0% -> 0%
where the time goes in v5:
time: 146 us
  waiting for transfers between devices  86.5 us (59%)
  Pallas kernels  25.6 us (18%)
  between operations  14.2 us (10%)
  starting transfers between devices  9.41 us (6%)
  local copies, waits for them, and re-layouts  8.06 us (6%)
  other arithmetic  2 us (1%)
    reduce_scatter x1, waiting for transfers between devices, shards(): got = lax.psum_scatter(far, 'ctx', scatter_dimension=0, tiled=True)  41.7 us
    all_gather x1, waiting for transfers between devices, shards(): kv_all = lax.all_gather(kv_own, 'ctx', axis=0, tiled=True)  34.2 us
    pallas_call x1, Pallas kernels, shards(): pl.pallas_call(kernel, grid_spec=grid_spec, out_shape=[jax.ShapeDtypeStru...  25.6 us
    all_to_all x1, waiting for transfers between devices, shards(): lax.all_to_all(kv_grad, 'uly', split_axis=0, concat_axis=1, tiled=True)  10.6 us
    all_to_all x1, starting transfers between devices, shards(): lax.all_to_all(dq, 'uly', split_axis=0, concat_axis=1, tiled=True)  4.74 us
    all_to_all x1, starting transfers between devices, shards(): lax.all_to_all(kv_grad, 'uly', split_axis=0, concat_axis=1, tiled=True)  4.59 us
  transfers between devices with their start and end apart: 4, of which 3 were waited for; matrix products, arithmetic and copies ran while one was open for 4% of the time, Pallas kernels for 0%

profile of v5, /device:TPU:0, one launch (start us, length us, event | category | flops | bytes accessed | tf_op | source)
XLA Modules:
  0.0 145.7 jit_solution(3819923186285713606)
XLA Ops:
  7.2 0.0 all-gather.2.cloned.1.call-start
  7.3 1.1 constant_dynamic-slice_fusion
  8.3 0.8 pad_maximum_fusion
  9.1 0.0 all-gather.2.cloned.1.call-update
  9.1 0.0 reduce-scatter.2.cloned.1.call-start
  9.2 0.0 copy-done.1
  9.2 0.1 select_select_fusion
  9.3 0.1 copy.19
  9.4 0.6 reshape.45.kind_ref
  10.0 0.1 copy.17
  10.1 0.6 reshape.43.blk_ref
  10.7 0.1 copy.18
  10.7 0.6 reshape.44.dst_ref
  11.3 34.2 %all-gather.2.cloned.1.call-done.k_ref.v_ref = bf16[3072,512]{1,0:T(8,128)(2,1)} async-done(((bf16[384,512]{1,0:T(8,128)(2,1)}), bf16[3072,512]{1,0:T(8,128)(2,1)}) %all-gather.2.cloned.1.call-update) | async-done | bytes 3145744 | tf_op jit(solution)/shard_map/all_gather | solution.py:99
  45.5 25.6 %shard_map.76 = (bf16[384,1536]{1,0:T(8,128)(2,1)}, f32[384,512]{1,0:T(8,128)}, bf16[3072,512]{1,0:T(8,128)(2,1)}) custom-call(s32[24]{0:T(128)} %reshape.43.blk_ref, s32[24]{0:T(128)} %reshape.44.dst_ref, s32[24]{0:T(128)} %reshape.45.kind_ref, bf16[384,1536]{1,0:T(8,128)(2,1)} %q_ref.1, bf16[384,1536]{1,0:T(8,128)(2,1)} %do_ref.1, ...), custom_call_target="tpu_custom_call" | custom-call | tf_op jit(solution)/shard_map/pallas_call | solution.py:133
  71.2 0.0 reduce-scatter.2.cloned.1.call-update
  71.2 4.7 %all-to-all-start = ((bf16[4,96,1536]{2,1,0:T(8,128)(2,1)}), bf16[4,96,1536]{2,1,0:T(8,128)(2,1)S(1)}, u32[]{:S(2)}, u32[]{:S(2)}) async-start(bf16[4,96,1536]{2,1,0:T(8,128)(2,1)} %bitcast), calls=%async_computation | async-start | bytes 2359296 | tf_op jit(solution)/shard_map/all_to_all | solution.py:148
  75.9 41.7 %reduce-scatter.2.cloned.1.call-done = bf16[384,512]{1,0:T(8,128)(2,1)} async-done(((bf16[3072,512]{1,0:T(8,128)(2,1)}), bf16[384,512]{1,0:T(8,128)(2,1)}) %reduce-scatter.2.cloned.1.call-update) | async-done | bytes 393232 | tf_op jit(solution)/shard_map/reduce_scatter | solution.py:144
  117.6 1.1 add_convert_fusion
  118.8 0.1 convert_element_type.18
  118.9 0.3 copy.21
  119.1 0.9 convert_element_type.20
  120.0 0.0 all-to-all-done
  120.0 4.6 %all-to-all-start.1 = ((bf16[4,96,512]{2,1,0:T(8,128)(2,1)}), bf16[4,96,512]{2,1,0:T(8,128)(2,1)S(1)}, u32[]{:S(2)}, u32[]{:S(2)}) async-start(bf16[4,96,512]{2,1,0:T(8,128)(2,1)} %convert_element_type.20), calls=%async_computation.2 | async-start | bytes 786432 | tf_op jit(solution)/shard_map/all_to_all | solution.py:149
  124.6 1.1 copy.24
  125.8 10.6 %all-to-all-done.1 = bf16[4,96,512]{2,1,0:T(8,128)(2,1)S(1)} async-done(((bf16[4,96,512]{2,1,0:T(8,128)(2,1)}), bf16[4,96,512]{2,1,0:T(8,128)(2,1)S(1)}, u32[]{:S(2)}, u32[]{:S(2)}) %all-to-all-start.1) | async-done | bytes 393248 | tf_op jit(solution)/shard_map/all_to_all | solution.py:149
  136.3 0.1 reshape.46
  136.4 0.5 fusion.2
  137.0 0.3 copy.23
  137.2 0.7 copy.26
  137.9 0.3 copy.22
  138.2 0.7 copy.25
  (5 shorter events, 0.0 us)
Async XLA Ops:
  7.2 2.0 %copy-start.1 = (s32[24,8]{0,1:T(8,128)S(1)}, s32[24,8]{0,1:T(8,128)}, u32[]{:S(2)}) copy-start(s32[24,8]{0,1:T(8,128)} %param.9) | copy-start | bytes 2308
  7.2 38.3 %all-gather.2.cloned.1.call-start = ((), (), s32[]{:S(2)}) async-start(), calls=%async_computation.3 | async-start | bytes 3538944 | tf_op jit(solution)/shard_map/all_gather | solution.py:99
  9.1 108.5 %reduce-scatter.2.cloned.1.call-start = ((), (), s32[]{:S(2)}) async-start(), calls=%async_computation.4 | async-start | bytes 3538944 | tf_op jit(solution)/shard_map/reduce_scatter | solution.py:144
  71.2 46.4 %copy-start = (f32[384,512]{1,0:T(8,128)S(1)}, f32[384,512]{1,0:T(8,128)}, u32[]{:S(2)}) copy-start(f32[384,512]{1,0:T(8,128)} %get-tuple-element.8) | copy-start | bytes 2359300
  71.2 48.8 %all-to-all-start = ((bf16[4,96,1536]{2,1,0:T(8,128)(2,1)}), bf16[4,96,1536]{2,1,0:T(8,128)(2,1)S(1)}, u32[]{:S(2)}, u32[]{:S(2)}) async-start(bf16[4,96,1536]{2,1,0:T(8,128)(2,1)} %bitcast), calls=%async_computation | async-start | bytes 2359296 | tf_op jit(solution)/shard_map/all_to_all | solution.py:148
  120.0 16.3 %all-to-all-start.1 = ((bf16[4,96,512]{2,1,0:T(8,128)(2,1)}), bf16[4,96,512]{2,1,0:T(8,128)(2,1)S(1)}, u32[]{:S(2)}, u32[]{:S(2)}) async-start(bf16[4,96,512]{2,1,0:T(8,128)(2,1)} %convert_element_type.20), calls=%async_computation.2 | async-start | bytes 786432 | tf_op jit(solution)/shard_map/all_to_all | solution.py:149
Sparse Core Ops, SparseCore 0:
  10.5 35.0 all-gather.1
  71.3 46.2 reduce-scatter.1

commit v6 on v5

--- a/solution.py
+++ b/solution.py
@@ -16,10 +16,10 @@
 
 
 def attention_kernel(
-    blk_ref, dst_ref, kind_ref,
-    q_ref, do_ref, k_ref, v_ref,
-    dq_ref, loc_ref, far_ref,
-    kc_ref, vc_ref, loc_acc, far_acc,
+    blk_ref, side_ref, dst_ref, kind_ref,
+    q_ref, do_ref, k_ref, v_ref, ko_ref, vo_ref,
+    dq_ref, loc_ref, far_ref, fo_ref,
+    kc_ref, vc_ref, loc_acc, far_acc, fo_acc,
     *, hpk, kv_here, nb,
 ):
     g = pl.program_id(0)
@@ -30,11 +30,16 @@
     def _():
         loc_acc[...] = jnp.zeros_like(loc_acc)
         far_acc[...] = jnp.zeros_like(far_acc)
+        fo_acc[...] = jnp.zeros_like(fo_acc)
 
     for s in range(SLOTS):
         row = pl.multiple_of(blk_ref[b * SLOTS + s] * BLK, BLK)
-        kc_ref[s * BLK:(s + 1) * BLK, :] = k_ref[pl.ds(row, BLK), :]
-        vc_ref[s * BLK:(s + 1) * BLK, :] = v_ref[pl.ds(row, BLK), :]
+        side = side_ref[b * SLOTS + s]
+        for code, tk, tv in ((0, k_ref, v_ref), (1, ko_ref, vo_ref)):
+            @pl.when(side == code)
+            def _():
+                kc_ref[s * BLK:(s + 1) * BLK, :] = tk[pl.ds(row, BLK), :]
+                vc_ref[s * BLK:(s + 1) * BLK, :] = tv[pl.ds(row, BLK), :]
 
     kc = kc_ref[...]
     vc = vc_ref[...]
@@ -71,16 +76,24 @@
             loc_acc[g, pl.ds(row, BLK), :] += kt
             loc_acc[kv_here + g, pl.ds(row, BLK), :] += vt
 
-        @pl.when(kind != 2)
+        side = side_ref[b * SLOTS + s]
+
+        @pl.when((kind != 2) & (side == 0))
         def _():
             far_acc[g, pl.ds(row, BLK), :] += kt
             far_acc[kv_here + g, pl.ds(row, BLK), :] += vt
+
+        @pl.when((kind != 2) & (side == 1))
+        def _():
+            fo_acc[g, pl.ds(row, BLK), :] += kt
+            fo_acc[kv_here + g, pl.ds(row, BLK), :] += vt
 
     @pl.when((g == kv_here - 1) & (b == nb - 1))
     def _():
         for j in range(2 * kv_here):
             loc_ref[:, j * HD:(j + 1) * HD] = loc_acc[j]
             far_ref[:, j * HD:(j + 1) * HD] = far_acc[j].astype(jnp.bfloat16)
+            fo_ref[:, j * HD:(j + 1) * HD] = fo_acc[j].astype(jnp.bfloat16)
 
 
 def shards(query_rows, key_rows, value_rows, out_grad, block_list):
@@ -96,7 +109,13 @@
     key_own = lax.dynamic_slice_in_dim(key_rows, first_kv * HD, kv_here * HD, axis=1)
     value_own = lax.dynamic_slice_in_dim(value_rows, first_kv * HD, kv_here * HD, axis=1)
     kv_own = jnp.concatenate([key_own, value_own], axis=1)
-    kv_all = lax.all_gather(kv_own, "ctx", axis=0, tiled=True)
+    shard_count = lax.axis_size("ctx")
+    groups = [[i for i in range(shard_count) if i % 2 == p] for p in range(2)]
+    partner = [(i, i ^ 1) for i in range(shard_count)]
+    core = shard_index % 2
+    kv_half = lax.all_gather(kv_own, "ctx", axis=0, tiled=True, axis_index_groups=groups)
+    kv_other = lax.ppermute(kv_half, "ctx", partner)
+    half = seq // 2
 
     rows = lax.dynamic_slice_in_dim(block_list, shard_index * nb, nb, axis=0).astype(jnp.int32)
     owner = rows // nb
@@ -105,43 +124,55 @@
     local = owner == shard_index
     remote = jnp.logical_not(local) & jnp.logical_not(is_global)
     kind = jnp.where(local, 2, jnp.where(remote, 0, 1)).astype(jnp.int32).reshape(-1)
-    dst = jnp.where(local, rows - shard_index * nb, rows).astype(jnp.int32).reshape(-1)
-    blk = rows.reshape(-1)
+    owner_side = (owner % 2 != core).astype(jnp.int32)
+    half_row = (owner // 2) * nb + rows % nb
+    dst = jnp.where(local, rows - shard_index * nb, half_row).astype(jnp.int32).reshape(-1)
+    blk = half_row.astype(jnp.int32).reshape(-1)
+    side = owner_side.reshape(-1)
 
     kernel = functools.partial(attention_kernel, hpk=hpk, kv_here=kv_here, nb=nb)
     grid_spec = pltpu.PrefetchScalarGridSpec(
-        num_scalar_prefetch=3,
+        num_scalar_prefetch=4,
         grid=(kv_here, nb),
         in_specs=[
             pl.BlockSpec((BLK, hpk * HD), lambda g, b, *_: (b, g)),
             pl.BlockSpec((BLK, hpk * HD), lambda g, b, *_: (b, g)),
-            pl.BlockSpec((seq, HD), lambda g, b, *_: (0, g)),
-            pl.BlockSpec((seq, HD), lambda g, b, *_: (0, kv_here + g)),
+            pl.BlockSpec((half, HD), lambda g, b, *_: (0, g)),
+            pl.BlockSpec((half, HD), lambda g, b, *_: (0, kv_here + g)),
+            pl.BlockSpec((half, HD), lambda g, b, *_: (0, g)),
+            pl.BlockSpec((half, HD), lambda g, b, *_: (0, kv_here + g)),
         ],
         out_specs=[
             pl.BlockSpec((BLK, hpk * HD), lambda g, b, *_: (b, g)),
             pl.BlockSpec((nb * BLK, width), lambda g, b, *_: (0, 0)),
-            pl.BlockSpec((seq, width), lambda g, b, *_: (0, 0)),
+            pl.BlockSpec((half, width), lambda g, b, *_: (0, 0)),
+            pl.BlockSpec((half, width), lambda g, b, *_: (0, 0)),
         ],
         scratch_shapes=[
             pltpu.VMEM((SLOTS * BLK, HD), jnp.bfloat16),
             pltpu.VMEM((SLOTS * BLK, HD), jnp.bfloat16),
             pltpu.VMEM((2 * kv_here, nb * BLK, HD), jnp.float32),
-            pltpu.VMEM((2 * kv_here, seq, HD), jnp.float32),
+            pltpu.VMEM((2 * kv_here, half, HD), jnp.float32),
+            pltpu.VMEM((2 * kv_here, half, HD), jnp.float32),
         ],
     )
-    dq, loc, far = pl.pallas_call(
+    dq, loc, far, far_other = pl.pallas_call(
         kernel,
         grid_spec=grid_spec,
         out_shape=[
             jax.ShapeDtypeStruct((nb * BLK, heads_here * HD), jnp.bfloat16),
             jax.ShapeDtypeStruct((nb * BLK, width), jnp.float32),
-            jax.ShapeDtypeStruct((seq, width), jnp.bfloat16),
+            jax.ShapeDtypeStruct((half, width), jnp.bfloat16),
+            jax.ShapeDtypeStruct((half, width), jnp.bfloat16),
         ],
         compiler_params=pltpu.CompilerParams(dimension_semantics=("arbitrary", "arbitrary")),
-    )(blk, dst, kind, query_rows, out_grad, kv_all, kv_all)
-
-    got = lax.psum_scatter(far, "ctx", scatter_dimension=0, tiled=True)
+    )(blk, side, dst, kind, query_rows, out_grad, kv_half, kv_half, kv_other, kv_other)
+
+    from_partner = lax.ppermute(far_other, "ctx", partner)
+    mine = (far.astype(jnp.float32) + from_partner.astype(jnp.float32)).astype(jnp.bfloat16)
+    got = lax.psum_scatter(
+        mine, "ctx", scatter_dimension=0, tiled=True, axis_index_groups=groups
+    )
     kv_sum = (got.astype(jnp.float32) + loc).reshape(nb, HD, 2 * kv_here, BLK)
     kv_grad = jnp.transpose(kv_sum, (0, 3, 2, 1)).reshape(nb * BLK, width).astype(jnp.bfloat16)
 

time: 146 us -> 142 us (0.973)
  waiting for transfers between devices: 86.5 us -> 76 us
  other arithmetic: 2 us -> 5.15 us
  local copies, waits for them, and re-layouts: 8.06 us -> 10 us
    reduce_scatter x1, waiting for transfers between devices: 41.7 us -> 26.4 us  [shards(): lax.psum_scatter(mine, 'ctx', scatter_dimension=0, tiled=True, axis_index...]
    ppermute x0 -> x2, waiting for transfers between devices: none -> 3.98 us  [the longest x1 3.46 us: shards(): from_partner = lax.ppermute(far_other, 'ctx', partner)]
    convert_element_type x0 -> x1, other arithmetic: none -> 2.98 us  [shards(): (far.astype(jnp.float32) + from_partner.astype(jnp.float32)).astype(jnp.b...]
  transfers between devices with their start and end apart: 4 -> 6, of which waited for: 3 -> 6; matrix products, arithmetic and copies ran while one was open for 4% -> 5% of each run, Pallas kernels for 0% -> 0%
where the time goes in v6:
time: 142 us; the launch traced here: 141 us
  waiting for transfers between devices  76 us (54%)
  Pallas kernels  26.6 us (19%)
  between operations  14.1 us (10%)
  local copies, waits for them, and re-layouts  10 us (7%)
  starting transfers between devices  9.58 us (7%)
  other arithmetic  5.15 us (4%)
    all_gather x1, waiting for transfers between devices, shards(): lax.all_gather(kv_own, 'ctx', axis=0, tiled=True, axis_index_groups=groups)  35 us
    pallas_call x1, Pallas kernels, shards(): pl.pallas_call(kernel, grid_spec=grid_spec, out_shape=[jax.ShapeDtypeStru...  26.6 us
    reduce_scatter x1, waiting for transfers between devices, shards(): lax.psum_scatter(mine, 'ctx', scatter_dimension=0, tiled=True, axis_index...  26.4 us
    all_to_all x1, waiting for transfers between devices, shards(): lax.all_to_all(kv_grad, 'uly', split_axis=0, concat_axis=1, tiled=True)  10.5 us
    all_to_all x1, starting transfers between devices, shards(): lax.all_to_all(dq, 'uly', split_axis=0, concat_axis=1, tiled=True)  4.75 us
    all_to_all x1, starting transfers between devices, shards(): lax.all_to_all(kv_grad, 'uly', split_axis=0, concat_axis=1, tiled=True)  4.52 us
    ppermute x1, waiting for transfers between devices, shards(): from_partner = lax.ppermute(far_other, 'ctx', partner)  3.46 us
    convert_element_type x1, other arithmetic, shards(): (far.astype(jnp.float32) + from_partner.astype(jnp.float32)).astype(jnp.b...  2.98 us
  transfers between devices with their start and end apart: 6, of which 6 were waited for; matrix products, arithmetic and copies ran while one was open for 5% of the time, Pallas kernels for 0%

profile of v6, /device:TPU:0, one launch (start us, length us, event | category | flops | bytes accessed | tf_op | source)
XLA Modules:
  0.0 141.4 jit_solution(12197978013480988813)
XLA Ops:
  7.3 1.1 constant_dynamic-slice_fusion
  8.3 0.8 pad_maximum_fusion
  9.2 35.0 %all-gather.2.cloned.1.call-done.k_ref.v_ref = bf16[1536,512]{1,0:T(8,128)(2,1)} async-done(((bf16[384,512]{1,0:T(8,128)(2,1)}), bf16[1536,512]{1,0:T(8,128)(2,1)}) %all-gather.2.cloned.1.call-update) | async-done | bytes 1572880 | tf_op jit(solution)/shard_map/all_gather | solution.py:116
  44.1 0.1 fusion.5
  44.2 0.1 copy.20
  44.3 0.6 reshape.55.side_ref
  44.9 0.1 select_select_fusion
  45.1 0.7 reshape.52.kind_ref
  45.8 0.1 subtract_select_fusion
  45.9 0.6 reshape.51.dst_ref
  46.6 0.6 reshape.48.blk_ref
  47.2 0.5 collective-permute-done.ko_ref.vo_ref
  47.8 1.2 copy-done
  48.9 26.6 %shard_map.76 = (bf16[384,1536]{1,0:T(8,128)(2,1)}, f32[384,512]{1,0:T(8,128)}, bf16[1536,512]{1,0:T(8,128)(2,1)}, bf16[1536,512]{1,0:T(8,128)(2,1)}) custom-call(s32[24]{0:T(128)} %reshape.48.blk_ref, s32[24]{0:T(128)} %reshape.55.side_ref, s32[24]{0:T(128)} %reshape.51.dst_ref, s32[24]{0:T(128)} %reshape.52.kind_ref, bf16[384,1536]{1,0:T(8,128)(2,1)} %q_ref.1, ...), custom_call_target="tpu_custom_call" | custom-call | tf_op jit(solution)/shard_map/pallas_call | solution.py:159
  75.5 0.2 collective-permute-start.1
  75.7 3.5 %collective-permute-done.1 = bf16[1536,512]{1,0:T(8,128)(2,1)S(1)} collective-permute-done((bf16[1536,512]{1,0:T(8,128)(2,1)}, bf16[1536,512]{1,0:T(8,128)(2,1)S(1)}, u32[]{:S(2)}, u32[]{:S(2)}) %collective-permute-start.1) | collective-permute-done | bytes 1572896 | tf_op jit(solution)/shard_map/ppermute | solution.py:171
  79.2 3.0 %add_convert_fusion = bf16[1536,512]{1,0:T(8,128)(2,1)} fusion(bf16[1536,512]{1,0:T(8,128)(2,1)S(1)} %collective-permute-done.1, bf16[1536,512]{1,0:T(8,128)(2,1)} %get-tuple-element.8), kind=kLoop, calls=%fused_computation | loop fusion | flops 3145728 | bytes 4718592 | tf_op jit(solution)/shard_map/convert_element_type | solution.py:172
  82.2 4.7 %all-to-all-start = ((bf16[4,96,1536]{2,1,0:T(8,128)(2,1)}), bf16[4,96,1536]{2,1,0:T(8,128)(2,1)S(1)}, u32[]{:S(2)}, u32[]{:S(2)}) async-start(bf16[4,96,1536]{2,1,0:T(8,128)(2,1)} %bitcast), calls=%async_computation | async-start | bytes 2359296 | tf_op jit(solution)/shard_map/all_to_all | solution.py:179
  86.9 26.4 %reduce-scatter.2.cloned.1.call-done = bf16[384,512]{1,0:T(8,128)(2,1)} async-done(((bf16[1536,512]{1,0:T(8,128)(2,1)}), bf16[384,512]{1,0:T(8,128)(2,1)}) %reduce-scatter.2.cloned.1.call-update) | async-done | bytes 393232 | tf_op jit(solution)/shard_map/reduce_scatter | solution.py:173
  113.3 1.1 add_convert_fusion.1
  114.4 0.1 convert_element_type.31
  114.5 0.3 copy.24
  114.8 0.9 convert_element_type.33
  115.8 4.5 %all-to-all-start.1 = ((bf16[4,96,512]{2,1,0:T(8,128)(2,1)}), bf16[4,96,512]{2,1,0:T(8,128)(2,1)S(1)}, u32[]{:S(2)}, u32[]{:S(2)}) async-start(bf16[4,96,512]{2,1,0:T(8,128)(2,1)} %convert_element_type.33), calls=%async_computation.2 | async-start | bytes 786432 | tf_op jit(solution)/shard_map/all_to_all | solution.py:180
  120.3 1.1 copy.27
  121.5 10.5 %all-to-all-done.1 = bf16[4,96,512]{2,1,0:T(8,128)(2,1)S(1)} async-done(((bf16[4,96,512]{2,1,0:T(8,128)(2,1)}), bf16[4,96,512]{2,1,0:T(8,128)(2,1)S(1)}, u32[]{:S(2)}, u32[]{:S(2)}) %all-to-all-start.1) | async-done | bytes 393248 | tf_op jit(solution)/shard_map/all_to_all | solution.py:180
  132.0 0.1 reshape.53
  132.1 0.5 fusion.8
  132.6 0.3 copy.26
  132.9 0.7 copy.29
  133.6 0.3 copy.25
  133.9 0.7 copy.28
  (15 shorter events, 0.5 us)
Async XLA Ops:
  7.2 37.0 %copy-start.2 = (s32[24,8]{0,1:T(8,128)S(1)}, s32[24,8]{0,1:T(8,128)}, u32[]{:S(2)}) copy-start(s32[24,8]{0,1:T(8,128)} %param.9) | copy-start | bytes 2308
  7.2 37.0 %all-gather.2.cloned.1.call-start = ((), (), s32[]{:S(2)}) async-start(), calls=%async_computation.3 | async-start | bytes 1966080 | tf_op jit(solution)/shard_map/all_gather | solution.py:116
  9.1 104.2 %reduce-scatter.2.cloned.1.call-start = ((), (), s32[]{:S(2)}) async-start(), calls=%async_computation.4 | async-start | bytes 1966080 | tf_op jit(solution)/shard_map/reduce_scatter | solution.py:173
  44.1 3.6 %collective-permute-start = (bf16[1536,512]{1,0:T(8,128)(2,1)}, bf16[1536,512]{1,0:T(8,128)(2,1)S(1)}, u32[]{:S(2)}, u32[]{:S(2)}) collective-permute-start(bf16[1536,512]{1,0:T(8,128)(2,1)} %all-gather.2.cloned.1.call-done.k_ref.v_ref), channel_id=1, source_target_pairs={{0,4},{4,0},{8,12},{12,8},{16,20},{20,16},{24,28},{28,24},{1,5},{5... | collective-permute-start | bytes 4718600 | tf_op jit(solution)/shard_map/ppermute | solution.py:117
  47.8 1.2 copy-start
  75.5 3.7 %collective-permute-start.1 = (bf16[1536,512]{1,0:T(8,128)(2,1)}, bf16[1536,512]{1,0:T(8,128)(2,1)S(1)}, u32[]{:S(2)}, u32[]{:S(2)}) collective-permute-start(bf16[1536,512]{1,0:T(8,128)(2,1)} %get-tuple-element.9), channel_id=1, source_target_pairs={{0,4},{4,0},{8,12},{12,8},{16,20},{20,16},{24,28},{28,24},{1,5},{5... | collective-permute-start | bytes 4718600 | tf_op jit(solution)/shard_map/ppermute | solution.py:171
  82.2 31.1 %copy-start.1 = (f32[384,512]{1,0:T(8,128)S(1)}, f32[384,512]{1,0:T(8,128)}, u32[]{:S(2)}) copy-start(f32[384,512]{1,0:T(8,128)} %get-tuple-element.10) | copy-start | bytes 2359300
  82.2 33.6 %all-to-all-start = ((bf16[4,96,1536]{2,1,0:T(8,128)(2,1)}), bf16[4,96,1536]{2,1,0:T(8,128)(2,1)S(1)}, u32[]{:S(2)}, u32[]{:S(2)}) async-start(bf16[4,96,1536]{2,1,0:T(8,128)(2,1)} %bitcast), calls=%async_computation | async-start | bytes 2359296 | tf_op jit(solution)/shard_map/all_to_all | solution.py:179
  115.8 16.2 %all-to-all-start.1 = ((bf16[4,96,512]{2,1,0:T(8,128)(2,1)}), bf16[4,96,512]{2,1,0:T(8,128)(2,1)S(1)}, u32[]{:S(2)}, u32[]{:S(2)}) async-start(bf16[4,96,512]{2,1,0:T(8,128)(2,1)} %convert_element_type.33), calls=%async_computation.2 | async-start | bytes 786432 | tf_op jit(solution)/shard_map/all_to_all | solution.py:180
Sparse Core Ops, SparseCore 0:
  10.4 33.6 all-gather.1
  82.3 30.9 reduce-scatter.1

commit v7 on v6

--- a/solution.py
+++ b/solution.py
@@ -110,10 +110,15 @@
     value_own = lax.dynamic_slice_in_dim(value_rows, first_kv * HD, kv_here * HD, axis=1)
     kv_own = jnp.concatenate([key_own, value_own], axis=1)
     shard_count = lax.axis_size("ctx")
-    groups = [[i for i in range(shard_count) if i % 2 == p] for p in range(2)]
     partner = [(i, i ^ 1) for i in range(shard_count)]
     core = shard_index % 2
-    kv_half = lax.all_gather(kv_own, "ctx", axis=0, tiled=True, axis_index_groups=groups)
+    members = shard_count // 2
+    member = shard_index // 2
+    gathered = [kv_own]
+    for d in range(1, members):
+        pairs = [(i, (i + 2 * d) % shard_count) for i in range(shard_count)]
+        gathered.append(lax.ppermute(kv_own, "ctx", pairs))
+    kv_half = jnp.concatenate(gathered, axis=0)
     kv_other = lax.ppermute(kv_half, "ctx", partner)
     half = seq // 2
 
@@ -125,7 +130,7 @@
     remote = jnp.logical_not(local) & jnp.logical_not(is_global)
     kind = jnp.where(local, 2, jnp.where(remote, 0, 1)).astype(jnp.int32).reshape(-1)
     owner_side = (owner % 2 != core).astype(jnp.int32)
-    half_row = (owner // 2) * nb + rows % nb
+    half_row = ((member - owner // 2) % members) * nb + rows % nb
     dst = jnp.where(local, rows - shard_index * nb, half_row).astype(jnp.int32).reshape(-1)
     blk = half_row.astype(jnp.int32).reshape(-1)
     side = owner_side.reshape(-1)
@@ -170,10 +175,13 @@
 
     from_partner = lax.ppermute(far_other, "ctx", partner)
     mine = (far.astype(jnp.float32) + from_partner.astype(jnp.float32)).astype(jnp.bfloat16)
-    got = lax.psum_scatter(
-        mine, "ctx", scatter_dimension=0, tiled=True, axis_index_groups=groups
-    )
-    kv_sum = (got.astype(jnp.float32) + loc).reshape(nb, HD, 2 * kv_here, BLK)
+    total = far[0:nb * BLK].astype(jnp.float32) + from_partner[0:nb * BLK].astype(jnp.float32)
+    for d in range(1, members):
+        pairs = [(i, (i - 2 * d) % shard_count) for i in range(shard_count)]
+        total = total + lax.ppermute(
+            mine[d * nb * BLK:(d + 1) * nb * BLK], "ctx", pairs
+        ).astype(jnp.float32)
+    kv_sum = (total + loc).reshape(nb, HD, 2 * kv_here, BLK)
     kv_grad = jnp.transpose(kv_sum, (0, 3, 2, 1)).reshape(nb * BLK, width).astype(jnp.bfloat16)
 
     query_out = lax.all_to_all(dq, "uly", split_axis=0, concat_axis=1, tiled=True)

time: 142 us -> 108 us (0.76)
  waiting for transfers between devices: 76 us -> 49.9 us
  between operations: 14.1 us -> 0.82 us
  starting transfers between devices: 9.58 us -> 16.5 us
  other arithmetic: 5.15 us -> 3.59 us
    ppermute x0 -> x6, waiting for transfers between devices: none -> 36.3 us  [the longest x3 18.4 us: shards(): lax.ppermute(mine[d * nb * BLK:(d + 1) * nb * BLK], 'ctx', pairs)]
    all_gather x1 -> x0, waiting for transfers between devices: 35 us -> none  [shards(): lax.all_gather(kv_own, 'ctx', axis=0, tiled=True, axis_index_groups=groups)]
    reduce_scatter x1 -> x0, waiting for transfers between devices: 26.4 us -> none  [shards(): lax.psum_scatter(mine, 'ctx', scatter_dimension=0, tiled=True, axis_index...]
    ppermute x0 -> x6, starting transfers between devices: none -> 7.63 us  [the longest x3 5.04 us: shards(): gathered.append(lax.ppermute(kv_own, 'ctx', pairs))]
    ppermute x1, waiting for transfers between devices: 3.46 us -> 0.01 us  [shards(): from_partner = lax.ppermute(far_other, 'ctx', partner)]
    all_to_all x1, waiting for transfers between devices: 0.08 us -> 3.44 us  [shards(): lax.all_to_all(dq, 'uly', split_axis=0, concat_axis=1, tiled=True)]
  transfers between devices with their start and end apart: 6 -> 10, of which waited for: 6 -> 8; matrix products, arithmetic and copies ran while one was open for 5% -> 8% of each run, Pallas kernels for 0% -> 0%
where the time goes in v7:
time: 108 us
  waiting for transfers between devices  49.9 us (46%)
  Pallas kernels  26.5 us (25%)
  starting transfers between devices  16.5 us (15%)
  local copies, waits for them, and re-layouts  10.3 us (10%)
  other arithmetic  3.59 us (3%)
    pallas_call x1, Pallas kernels, shards(): pl.pallas_call(kernel, grid_spec=grid_spec, out_shape=[jax.ShapeDtypeStru...  26.5 us
    ppermute x3, waiting for transfers between devices, shards(): lax.ppermute(mine[d * nb * BLK:(d + 1) * nb * BLK], 'ctx', pairs)  18.4 us
    ppermute x3, waiting for transfers between devices, shards(): gathered.append(lax.ppermute(kv_own, 'ctx', pairs))  17.9 us
    all_to_all x1, waiting for transfers between devices, shards(): lax.all_to_all(kv_grad, 'uly', split_axis=0, concat_axis=1, tiled=True)  10.1 us
    ppermute x3, starting transfers between devices, shards(): gathered.append(lax.ppermute(kv_own, 'ctx', pairs))  5.04 us
    all_to_all x1, starting transfers between devices, shards(): lax.all_to_all(dq, 'uly', split_axis=0, concat_axis=1, tiled=True)  5 us
    all_to_all x1, starting transfers between devices, shards(): lax.all_to_all(kv_grad, 'uly', split_axis=0, concat_axis=1, tiled=True)  3.46 us
    all_to_all x1, waiting for transfers between devices, shards(): lax.all_to_all(dq, 'uly', split_axis=0, concat_axis=1, tiled=True)  3.44 us
  transfers between devices with their start and end apart: 10, of which 8 were waited for; matrix products, arithmetic and copies ran while one was open for 8% of the time, Pallas kernels for 0%

profile of v7, /device:TPU:0, one launch (start us, length us, event | category | flops | bytes accessed | tf_op | source)
XLA Modules:
  0.0 107.6 jit_solution(11993078252327532500)
XLA Ops:
  0.7 1.1 constant_dynamic-slice_fusion
  1.8 3.9 %collective-permute-start.2 = (bf16[384,512]{1,0:T(8,128)(2,1)S(1)}, bf16[384,512]{1,0:T(8,128)(2,1)S(1)}, u32[]{:S(2)}, u32[]{:S(2)}) collective-permute-start(bf16[384,512]{1,0:T(8,128)(2,1)S(1)} %pad_maximum_fusion.1), channel_id=1, source_target_pairs={{0,24},{4,28},{8,0},{12,4},{16,8},{20,12},{24,16},{28,20},{1,25},{... | collective-permute-start | bytes 1179656 | tf_op jit(solution)/shard_map/ppermute | solution.py:120
  5.7 0.5 collective-permute-start.1
  6.2 0.6 collective-permute-start
  6.8 8.4 %collective-permute-done.2 = bf16[384,512]{1,0:T(8,128)(2,1)S(1)} collective-permute-done((bf16[384,512]{1,0:T(8,128)(2,1)S(1)}, bf16[384,512]{1,0:T(8,128)(2,1)S(1)}, u32[]{:S(2)}, u32[]{:S(2)}) %collective-permute-start.2) | collective-permute-done | bytes 393248 | tf_op jit(solution)/shard_map/ppermute | solution.py:120
  15.2 9.5 %collective-permute-done.1 = bf16[384,512]{1,0:T(8,128)(2,1)S(1)} collective-permute-done((bf16[384,512]{1,0:T(8,128)(2,1)S(1)}, bf16[384,512]{1,0:T(8,128)(2,1)S(1)}, u32[]{:S(2)}, u32[]{:S(2)}) %collective-permute-start.1) | collective-permute-done | bytes 393248 | tf_op jit(solution)/shard_map/ppermute | solution.py:120
  25.1 0.7 reshape.55.side_ref
  26.0 0.7 reshape.52.kind_ref
  26.9 0.6 reshape.51.dst_ref
  27.6 0.6 reshape.48.blk_ref
  28.3 1.2 %copy-done.1 = bf16[1536,512]{1,0:T(8,128)(2,1)} copy-done((bf16[1536,512]{1,0:T(8,128)(2,1)}, bf16[1536,512]{1,0:T(8,128)(2,1)S(1)}, u32[]{:S(2)}) %copy-start.1) | copy-done | bytes 1572888
  29.5 26.5 %shard_map.76 = (bf16[384,1536]{1,0:T(8,128)(2,1)}, f32[384,512]{1,0:T(8,128)}, bf16[1536,512]{1,0:T(8,128)(2,1)}, bf16[1536,512]{1,0:T(8,128)(2,1)}) custom-call(s32[24]{0:T(128)} %reshape.48.blk_ref, s32[24]{0:T(128)} %reshape.55.side_ref, s32[24]{0:T(128)} %reshape.51.dst_ref, s32[24]{0:T(128)} %reshape.52.kind_ref, bf16[384,1536]{1,0:T(8,128)(2,1)} %q_ref.1, ...), custom_call_target="tpu_custom_call" | custom-call | tf_op jit(solution)/shard_map/pallas_call | solution.py:164
  56.0 0.3 collective-permute-start.4
  56.4 5.0 %all-to-all-start = ((bf16[4,96,1536]{2,1,0:T(8,128)(2,1)}), bf16[4,96,1536]{2,1,0:T(8,128)(2,1)S(1)}, u32[]{:S(2)}, u32[]{:S(2)}) async-start(bf16[4,96,1536]{2,1,0:T(8,128)(2,1)} %bitcast.19), calls=%async_computation | async-start | bytes 2359296 | tf_op jit(solution)/shard_map/all_to_all | solution.py:187
  61.4 1.8 %add_convert_fusion = bf16[1536,512]{1,0:T(8,128)(2,1)S(1)} fusion(bf16[1536,512]{1,0:T(8,128)(2,1)} %collective-permute-done.4, bf16[1536,512]{1,0:T(8,128)(2,1)S(1)} %copy-done.2), kind=kLoop, calls=%fused_computation | loop fusion | flops 3145728 | bytes 4718592 | tf_op jit(solution)/shard_map/convert_element_type | solution.py:177
  63.3 0.6 collective-permute-start.5
  63.9 1.5 %collective-permute-start.7 = (bf16[384,512]{1,0:T(8,128)(2,1)S(1)}, bf16[384,512]{1,0:T(8,128)(2,1)S(1)}, u32[]{:S(2)}, u32[]{:S(2)}) collective-permute-start(bf16[384,512]{1,0:T(8,128)(2,1)S(1)} %get-tuple-element.16), channel_id=1, source_target_pairs={{0,8},{4,12},{8,16},{12,20},{16,24},{20,28},{24,0},{28,4},{1,9},{5... | collective-permute-start | bytes 1179656 | tf_op jit(solution)/shard_map/ppermute | solution.py:181
  65.4 0.5 collective-permute-start.6
  65.9 9.4 %collective-permute-done.5 = bf16[384,512]{1,0:T(8,128)(2,1)S(1)} collective-permute-done((bf16[384,512]{1,0:T(8,128)(2,1)S(1)}, bf16[384,512]{1,0:T(8,128)(2,1)S(1)}, u32[]{:S(2)}, u32[]{:S(2)}) %collective-permute-start.5) | collective-permute-done | bytes 393248 | tf_op jit(solution)/shard_map/ppermute | solution.py:181
  75.4 7.5 %collective-permute-done.7 = bf16[384,512]{1,0:T(8,128)(2,1)S(1)} collective-permute-done((bf16[384,512]{1,0:T(8,128)(2,1)S(1)}, bf16[384,512]{1,0:T(8,128)(2,1)S(1)}, u32[]{:S(2)}, u32[]{:S(2)}) %collective-permute-start.7) | collective-permute-done | bytes 393248 | tf_op jit(solution)/shard_map/ppermute | solution.py:181
  82.9 1.4 %collective-permute-done.6 = bf16[384,512]{1,0:T(8,128)(2,1)S(1)} collective-permute-done((bf16[384,512]{1,0:T(8,128)(2,1)S(1)}, bf16[384,512]{1,0:T(8,128)(2,1)S(1)}, u32[]{:S(2)}, u32[]{:S(2)}) %collective-permute-start.6) | collective-permute-done | bytes 393248 | tf_op jit(solution)/shard_map/ppermute | solution.py:181
  84.3 1.3 %add_convert_fusion.1 = bf16[384,512]{1,0:T(8,128)(2,1)S(1)} fusion(f32[384,512]{1,0:T(8,128)S(1)} %copy-done.3, bf16[384,512]{1,0:T(8,128)(2,1)S(1)} %collective-permute-done.7, bf16[384,512]{1,0:T(8,128)(2,1)S(1)} %collective-permute-done.6, bf16[384,512]{1,0:T(8,128)(2,1)S(1)} %collective-permute-done.5, bf16[1536,512]{1,0:T(8,128)(2,1)} %collective-permute-done.4, ...), kind=kLoop, calls=%fused_computation.2 | loop fusion | flops 2162688 | bytes 3145728 | tf_op jit(solution)/shard_map/convert_element_type | solution.py:185
  85.7 0.3 copy.24
  86.0 0.9 convert_element_type.49
  86.9 3.4 %all-to-all-done = bf16[4,96,1536]{2,1,0:T(8,128)(2,1)S(1)} async-done(((bf16[4,96,1536]{2,1,0:T(8,128)(2,1)}), bf16[4,96,1536]{2,1,0:T(8,128)(2,1)S(1)}, u32[]{:S(2)}, u32[]{:S(2)}) %all-to-all-start) | async-done | bytes 1179680 | tf_op jit(solution)/shard_map/all_to_all | solution.py:187
  90.3 3.5 %all-to-all-start.1 = ((bf16[4,96,512]{2,1,0:T(8,128)(2,1)}), bf16[4,96,512]{2,1,0:T(8,128)(2,1)S(1)}, u32[]{:S(2)}, u32[]{:S(2)}) async-start(bf16[4,96,512]{2,1,0:T(8,128)(2,1)} %convert_element_type.49), calls=%async_computation.1 | async-start | bytes 786432 | tf_op jit(solution)/shard_map/all_to_all | solution.py:188
  93.8 1.1 %copy.27 = bf16[4,12,8,1536]{3,2,0,1:T(8,128)(2,1)} copy(bf16[4,12,8,1536]{3,2,1,0:T(8,128)(2,1)S(1)} %bitcast.16) | data formatting | bytes 2359296 | tf_op jit(solution)/shard_map/all_to_all | solution.py:187
  94.9 10.1 %all-to-all-done.1 = bf16[4,96,512]{2,1,0:T(8,128)(2,1)S(1)} async-done(((bf16[4,96,512]{2,1,0:T(8,128)(2,1)}), bf16[4,96,512]{2,1,0:T(8,128)(2,1)S(1)}, u32[]{:S(2)}, u32[]{:S(2)}) %all-to-all-start.1) | async-done | bytes 393248 | tf_op jit(solution)/shard_map/all_to_all | solution.py:188
  105.1 0.5 fusion.11
  105.7 0.3 copy.26
  105.9 0.7 copy.29
  106.9 0.7 copy.28
  (27 shorter events, 1.5 us)
Async XLA Ops:
  1.8 23.2 %copy-start.4 = (s32[24,8]{0,1:T(8,128)S(1)}, s32[24,8]{0,1:T(8,128)}, u32[]{:S(2)}) copy-start(s32[24,8]{0,1:T(8,128)} %param.9) | copy-start | bytes 2308
  1.8 13.5 %collective-permute-start.2 = (bf16[384,512]{1,0:T(8,128)(2,1)S(1)}, bf16[384,512]{1,0:T(8,128)(2,1)S(1)}, u32[]{:S(2)}, u32[]{:S(2)}) collective-permute-start(bf16[384,512]{1,0:T(8,128)(2,1)S(1)} %pad_maximum_fusion.1), channel_id=1, source_target_pairs={{0,24},{4,28},{8,0},{12,4},{16,8},{20,12},{24,16},{28,20},{1,25},{... | collective-permute-start | bytes 1179656 | tf_op jit(solution)/shard_map/ppermute | solution.py:120
  5.7 19.0 %collective-permute-start.1 = (bf16[384,512]{1,0:T(8,128)(2,1)S(1)}, bf16[384,512]{1,0:T(8,128)(2,1)S(1)}, u32[]{:S(2)}, u32[]{:S(2)}) collective-permute-start(bf16[384,512]{1,0:T(8,128)(2,1)S(1)} %pad_maximum_fusion.1), channel_id=1, source_target_pairs={{0,16},{4,20},{8,24},{12,28},{16,0},{20,4},{24,8},{28,12},{1,17},{... | collective-permute-start | bytes 1179656 | tf_op jit(solution)/shard_map/ppermute | solution.py:120
  6.2 18.5 %collective-permute-start = (bf16[384,512]{1,0:T(8,128)(2,1)S(1)}, bf16[384,512]{1,0:T(8,128)(2,1)S(1)}, u32[]{:S(2)}, u32[]{:S(2)}) collective-permute-start(bf16[384,512]{1,0:T(8,128)(2,1)S(1)} %pad_maximum_fusion.1), channel_id=1, source_target_pairs={{0,8},{4,12},{8,16},{12,20},{16,24},{20,28},{24,0},{28,4},{1,9},{5... | collective-permute-start | bytes 1179656 | tf_op jit(solution)/shard_map/ppermute | solution.py:120
  24.8 3.5 %copy-start = (bf16[1536,512]{1,0:T(8,128)(2,1)}, bf16[1536,512]{1,0:T(8,128)(2,1)S(1)}, u32[]{:S(2)}) copy-start(bf16[1536,512]{1,0:T(8,128)(2,1)S(1)} %pad_maximum_fusion.k_ref.v_ref) | copy-start | bytes 4718596
  24.8 3.5 %collective-permute-start.3 = (bf16[1536,512]{1,0:T(8,128)(2,1)S(1)}, bf16[1536,512]{1,0:T(8,128)(2,1)S(1)}, u32[]{:S(2)}, u32[]{:S(2)}) collective-permute-start(bf16[1536,512]{1,0:T(8,128)(2,1)S(1)} %pad_maximum_fusion.k_ref.v_ref), channel_id=1, source_target_pairs={{0,4},{4,0},{8,12},{12,8},{16,20},{20,16},{24,28},{28,24},{1,5},{5... | collective-permute-start | bytes 4718600 | tf_op jit(solution)/shard_map/ppermute | solution.py:122
  28.3 1.2 %copy-start.1 = (bf16[1536,512]{1,0:T(8,128)(2,1)}, bf16[1536,512]{1,0:T(8,128)(2,1)S(1)}, u32[]{:S(2)}) copy-start(bf16[1536,512]{1,0:T(8,128)(2,1)S(1)} %collective-permute-done.3.ko_ref.vo_ref) | copy-start | bytes 4718596
  56.0 5.3 %copy-start.2 = (bf16[1536,512]{1,0:T(8,128)(2,1)S(1)}, bf16[1536,512]{1,0:T(8,128)(2,1)}, u32[]{:S(2)}) copy-start(bf16[1536,512]{1,0:T(8,128)(2,1)} %get-tuple-element.8) | copy-start | bytes 4718596
  56.0 5.3 %collective-permute-start.4 = (bf16[1536,512]{1,0:T(8,128)(2,1)}, bf16[1536,512]{1,0:T(8,128)(2,1)}, u32[]{:S(2)}, u32[]{:S(2)}) collective-permute-start(bf16[1536,512]{1,0:T(8,128)(2,1)} %get-tuple-element.9), channel_id=1, source_target_pairs={{0,4},{4,0},{8,12},{12,8},{16,20},{20,16},{24,28},{28,24},{1,5},{5... | collective-permute-start | bytes 4718600 | tf_op jit(solution)/shard_map/ppermute | solution.py:176
  56.4 34.0 %all-to-all-start = ((bf16[4,96,1536]{2,1,0:T(8,128)(2,1)}), bf16[4,96,1536]{2,1,0:T(8,128)(2,1)S(1)}, u32[]{:S(2)}, u32[]{:S(2)}) async-start(bf16[4,96,1536]{2,1,0:T(8,128)(2,1)} %bitcast.19), calls=%async_computation | async-start | bytes 2359296 | tf_op jit(solution)/shard_map/all_to_all | solution.py:187
  63.2 21.0 %copy-start.3 = (f32[384,512]{1,0:T(8,128)S(1)}, f32[384,512]{1,0:T(8,128)}, u32[]{:S(2)}) copy-start(f32[384,512]{1,0:T(8,128)} %get-tuple-element.10) | copy-start | bytes 2359300
  63.3 12.0 %collective-permute-start.5 = (bf16[384,512]{1,0:T(8,128)(2,1)S(1)}, bf16[384,512]{1,0:T(8,128)(2,1)S(1)}, u32[]{:S(2)}, u32[]{:S(2)}) collective-permute-start(bf16[384,512]{1,0:T(8,128)(2,1)S(1)} %get-tuple-element.15), channel_id=1, source_target_pairs={{0,24},{4,28},{8,0},{12,4},{16,8},{20,12},{24,16},{28,20},{1,25},{... | collective-permute-start | bytes 1179656 | tf_op jit(solution)/shard_map/ppermute | solution.py:181
  63.9 19.0 %collective-permute-start.7 = (bf16[384,512]{1,0:T(8,128)(2,1)S(1)}, bf16[384,512]{1,0:T(8,128)(2,1)S(1)}, u32[]{:S(2)}, u32[]{:S(2)}) collective-permute-start(bf16[384,512]{1,0:T(8,128)(2,1)S(1)} %get-tuple-element.16), channel_id=1, source_target_pairs={{0,8},{4,12},{8,16},{12,20},{16,24},{20,28},{24,0},{28,4},{1,9},{5... | collective-permute-start | bytes 1179656 | tf_op jit(solution)/shard_map/ppermute | solution.py:181
  65.4 18.9 %collective-permute-start.6 = (bf16[384,512]{1,0:T(8,128)(2,1)S(1)}, bf16[384,512]{1,0:T(8,128)(2,1)S(1)}, u32[]{:S(2)}, u32[]{:S(2)}) collective-permute-start(bf16[384,512]{1,0:T(8,128)(2,1)S(1)} %get-tuple-element.17), channel_id=1, source_target_pairs={{0,16},{4,20},{8,24},{12,28},{16,0},{20,4},{24,8},{28,12},{1,17},{... | collective-permute-start | bytes 1179656 | tf_op jit(solution)/shard_map/ppermute | solution.py:181
  90.3 14.7 %all-to-all-start.1 = ((bf16[4,96,512]{2,1,0:T(8,128)(2,1)}), bf16[4,96,512]{2,1,0:T(8,128)(2,1)S(1)}, u32[]{:S(2)}, u32[]{:S(2)}) async-start(bf16[4,96,512]{2,1,0:T(8,128)(2,1)} %convert_element_type.49), calls=%async_computation.1 | async-start | bytes 786432 | tf_op jit(solution)/shard_map/all_to_all | solution.py:188

commit v8 on v7

--- a/solution.py
+++ b/solution.py
@@ -16,7 +16,7 @@
 
 
 def attention_kernel(
-    blk_ref, side_ref, dst_ref, kind_ref,
+    tbl_ref,
     q_ref, do_ref, k_ref, v_ref, ko_ref, vo_ref,
     dq_ref, loc_ref, far_ref, fo_ref,
     kc_ref, vc_ref, loc_acc, far_acc, fo_acc,
@@ -25,6 +25,19 @@
     g = pl.program_id(0)
     b = pl.program_id(1)
     scale = 1.0 / math.sqrt(HD)
+    count = nb * SLOTS
+
+    def blk_ref(i):
+        return tbl_ref[i]
+
+    def side_ref(i):
+        return tbl_ref[count + i]
+
+    def dst_ref(i):
+        return tbl_ref[2 * count + i]
+
+    def kind_ref(i):
+        return tbl_ref[3 * count + i]
 
     @pl.when((g == 0) & (b == 0))
     def _():
@@ -33,8 +46,8 @@
         fo_acc[...] = jnp.zeros_like(fo_acc)
 
     for s in range(SLOTS):
-        row = pl.multiple_of(blk_ref[b * SLOTS + s] * BLK, BLK)
-        side = side_ref[b * SLOTS + s]
+        row = pl.multiple_of(blk_ref(b * SLOTS + s) * BLK, BLK)
+        side = side_ref(b * SLOTS + s)
         for code, tk, tv in ((0, k_ref, v_ref), (1, ko_ref, vo_ref)):
             @pl.when(side == code)
             def _():
@@ -63,8 +76,8 @@
     vterm = lax.dot_general(dos, probs_b, tn, preferred_element_type=jnp.float32)
 
     for s in range(SLOTS):
-        kind = kind_ref[b * SLOTS + s]
-        row = pl.multiple_of(dst_ref[b * SLOTS + s] * BLK, BLK)
+        kind = kind_ref(b * SLOTS + s)
+        row = pl.multiple_of(dst_ref(b * SLOTS + s) * BLK, BLK)
         kt = kterm[:, s * BLK:(s + 1) * BLK]
         vt = vterm[:, s * BLK:(s + 1) * BLK]
         rounded = kind == 0
@@ -76,7 +89,7 @@
             loc_acc[g, pl.ds(row, BLK), :] += kt
             loc_acc[kv_here + g, pl.ds(row, BLK), :] += vt
 
-        side = side_ref[b * SLOTS + s]
+        side = side_ref(b * SLOTS + s)
 
         @pl.when((kind != 2) & (side == 0))
         def _():
@@ -119,7 +132,7 @@
         pairs = [(i, (i + 2 * d) % shard_count) for i in range(shard_count)]
         gathered.append(lax.ppermute(kv_own, "ctx", pairs))
     kv_half = jnp.concatenate(gathered, axis=0)
-    kv_other = lax.ppermute(kv_half, "ctx", partner)
+    kv_other = jnp.concatenate([lax.ppermute(p, "ctx", partner) for p in gathered], axis=0)
     half = seq // 2
 
     rows = lax.dynamic_slice_in_dim(block_list, shard_index * nb, nb, axis=0).astype(jnp.int32)
@@ -134,10 +147,11 @@
     dst = jnp.where(local, rows - shard_index * nb, half_row).astype(jnp.int32).reshape(-1)
     blk = half_row.astype(jnp.int32).reshape(-1)
     side = owner_side.reshape(-1)
+    table = jnp.concatenate([blk, side, dst, kind]).astype(jnp.int32)
 
     kernel = functools.partial(attention_kernel, hpk=hpk, kv_here=kv_here, nb=nb)
     grid_spec = pltpu.PrefetchScalarGridSpec(
-        num_scalar_prefetch=4,
+        num_scalar_prefetch=1,
         grid=(kv_here, nb),
         in_specs=[
             pl.BlockSpec((BLK, hpk * HD), lambda g, b, *_: (b, g)),
@@ -171,16 +185,19 @@
             jax.ShapeDtypeStruct((half, width), jnp.bfloat16),
         ],
         compiler_params=pltpu.CompilerParams(dimension_semantics=("arbitrary", "arbitrary")),
-    )(blk, side, dst, kind, query_rows, out_grad, kv_half, kv_half, kv_other, kv_other)
-
-    from_partner = lax.ppermute(far_other, "ctx", partner)
-    mine = (far.astype(jnp.float32) + from_partner.astype(jnp.float32)).astype(jnp.bfloat16)
-    total = far[0:nb * BLK].astype(jnp.float32) + from_partner[0:nb * BLK].astype(jnp.float32)
+    )(table, query_rows, out_grad, kv_half, kv_half, kv_other, kv_other)
+
+    span = nb * BLK
+
+    def partner_sum(pos):
+        swapped = lax.ppermute(far_other[pos * span:(pos + 1) * span], "ctx", partner)
+        return far[pos * span:(pos + 1) * span].astype(jnp.float32) + swapped.astype(jnp.float32)
+
+    total = partner_sum(0)
     for d in range(1, members):
         pairs = [(i, (i - 2 * d) % shard_count) for i in range(shard_count)]
-        total = total + lax.ppermute(
-            mine[d * nb * BLK:(d + 1) * nb * BLK], "ctx", pairs
-        ).astype(jnp.float32)
+        chunk = partner_sum(d).astype(jnp.bfloat16)
+        total = total + lax.ppermute(chunk, "ctx", pairs).astype(jnp.float32)
     kv_sum = (total + loc).reshape(nb, HD, 2 * kv_here, BLK)
     kv_grad = jnp.transpose(kv_sum, (0, 3, 2, 1)).reshape(nb * BLK, width).astype(jnp.bfloat16)
 

time: 108 us -> 131 us (1.21)
  blocking collectives: 0 us -> 14.4 us
  waiting for transfers between devices: 49.9 us -> 62 us
  starting transfers between devices: 16.5 us -> 12.9 us
  other arithmetic: 3.59 us -> 5.32 us
  local copies, waits for them, and re-layouts: 10.3 us -> 8.71 us
    all_to_all x1, waiting for transfers between devices: 3.44 us -> 23.9 us  [shards(): lax.all_to_all(dq, 'uly', split_axis=0, concat_axis=1, tiled=True)]
    all_to_all x0 -> x1, blocking collectives: none -> 14.4 us  [shards(): lax.all_to_all(kv_grad, 'uly', split_axis=0, concat_axis=1, tiled=True)]
    all_to_all x1 -> x0, waiting for transfers between devices: 10.1 us -> none  [shards(): lax.all_to_all(kv_grad, 'uly', split_axis=0, concat_axis=1, tiled=True)]
    all_to_all x1 -> x0, starting transfers between devices: 3.46 us -> none  [shards(): lax.all_to_all(kv_grad, 'uly', split_axis=0, concat_axis=1, tiled=True)]
    concatenate x0 -> x2, other arithmetic: none -> 2.5 us  [the longest x1 1.25 us: shards(): jnp.concatenate([lax.ppermute(p, 'ctx', partner) for p in gathered], axis=0)]
    ppermute x5 -> x11, waiting for transfers between devices: 18.5 us -> 20.3 us  [the longest x3 18.5 us: shards(): total = total + lax.ppermute(chunk, 'ctx', pairs).astype(jnp.float32)]
    ppermute x5 -> x11, starting transfers between devices: 2.99 us -> 4.72 us  [the longest x3 2.61 us: shards(): total = total + lax.ppermute(chunk, 'ctx', pairs).astype(jnp.float32)]
    slice x1, local copies, waits for them, and re-layouts: 0.08 us -> 1.57 us  [partner_sum(): far_other[pos * span:(pos + 1) * span]]
  transfers between devices with their start and end apart: 10 -> 15, of which waited for: 8 -> 9; matrix products, arithmetic and copies ran while one was open for 8% -> 6% of each run, Pallas kernels for 0% -> 0%
where the time goes in v8:
time: 131 us
  waiting for transfers between devices  62 us (47%)
  Pallas kernels  26.5 us (20%)
  blocking collectives  14.4 us (11%)
  starting transfers between devices  12.9 us (10%)
  local copies, waits for them, and re-layouts  8.71 us (7%)
  other arithmetic  5.32 us (4%)
    pallas_call x1, Pallas kernels, shards(): pl.pallas_call(kernel, grid_spec=grid_spec, out_shape=[jax.ShapeDtypeStru...  26.5 us
    all_to_all x1, waiting for transfers between devices, shards(): lax.all_to_all(dq, 'uly', split_axis=0, concat_axis=1, tiled=True)  23.9 us
    ppermute x3, waiting for transfers between devices, shards(): total = total + lax.ppermute(chunk, 'ctx', pairs).astype(jnp.float32)  18.5 us
    ppermute x3, waiting for transfers between devices, shards(): gathered.append(lax.ppermute(kv_own, 'ctx', pairs))  17.7 us
    all_to_all x1, blocking collectives, shards(): lax.all_to_all(kv_grad, 'uly', split_axis=0, concat_axis=1, tiled=True)  14.4 us
    ppermute x3, starting transfers between devices, shards(): gathered.append(lax.ppermute(kv_own, 'ctx', pairs))  4.61 us
    all_to_all x1, starting transfers between devices, shards(): lax.all_to_all(dq, 'uly', split_axis=0, concat_axis=1, tiled=True)  3.53 us
  transfers between devices with their start and end apart: 15, of which 9 were waited for; matrix products, arithmetic and copies ran while one was open for 6% of the time, Pallas kernels for 0%

profile of v8, /device:TPU:0, one launch (start us, length us, event | category | flops | bytes accessed | tf_op | source)
XLA Modules:
  0.0 130.6 jit_solution(7172213653136881165)
XLA Ops:
  0.7 1.1 constant_dynamic-slice_fusion
  1.8 0.5 collective-permute-start.3
  2.3 3.5 %collective-permute-start.2 = (bf16[384,512]{1,0:T(8,128)(2,1)S(1)}, bf16[384,512]{1,0:T(8,128)(2,1)S(1)}, u32[]{:S(2)}, u32[]{:S(2)}) collective-permute-start(bf16[384,512]{1,0:T(8,128)(2,1)S(1)} %pad_maximum_fusion.2), channel_id=1, source_target_pairs={{0,24},{4,28},{8,0},{12,4},{16,8},{20,12},{24,16},{28,20},{1,25},{... | collective-permute-start | bytes 1179656 | tf_op jit(solution)/shard_map/ppermute | solution.py:133
  5.8 0.5 collective-permute-start.1
  6.3 0.6 collective-permute-start
  6.9 0.7 subtract_select_fusion
  7.7 7.6 %collective-permute-done.2 = bf16[384,512]{1,0:T(8,128)(2,1)S(1)} collective-permute-done((bf16[384,512]{1,0:T(8,128)(2,1)S(1)}, bf16[384,512]{1,0:T(8,128)(2,1)S(1)}, u32[]{:S(2)}, u32[]{:S(2)}) %collective-permute-start.2) | collective-permute-done | bytes 393248 | tf_op jit(solution)/shard_map/ppermute | solution.py:133
  15.3 10.1 %collective-permute-done.1 = bf16[384,512]{1,0:T(8,128)(2,1)S(1)} collective-permute-done((bf16[384,512]{1,0:T(8,128)(2,1)S(1)}, bf16[384,512]{1,0:T(8,128)(2,1)S(1)}, u32[]{:S(2)}, u32[]{:S(2)}) %collective-permute-start.1) | collective-permute-done | bytes 393248 | tf_op jit(solution)/shard_map/ppermute | solution.py:133
  25.4 0.5 collective-permute-start.4
  26.2 0.8 copy.21
  26.9 0.6 reshape.52
  27.9 1.2 pad_add_fusion.tbl_ref
  29.1 1.3 pad_maximum_fusion.k_ref.v_ref
  30.4 1.3 pad_maximum_fusion.1.ko_ref.vo_ref
  31.7 26.5 %shard_map.76 = (bf16[384,1536]{1,0:T(8,128)(2,1)}, f32[384,512]{1,0:T(8,128)}, bf16[1536,512]{1,0:T(8,128)(2,1)}, bf16[1536,512]{1,0:T(8,128)(2,1)}) custom-call(s32[96]{0:T(128)} %pad_add_fusion.tbl_ref, bf16[384,1536]{1,0:T(8,128)(2,1)} %q_ref.1, bf16[384,1536]{1,0:T(8,128)(2,1)} %do_ref.1, bf16[1536,512]{1,0:T(8,128)(2,1)} %pad_maximum_fusion.k_ref.v_ref, ...), custom_call_target="tpu_custom_call" | custom-call | tf_op jit(solution)/shard_map/pallas_call | solution.py:178
  58.2 1.6 %fusion.10 = (bf16[384,512]{1,0:T(8,128)(2,1)S(1)}, bf16[384,512]{1,0:T(8,128)(2,1)S(1)}, bf16[384,512]{1,0:T(8,128)(2,1)S(1)}, bf16[384,512]{1,0:T(8,128)(2,1)S(1)}) fusion(bf16[1536,512]{1,0:T(8,128)(2,1)} %get-tuple-element.9), kind=kLoop, calls=%fused_computation.36 | loop fusion | bytes 3145728 | tf_op jit(solution)/shard_map/slice | solution.py:193
  60.8 0.7 collective-permute-done.12
  61.5 0.6 collective-permute-done.10
  62.1 0.6 collective-permute-done.8
  63.0 0.6 collective-permute-start.9
  63.7 1.5 %collective-permute-start.13 = (bf16[384,512]{1,0:T(8,128)(2,1)S(1)}, bf16[384,512]{1,0:T(8,128)(2,1)S(1)}, u32[]{:S(2)}, u32[]{:S(2)}) collective-permute-start(bf16[384,512]{1,0:T(8,128)(2,1)S(1)} %get-tuple-element.19), channel_id=1, source_target_pairs={{0,8},{4,12},{8,16},{12,20},{16,24},{20,28},{24,0},{28,4},{1,9},{5... | collective-permute-start | bytes 1179656 | tf_op jit(solution)/shard_map/ppermute | solution.py:200
  65.1 0.5 collective-permute-start.11
  65.7 9.4 %collective-permute-done.9 = bf16[384,512]{1,0:T(8,128)(2,1)S(1)} collective-permute-done((bf16[384,512]{1,0:T(8,128)(2,1)S(1)}, bf16[384,512]{1,0:T(8,128)(2,1)S(1)}, u32[]{:S(2)}, u32[]{:S(2)}) %collective-permute-start.9) | collective-permute-done | bytes 393248 | tf_op jit(solution)/shard_map/ppermute | solution.py:200
  75.1 7.7 %collective-permute-done.13 = bf16[384,512]{1,0:T(8,128)(2,1)S(1)} collective-permute-done((bf16[384,512]{1,0:T(8,128)(2,1)S(1)}, bf16[384,512]{1,0:T(8,128)(2,1)S(1)}, u32[]{:S(2)}, u32[]{:S(2)}) %collective-permute-start.13) | collective-permute-done | bytes 393248 | tf_op jit(solution)/shard_map/ppermute | solution.py:200
  82.8 1.4 %collective-permute-done.11 = bf16[384,512]{1,0:T(8,128)(2,1)S(1)} collective-permute-done((bf16[384,512]{1,0:T(8,128)(2,1)S(1)}, bf16[384,512]{1,0:T(8,128)(2,1)S(1)}, u32[]{:S(2)}, u32[]{:S(2)}) %collective-permute-start.11) | collective-permute-done | bytes 393248 | tf_op jit(solution)/shard_map/ppermute | solution.py:200
  85.0 14.4 %all_to_all.32 = bf16[4,96,512]{2,1,0:T(8,128)(2,1)S(1)} all-to-all(bf16[4,96,512]{2,1,0:T(8,128)(2,1)S(1)} %convert_element_type.73), channel_id=1, replica_groups=mesh['ctx'=8,'uly'=4] {'uly'}, dimensions={0} | all-to-all | bytes 786432 | tf_op jit(solution)/shard_map/all_to_all | solution.py:205
  99.4 3.5 %all-to-all-start = ((bf16[4,96,1536]{2,1,0:T(8,128)(2,1)}), bf16[4,96,1536]{2,1,0:T(8,128)(2,1)S(1)}, u32[]{:S(2)}, u32[]{:S(2)}) async-start(bf16[4,96,1536]{2,1,0:T(8,128)(2,1)} %bitcast), calls=%async_computation | async-start | bytes 2359296 | tf_op jit(solution)/shard_map/all_to_all | solution.py:204
  103.0 0.5 fusion.11
  103.8 0.7 copy.29
  104.8 0.7 copy.28
  105.5 23.9 %all-to-all-done = bf16[4,96,1536]{2,1,0:T(8,128)(2,1)S(1)} async-done(((bf16[4,96,1536]{2,1,0:T(8,128)(2,1)}), bf16[4,96,1536]{2,1,0:T(8,128)(2,1)S(1)}, u32[]{:S(2)}, u32[]{:S(2)}) %all-to-all-start) | async-done | bytes 1179680 | tf_op jit(solution)/shard_map/all_to_all | solution.py:204
  129.4 1.1 copy.27
  (36 shorter events, 3.6 us)
Async XLA Ops:
  0.6 6.3 %copy-start.2 = (s32[24,8]{0,1:T(8,128)S(1)}, s32[24,8]{0,1:T(8,128)}, u32[]{:S(2)}) copy-start(s32[24,8]{0,1:T(8,128)} %param.9) | copy-start | bytes 2308
  1.8 28.6 %collective-permute-start.3 = (bf16[384,512]{1,0:T(8,128)(2,1)S(1)}, bf16[384,512]{1,0:T(8,128)(2,1)S(1)}, u32[]{:S(2)}, u32[]{:S(2)}) collective-permute-start(bf16[384,512]{1,0:T(8,128)(2,1)S(1)} %pad_maximum_fusion.2), channel_id=1, source_target_pairs={{0,4},{4,0},{8,12},{12,8},{16,20},{20,16},{24,28},{28,24},{1,5},{5... | collective-permute-start | bytes 1179656 | tf_op jit(solution)/shard_map/ppermute | solution.py:135
  2.3 13.0 %collective-permute-start.2 = (bf16[384,512]{1,0:T(8,128)(2,1)S(1)}, bf16[384,512]{1,0:T(8,128)(2,1)S(1)}, u32[]{:S(2)}, u32[]{:S(2)}) collective-permute-start(bf16[384,512]{1,0:T(8,128)(2,1)S(1)} %pad_maximum_fusion.2), channel_id=1, source_target_pairs={{0,24},{4,28},{8,0},{12,4},{16,8},{20,12},{24,16},{28,20},{1,25},{... | collective-permute-start | bytes 1179656 | tf_op jit(solution)/shard_map/ppermute | solution.py:133
  5.8 19.6 %collective-permute-start.1 = (bf16[384,512]{1,0:T(8,128)(2,1)S(1)}, bf16[384,512]{1,0:T(8,128)(2,1)S(1)}, u32[]{:S(2)}, u32[]{:S(2)}) collective-permute-start(bf16[384,512]{1,0:T(8,128)(2,1)S(1)} %pad_maximum_fusion.2), channel_id=1, source_target_pairs={{0,16},{4,20},{8,24},{12,28},{16,0},{20,4},{24,8},{28,12},{1,17},{... | collective-permute-start | bytes 1179656 | tf_op jit(solution)/shard_map/ppermute | solution.py:133
  6.3 19.1 %collective-permute-start = (bf16[384,512]{1,0:T(8,128)(2,1)S(1)}, bf16[384,512]{1,0:T(8,128)(2,1)S(1)}, u32[]{:S(2)}, u32[]{:S(2)}) collective-permute-start(bf16[384,512]{1,0:T(8,128)(2,1)S(1)} %pad_maximum_fusion.2), channel_id=1, source_target_pairs={{0,8},{4,12},{8,16},{12,20},{16,24},{20,28},{24,0},{28,4},{1,9},{5... | collective-permute-start | bytes 1179656 | tf_op jit(solution)/shard_map/ppermute | solution.py:133
  15.3 15.1 %collective-permute-start.6 = (bf16[384,512]{1,0:T(8,128)(2,1)S(1)}, bf16[384,512]{1,0:T(8,128)(2,1)S(1)}, u32[]{:S(2)}, u32[]{:S(2)}) collective-permute-start(bf16[384,512]{1,0:T(8,128)(2,1)S(1)} %collective-permute-done.2), channel_id=1, source_target_pairs={{0,4},{4,0},{8,12},{12,8},{16,20},{20,16},{24,28},{28,24},{1,5},{5... | collective-permute-start | bytes 1179656 | tf_op jit(solution)/shard_map/ppermute | solution.py:135
  25.4 5.0 %collective-permute-start.5 = (bf16[384,512]{1,0:T(8,128)(2,1)S(1)}, bf16[384,512]{1,0:T(8,128)(2,1)S(1)}, u32[]{:S(2)}, u32[]{:S(2)}) collective-permute-start(bf16[384,512]{1,0:T(8,128)(2,1)S(1)} %collective-permute-done.1), channel_id=1, source_target_pairs={{0,4},{4,0},{8,12},{12,8},{16,20},{20,16},{24,28},{28,24},{1,5},{5... | collective-permute-start | bytes 1179656 | tf_op jit(solution)/shard_map/ppermute | solution.py:135
  25.4 5.0 %collective-permute-start.4 = (bf16[384,512]{1,0:T(8,128)(2,1)S(1)}, bf16[384,512]{1,0:T(8,128)(2,1)S(1)}, u32[]{:S(2)}, u32[]{:S(2)}) collective-permute-start(bf16[384,512]{1,0:T(8,128)(2,1)S(1)} %collective-permute-done), channel_id=1, source_target_pairs={{0,4},{4,0},{8,12},{12,8},{16,20},{20,16},{24,28},{28,24},{1,5},{5... | collective-permute-start | bytes 1179656 | tf_op jit(solution)/shard_map/ppermute | solution.py:135
  58.2 4.5 %copy-start = (bf16[1536,512]{1,0:T(8,128)(2,1)S(1)}, bf16[1536,512]{1,0:T(8,128)(2,1)}, u32[]{:S(2)}) copy-start(bf16[1536,512]{1,0:T(8,128)(2,1)} %get-tuple-element.8) | copy-start | bytes 4718596
  59.8 1.8 %collective-permute-start.12 = (bf16[384,512]{1,0:T(8,128)(2,1)S(1)}, bf16[384,512]{1,0:T(8,128)(2,1)S(1)}, u32[]{:S(2)}, u32[]{:S(2)}) collective-permute-start(bf16[384,512]{1,0:T(8,128)(2,1)S(1)} %get-tuple-element.15), channel_id=1, source_target_pairs={{0,4},{4,0},{8,12},{12,8},{16,20},{20,16},{24,28},{28,24},{1,5},{5... | collective-permute-start | bytes 1179656 | tf_op jit(solution)/shard_map/ppermute | solution.py:193
  59.8 2.3 %collective-permute-start.10 = (bf16[384,512]{1,0:T(8,128)(2,1)S(1)}, bf16[384,512]{1,0:T(8,128)(2,1)S(1)}, u32[]{:S(2)}, u32[]{:S(2)}) collective-permute-start(bf16[384,512]{1,0:T(8,128)(2,1)S(1)} %get-tuple-element.16), channel_id=1, source_target_pairs={{0,4},{4,0},{8,12},{12,8},{16,20},{20,16},{24,28},{28,24},{1,5},{5... | collective-permute-start | bytes 1179656 | tf_op jit(solution)/shard_map/ppermute | solution.py:193
  60.3 2.3 %collective-permute-start.8 = (bf16[384,512]{1,0:T(8,128)(2,1)S(1)}, bf16[384,512]{1,0:T(8,128)(2,1)S(1)}, u32[]{:S(2)}, u32[]{:S(2)}) collective-permute-start(bf16[384,512]{1,0:T(8,128)(2,1)S(1)} %get-tuple-element.17), channel_id=1, source_target_pairs={{0,4},{4,0},{8,12},{12,8},{16,20},{20,16},{24,28},{28,24},{1,5},{5... | collective-permute-start | bytes 1179656 | tf_op jit(solution)/shard_map/ppermute | solution.py:193
  60.4 5.2 %collective-permute-start.7 = (bf16[384,512]{1,0:T(8,128)(2,1)S(1)}, bf16[384,512]{1,0:T(8,128)(2,1)S(1)}, u32[]{:S(2)}, u32[]{:S(2)}) collective-permute-start(bf16[384,512]{1,0:T(8,128)(2,1)S(1)} %get-tuple-element.14), channel_id=1, source_target_pairs={{0,4},{4,0},{8,12},{12,8},{16,20},{20,16},{24,28},{28,24},{1,5},{5... | collective-permute-start | bytes 1179656 | tf_op jit(solution)/shard_map/ppermute | solution.py:193
  62.7 21.5 %copy-start.1 = (f32[384,512]{1,0:T(8,128)S(1)}, f32[384,512]{1,0:T(8,128)}, u32[]{:S(2)}) copy-start(f32[384,512]{1,0:T(8,128)} %get-tuple-element.10) | copy-start | bytes 2359300
  63.0 12.0 %collective-permute-start.9 = (bf16[384,512]{1,0:T(8,128)(2,1)S(1)}, bf16[384,512]{1,0:T(8,128)(2,1)S(1)}, u32[]{:S(2)}, u32[]{:S(2)}) collective-permute-start(bf16[384,512]{1,0:T(8,128)(2,1)S(1)} %get-tuple-element.18), channel_id=1, source_target_pairs={{0,24},{4,28},{8,0},{12,4},{16,8},{20,12},{24,16},{28,20},{1,25},{... | collective-permute-start | bytes 1179656 | tf_op jit(solution)/shard_map/ppermute | solution.py:200
  63.7 19.1 %collective-permute-start.13 = (bf16[384,512]{1,0:T(8,128)(2,1)S(1)}, bf16[384,512]{1,0:T(8,128)(2,1)S(1)}, u32[]{:S(2)}, u32[]{:S(2)}) collective-permute-start(bf16[384,512]{1,0:T(8,128)(2,1)S(1)} %get-tuple-element.19), channel_id=1, source_target_pairs={{0,8},{4,12},{8,16},{12,20},{16,24},{20,28},{24,0},{28,4},{1,9},{5... | collective-permute-start | bytes 1179656 | tf_op jit(solution)/shard_map/ppermute | solution.py:200
  65.1 19.0 %collective-permute-start.11 = (bf16[384,512]{1,0:T(8,128)(2,1)S(1)}, bf16[384,512]{1,0:T(8,128)(2,1)S(1)}, u32[]{:S(2)}, u32[]{:S(2)}) collective-permute-start(bf16[384,512]{1,0:T(8,128)(2,1)S(1)} %get-tuple-element.20), channel_id=1, source_target_pairs={{0,16},{4,20},{8,24},{12,28},{16,0},{20,4},{24,8},{28,12},{1,17},{... | collective-permute-start | bytes 1179656 | tf_op jit(solution)/shard_map/ppermute | solution.py:200
  99.4 30.1 %all-to-all-start = ((bf16[4,96,1536]{2,1,0:T(8,128)(2,1)}), bf16[4,96,1536]{2,1,0:T(8,128)(2,1)S(1)}, u32[]{:S(2)}, u32[]{:S(2)}) async-start(bf16[4,96,1536]{2,1,0:T(8,128)(2,1)} %bitcast), calls=%async_computation | async-start | bytes 2359296 | tf_op jit(solution)/shard_map/all_to_all | solution.py:204

commit v9 on v8

--- a/solution.py
+++ b/solution.py
@@ -107,6 +107,21 @@
             loc_ref[:, j * HD:(j + 1) * HD] = loc_acc[j]
             far_ref[:, j * HD:(j + 1) * HD] = far_acc[j].astype(jnp.bfloat16)
             fo_ref[:, j * HD:(j + 1) * HD] = fo_acc[j].astype(jnp.bfloat16)
+
+
+def lane_transpose(x, lane, lanes):
+    rows = x.shape[0] // lanes
+    cols = x.shape[1]
+    chunks = x.reshape(lanes, rows, cols)
+    out = jnp.zeros((rows, lanes * cols), x.dtype)
+    own = lax.dynamic_index_in_dim(chunks, lane, 0, keepdims=False)
+    out = lax.dynamic_update_slice(out, own, (0, lane * cols))
+    for e in range(1, lanes):
+        send = lax.dynamic_index_in_dim(chunks, (lane + e) % lanes, 0, keepdims=False)
+        pairs = [(i, (i + e) % lanes) for i in range(lanes)]
+        got = lax.ppermute(send, "uly", pairs)
+        out = lax.dynamic_update_slice(out, got, (0, ((lane - e) % lanes) * cols))
+    return out
 
 
 def shards(query_rows, key_rows, value_rows, out_grad, block_list):
@@ -201,8 +216,9 @@
     kv_sum = (total + loc).reshape(nb, HD, 2 * kv_here, BLK)
     kv_grad = jnp.transpose(kv_sum, (0, 3, 2, 1)).reshape(nb * BLK, width).astype(jnp.bfloat16)
 
-    query_out = lax.all_to_all(dq, "uly", split_axis=0, concat_axis=1, tiled=True)
-    kv_seq = lax.all_to_all(kv_grad, "uly", split_axis=0, concat_axis=1, tiled=True)
+    lanes = lax.axis_size("uly")
+    query_out = lane_transpose(dq, lane_index, lanes)
+    kv_seq = lane_transpose(kv_grad, lane_index, lanes)
     rows_here = kv_seq.shape[0]
     lane_count = kv_seq.shape[1] // width
     spread = kv_seq.reshape(rows_here, lane_count, 2, kv_here * HD)

time: 131 us -> 116 us (0.89)
  blocking collectives: 14.4 us -> 0 us
  waiting for transfers between devices: 62 us -> 47.9 us
  starting transfers between devices: 12.9 us -> 25.4 us
  local copies, waits for them, and re-layouts: 8.71 us -> 10.7 us
    all_to_all x1 -> x0, waiting for transfers between devices: 23.9 us -> none  [shards(): lax.all_to_all(dq, 'uly', split_axis=0, concat_axis=1, tiled=True)]
    ppermute x0 -> x6, waiting for transfers between devices: none -> 22.2 us  [lane_transpose(): got = lax.ppermute(send, 'uly', pairs)]
    all_to_all x1 -> x0, blocking collectives: 14.4 us -> none  [shards(): lax.all_to_all(kv_grad, 'uly', split_axis=0, concat_axis=1, tiled=True)]
    ppermute x0 -> x6, starting transfers between devices: none -> 13.3 us  [lane_transpose(): got = lax.ppermute(send, 'uly', pairs)]
    ppermute x3, waiting for transfers between devices: 18.5 us -> 10.1 us  [shards(): total = total + lax.ppermute(chunk, 'ctx', pairs).astype(jnp.float32)]
    all_to_all x1 -> x0, starting transfers between devices: 3.53 us -> none  [shards(): lax.all_to_all(dq, 'uly', split_axis=0, concat_axis=1, tiled=True)]
    ppermute x3, waiting for transfers between devices: 17.7 us -> 15.5 us  [shards(): gathered.append(lax.ppermute(kv_own, 'ctx', pairs))]
    ppermute x3, starting transfers between devices: 2.61 us -> 4.81 us  [shards(): total = total + lax.ppermute(chunk, 'ctx', pairs).astype(jnp.float32)]
  transfers between devices with their start and end apart: 15 -> 20, of which waited for: 9 -> 9; matrix products, arithmetic and copies ran while one was open for 6% -> 6% of each run, Pallas kernels for 0% -> 0%
where the time goes in v9:
time: 116 us
  waiting for transfers between devices  47.9 us (41%)
  Pallas kernels  26.5 us (23%)
  starting transfers between devices  25.4 us (22%)
  local copies, waits for them, and re-layouts  10.7 us (9%)
  other arithmetic  4.73 us (4%)
    pallas_call x1, Pallas kernels, shards(): pl.pallas_call(kernel, grid_spec=grid_spec, out_shape=[jax.ShapeDtypeStru...  26.5 us
    ppermute x6, waiting for transfers between devices, lane_transpose(): got = lax.ppermute(send, 'uly', pairs)  22.2 us
    ppermute x3, waiting for transfers between devices, shards(): gathered.append(lax.ppermute(kv_own, 'ctx', pairs))  15.5 us
    ppermute x6, starting transfers between devices, lane_transpose(): got = lax.ppermute(send, 'uly', pairs)  13.3 us
    ppermute x3, waiting for transfers between devices, shards(): total = total + lax.ppermute(chunk, 'ctx', pairs).astype(jnp.float32)  10.1 us
    ppermute x3, starting transfers between devices, shards(): gathered.append(lax.ppermute(kv_own, 'ctx', pairs))  5.94 us
    ppermute x3, starting transfers between devices, shards(): total = total + lax.ppermute(chunk, 'ctx', pairs).astype(jnp.float32)  4.81 us
  transfers between devices with their start and end apart: 20, of which 9 were waited for; matrix products, arithmetic and copies ran while one was open for 6% of the time, Pallas kernels for 0%

profile of v9, /device:TPU:0, one launch (start us, length us, event | category | flops | bytes accessed | tf_op | source)
XLA Modules:
  0.0 116.2 jit_solution(3245037847236301447)
XLA Ops:
  0.7 1.1 constant_dynamic-slice_fusion
  1.8 3.0 %collective-permute-start = (bf16[384,512]{1,0:T(8,128)(2,1)S(1)}, bf16[384,512]{1,0:T(8,128)(2,1)S(1)}, u32[]{:S(2)}, u32[]{:S(2)}) collective-permute-start(bf16[384,512]{1,0:T(8,128)(2,1)S(1)} %pad_maximum_fusion.2), channel_id=1, source_target_pairs={{0,8},{4,12},{8,16},{12,20},{16,24},{20,28},{24,0},{28,4},{1,9},{5... | collective-permute-start | bytes 1179656 | tf_op jit(solution)/shard_map/ppermute | solution.py:148
  4.8 1.5 %collective-permute-start.1 = (bf16[384,512]{1,0:T(8,128)(2,1)S(1)}, bf16[384,512]{1,0:T(8,128)(2,1)S(1)}, u32[]{:S(2)}, u32[]{:S(2)}) collective-permute-start(bf16[384,512]{1,0:T(8,128)(2,1)S(1)} %pad_maximum_fusion.2), channel_id=1, source_target_pairs={{0,16},{4,20},{8,24},{12,28},{16,0},{20,4},{24,8},{28,12},{1,17},{... | collective-permute-start | bytes 1179656 | tf_op jit(solution)/shard_map/ppermute | solution.py:148
  6.3 1.4 %collective-permute-start.2 = (bf16[384,512]{1,0:T(8,128)(2,1)S(1)}, bf16[384,512]{1,0:T(8,128)(2,1)S(1)}, u32[]{:S(2)}, u32[]{:S(2)}) collective-permute-start(bf16[384,512]{1,0:T(8,128)(2,1)S(1)} %pad_maximum_fusion.2), channel_id=1, source_target_pairs={{0,24},{4,28},{8,0},{12,4},{16,8},{20,12},{24,16},{28,20},{1,25},{... | collective-permute-start | bytes 1179656 | tf_op jit(solution)/shard_map/ppermute | solution.py:148
  8.0 7.7 %collective-permute-done = bf16[384,512]{1,0:T(8,128)(2,1)S(1)} collective-permute-done((bf16[384,512]{1,0:T(8,128)(2,1)S(1)}, bf16[384,512]{1,0:T(8,128)(2,1)S(1)}, u32[]{:S(2)}, u32[]{:S(2)}) %collective-permute-start) | collective-permute-done | bytes 393248 | tf_op jit(solution)/shard_map/ppermute | solution.py:148
  15.7 7.6 %collective-permute-done.1 = bf16[384,512]{1,0:T(8,128)(2,1)S(1)} collective-permute-done((bf16[384,512]{1,0:T(8,128)(2,1)S(1)}, bf16[384,512]{1,0:T(8,128)(2,1)S(1)}, u32[]{:S(2)}, u32[]{:S(2)}) %collective-permute-start.1) | collective-permute-done | bytes 393248 | tf_op jit(solution)/shard_map/ppermute | solution.py:148
  23.8 0.7 copy.18
  24.4 1.3 %reshape.54 = s32[24]{0:T(128)} reshape(s32[3,8]{1,0:T(4,128)} %copy.18) | data formatting | bytes 192 | tf_op jit(solution)/shard_map/reshape | solution.py:164
  25.9 0.6 reshape.46
  26.7 1.2 %pad_add_fusion.tbl_ref = s32[96]{0:T(128)} fusion(s32[24]{0:T(128)S(1)} %reshape.50, s32[24]{0:T(128)S(1)} %reshape.49, s32[24]{0:T(128)} %reshape.54, s32[24]{0:T(128)} %reshape.46), kind=kLoop, calls=%fused_computation.52 | loop fusion | flops 288 | bytes 768 | tf_op jit(solution)/shard_map/concatenate | solution.py:165
  27.9 1.3 %pad_maximum_fusion.k_ref.v_ref = bf16[1536,512]{1,0:T(8,128)(2,1)} fusion(bf16[384,512]{1,0:T(8,128)(2,1)S(1)} %collective-permute-done.2, bf16[384,512]{1,0:T(8,128)(2,1)S(1)} %collective-permute-done.1, bf16[384,512]{1,0:T(8,128)(2,1)S(1)} %collective-permute-done, bf16[384,256]{1,0:T(8,128)(2,1)S(1)} %get-tuple-element.29, ...), kind=kLoop, calls=%fused_computation | loop fusion | flops 7864320 | bytes 3145728 | tf_op jit(solution)/shard_map/concatenate | solution.py:149
  29.2 1.3 %pad_maximum_fusion.1.ko_ref.vo_ref = bf16[1536,512]{1,0:T(8,128)(2,1)} fusion(bf16[384,512]{1,0:T(8,128)(2,1)S(1)} %collective-permute-done.6, bf16[384,512]{1,0:T(8,128)(2,1)S(1)} %collective-permute-done.5, bf16[384,512]{1,0:T(8,128)(2,1)S(1)} %collective-permute-done.4, bf16[384,512]{1,0:T(8,128)(2,1)S(1)} %collective-permute-done.3), kind=kLoop, calls=%fused_computation.1 | loop fusion | flops 6291456 | bytes 3145728 | tf_op jit(solution)/shard_map/concatenate | solution.py:150
  30.5 26.5 %shard_map.76 = (bf16[384,1536]{1,0:T(8,128)(2,1)}, f32[384,512]{1,0:T(8,128)}, bf16[1536,512]{1,0:T(8,128)(2,1)}, bf16[1536,512]{1,0:T(8,128)(2,1)}) custom-call(s32[96]{0:T(128)} %pad_add_fusion.tbl_ref, bf16[384,1536]{1,0:T(8,128)(2,1)} %q_ref.1, bf16[384,1536]{1,0:T(8,128)(2,1)} %do_ref.1, bf16[1536,512]{1,0:T(8,128)(2,1)} %pad_maximum_fusion.k_ref.v_ref, ...), custom_call_target="tpu_custom_call" | custom-call | tf_op jit(solution)/shard_map/pallas_call | solution.py:193
  57.0 1.3 %dynamic-slice_bitcast_fusion = (bf16[96,1536]{1,0:T(8,128)(2,1)S(1)}, bf16[96,1536]{1,0:T(8,128)(2,1)S(1)}, bf16[96,1536]{1,0:T(8,128)(2,1)S(1)}) fusion(bf16[4,96,1536]{2,1,0:T(8,128)(2,1)} %bitcast.23, s32[]{:T(128)S(6)} %select_n.156, s32[]{:T(128)S(6)} %select_n.152, s32[]{:T(128)S(6)} %select_n.148), kind=kLoop, calls=%fused_computation.10 | loop fusion | bytes 1769484 | tf_op jit(solution)/shard_map/jit(dynamic_index_in_dim)/squeeze | solution.py:120
  58.4 1.8 %collective-permute-start.7 = (bf16[96,1536]{1,0:T(8,128)(2,1)S(1)}, bf16[96,1536]{1,0:T(8,128)(2,1)S(1)}, u32[]{:S(2)}, u32[]{:S(2)}) collective-permute-start(bf16[96,1536]{1,0:T(8,128)(2,1)S(1)} %get-tuple-element.25), channel_id=1, source_target_pairs={{0,1},{1,2},{2,3},{3,0},{4,5},{5,6},{6,7},{7,4},{8,9},{9,10},{10,1... | collective-permute-start | bytes 884744 | tf_op jit(solution)/shard_map/ppermute | solution.py:122
  60.4 0.5 collective-permute-start.13
  61.5 1.0 bitcast_dynamic-update-slice_fusion
  62.5 7.0 %collective-permute-done.7 = bf16[96,1536]{1,0:T(8,128)(2,1)S(1)} collective-permute-done((bf16[96,1536]{1,0:T(8,128)(2,1)S(1)}, bf16[96,1536]{1,0:T(8,128)(2,1)S(1)}, u32[]{:S(2)}, u32[]{:S(2)}) %collective-permute-start.7) | collective-permute-done | bytes 294944 | tf_op jit(solution)/shard_map/ppermute | solution.py:122
  69.5 0.7 collective-permute-start.8
  70.3 1.4 %collective-permute-start.9 = (bf16[96,1536]{1,0:T(8,128)(2,1)S(1)}, bf16[96,1536]{1,0:T(8,128)(2,1)S(1)}, u32[]{:S(2)}, u32[]{:S(2)}) collective-permute-start(bf16[96,1536]{1,0:T(8,128)(2,1)S(1)} %get-tuple-element.23), channel_id=1, source_target_pairs={{0,3},{1,0},{2,1},{3,2},{4,7},{5,4},{6,5},{7,6},{8,11},{9,8},{10,9... | collective-permute-start | bytes 884744 | tf_op jit(solution)/shard_map/ppermute | solution.py:122
  72.0 1.7 %collective-permute-start.12 = (bf16[384,512]{1,0:T(8,128)(2,1)S(1)}, bf16[384,512]{1,0:T(8,128)(2,1)S(1)}, u32[]{:S(2)}, u32[]{:S(2)}) collective-permute-start(bf16[384,512]{1,0:T(8,128)(2,1)S(1)} %get-tuple-element.20), channel_id=1, source_target_pairs={{0,24},{4,28},{8,0},{12,4},{16,8},{20,12},{24,16},{28,20},{1,25},{... | collective-permute-start | bytes 1179656 | tf_op jit(solution)/shard_map/ppermute | solution.py:215
  73.7 1.5 %collective-permute-start.14 = (bf16[384,512]{1,0:T(8,128)(2,1)S(1)}, bf16[384,512]{1,0:T(8,128)(2,1)S(1)}, u32[]{:S(2)}, u32[]{:S(2)}) collective-permute-start(bf16[384,512]{1,0:T(8,128)(2,1)S(1)} %get-tuple-element.22), channel_id=1, source_target_pairs={{0,16},{4,20},{8,24},{12,28},{16,0},{20,4},{24,8},{28,12},{1,17},{... | collective-permute-start | bytes 1179656 | tf_op jit(solution)/shard_map/ppermute | solution.py:215
  75.3 8.9 %collective-permute-done.8 = bf16[96,1536]{1,0:T(8,128)(2,1)S(1)} collective-permute-done((bf16[96,1536]{1,0:T(8,128)(2,1)S(1)}, bf16[96,1536]{1,0:T(8,128)(2,1)S(1)}, u32[]{:S(2)}, u32[]{:S(2)}) %collective-permute-start.8) | collective-permute-done | bytes 294944 | tf_op jit(solution)/shard_map/ppermute | solution.py:122
  84.2 1.6 %collective-permute-start.16 = (bf16[384,512]{1,0:T(8,128)(2,1)S(1)}, bf16[384,512]{1,0:T(8,128)(2,1)S(1)}, u32[]{:S(2)}, u32[]{:S(2)}) collective-permute-start(bf16[384,512]{1,0:T(8,128)(2,1)S(1)} %get-tuple-element.21), channel_id=1, source_target_pairs={{0,8},{4,12},{8,16},{12,20},{16,24},{20,28},{24,0},{28,4},{1,9},{5... | collective-permute-start | bytes 1179656 | tf_op jit(solution)/shard_map/ppermute | solution.py:215
  85.9 10.1 %collective-permute-done.16 = bf16[384,512]{1,0:T(8,128)(2,1)S(1)} collective-permute-done((bf16[384,512]{1,0:T(8,128)(2,1)S(1)}, bf16[384,512]{1,0:T(8,128)(2,1)S(1)}, u32[]{:S(2)}, u32[]{:S(2)}) %collective-permute-start.16) | collective-permute-done | bytes 393248 | tf_op jit(solution)/shard_map/ppermute | solution.py:215
  97.0 6.0 %collective-permute-start.17 = (bf16[96,512]{1,0:T(8,128)(2,1)S(1)}, bf16[96,512]{1,0:T(8,128)(2,1)S(1)}, u32[]{:S(2)}, u32[]{:S(2)}) collective-permute-start(bf16[96,512]{1,0:T(8,128)(2,1)S(1)} %get-tuple-element.28), channel_id=1, source_target_pairs={{0,1},{1,2},{2,3},{3,0},{4,5},{5,6},{6,7},{7,4},{8,9},{9,10},{10,1... | collective-permute-start | bytes 294920 | tf_op jit(solution)/shard_map/ppermute | solution.py:122
  103.0 3.4 %collective-permute-start.18 = (bf16[96,512]{1,0:T(8,128)(2,1)S(1)}, bf16[96,512]{1,0:T(8,128)(2,1)S(1)}, u32[]{:S(2)}, u32[]{:S(2)}) collective-permute-start(bf16[96,512]{1,0:T(8,128)(2,1)S(1)} %get-tuple-element.27), channel_id=1, source_target_pairs={{0,2},{1,3},{2,0},{3,1},{4,6},{5,7},{6,4},{7,5},{8,10},{9,11},{10,... | collective-permute-start | bytes 294920 | tf_op jit(solution)/shard_map/ppermute | solution.py:122
  106.4 3.2 %collective-permute-done.17 = bf16[96,512]{1,0:T(8,128)(2,1)S(1)} collective-permute-done((bf16[96,512]{1,0:T(8,128)(2,1)S(1)}, bf16[96,512]{1,0:T(8,128)(2,1)S(1)}, u32[]{:S(2)}, u32[]{:S(2)}) %collective-permute-start.17) | collective-permute-done | bytes 98336 | tf_op jit(solution)/shard_map/ppermute | solution.py:122
  109.6 2.7 %collective-permute-done.18 = bf16[96,512]{1,0:T(8,128)(2,1)S(1)} collective-permute-done((bf16[96,512]{1,0:T(8,128)(2,1)S(1)}, bf16[96,512]{1,0:T(8,128)(2,1)S(1)}, u32[]{:S(2)}, u32[]{:S(2)}) %collective-permute-start.18) | collective-permute-done | bytes 98336 | tf_op jit(solution)/shard_map/ppermute | solution.py:122
  113.0 1.8 %slice_reduce_fusion = (bf16[96,4,256]{2,1,0:T(4,128)(2,1)S(1)}, bf16[96,4,256]{2,1,0:T(4,128)(2,1)S(1)}) fusion(bf16[96,4,2,256]{3,2,1,0:T(2,128)(2,1)S(1)} %reshape.52), kind=kLoop, calls=%fused_computation.6 | loop fusion | bytes 786432 | tf_op jit(solution)/shard_map/slice | solution.py:233
  114.8 0.7 copy.22
  115.5 0.7 copy.23
  (58 shorter events, 4.1 us)
Async XLA Ops:
  0.6 7.1 %copy-start.4 = (s32[24,8]{0,1:T(8,128)S(1)}, s32[24,8]{0,1:T(8,128)}, u32[]{:S(2)}) copy-start(s32[24,8]{0,1:T(8,128)} %param.9) | copy-start | bytes 2308
  1.8 13.9 %collective-permute-start = (bf16[384,512]{1,0:T(8,128)(2,1)S(1)}, bf16[384,512]{1,0:T(8,128)(2,1)S(1)}, u32[]{:S(2)}, u32[]{:S(2)}) collective-permute-start(bf16[384,512]{1,0:T(8,128)(2,1)S(1)} %pad_maximum_fusion.2), channel_id=1, source_target_pairs={{0,8},{4,12},{8,16},{12,20},{16,24},{20,28},{24,0},{28,4},{1,9},{5... | collective-permute-start | bytes 1179656 | tf_op jit(solution)/shard_map/ppermute | solution.py:148
  4.8 18.5 %collective-permute-start.1 = (bf16[384,512]{1,0:T(8,128)(2,1)S(1)}, bf16[384,512]{1,0:T(8,128)(2,1)S(1)}, u32[]{:S(2)}, u32[]{:S(2)}) collective-permute-start(bf16[384,512]{1,0:T(8,128)(2,1)S(1)} %pad_maximum_fusion.2), channel_id=1, source_target_pairs={{0,16},{4,20},{8,24},{12,28},{16,0},{20,4},{24,8},{28,12},{1,17},{... | collective-permute-start | bytes 1179656 | tf_op jit(solution)/shard_map/ppermute | solution.py:148
  6.3 17.3 %collective-permute-start.2 = (bf16[384,512]{1,0:T(8,128)(2,1)S(1)}, bf16[384,512]{1,0:T(8,128)(2,1)S(1)}, u32[]{:S(2)}, u32[]{:S(2)}) collective-permute-start(bf16[384,512]{1,0:T(8,128)(2,1)S(1)} %pad_maximum_fusion.2), channel_id=1, source_target_pairs={{0,24},{4,28},{8,0},{12,4},{16,8},{20,12},{24,16},{28,20},{1,25},{... | collective-permute-start | bytes 1179656 | tf_op jit(solution)/shard_map/ppermute | solution.py:148
  7.7 21.5 %collective-permute-start.3 = (bf16[384,512]{1,0:T(8,128)(2,1)S(1)}, bf16[384,512]{1,0:T(8,128)(2,1)S(1)}, u32[]{:S(2)}, u32[]{:S(2)}) collective-permute-start(bf16[384,512]{1,0:T(8,128)(2,1)S(1)} %pad_maximum_fusion.2), channel_id=1, source_target_pairs={{0,4},{4,0},{8,12},{12,8},{16,20},{20,16},{24,28},{28,24},{1,5},{5... | collective-permute-start | bytes 1179656 | tf_op jit(solution)/shard_map/ppermute | solution.py:150
  15.7 13.5 %collective-permute-start.4 = (bf16[384,512]{1,0:T(8,128)(2,1)S(1)}, bf16[384,512]{1,0:T(8,128)(2,1)S(1)}, u32[]{:S(2)}, u32[]{:S(2)}) collective-permute-start(bf16[384,512]{1,0:T(8,128)(2,1)S(1)} %collective-permute-done), channel_id=1, source_target_pairs={{0,4},{4,0},{8,12},{12,8},{16,20},{20,16},{24,28},{28,24},{1,5},{5... | collective-permute-start | bytes 1179656 | tf_op jit(solution)/shard_map/ppermute | solution.py:150
  23.3 6.0 %collective-permute-start.5 = (bf16[384,512]{1,0:T(8,128)(2,1)S(1)}, bf16[384,512]{1,0:T(8,128)(2,1)S(1)}, u32[]{:S(2)}, u32[]{:S(2)}) collective-permute-start(bf16[384,512]{1,0:T(8,128)(2,1)S(1)} %collective-permute-done.1), channel_id=1, source_target_pairs={{0,4},{4,0},{8,12},{12,8},{16,20},{20,16},{24,28},{28,24},{1,5},{5... | collective-permute-start | bytes 1179656 | tf_op jit(solution)/shard_map/ppermute | solution.py:150
  23.5 5.7 %collective-permute-start.6 = (bf16[384,512]{1,0:T(8,128)(2,1)S(1)}, bf16[384,512]{1,0:T(8,128)(2,1)S(1)}, u32[]{:S(2)}, u32[]{:S(2)}) collective-permute-start(bf16[384,512]{1,0:T(8,128)(2,1)S(1)} %collective-permute-done.2), channel_id=1, source_target_pairs={{0,4},{4,0},{8,12},{12,8},{16,20},{20,16},{24,28},{28,24},{1,5},{5... | collective-permute-start | bytes 1179656 | tf_op jit(solution)/shard_map/ppermute | solution.py:150
  57.0 3.2 %copy-start.1 = (bf16[1536,512]{1,0:T(8,128)(2,1)S(1)}, bf16[1536,512]{1,0:T(8,128)(2,1)}, u32[]{:S(2)}) copy-start(bf16[1536,512]{1,0:T(8,128)(2,1)} %get-tuple-element.9) | copy-start | bytes 4718596
  58.4 11.1 %collective-permute-start.7 = (bf16[96,1536]{1,0:T(8,128)(2,1)S(1)}, bf16[96,1536]{1,0:T(8,128)(2,1)S(1)}, u32[]{:S(2)}, u32[]{:S(2)}) collective-permute-start(bf16[96,1536]{1,0:T(8,128)(2,1)S(1)} %get-tuple-element.25), channel_id=1, source_target_pairs={{0,1},{1,2},{2,3},{3,0},{4,5},{5,6},{6,7},{7,4},{8,9},{9,10},{10,1... | collective-permute-start | bytes 884744 | tf_op jit(solution)/shard_map/ppermute | solution.py:122
  60.3 11.4 %copy-start = (bf16[1536,512]{1,0:T(8,128)(2,1)S(1)}, bf16[1536,512]{1,0:T(8,128)(2,1)}, u32[]{:S(2)}) copy-start(bf16[1536,512]{1,0:T(8,128)(2,1)} %get-tuple-element.8) | copy-start | bytes 4718596
  60.3 10.0 %collective-permute-start.11 = (bf16[384,512]{1,0:T(8,128)(2,1)S(1)}, bf16[384,512]{1,0:T(8,128)(2,1)S(1)}, u32[]{:S(2)}, u32[]{:S(2)}) collective-permute-start(bf16[384,512]{1,0:T(8,128)(2,1)S(1)} %get-tuple-element.19), channel_id=1, source_target_pairs={{0,4},{4,0},{8,12},{12,8},{16,20},{20,16},{24,28},{28,24},{1,5},{5... | collective-permute-start | bytes 1179656 | tf_op jit(solution)/shard_map/ppermute | solution.py:208
  60.4 11.3 %collective-permute-start.13 = (bf16[384,512]{1,0:T(8,128)(2,1)S(1)}, bf16[384,512]{1,0:T(8,128)(2,1)S(1)}, u32[]{:S(2)}, u32[]{:S(2)}) collective-permute-start(bf16[384,512]{1,0:T(8,128)(2,1)S(1)} %get-tuple-element.18), channel_id=1, source_target_pairs={{0,4},{4,0},{8,12},{12,8},{16,20},{20,16},{24,28},{28,24},{1,5},{5... | collective-permute-start | bytes 1179656 | tf_op jit(solution)/shard_map/ppermute | solution.py:208
  60.9 10.8 %collective-permute-start.15 = (bf16[384,512]{1,0:T(8,128)(2,1)S(1)}, bf16[384,512]{1,0:T(8,128)(2,1)S(1)}, u32[]{:S(2)}, u32[]{:S(2)}) collective-permute-start(bf16[384,512]{1,0:T(8,128)(2,1)S(1)} %get-tuple-element.17), channel_id=1, source_target_pairs={{0,4},{4,0},{8,12},{12,8},{16,20},{20,16},{24,28},{28,24},{1,5},{5... | collective-permute-start | bytes 1179656 | tf_op jit(solution)/shard_map/ppermute | solution.py:208
  61.0 24.9 %collective-permute-start.10 = (bf16[384,512]{1,0:T(8,128)(2,1)S(1)}, bf16[384,512]{1,0:T(8,128)(2,1)S(1)}, u32[]{:S(2)}, u32[]{:S(2)}) collective-permute-start(bf16[384,512]{1,0:T(8,128)(2,1)S(1)} %get-tuple-element.16), channel_id=1, source_target_pairs={{0,4},{4,0},{8,12},{12,8},{16,20},{20,16},{24,28},{28,24},{1,5},{5... | collective-permute-start | bytes 1179656 | tf_op jit(solution)/shard_map/ppermute | solution.py:208
  69.5 14.7 %collective-permute-start.8 = (bf16[96,1536]{1,0:T(8,128)(2,1)S(1)}, bf16[96,1536]{1,0:T(8,128)(2,1)S(1)}, u32[]{:S(2)}, u32[]{:S(2)}) collective-permute-start(bf16[96,1536]{1,0:T(8,128)(2,1)S(1)} %get-tuple-element.24), channel_id=1, source_target_pairs={{0,2},{1,3},{2,0},{3,1},{4,6},{5,7},{6,4},{7,5},{8,10},{9,11},{10,... | collective-permute-start | bytes 884744 | tf_op jit(solution)/shard_map/ppermute | solution.py:122
  70.3 15.6 %collective-permute-start.9 = (bf16[96,1536]{1,0:T(8,128)(2,1)S(1)}, bf16[96,1536]{1,0:T(8,128)(2,1)S(1)}, u32[]{:S(2)}, u32[]{:S(2)}) collective-permute-start(bf16[96,1536]{1,0:T(8,128)(2,1)S(1)} %get-tuple-element.23), channel_id=1, source_target_pairs={{0,3},{1,0},{2,1},{3,2},{4,7},{5,4},{6,5},{7,6},{8,11},{9,8},{10,9... | collective-permute-start | bytes 884744 | tf_op jit(solution)/shard_map/ppermute | solution.py:122
  71.7 24.4 %copy-start.3 = (f32[384,512]{1,0:T(8,128)S(1)}, f32[384,512]{1,0:T(8,128)}, u32[]{:S(2)}) copy-start(f32[384,512]{1,0:T(8,128)} %get-tuple-element.10) | copy-start | bytes 2359300
  72.0 13.9 %collective-permute-start.12 = (bf16[384,512]{1,0:T(8,128)(2,1)S(1)}, bf16[384,512]{1,0:T(8,128)(2,1)S(1)}, u32[]{:S(2)}, u32[]{:S(2)}) collective-permute-start(bf16[384,512]{1,0:T(8,128)(2,1)S(1)} %get-tuple-element.20), channel_id=1, source_target_pairs={{0,24},{4,28},{8,0},{12,4},{16,8},{20,12},{24,16},{28,20},{1,25},{... | collective-permute-start | bytes 1179656 | tf_op jit(solution)/shard_map/ppermute | solution.py:215
  73.7 12.2 %collective-permute-start.14 = (bf16[384,512]{1,0:T(8,128)(2,1)S(1)}, bf16[384,512]{1,0:T(8,128)(2,1)S(1)}, u32[]{:S(2)}, u32[]{:S(2)}) collective-permute-start(bf16[384,512]{1,0:T(8,128)(2,1)S(1)} %get-tuple-element.22), channel_id=1, source_target_pairs={{0,16},{4,20},{8,24},{12,28},{16,0},{20,4},{24,8},{28,12},{1,17},{... | collective-permute-start | bytes 1179656 | tf_op jit(solution)/shard_map/ppermute | solution.py:215
  84.2 11.8 %collective-permute-start.16 = (bf16[384,512]{1,0:T(8,128)(2,1)S(1)}, bf16[384,512]{1,0:T(8,128)(2,1)S(1)}, u32[]{:S(2)}, u32[]{:S(2)}) collective-permute-start(bf16[384,512]{1,0:T(8,128)(2,1)S(1)} %get-tuple-element.21), channel_id=1, source_target_pairs={{0,8},{4,12},{8,16},{12,20},{16,24},{20,28},{24,0},{28,4},{1,9},{5... | collective-permute-start | bytes 1179656 | tf_op jit(solution)/shard_map/ppermute | solution.py:215
  85.9 10.5 %copy-start.2 = (bf16[96,6144]{1,0:T(8,128)(2,1)}, bf16[96,6144]{1,0:T(8,128)(2,1)S(1)}, u32[]{:S(2)}) copy-start(bf16[96,6144]{1,0:T(8,128)(2,1)S(1)} %constant_dynamic-update-slice_fusion.3) | copy-start | bytes 3538948
  97.0 12.6 %collective-permute-start.17 = (bf16[96,512]{1,0:T(8,128)(2,1)S(1)}, bf16[96,512]{1,0:T(8,128)(2,1)S(1)}, u32[]{:S(2)}, u32[]{:S(2)}) collective-permute-start(bf16[96,512]{1,0:T(8,128)(2,1)S(1)} %get-tuple-element.28), channel_id=1, source_target_pairs={{0,1},{1,2},{2,3},{3,0},{4,5},{5,6},{6,7},{7,4},{8,9},{9,10},{10,1... | collective-permute-start | bytes 294920 | tf_op jit(solution)/shard_map/ppermute | solution.py:122
  103.0 9.3 %collective-permute-start.18 = (bf16[96,512]{1,0:T(8,128)(2,1)S(1)}, bf16[96,512]{1,0:T(8,128)(2,1)S(1)}, u32[]{:S(2)}, u32[]{:S(2)}) collective-permute-start(bf16[96,512]{1,0:T(8,128)(2,1)S(1)} %get-tuple-element.27), channel_id=1, source_target_pairs={{0,2},{1,3},{2,0},{3,1},{4,6},{5,7},{6,4},{7,5},{8,10},{9,11},{10,... | collective-permute-start | bytes 294920 | tf_op jit(solution)/shard_map/ppermute | solution.py:122
  106.3 6.3 %collective-permute-start.19 = (bf16[96,512]{1,0:T(8,128)(2,1)S(1)}, bf16[96,512]{1,0:T(8,128)(2,1)S(1)}, u32[]{:S(2)}, u32[]{:S(2)}) collective-permute-start(bf16[96,512]{1,0:T(8,128)(2,1)S(1)} %get-tuple-element.26), channel_id=1, source_target_pairs={{0,3},{1,0},{2,1},{3,2},{4,7},{5,4},{6,5},{7,6},{8,11},{9,8},{10,9... | collective-permute-start | bytes 294920 | tf_op jit(solution)/shard_map/ppermute | solution.py:122

commit v10 on v8

--- a/solution.py
+++ b/solution.py
@@ -132,7 +132,7 @@
         pairs = [(i, (i + 2 * d) % shard_count) for i in range(shard_count)]
         gathered.append(lax.ppermute(kv_own, "ctx", pairs))
     kv_half = jnp.concatenate(gathered, axis=0)
-    kv_other = jnp.concatenate([lax.ppermute(p, "ctx", partner) for p in gathered], axis=0)
+    kv_other = lax.ppermute(kv_half, "ctx", partner)
     half = seq // 2
 
     rows = lax.dynamic_slice_in_dim(block_list, shard_index * nb, nb, axis=0).astype(jnp.int32)
@@ -187,17 +187,14 @@
         compiler_params=pltpu.CompilerParams(dimension_semantics=("arbitrary", "arbitrary")),
     )(table, query_rows, out_grad, kv_half, kv_half, kv_other, kv_other)
 
-    span = nb * BLK
-
-    def partner_sum(pos):
-        swapped = lax.ppermute(far_other[pos * span:(pos + 1) * span], "ctx", partner)
-        return far[pos * span:(pos + 1) * span].astype(jnp.float32) + swapped.astype(jnp.float32)
-
-    total = partner_sum(0)
+    from_partner = lax.ppermute(far_other, "ctx", partner)
+    mine = (far.astype(jnp.float32) + from_partner.astype(jnp.float32)).astype(jnp.bfloat16)
+    total = far[0:nb * BLK].astype(jnp.float32) + from_partner[0:nb * BLK].astype(jnp.float32)
     for d in range(1, members):
         pairs = [(i, (i - 2 * d) % shard_count) for i in range(shard_count)]
-        chunk = partner_sum(d).astype(jnp.bfloat16)
-        total = total + lax.ppermute(chunk, "ctx", pairs).astype(jnp.float32)
+        total = total + lax.ppermute(
+            mine[d * nb * BLK:(d + 1) * nb * BLK], "ctx", pairs
+        ).astype(jnp.float32)
     kv_sum = (total + loc).reshape(nb, HD, 2 * kv_here, BLK)
     kv_grad = jnp.transpose(kv_sum, (0, 3, 2, 1)).reshape(nb * BLK, width).astype(jnp.bfloat16)
 

time: 131 us -> 108 us (0.82)
  blocking collectives: 14.4 us -> 0 us
  waiting for transfers between devices: 62 us -> 51.8 us
  starting transfers between devices: 12.9 us -> 16.4 us
    all_to_all x1, waiting for transfers between devices: 23.9 us -> 3.45 us  [shards(): lax.all_to_all(dq, 'uly', split_axis=0, concat_axis=1, tiled=True)]
    all_to_all x1 -> x0, blocking collectives: 14.4 us -> none  [shards(): lax.all_to_all(kv_grad, 'uly', split_axis=0, concat_axis=1, tiled=True)]
    all_to_all x0 -> x1, waiting for transfers between devices: none -> 10.2 us  [shards(): lax.all_to_all(kv_grad, 'uly', split_axis=0, concat_axis=1, tiled=True)]
    all_to_all x0 -> x1, starting transfers between devices: none -> 3.46 us  [shards(): lax.all_to_all(kv_grad, 'uly', split_axis=0, concat_axis=1, tiled=True)]
    ppermute x11 -> x5, starting transfers between devices: 4.72 us -> 2.9 us  [the longest x3 2.6 us: shards(): lax.ppermute(mine[d * nb * BLK:(d + 1) * nb * BLK], 'ctx', pairs)]
    slice x1, local copies, waits for them, and re-layouts: 1.57 us -> 0.08 us  [shards(): mine[d * nb * BLK:(d + 1) * nb * BLK]]
    convert_element_type x1, other arithmetic: 0.37 us -> 1.84 us  [shards(): (far.astype(jnp.float32) + from_partner.astype(jnp.float32)).astype(jnp.b...]
    all_to_all x1, starting transfers between devices: 3.53 us -> 5 us  [shards(): lax.all_to_all(dq, 'uly', split_axis=0, concat_axis=1, tiled=True)]
  transfers between devices with their start and end apart: 15 -> 10, of which waited for: 9 -> 8; matrix products, arithmetic and copies ran while one was open for 6% -> 7% of each run, Pallas kernels for 0% -> 0%
where the time goes in v10:
time: 108 us
  waiting for transfers between devices  51.8 us (48%)
  Pallas kernels  26.5 us (25%)
  starting transfers between devices  16.4 us (15%)
  local copies, waits for them, and re-layouts  7.98 us (7%)
  other arithmetic  4.18 us (4%)
    pallas_call x1, Pallas kernels, shards(): pl.pallas_call(kernel, grid_spec=grid_spec, out_shape=[jax.ShapeDtypeStru...  26.5 us
    ppermute x3, waiting for transfers between devices, shards(): lax.ppermute(mine[d * nb * BLK:(d + 1) * nb * BLK], 'ctx', pairs)  18.4 us
    ppermute x3, waiting for transfers between devices, shards(): gathered.append(lax.ppermute(kv_own, 'ctx', pairs))  17.9 us
    all_to_all x1, waiting for transfers between devices, shards(): lax.all_to_all(kv_grad, 'uly', split_axis=0, concat_axis=1, tiled=True)  10.2 us
    ppermute x3, starting transfers between devices, shards(): gathered.append(lax.ppermute(kv_own, 'ctx', pairs))  5.04 us
    all_to_all x1, starting transfers between devices, shards(): lax.all_to_all(dq, 'uly', split_axis=0, concat_axis=1, tiled=True)  5 us
    all_to_all x1, starting transfers between devices, shards(): lax.all_to_all(kv_grad, 'uly', split_axis=0, concat_axis=1, tiled=True)  3.46 us
    all_to_all x1, waiting for transfers between devices, shards(): lax.all_to_all(dq, 'uly', split_axis=0, concat_axis=1, tiled=True)  3.45 us
  transfers between devices with their start and end apart: 10, of which 8 were waited for; matrix products, arithmetic and copies ran while one was open for 7% of the time, Pallas kernels for 0%

profile of v10, /device:TPU:0, one launch (start us, length us, event | category | flops | bytes accessed | tf_op | source)
XLA Modules:
  0.0 107.6 jit_solution(12715338063503313848)
XLA Ops:
  0.7 1.1 constant_dynamic-slice_fusion
  1.8 3.9 %collective-permute-start.2 = (bf16[384,512]{1,0:T(8,128)(2,1)S(1)}, bf16[384,512]{1,0:T(8,128)(2,1)S(1)}, u32[]{:S(2)}, u32[]{:S(2)}) collective-permute-start(bf16[384,512]{1,0:T(8,128)(2,1)S(1)} %pad_maximum_fusion.1), channel_id=1, source_target_pairs={{0,24},{4,28},{8,0},{12,4},{16,8},{20,12},{24,16},{28,20},{1,25},{... | collective-permute-start | bytes 1179656 | tf_op jit(solution)/shard_map/ppermute | solution.py:133
  5.7 0.5 collective-permute-start.1
  6.2 0.6 collective-permute-start
  6.8 8.4 %collective-permute-done.2 = bf16[384,512]{1,0:T(8,128)(2,1)S(1)} collective-permute-done((bf16[384,512]{1,0:T(8,128)(2,1)S(1)}, bf16[384,512]{1,0:T(8,128)(2,1)S(1)}, u32[]{:S(2)}, u32[]{:S(2)}) %collective-permute-start.2) | collective-permute-done | bytes 393248 | tf_op jit(solution)/shard_map/ppermute | solution.py:133
  15.2 9.5 %collective-permute-done.1 = bf16[384,512]{1,0:T(8,128)(2,1)S(1)} collective-permute-done((bf16[384,512]{1,0:T(8,128)(2,1)S(1)}, bf16[384,512]{1,0:T(8,128)(2,1)S(1)}, u32[]{:S(2)}, u32[]{:S(2)}) %collective-permute-start.1) | collective-permute-done | bytes 393248 | tf_op jit(solution)/shard_map/ppermute | solution.py:133
  24.7 0.1 pad_maximum_fusion.k_ref.v_ref
  25.9 0.6 pad_add_fusion.tbl_ref
  26.5 1.8 %collective-permute-done.3.ko_ref.vo_ref = bf16[1536,512]{1,0:T(8,128)(2,1)S(1)} collective-permute-done((bf16[1536,512]{1,0:T(8,128)(2,1)S(1)}, bf16[1536,512]{1,0:T(8,128)(2,1)S(1)}, u32[]{:S(2)}, u32[]{:S(2)}) %collective-permute-start.3) | collective-permute-done | bytes 1572896 | tf_op jit(solution)/shard_map/ppermute | solution.py:135
  28.3 1.2 %copy-done.1 = bf16[1536,512]{1,0:T(8,128)(2,1)} copy-done((bf16[1536,512]{1,0:T(8,128)(2,1)}, bf16[1536,512]{1,0:T(8,128)(2,1)S(1)}, u32[]{:S(2)}) %copy-start.1) | copy-done | bytes 1572888
  29.5 26.5 %shard_map.76 = (bf16[384,1536]{1,0:T(8,128)(2,1)}, f32[384,512]{1,0:T(8,128)}, bf16[1536,512]{1,0:T(8,128)(2,1)}, bf16[1536,512]{1,0:T(8,128)(2,1)}) custom-call(s32[96]{0:T(128)} %pad_add_fusion.tbl_ref, bf16[384,1536]{1,0:T(8,128)(2,1)} %q_ref.1, bf16[384,1536]{1,0:T(8,128)(2,1)} %do_ref.1, bf16[1536,512]{1,0:T(8,128)(2,1)} %copy-done, ...), custom_call_target="tpu_custom_call" | custom-call | tf_op jit(solution)/shard_map/pallas_call | solution.py:178
  56.0 0.2 collective-permute-start.4
  56.2 5.0 %all-to-all-start = ((bf16[4,96,1536]{2,1,0:T(8,128)(2,1)}), bf16[4,96,1536]{2,1,0:T(8,128)(2,1)S(1)}, u32[]{:S(2)}, u32[]{:S(2)}) async-start(bf16[4,96,1536]{2,1,0:T(8,128)(2,1)} %bitcast.19), calls=%async_computation | async-start | bytes 2359296 | tf_op jit(solution)/shard_map/all_to_all | solution.py:201
  61.2 1.8 %add_convert_fusion = bf16[1536,512]{1,0:T(8,128)(2,1)S(1)} fusion(bf16[1536,512]{1,0:T(8,128)(2,1)} %collective-permute-done.4, bf16[1536,512]{1,0:T(8,128)(2,1)S(1)} %copy-done.2), kind=kLoop, calls=%fused_computation | loop fusion | flops 3145728 | bytes 4718592 | tf_op jit(solution)/shard_map/convert_element_type | solution.py:191
  63.2 0.6 collective-permute-start.5
  63.8 1.5 %collective-permute-start.7 = (bf16[384,512]{1,0:T(8,128)(2,1)S(1)}, bf16[384,512]{1,0:T(8,128)(2,1)S(1)}, u32[]{:S(2)}, u32[]{:S(2)}) collective-permute-start(bf16[384,512]{1,0:T(8,128)(2,1)S(1)} %get-tuple-element.15), channel_id=1, source_target_pairs={{0,8},{4,12},{8,16},{12,20},{16,24},{20,28},{24,0},{28,4},{1,9},{5... | collective-permute-start | bytes 1179656 | tf_op jit(solution)/shard_map/ppermute | solution.py:195
  65.3 0.5 collective-permute-start.6
  65.8 9.4 %collective-permute-done.5 = bf16[384,512]{1,0:T(8,128)(2,1)S(1)} collective-permute-done((bf16[384,512]{1,0:T(8,128)(2,1)S(1)}, bf16[384,512]{1,0:T(8,128)(2,1)S(1)}, u32[]{:S(2)}, u32[]{:S(2)}) %collective-permute-start.5) | collective-permute-done | bytes 393248 | tf_op jit(solution)/shard_map/ppermute | solution.py:195
  75.2 7.6 %collective-permute-done.7 = bf16[384,512]{1,0:T(8,128)(2,1)S(1)} collective-permute-done((bf16[384,512]{1,0:T(8,128)(2,1)S(1)}, bf16[384,512]{1,0:T(8,128)(2,1)S(1)}, u32[]{:S(2)}, u32[]{:S(2)}) %collective-permute-start.7) | collective-permute-done | bytes 393248 | tf_op jit(solution)/shard_map/ppermute | solution.py:195
  82.8 1.4 %collective-permute-done.6 = bf16[384,512]{1,0:T(8,128)(2,1)S(1)} collective-permute-done((bf16[384,512]{1,0:T(8,128)(2,1)S(1)}, bf16[384,512]{1,0:T(8,128)(2,1)S(1)}, u32[]{:S(2)}, u32[]{:S(2)}) %collective-permute-start.6) | collective-permute-done | bytes 393248 | tf_op jit(solution)/shard_map/ppermute | solution.py:195
  84.2 1.3 %add_convert_fusion.1 = bf16[384,512]{1,0:T(8,128)(2,1)S(1)} fusion(f32[384,512]{1,0:T(8,128)S(1)} %copy-done.3, bf16[384,512]{1,0:T(8,128)(2,1)S(1)} %collective-permute-done.7, bf16[384,512]{1,0:T(8,128)(2,1)S(1)} %collective-permute-done.6, bf16[384,512]{1,0:T(8,128)(2,1)S(1)} %collective-permute-done.5, bf16[1536,512]{1,0:T(8,128)(2,1)} %collective-permute-done.4, ...), kind=kLoop, calls=%fused_computation.2 | loop fusion | flops 2162688 | bytes 3145728 | tf_op jit(solution)/shard_map/convert_element_type | solution.py:199
  85.6 0.3 copy.24
  85.9 0.9 convert_element_type.49
  86.8 3.4 %all-to-all-done = bf16[4,96,1536]{2,1,0:T(8,128)(2,1)S(1)} async-done(((bf16[4,96,1536]{2,1,0:T(8,128)(2,1)}), bf16[4,96,1536]{2,1,0:T(8,128)(2,1)S(1)}, u32[]{:S(2)}, u32[]{:S(2)}) %all-to-all-start) | async-done | bytes 1179680 | tf_op jit(solution)/shard_map/all_to_all | solution.py:201
  90.3 3.5 %all-to-all-start.1 = ((bf16[4,96,512]{2,1,0:T(8,128)(2,1)}), bf16[4,96,512]{2,1,0:T(8,128)(2,1)S(1)}, u32[]{:S(2)}, u32[]{:S(2)}) async-start(bf16[4,96,512]{2,1,0:T(8,128)(2,1)} %convert_element_type.49), calls=%async_computation.1 | async-start | bytes 786432 | tf_op jit(solution)/shard_map/all_to_all | solution.py:202
  93.7 1.1 %copy.27 = bf16[4,12,8,1536]{3,2,0,1:T(8,128)(2,1)} copy(bf16[4,12,8,1536]{3,2,1,0:T(8,128)(2,1)S(1)} %bitcast.16) | data formatting | bytes 2359296 | tf_op jit(solution)/shard_map/all_to_all | solution.py:201
  94.9 10.2 %all-to-all-done.1 = bf16[4,96,512]{2,1,0:T(8,128)(2,1)S(1)} async-done(((bf16[4,96,512]{2,1,0:T(8,128)(2,1)}), bf16[4,96,512]{2,1,0:T(8,128)(2,1)S(1)}, u32[]{:S(2)}, u32[]{:S(2)}) %all-to-all-start.1) | async-done | bytes 393248 | tf_op jit(solution)/shard_map/all_to_all | solution.py:202
  105.2 0.5 fusion.11
  105.7 0.3 copy.26
  106.0 0.7 copy.29
  106.7 0.3 copy.25
  106.9 0.7 copy.28
  (28 shorter events, 1.3 us)
Async XLA Ops:
  1.8 23.2 %copy-start.4 = (s32[24,8]{0,1:T(8,128)S(1)}, s32[24,8]{0,1:T(8,128)}, u32[]{:S(2)}) copy-start(s32[24,8]{0,1:T(8,128)} %param.9) | copy-start | bytes 2308
  1.8 13.5 %collective-permute-start.2 = (bf16[384,512]{1,0:T(8,128)(2,1)S(1)}, bf16[384,512]{1,0:T(8,128)(2,1)S(1)}, u32[]{:S(2)}, u32[]{:S(2)}) collective-permute-start(bf16[384,512]{1,0:T(8,128)(2,1)S(1)} %pad_maximum_fusion.1), channel_id=1, source_target_pairs={{0,24},{4,28},{8,0},{12,4},{16,8},{20,12},{24,16},{28,20},{1,25},{... | collective-permute-start | bytes 1179656 | tf_op jit(solution)/shard_map/ppermute | solution.py:133
  5.7 19.0 %collective-permute-start.1 = (bf16[384,512]{1,0:T(8,128)(2,1)S(1)}, bf16[384,512]{1,0:T(8,128)(2,1)S(1)}, u32[]{:S(2)}, u32[]{:S(2)}) collective-permute-start(bf16[384,512]{1,0:T(8,128)(2,1)S(1)} %pad_maximum_fusion.1), channel_id=1, source_target_pairs={{0,16},{4,20},{8,24},{12,28},{16,0},{20,4},{24,8},{28,12},{1,17},{... | collective-permute-start | bytes 1179656 | tf_op jit(solution)/shard_map/ppermute | solution.py:133
  6.2 18.5 %collective-permute-start = (bf16[384,512]{1,0:T(8,128)(2,1)S(1)}, bf16[384,512]{1,0:T(8,128)(2,1)S(1)}, u32[]{:S(2)}, u32[]{:S(2)}) collective-permute-start(bf16[384,512]{1,0:T(8,128)(2,1)S(1)} %pad_maximum_fusion.1), channel_id=1, source_target_pairs={{0,8},{4,12},{8,16},{12,20},{16,24},{20,28},{24,0},{28,4},{1,9},{5... | collective-permute-start | bytes 1179656 | tf_op jit(solution)/shard_map/ppermute | solution.py:133
  24.8 3.5 %copy-start = (bf16[1536,512]{1,0:T(8,128)(2,1)}, bf16[1536,512]{1,0:T(8,128)(2,1)S(1)}, u32[]{:S(2)}) copy-start(bf16[1536,512]{1,0:T(8,128)(2,1)S(1)} %pad_maximum_fusion.k_ref.v_ref) | copy-start | bytes 4718596
  24.8 3.5 %collective-permute-start.3 = (bf16[1536,512]{1,0:T(8,128)(2,1)S(1)}, bf16[1536,512]{1,0:T(8,128)(2,1)S(1)}, u32[]{:S(2)}, u32[]{:S(2)}) collective-permute-start(bf16[1536,512]{1,0:T(8,128)(2,1)S(1)} %pad_maximum_fusion.k_ref.v_ref), channel_id=1, source_target_pairs={{0,4},{4,0},{8,12},{12,8},{16,20},{20,16},{24,28},{28,24},{1,5},{5... | collective-permute-start | bytes 4718600 | tf_op jit(solution)/shard_map/ppermute | solution.py:135
  28.3 1.2 %copy-start.1 = (bf16[1536,512]{1,0:T(8,128)(2,1)}, bf16[1536,512]{1,0:T(8,128)(2,1)S(1)}, u32[]{:S(2)}) copy-start(bf16[1536,512]{1,0:T(8,128)(2,1)S(1)} %collective-permute-done.3.ko_ref.vo_ref) | copy-start | bytes 4718596
  56.0 5.2 %copy-start.2 = (bf16[1536,512]{1,0:T(8,128)(2,1)S(1)}, bf16[1536,512]{1,0:T(8,128)(2,1)}, u32[]{:S(2)}) copy-start(bf16[1536,512]{1,0:T(8,128)(2,1)} %get-tuple-element.8) | copy-start | bytes 4718596
  56.0 5.2 %collective-permute-start.4 = (bf16[1536,512]{1,0:T(8,128)(2,1)}, bf16[1536,512]{1,0:T(8,128)(2,1)}, u32[]{:S(2)}, u32[]{:S(2)}) collective-permute-start(bf16[1536,512]{1,0:T(8,128)(2,1)} %get-tuple-element.9), channel_id=1, source_target_pairs={{0,4},{4,0},{8,12},{12,8},{16,20},{20,16},{24,28},{28,24},{1,5},{5... | collective-permute-start | bytes 4718600 | tf_op jit(solution)/shard_map/ppermute | solution.py:190
  56.2 34.1 %all-to-all-start = ((bf16[4,96,1536]{2,1,0:T(8,128)(2,1)}), bf16[4,96,1536]{2,1,0:T(8,128)(2,1)S(1)}, u32[]{:S(2)}, u32[]{:S(2)}) async-start(bf16[4,96,1536]{2,1,0:T(8,128)(2,1)} %bitcast.19), calls=%async_computation | async-start | bytes 2359296 | tf_op jit(solution)/shard_map/all_to_all | solution.py:201
  63.1 21.1 %copy-start.3 = (f32[384,512]{1,0:T(8,128)S(1)}, f32[384,512]{1,0:T(8,128)}, u32[]{:S(2)}) copy-start(f32[384,512]{1,0:T(8,128)} %get-tuple-element.10) | copy-start | bytes 2359300
  63.2 12.0 %collective-permute-start.5 = (bf16[384,512]{1,0:T(8,128)(2,1)S(1)}, bf16[384,512]{1,0:T(8,128)(2,1)S(1)}, u32[]{:S(2)}, u32[]{:S(2)}) collective-permute-start(bf16[384,512]{1,0:T(8,128)(2,1)S(1)} %get-tuple-element.14), channel_id=1, source_target_pairs={{0,24},{4,28},{8,0},{12,4},{16,8},{20,12},{24,16},{28,20},{1,25},{... | collective-permute-start | bytes 1179656 | tf_op jit(solution)/shard_map/ppermute | solution.py:195
  63.8 19.0 %collective-permute-start.7 = (bf16[384,512]{1,0:T(8,128)(2,1)S(1)}, bf16[384,512]{1,0:T(8,128)(2,1)S(1)}, u32[]{:S(2)}, u32[]{:S(2)}) collective-permute-start(bf16[384,512]{1,0:T(8,128)(2,1)S(1)} %get-tuple-element.15), channel_id=1, source_target_pairs={{0,8},{4,12},{8,16},{12,20},{16,24},{20,28},{24,0},{28,4},{1,9},{5... | collective-permute-start | bytes 1179656 | tf_op jit(solution)/shard_map/ppermute | solution.py:195
  65.3 19.0 %collective-permute-start.6 = (bf16[384,512]{1,0:T(8,128)(2,1)S(1)}, bf16[384,512]{1,0:T(8,128)(2,1)S(1)}, u32[]{:S(2)}, u32[]{:S(2)}) collective-permute-start(bf16[384,512]{1,0:T(8,128)(2,1)S(1)} %get-tuple-element.16), channel_id=1, source_target_pairs={{0,16},{4,20},{8,24},{12,28},{16,0},{20,4},{24,8},{28,12},{1,17},{... | collective-permute-start | bytes 1179656 | tf_op jit(solution)/shard_map/ppermute | solution.py:195
  90.3 14.8 %all-to-all-start.1 = ((bf16[4,96,512]{2,1,0:T(8,128)(2,1)}), bf16[4,96,512]{2,1,0:T(8,128)(2,1)S(1)}, u32[]{:S(2)}, u32[]{:S(2)}) async-start(bf16[4,96,512]{2,1,0:T(8,128)(2,1)} %convert_element_type.49), calls=%async_computation.1 | async-start | bytes 786432 | tf_op jit(solution)/shard_map/all_to_all | solution.py:202

commit v11 on v10

--- a/solution.py
+++ b/solution.py
@@ -17,7 +17,7 @@
 
 def attention_kernel(
     tbl_ref,
-    q_ref, do_ref, k_ref, v_ref, ko_ref, vo_ref,
+    q_ref, do_ref, k_ref, v_ref, ko_ref, vo_ref, dq_in,
     dq_ref, loc_ref, far_ref, fo_ref,
     kc_ref, vc_ref, loc_acc, far_acc, fo_acc,
     *, hpk, kv_here, nb,
@@ -119,21 +119,13 @@
     hpk = heads_here // kv_here
     width = 2 * kv_here * HD
     first_kv = lane_index * heads_here // GROUP
-    key_own = lax.dynamic_slice_in_dim(key_rows, first_kv * HD, kv_here * HD, axis=1)
-    value_own = lax.dynamic_slice_in_dim(value_rows, first_kv * HD, kv_here * HD, axis=1)
-    kv_own = jnp.concatenate([key_own, value_own], axis=1)
     shard_count = lax.axis_size("ctx")
     partner = [(i, i ^ 1) for i in range(shard_count)]
     core = shard_index % 2
     members = shard_count // 2
     member = shard_index // 2
-    gathered = [kv_own]
-    for d in range(1, members):
-        pairs = [(i, (i + 2 * d) % shard_count) for i in range(shard_count)]
-        gathered.append(lax.ppermute(kv_own, "ctx", pairs))
-    kv_half = jnp.concatenate(gathered, axis=0)
-    kv_other = lax.ppermute(kv_half, "ctx", partner)
     half = seq // 2
+    span = nb * BLK
 
     rows = lax.dynamic_slice_in_dim(block_list, shard_index * nb, nb, axis=0).astype(jnp.int32)
     owner = rows // nb
@@ -149,54 +141,74 @@
     side = owner_side.reshape(-1)
     table = jnp.concatenate([blk, side, dst, kind]).astype(jnp.int32)
 
-    kernel = functools.partial(attention_kernel, hpk=hpk, kv_here=kv_here, nb=nb)
-    grid_spec = pltpu.PrefetchScalarGridSpec(
-        num_scalar_prefetch=1,
-        grid=(kv_here, nb),
-        in_specs=[
-            pl.BlockSpec((BLK, hpk * HD), lambda g, b, *_: (b, g)),
-            pl.BlockSpec((BLK, hpk * HD), lambda g, b, *_: (b, g)),
-            pl.BlockSpec((half, HD), lambda g, b, *_: (0, g)),
-            pl.BlockSpec((half, HD), lambda g, b, *_: (0, kv_here + g)),
-            pl.BlockSpec((half, HD), lambda g, b, *_: (0, g)),
-            pl.BlockSpec((half, HD), lambda g, b, *_: (0, kv_here + g)),
-        ],
-        out_specs=[
-            pl.BlockSpec((BLK, hpk * HD), lambda g, b, *_: (b, g)),
-            pl.BlockSpec((nb * BLK, width), lambda g, b, *_: (0, 0)),
-            pl.BlockSpec((half, width), lambda g, b, *_: (0, 0)),
-            pl.BlockSpec((half, width), lambda g, b, *_: (0, 0)),
-        ],
-        scratch_shapes=[
-            pltpu.VMEM((SLOTS * BLK, HD), jnp.bfloat16),
-            pltpu.VMEM((SLOTS * BLK, HD), jnp.bfloat16),
-            pltpu.VMEM((2 * kv_here, nb * BLK, HD), jnp.float32),
-            pltpu.VMEM((2 * kv_here, half, HD), jnp.float32),
-            pltpu.VMEM((2 * kv_here, half, HD), jnp.float32),
-        ],
-    )
-    dq, loc, far, far_other = pl.pallas_call(
-        kernel,
-        grid_spec=grid_spec,
-        out_shape=[
-            jax.ShapeDtypeStruct((nb * BLK, heads_here * HD), jnp.bfloat16),
-            jax.ShapeDtypeStruct((nb * BLK, width), jnp.float32),
-            jax.ShapeDtypeStruct((half, width), jnp.bfloat16),
-            jax.ShapeDtypeStruct((half, width), jnp.bfloat16),
-        ],
-        compiler_params=pltpu.CompilerParams(dimension_semantics=("arbitrary", "arbitrary")),
-    )(table, query_rows, out_grad, kv_half, kv_half, kv_other, kv_other)
-
-    from_partner = lax.ppermute(far_other, "ctx", partner)
-    mine = (far.astype(jnp.float32) + from_partner.astype(jnp.float32)).astype(jnp.bfloat16)
-    total = far[0:nb * BLK].astype(jnp.float32) + from_partner[0:nb * BLK].astype(jnp.float32)
-    for d in range(1, members):
-        pairs = [(i, (i - 2 * d) % shard_count) for i in range(shard_count)]
-        total = total + lax.ppermute(
-            mine[d * nb * BLK:(d + 1) * nb * BLK], "ctx", pairs
-        ).astype(jnp.float32)
-    kv_sum = (total + loc).reshape(nb, HD, 2 * kv_here, BLK)
-    kv_grad = jnp.transpose(kv_sum, (0, 3, 2, 1)).reshape(nb * BLK, width).astype(jnp.bfloat16)
+    kernel = functools.partial(attention_kernel, hpk=hpk, kv_here=1, nb=nb)
+    dq = jnp.zeros((nb * BLK, heads_here * HD), jnp.bfloat16)
+    sums = []
+    for g in range(kv_here):
+        col = (first_kv + g) * HD
+        kv_own = jnp.concatenate(
+            [
+                lax.dynamic_slice_in_dim(key_rows, col, HD, axis=1),
+                lax.dynamic_slice_in_dim(value_rows, col, HD, axis=1),
+            ],
+            axis=1,
+        )
+        gathered = [kv_own]
+        for d in range(1, members):
+            pairs = [(i, (i + 2 * d) % shard_count) for i in range(shard_count)]
+            gathered.append(lax.ppermute(kv_own, "ctx", pairs))
+        kv_half = jnp.concatenate(gathered, axis=0)
+        kv_other = lax.ppermute(kv_half, "ctx", partner)
+        grid_spec = pltpu.PrefetchScalarGridSpec(
+            num_scalar_prefetch=1,
+            grid=(1, nb),
+            in_specs=[
+                pl.BlockSpec((BLK, hpk * HD), lambda z, b, *_, g=g: (b, g)),
+                pl.BlockSpec((BLK, hpk * HD), lambda z, b, *_, g=g: (b, g)),
+                pl.BlockSpec((half, HD), lambda z, b, *_: (0, 0)),
+                pl.BlockSpec((half, HD), lambda z, b, *_: (0, 1)),
+                pl.BlockSpec((half, HD), lambda z, b, *_: (0, 0)),
+                pl.BlockSpec((half, HD), lambda z, b, *_: (0, 1)),
+                pl.BlockSpec(memory_space=pl.ANY),
+            ],
+            out_specs=[
+                pl.BlockSpec((BLK, hpk * HD), lambda z, b, *_, g=g: (b, g)),
+                pl.BlockSpec((span, 2 * HD), lambda z, b, *_: (0, 0)),
+                pl.BlockSpec((half, 2 * HD), lambda z, b, *_: (0, 0)),
+                pl.BlockSpec((half, 2 * HD), lambda z, b, *_: (0, 0)),
+            ],
+            scratch_shapes=[
+                pltpu.VMEM((SLOTS * BLK, HD), jnp.bfloat16),
+                pltpu.VMEM((SLOTS * BLK, HD), jnp.bfloat16),
+                pltpu.VMEM((2, span, HD), jnp.float32),
+                pltpu.VMEM((2, half, HD), jnp.float32),
+                pltpu.VMEM((2, half, HD), jnp.float32),
+            ],
+        )
+        dq, loc, far, far_other = pl.pallas_call(
+            kernel,
+            grid_spec=grid_spec,
+            out_shape=[
+                jax.ShapeDtypeStruct((nb * BLK, heads_here * HD), jnp.bfloat16),
+                jax.ShapeDtypeStruct((span, 2 * HD), jnp.float32),
+                jax.ShapeDtypeStruct((half, 2 * HD), jnp.bfloat16),
+                jax.ShapeDtypeStruct((half, 2 * HD), jnp.bfloat16),
+            ],
+            input_output_aliases={7: 0},
+            compiler_params=pltpu.CompilerParams(dimension_semantics=("arbitrary", "arbitrary")),
+        )(table, query_rows, out_grad, kv_half, kv_half, kv_other, kv_other, dq)
+        from_partner = lax.ppermute(far_other, "ctx", partner)
+        mine = (far.astype(jnp.float32) + from_partner.astype(jnp.float32)).astype(jnp.bfloat16)
+        total = far[0:span].astype(jnp.float32) + from_partner[0:span].astype(jnp.float32)
+        for d in range(1, members):
+            pairs = [(i, (i - 2 * d) % shard_count) for i in range(shard_count)]
+            total = total + lax.ppermute(
+                mine[d * span:(d + 1) * span], "ctx", pairs
+            ).astype(jnp.float32)
+        sums.append((total + loc).reshape(nb, HD, 2, BLK))
+    stacked = jnp.stack([s[:, :, 0] for s in sums] + [s[:, :, 1] for s in sums], axis=2)
+    kv_grad = jnp.transpose(stacked, (0, 3, 2, 1)).reshape(span, 2 * kv_here * HD).astype(jnp.bfloat16)
+    width = 2 * kv_here * HD
 
     query_out = lax.all_to_all(dq, "uly", split_axis=0, concat_axis=1, tiled=True)
     kv_seq = lax.all_to_all(kv_grad, "uly", split_axis=0, concat_axis=1, tiled=True)

time: 108 us -> 131 us (1.21)
  blocking collectives: 0 us -> 15.8 us
  Pallas kernels: 26.5 us -> 29 us
  starting transfers between devices: 16.4 us -> 18.9 us
  local copies, waits for them, and re-layouts: 7.98 us -> 9.93 us
  waiting for transfers between devices: 51.8 us -> 49.9 us
  other arithmetic: 4.18 us -> 5.82 us
    all_to_all x1, waiting for transfers between devices: 3.45 us -> 24.7 us  [shards(): lax.all_to_all(dq, 'uly', split_axis=0, concat_axis=1, tiled=True)]
    all_to_all x0 -> x1, blocking collectives: none -> 15.8 us  [shards(): lax.all_to_all(kv_grad, 'uly', split_axis=0, concat_axis=1, tiled=True)]
    all_to_all x1 -> x0, waiting for transfers between devices: 10.2 us -> none  [shards(): lax.all_to_all(kv_grad, 'uly', split_axis=0, concat_axis=1, tiled=True)]
    ppermute x3 -> x6, waiting for transfers between devices: 17.9 us -> 11.6 us  [shards(): gathered.append(lax.ppermute(kv_own, 'ctx', pairs))]
    ppermute x3 -> x6, waiting for transfers between devices: 18.4 us -> 13.7 us  [shards(): lax.ppermute(mine[d * span:(d + 1) * span], 'ctx', pairs)]
    ppermute x3 -> x6, starting transfers between devices: 5.04 us -> 9.11 us  [shards(): gathered.append(lax.ppermute(kv_own, 'ctx', pairs))]
    all_to_all x1 -> x0, starting transfers between devices: 3.46 us -> none  [shards(): lax.all_to_all(kv_grad, 'uly', split_axis=0, concat_axis=1, tiled=True)]
    ppermute x3 -> x6, starting transfers between devices: 2.6 us -> 5.58 us  [shards(): lax.ppermute(mine[d * span:(d + 1) * span], 'ctx', pairs)]
  transfers between devices with their start and end apart: 10 -> 17, of which waited for: 8 -> 11; matrix products, arithmetic and copies ran while one was open for 7% -> 7% of each run, Pallas kernels for 0% -> 22%
where the time goes in v11:
time: 131 us; the launch traced here: 130 us
  waiting for transfers between devices  49.9 us (38%)
  Pallas kernels  29 us (22%)
  starting transfers between devices  18.9 us (14%)
  blocking collectives  15.8 us (12%)
  local copies, waits for them, and re-layouts  9.93 us (8%)
  other arithmetic  5.82 us (4%)
    pallas_call x2, Pallas kernels, shards(): pl.pallas_call(kernel, grid_spec=grid_spec, out_shape=[jax.ShapeDtypeStru...  29 us
    all_to_all x1, waiting for transfers between devices, shards(): lax.all_to_all(dq, 'uly', split_axis=0, concat_axis=1, tiled=True)  24.7 us
    all_to_all x1, blocking collectives, shards(): lax.all_to_all(kv_grad, 'uly', split_axis=0, concat_axis=1, tiled=True)  15.8 us
    ppermute x6, waiting for transfers between devices, shards(): lax.ppermute(mine[d * span:(d + 1) * span], 'ctx', pairs)  13.7 us
    ppermute x6, waiting for transfers between devices, shards(): gathered.append(lax.ppermute(kv_own, 'ctx', pairs))  11.6 us
    ppermute x6, starting transfers between devices, shards(): gathered.append(lax.ppermute(kv_own, 'ctx', pairs))  9.11 us
    ppermute x6, starting transfers between devices, shards(): lax.ppermute(mine[d * span:(d + 1) * span], 'ctx', pairs)  5.58 us
    all_to_all x1, starting transfers between devices, shards(): lax.all_to_all(dq, 'uly', split_axis=0, concat_axis=1, tiled=True)  3.53 us
  transfers between devices with their start and end apart: 17, of which 11 were waited for; matrix products, arithmetic and copies ran while one was open for 7% of the time, Pallas kernels for 22%

profile of v11, /device:TPU:0, one launch (start us, length us, event | category | flops | bytes accessed | tf_op | source)
XLA Modules:
  0.0 130.4 jit_solution(13469668794611380807)
XLA Ops:
  0.7 1.1 constant_dynamic-slice_fusion
  1.8 3.0 %collective-permute-start.4 = (bf16[384,256]{1,0:T(8,128)(2,1)S(1)}, bf16[384,256]{1,0:T(8,128)(2,1)S(1)}, u32[]{:S(2)}, u32[]{:S(2)}) collective-permute-start(bf16[384,256]{1,0:T(8,128)(2,1)S(1)} %pad_maximum_fusion.3), channel_id=1, source_target_pairs={{0,8},{4,12},{8,16},{12,20},{16,24},{20,28},{24,0},{28,4},{1,9},{5... | collective-permute-start | bytes 589832 | tf_op jit(solution)/shard_map/ppermute | solution.py:159
  4.8 1.5 %collective-permute-start.5 = (bf16[384,256]{1,0:T(8,128)(2,1)S(1)}, bf16[384,256]{1,0:T(8,128)(2,1)S(1)}, u32[]{:S(2)}, u32[]{:S(2)}) collective-permute-start(bf16[384,256]{1,0:T(8,128)(2,1)S(1)} %pad_maximum_fusion.3), channel_id=1, source_target_pairs={{0,16},{4,20},{8,24},{12,28},{16,0},{20,4},{24,8},{28,12},{1,17},{... | collective-permute-start | bytes 589832 | tf_op jit(solution)/shard_map/ppermute | solution.py:159
  6.3 1.4 %collective-permute-start.6 = (bf16[384,256]{1,0:T(8,128)(2,1)S(1)}, bf16[384,256]{1,0:T(8,128)(2,1)S(1)}, u32[]{:S(2)}, u32[]{:S(2)}) collective-permute-start(bf16[384,256]{1,0:T(8,128)(2,1)S(1)} %pad_maximum_fusion.3), channel_id=1, source_target_pairs={{0,24},{4,28},{8,0},{12,4},{16,8},{20,12},{24,16},{28,20},{1,25},{... | collective-permute-start | bytes 589832 | tf_op jit(solution)/shard_map/ppermute | solution.py:159
  9.2 2.3 %collective-permute-done.4 = bf16[384,256]{1,0:T(8,128)(2,1)S(1)} collective-permute-done((bf16[384,256]{1,0:T(8,128)(2,1)S(1)}, bf16[384,256]{1,0:T(8,128)(2,1)S(1)}, u32[]{:S(2)}, u32[]{:S(2)}) %collective-permute-start.4) | collective-permute-done | bytes 196640 | tf_op jit(solution)/shard_map/ppermute | solution.py:159
  11.5 2.0 %collective-permute-start.2 = (bf16[384,256]{1,0:T(8,128)(2,1)S(1)}, bf16[384,256]{1,0:T(8,128)(2,1)S(1)}, u32[]{:S(2)}, u32[]{:S(2)}) collective-permute-start(bf16[384,256]{1,0:T(8,128)(2,1)S(1)} %pad_maximum_fusion.2), channel_id=1, source_target_pairs={{0,24},{4,28},{8,0},{12,4},{16,8},{20,12},{24,16},{28,20},{1,25},{... | collective-permute-start | bytes 589832 | tf_op jit(solution)/shard_map/ppermute | solution.py:159
  13.5 2.3 %collective-permute-done.5 = bf16[384,256]{1,0:T(8,128)(2,1)S(1)} collective-permute-done((bf16[384,256]{1,0:T(8,128)(2,1)S(1)}, bf16[384,256]{1,0:T(8,128)(2,1)S(1)}, u32[]{:S(2)}, u32[]{:S(2)}) %collective-permute-start.5) | collective-permute-done | bytes 196640 | tf_op jit(solution)/shard_map/ppermute | solution.py:159
  17.1 2.8 %collective-permute-done = bf16[384,256]{1,0:T(8,128)(2,1)S(1)} collective-permute-done((bf16[384,256]{1,0:T(8,128)(2,1)S(1)}, bf16[384,256]{1,0:T(8,128)(2,1)S(1)}, u32[]{:S(2)}, u32[]{:S(2)}) %collective-permute-start) | collective-permute-done | bytes 196640 | tf_op jit(solution)/shard_map/ppermute | solution.py:159
  20.0 3.3 %collective-permute-done.1 = bf16[384,256]{1,0:T(8,128)(2,1)S(1)} collective-permute-done((bf16[384,256]{1,0:T(8,128)(2,1)S(1)}, bf16[384,256]{1,0:T(8,128)(2,1)S(1)}, u32[]{:S(2)}, u32[]{:S(2)}) %collective-permute-start.1) | collective-permute-done | bytes 196640 | tf_op jit(solution)/shard_map/ppermute | solution.py:159
  23.8 0.7 pad_add_fusion.tbl_ref
  24.5 1.2 broadcast_in_dim.10.dq_in
  25.7 14.4 %shard_map.76 = (bf16[384,1536]{1,0:T(8,128)(2,1)}, f32[384,256]{1,0:T(8,128)}, bf16[1536,256]{1,0:T(8,128)(2,1)}, bf16[1536,256]{1,0:T(8,128)(2,1)}) custom-call(s32[96]{0:T(128)} %pad_add_fusion.tbl_ref, bf16[384,1536]{1,0:T(8,128)(2,1)} %q_ref.3, bf16[384,1536]{1,0:T(8,128)(2,1)} %do_ref.3, ...), custom_call_target="tpu_custom_call", output_to_operand_aliasing={{0}: (7, {})} | custom-call | tf_op jit(solution)/shard_map/pallas_call | solution.py:188
  40.6 0.9 copy-done.3
  41.5 14.6 %shard_map.77 = (bf16[384,1536]{1,0:T(8,128)(2,1)}, f32[384,256]{1,0:T(8,128)}, bf16[1536,256]{1,0:T(8,128)(2,1)}, bf16[1536,256]{1,0:T(8,128)(2,1)}) custom-call(s32[96]{0:T(128)} %pad_add_fusion.tbl_ref, bf16[384,1536]{1,0:T(8,128)(2,1)} %q_ref.3, bf16[384,1536]{1,0:T(8,128)(2,1)} %do_ref.3, ...), custom_call_target="tpu_custom_call", output_to_operand_aliasing={{0}: (7, {})} | custom-call | tf_op jit(solution)/shard_map/pallas_call | solution.py:188
  56.2 1.4 %add_convert_fusion.1 = bf16[1536,256]{1,0:T(8,128)(2,1)S(1)} fusion(bf16[1536,256]{1,0:T(8,128)(2,1)} %collective-permute-done.8, bf16[1536,256]{1,0:T(8,128)(2,1)S(1)} %copy-done.5), kind=kLoop, calls=%fused_computation.1 | loop fusion | flops 1572864 | bytes 2359296 | tf_op jit(solution)/shard_map/convert_element_type | solution.py:201
  57.7 1.4 %collective-permute-start.10 = (bf16[384,256]{1,0:T(8,128)(2,1)S(1)}, bf16[384,256]{1,0:T(8,128)(2,1)S(1)}, u32[]{:S(2)}, u32[]{:S(2)}) collective-permute-start(bf16[384,256]{1,0:T(8,128)(2,1)S(1)} %get-tuple-element.24), channel_id=1, source_target_pairs={{0,16},{4,20},{8,24},{12,28},{16,0},{20,4},{24,8},{28,12},{1,17},{... | collective-permute-start | bytes 589832 | tf_op jit(solution)/shard_map/ppermute | solution.py:205
  59.7 2.3 %collective-permute-start.9 = (bf16[384,256]{1,0:T(8,128)(2,1)S(1)}, bf16[384,256]{1,0:T(8,128)(2,1)S(1)}, u32[]{:S(2)}, u32[]{:S(2)}) collective-permute-start(bf16[384,256]{1,0:T(8,128)(2,1)S(1)} %get-tuple-element.22), channel_id=1, source_target_pairs={{0,24},{4,28},{8,0},{12,4},{16,8},{20,12},{24,16},{28,20},{1,25},{... | collective-permute-start | bytes 589832 | tf_op jit(solution)/shard_map/ppermute | solution.py:205
  62.2 0.7 fusion.11
  62.9 0.8 collective-permute-start.13
  64.2 5.5 %collective-permute-done.10 = bf16[384,256]{1,0:T(8,128)(2,1)S(1)} collective-permute-done((bf16[384,256]{1,0:T(8,128)(2,1)S(1)}, bf16[384,256]{1,0:T(8,128)(2,1)S(1)}, u32[]{:S(2)}, u32[]{:S(2)}) %collective-permute-start.10) | collective-permute-done | bytes 196640 | tf_op jit(solution)/shard_map/ppermute | solution.py:205
  69.6 1.5 %collective-permute-done.9 = bf16[384,256]{1,0:T(8,128)(2,1)S(1)} collective-permute-done((bf16[384,256]{1,0:T(8,128)(2,1)S(1)}, bf16[384,256]{1,0:T(8,128)(2,1)S(1)}, u32[]{:S(2)}, u32[]{:S(2)}) %collective-permute-start.9) | collective-permute-done | bytes 196640 | tf_op jit(solution)/shard_map/ppermute | solution.py:205
  71.2 1.2 add_convert_fusion.3
  73.1 2.3 %collective-permute-done.13 = bf16[384,256]{1,0:T(8,128)(2,1)S(1)} collective-permute-done((bf16[384,256]{1,0:T(8,128)(2,1)}, bf16[384,256]{1,0:T(8,128)(2,1)S(1)}, u32[]{:S(2)}, u32[]{:S(2)}) %collective-permute-start.13) | collective-permute-done | bytes 196640 | tf_op jit(solution)/shard_map/ppermute | solution.py:205
  75.4 4.3 %collective-permute-done.15 = bf16[384,256]{1,0:T(8,128)(2,1)} collective-permute-done((bf16[384,256]{1,0:T(8,128)(2,1)S(1)}, bf16[384,256]{1,0:T(8,128)(2,1)}, u32[]{:S(2)}, u32[]{:S(2)}) %collective-permute-start.15) | collective-permute-done | bytes 196640 | tf_op jit(solution)/shard_map/ppermute | solution.py:205
  79.7 1.1 add_convert_fusion.2
  81.5 0.9 maximum_bitcast_fusion
  82.6 15.8 %all_to_all.32 = bf16[4,96,512]{2,1,0:T(8,128)(2,1)S(1)} all-to-all(bf16[4,96,512]{2,1,0:T(8,128)(2,1)S(1)} %convert_element_type.74), channel_id=1, replica_groups=mesh['ctx'=8,'uly'=4] {'uly'}, dimensions={0} | all-to-all | bytes 786432 | tf_op jit(solution)/shard_map/all_to_all | solution.py:214
  98.4 3.5 %all-to-all-start = ((bf16[4,96,1536]{2,1,0:T(8,128)(2,1)}), bf16[4,96,1536]{2,1,0:T(8,128)(2,1)S(1)}, u32[]{:S(2)}, u32[]{:S(2)}) async-start(bf16[4,96,1536]{2,1,0:T(8,128)(2,1)} %bitcast), calls=%async_computation | async-start | bytes 2359296 | tf_op jit(solution)/shard_map/all_to_all | solution.py:213
  102.9 0.7 copy.40
  103.8 0.7 copy.41
  104.5 24.7 %all-to-all-done = bf16[4,96,1536]{2,1,0:T(8,128)(2,1)S(1)} async-done(((bf16[4,96,1536]{2,1,0:T(8,128)(2,1)}), bf16[4,96,1536]{2,1,0:T(8,128)(2,1)S(1)}, u32[]{:S(2)}, u32[]{:S(2)}) %all-to-all-start) | async-done | bytes 1179680 | tf_op jit(solution)/shard_map/all_to_all | solution.py:213
  129.2 1.1 copy.39
  (65 shorter events, 7.9 us)
Async XLA Ops:
  0.6 8.3 %copy-start.8 = (s32[24,8]{0,1:T(8,128)S(1)}, s32[24,8]{0,1:T(8,128)}, u32[]{:S(2)}) copy-start(s32[24,8]{0,1:T(8,128)} %param.9) | copy-start | bytes 2308
  1.8 9.7 %collective-permute-start.4 = (bf16[384,256]{1,0:T(8,128)(2,1)S(1)}, bf16[384,256]{1,0:T(8,128)(2,1)S(1)}, u32[]{:S(2)}, u32[]{:S(2)}) collective-permute-start(bf16[384,256]{1,0:T(8,128)(2,1)S(1)} %pad_maximum_fusion.3), channel_id=1, source_target_pairs={{0,8},{4,12},{8,16},{12,20},{16,24},{20,28},{24,0},{28,4},{1,9},{5... | collective-permute-start | bytes 589832 | tf_op jit(solution)/shard_map/ppermute | solution.py:159
  4.8 11.0 %collective-permute-start.5 = (bf16[384,256]{1,0:T(8,128)(2,1)S(1)}, bf16[384,256]{1,0:T(8,128)(2,1)S(1)}, u32[]{:S(2)}, u32[]{:S(2)}) collective-permute-start(bf16[384,256]{1,0:T(8,128)(2,1)S(1)} %pad_maximum_fusion.3), channel_id=1, source_target_pairs={{0,16},{4,20},{8,24},{12,28},{16,0},{20,4},{24,8},{28,12},{1,17},{... | collective-permute-start | bytes 589832 | tf_op jit(solution)/shard_map/ppermute | solution.py:159
  6.3 10.0 %collective-permute-start.6 = (bf16[384,256]{1,0:T(8,128)(2,1)S(1)}, bf16[384,256]{1,0:T(8,128)(2,1)S(1)}, u32[]{:S(2)}, u32[]{:S(2)}) collective-permute-start(bf16[384,256]{1,0:T(8,128)(2,1)S(1)} %pad_maximum_fusion.3), channel_id=1, source_target_pairs={{0,24},{4,28},{8,0},{12,4},{16,8},{20,12},{24,16},{28,20},{1,25},{... | collective-permute-start | bytes 589832 | tf_op jit(solution)/shard_map/ppermute | solution.py:159
  7.8 12.2 %collective-permute-start = (bf16[384,256]{1,0:T(8,128)(2,1)S(1)}, bf16[384,256]{1,0:T(8,128)(2,1)S(1)}, u32[]{:S(2)}, u32[]{:S(2)}) collective-permute-start(bf16[384,256]{1,0:T(8,128)(2,1)S(1)} %pad_maximum_fusion.2), channel_id=1, source_target_pairs={{0,8},{4,12},{8,16},{12,20},{16,24},{20,28},{24,0},{28,4},{1,9},{5... | collective-permute-start | bytes 589832 | tf_op jit(solution)/shard_map/ppermute | solution.py:159
  8.4 14.9 %collective-permute-start.1 = (bf16[384,256]{1,0:T(8,128)(2,1)S(1)}, bf16[384,256]{1,0:T(8,128)(2,1)S(1)}, u32[]{:S(2)}, u32[]{:S(2)}) collective-permute-start(bf16[384,256]{1,0:T(8,128)(2,1)S(1)} %pad_maximum_fusion.2), channel_id=1, source_target_pairs={{0,16},{4,20},{8,24},{12,28},{16,0},{20,4},{24,8},{28,12},{1,17},{... | collective-permute-start | bytes 589832 | tf_op jit(solution)/shard_map/ppermute | solution.py:159
  11.5 12.1 %collective-permute-start.2 = (bf16[384,256]{1,0:T(8,128)(2,1)S(1)}, bf16[384,256]{1,0:T(8,128)(2,1)S(1)}, u32[]{:S(2)}, u32[]{:S(2)}) collective-permute-start(bf16[384,256]{1,0:T(8,128)(2,1)S(1)} %pad_maximum_fusion.2), channel_id=1, source_target_pairs={{0,24},{4,28},{8,0},{12,4},{16,8},{20,12},{24,16},{28,20},{1,25},{... | collective-permute-start | bytes 589832 | tf_op jit(solution)/shard_map/ppermute | solution.py:159
  16.4 9.3 %copy-start = (bf16[1536,256]{1,0:T(8,128)(2,1)}, bf16[1536,256]{1,0:T(8,128)(2,1)S(1)}, u32[]{:S(2)}) copy-start(bf16[1536,256]{1,0:T(8,128)(2,1)S(1)} %pad_maximum_fusion.1.k_ref.v_ref) | copy-start | bytes 2359300
  16.4 8.1 %collective-permute-start.7 = (bf16[1536,256]{1,0:T(8,128)(2,1)S(1)}, bf16[1536,256]{1,0:T(8,128)(2,1)S(1)}, u32[]{:S(2)}, u32[]{:S(2)}) collective-permute-start(bf16[1536,256]{1,0:T(8,128)(2,1)S(1)} %pad_maximum_fusion.1.k_ref.v_ref), channel_id=1, source_target_pairs={{0,4},{4,0},{8,12},{12,8},{16,20},{20,16},{24,28},{28,24},{1,5},{5... | collective-permute-start | bytes 2359304 | tf_op jit(solution)/shard_map/ppermute | solution.py:161
  23.7 16.5 %copy-start.1 = (bf16[1536,256]{1,0:T(8,128)(2,1)}, bf16[1536,256]{1,0:T(8,128)(2,1)S(1)}, u32[]{:S(2)}) copy-start(bf16[1536,256]{1,0:T(8,128)(2,1)S(1)} %pad_maximum_fusion.k_ref.v_ref) | copy-start | bytes 2359300
  23.7 16.9 %collective-permute-start.3 = (bf16[1536,256]{1,0:T(8,128)(2,1)S(1)}, bf16[1536,256]{1,0:T(8,128)(2,1)S(1)}, u32[]{:S(2)}, u32[]{:S(2)}) collective-permute-start(bf16[1536,256]{1,0:T(8,128)(2,1)S(1)} %pad_maximum_fusion.k_ref.v_ref), channel_id=1, source_target_pairs={{0,4},{4,0},{8,12},{12,8},{16,20},{20,16},{24,28},{28,24},{1,5},{5... | collective-permute-start | bytes 2359304 | tf_op jit(solution)/shard_map/ppermute | solution.py:161
  24.5 1.3 copy-start.2
  40.2 16.1 %collective-permute-start.8 = (bf16[1536,256]{1,0:T(8,128)(2,1)}, bf16[1536,256]{1,0:T(8,128)(2,1)}, u32[]{:S(2)}, u32[]{:S(2)}) collective-permute-start(bf16[1536,256]{1,0:T(8,128)(2,1)} %get-tuple-element.14), channel_id=1, source_target_pairs={{0,4},{4,0},{8,12},{12,8},{16,20},{20,16},{24,28},{28,24},{1,5},{5... | collective-permute-start | bytes 2359304 | tf_op jit(solution)/shard_map/ppermute | solution.py:200
  40.6 0.9 copy-start.3
  41.5 14.7 %copy-start.5 = (bf16[1536,256]{1,0:T(8,128)(2,1)S(1)}, bf16[1536,256]{1,0:T(8,128)(2,1)}, u32[]{:S(2)}) copy-start(bf16[1536,256]{1,0:T(8,128)(2,1)} %get-tuple-element.13) | copy-start | bytes 2359300
  56.1 5.9 %collective-permute-start.12 = (bf16[1536,256]{1,0:T(8,128)(2,1)}, bf16[1536,256]{1,0:T(8,128)(2,1)S(1)}, u32[]{:S(2)}, u32[]{:S(2)}) collective-permute-start(bf16[1536,256]{1,0:T(8,128)(2,1)} %get-tuple-element.17), channel_id=1, source_target_pairs={{0,4},{4,0},{8,12},{12,8},{16,20},{20,16},{24,28},{28,24},{1,5},{5... | collective-permute-start | bytes 2359304 | tf_op jit(solution)/shard_map/ppermute | solution.py:200
  57.6 4.4 %copy-start.4 = (bf16[1536,256]{1,0:T(8,128)(2,1)S(1)}, bf16[1536,256]{1,0:T(8,128)(2,1)}, u32[]{:S(2)}) copy-start(bf16[1536,256]{1,0:T(8,128)(2,1)} %get-tuple-element.16) | copy-start | bytes 2359300
  57.7 12.0 %collective-permute-start.10 = (bf16[384,256]{1,0:T(8,128)(2,1)S(1)}, bf16[384,256]{1,0:T(8,128)(2,1)S(1)}, u32[]{:S(2)}, u32[]{:S(2)}) collective-permute-start(bf16[384,256]{1,0:T(8,128)(2,1)S(1)} %get-tuple-element.24), channel_id=1, source_target_pairs={{0,16},{4,20},{8,24},{12,28},{16,0},{20,4},{24,8},{28,12},{1,17},{... | collective-permute-start | bytes 589832 | tf_op jit(solution)/shard_map/ppermute | solution.py:205
  59.1 10.6 %collective-permute-start.11 = (bf16[384,256]{1,0:T(8,128)(2,1)S(1)}, bf16[384,256]{1,0:T(8,128)(2,1)S(1)}, u32[]{:S(2)}, u32[]{:S(2)}) collective-permute-start(bf16[384,256]{1,0:T(8,128)(2,1)S(1)} %get-tuple-element.23), channel_id=1, source_target_pairs={{0,8},{4,12},{8,16},{12,20},{16,24},{20,28},{24,0},{28,4},{1,9},{5... | collective-permute-start | bytes 589832 | tf_op jit(solution)/shard_map/ppermute | solution.py:205
  59.7 11.4 %collective-permute-start.9 = (bf16[384,256]{1,0:T(8,128)(2,1)S(1)}, bf16[384,256]{1,0:T(8,128)(2,1)S(1)}, u32[]{:S(2)}, u32[]{:S(2)}) collective-permute-start(bf16[384,256]{1,0:T(8,128)(2,1)S(1)} %get-tuple-element.22), channel_id=1, source_target_pairs={{0,24},{4,28},{8,0},{12,4},{16,8},{20,12},{24,16},{28,20},{1,25},{... | collective-permute-start | bytes 589832 | tf_op jit(solution)/shard_map/ppermute | solution.py:205
  62.2 9.0 %copy-start.7 = (f32[384,256]{1,0:T(8,128)S(1)}, f32[384,256]{1,0:T(8,128)}, u32[]{:S(2)}) copy-start(f32[384,256]{1,0:T(8,128)} %get-tuple-element.15) | copy-start | bytes 1179652
  62.9 12.5 %collective-permute-start.13 = (bf16[384,256]{1,0:T(8,128)(2,1)}, bf16[384,256]{1,0:T(8,128)(2,1)S(1)}, u32[]{:S(2)}, u32[]{:S(2)}) collective-permute-start(bf16[384,256]{1,0:T(8,128)(2,1)} %get-tuple-element.25), channel_id=1, source_target_pairs={{0,24},{4,28},{8,0},{12,4},{16,8},{20,12},{24,16},{28,20},{1,25},{... | collective-permute-start | bytes 589832 | tf_op jit(solution)/shard_map/ppermute | solution.py:205
  63.8 11.6 %collective-permute-start.14 = (bf16[384,256]{1,0:T(8,128)(2,1)S(1)}, bf16[384,256]{1,0:T(8,128)(2,1)S(1)}, u32[]{:S(2)}, u32[]{:S(2)}) collective-permute-start(bf16[384,256]{1,0:T(8,128)(2,1)S(1)} %get-tuple-element.27), channel_id=1, source_target_pairs={{0,16},{4,20},{8,24},{12,28},{16,0},{20,4},{24,8},{28,12},{1,17},{... | collective-permute-start | bytes 589832 | tf_op jit(solution)/shard_map/ppermute | solution.py:205
  69.6 10.1 %collective-permute-start.15 = (bf16[384,256]{1,0:T(8,128)(2,1)S(1)}, bf16[384,256]{1,0:T(8,128)(2,1)}, u32[]{:S(2)}, u32[]{:S(2)}) collective-permute-start(bf16[384,256]{1,0:T(8,128)(2,1)S(1)} %get-tuple-element.26), channel_id=1, source_target_pairs={{0,8},{4,12},{8,16},{12,20},{16,24},{20,28},{24,0},{28,4},{1,9},{5... | collective-permute-start | bytes 589832 | tf_op jit(solution)/shard_map/ppermute | solution.py:205
  72.4 7.4 %copy-start.6 = (f32[384,256]{1,0:T(8,128)S(1)}, f32[384,256]{1,0:T(8,128)}, u32[]{:S(2)}) copy-start(f32[384,256]{1,0:T(8,128)} %get-tuple-element.18) | copy-start | bytes 1179652
  98.4 30.8 %all-to-all-start = ((bf16[4,96,1536]{2,1,0:T(8,128)(2,1)}), bf16[4,96,1536]{2,1,0:T(8,128)(2,1)S(1)}, u32[]{:S(2)}, u32[]{:S(2)}) async-start(bf16[4,96,1536]{2,1,0:T(8,128)(2,1)} %bitcast), calls=%async_computation | async-start | bytes 2359296 | tf_op jit(solution)/shard_map/all_to_all | solution.py:213

commit v12 on v11

--- a/solution.py
+++ b/solution.py
@@ -211,6 +211,7 @@
     width = 2 * kv_here * HD
 
     query_out = lax.all_to_all(dq, "uly", split_axis=0, concat_axis=1, tiled=True)
+    query_out, kv_grad = lax.optimization_barrier((query_out, kv_grad))
     kv_seq = lax.all_to_all(kv_grad, "uly", split_axis=0, concat_axis=1, tiled=True)
     rows_here = kv_seq.shape[0]
     lane_count = kv_seq.shape[1] // width

time: 131 us -> 108 us (0.82)
  waiting for transfers between devices: 49.9 us -> 27.7 us
  blocking collectives: 15.8 us -> 13.8 us
  starting transfers between devices: 18.9 us -> 20.5 us
    all_to_all x1, waiting for transfers between devices: 24.7 us -> 2.95 us  [shards(): lax.all_to_all(dq, 'uly', split_axis=0, concat_axis=1, tiled=True)]
    all_to_all x1, blocking collectives: 15.8 us -> 13.8 us  [shards(): lax.all_to_all(kv_grad, 'uly', split_axis=0, concat_axis=1, tiled=True)]
    all_to_all x1, starting transfers between devices: 3.53 us -> 5 us  [shards(): lax.all_to_all(dq, 'uly', split_axis=0, concat_axis=1, tiled=True)]
    another operation x2 -> x3, other arithmetic: 2.22 us -> 3.36 us
    unnamed x24 -> x23, local copies, waits for them, and re-layouts: 3.15 us -> 3.2 us
  transfers between devices with their start and end apart: 17 -> 17, of which waited for: 11 -> 11; matrix products, arithmetic and copies ran while one was open for 7% -> 9% of each run, Pallas kernels for 22% -> 27%
where the time goes in v12:
time: 108 us
  Pallas kernels  28.9 us (27%)
  waiting for transfers between devices  27.7 us (26%)
  starting transfers between devices  20.5 us (19%)
  blocking collectives  13.8 us (13%)
  local copies, waits for them, and re-layouts  9.94 us (9%)
  other arithmetic  6.02 us (6%)
    pallas_call x2, Pallas kernels, shards(): pl.pallas_call(kernel, grid_spec=grid_spec, out_shape=[jax.ShapeDtypeStru...  28.9 us
    all_to_all x1, blocking collectives, shards(): lax.all_to_all(kv_grad, 'uly', split_axis=0, concat_axis=1, tiled=True)  13.8 us
    ppermute x6, waiting for transfers between devices, shards(): lax.ppermute(mine[d * span:(d + 1) * span], 'ctx', pairs)  13.2 us
    ppermute x6, waiting for transfers between devices, shards(): gathered.append(lax.ppermute(kv_own, 'ctx', pairs))  11.6 us
    ppermute x6, starting transfers between devices, shards(): gathered.append(lax.ppermute(kv_own, 'ctx', pairs))  9.11 us
    ppermute x6, starting transfers between devices, shards(): lax.ppermute(mine[d * span:(d + 1) * span], 'ctx', pairs)  5.71 us
    all_to_all x1, starting transfers between devices, shards(): lax.all_to_all(dq, 'uly', split_axis=0, concat_axis=1, tiled=True)  5 us
    unnamed x23, local copies, waits for them, and re-layouts  3.2 us
  transfers between devices with their start and end apart: 17, of which 11 were waited for; matrix products, arithmetic and copies ran while one was open for 9% of the time, Pallas kernels for 27%

profile of v12, /device:TPU:0, one launch (start us, length us, event | category | flops | bytes accessed | tf_op | source)
XLA Modules:
  0.0 107.8 jit_solution(6973109403573841436)
XLA Ops:
  0.7 1.1 %constant_dynamic-slice_fusion = (bf16[384,128]{1,0:T(8,128)(2,1)S(1)}, bf16[384,128]{1,0:T(8,128)(2,1)S(1)}, bf16[384,128]{1,0:T(8,128)(2,1)S(1)}, bf16[384,128]{1,0:T(8,128)(2,1)S(1)}) fusion(bf16[384,1024]{1,0:T(8,128)(2,1)} %param.7, s32[]{:T(128)S(6)} %select_n.71, s32[]{:T(128)S(6)} %select_n.70, bf16[384,1024]{1,0:T(8,128)(2,1)} %param.6), kind=kLoop, calls=%fused_computation.36 | loop fusion | bytes 786440 | tf_op jit(solution)/shard_map/dynamic_slice | solution.py:152
  1.8 3.0 %collective-permute-start.4 = (bf16[384,256]{1,0:T(8,128)(2,1)S(1)}, bf16[384,256]{1,0:T(8,128)(2,1)S(1)}, u32[]{:S(2)}, u32[]{:S(2)}) collective-permute-start(bf16[384,256]{1,0:T(8,128)(2,1)S(1)} %pad_maximum_fusion.4), channel_id=1, source_target_pairs={{0,8},{4,12},{8,16},{12,20},{16,24},{20,28},{24,0},{28,4},{1,9},{5... | collective-permute-start | bytes 589832 | tf_op jit(solution)/shard_map/ppermute | solution.py:159
  4.8 1.5 %collective-permute-start.5 = (bf16[384,256]{1,0:T(8,128)(2,1)S(1)}, bf16[384,256]{1,0:T(8,128)(2,1)S(1)}, u32[]{:S(2)}, u32[]{:S(2)}) collective-permute-start(bf16[384,256]{1,0:T(8,128)(2,1)S(1)} %pad_maximum_fusion.4), channel_id=1, source_target_pairs={{0,16},{4,20},{8,24},{12,28},{16,0},{20,4},{24,8},{28,12},{1,17},{... | collective-permute-start | bytes 589832 | tf_op jit(solution)/shard_map/ppermute | solution.py:159
  6.3 1.4 %collective-permute-start.6 = (bf16[384,256]{1,0:T(8,128)(2,1)S(1)}, bf16[384,256]{1,0:T(8,128)(2,1)S(1)}, u32[]{:S(2)}, u32[]{:S(2)}) collective-permute-start(bf16[384,256]{1,0:T(8,128)(2,1)S(1)} %pad_maximum_fusion.4), channel_id=1, source_target_pairs={{0,24},{4,28},{8,0},{12,4},{16,8},{20,12},{24,16},{28,20},{1,25},{... | collective-permute-start | bytes 589832 | tf_op jit(solution)/shard_map/ppermute | solution.py:159
  9.2 2.3 %collective-permute-done.4 = bf16[384,256]{1,0:T(8,128)(2,1)S(1)} collective-permute-done((bf16[384,256]{1,0:T(8,128)(2,1)S(1)}, bf16[384,256]{1,0:T(8,128)(2,1)S(1)}, u32[]{:S(2)}, u32[]{:S(2)}) %collective-permute-start.4) | collective-permute-done | bytes 196640 | tf_op jit(solution)/shard_map/ppermute | solution.py:159
  11.5 2.0 %collective-permute-start.2 = (bf16[384,256]{1,0:T(8,128)(2,1)S(1)}, bf16[384,256]{1,0:T(8,128)(2,1)S(1)}, u32[]{:S(2)}, u32[]{:S(2)}) collective-permute-start(bf16[384,256]{1,0:T(8,128)(2,1)S(1)} %pad_maximum_fusion.3), channel_id=1, source_target_pairs={{0,24},{4,28},{8,0},{12,4},{16,8},{20,12},{24,16},{28,20},{1,25},{... | collective-permute-start | bytes 589832 | tf_op jit(solution)/shard_map/ppermute | solution.py:159
  13.5 2.3 %collective-permute-done.5 = bf16[384,256]{1,0:T(8,128)(2,1)S(1)} collective-permute-done((bf16[384,256]{1,0:T(8,128)(2,1)S(1)}, bf16[384,256]{1,0:T(8,128)(2,1)S(1)}, u32[]{:S(2)}, u32[]{:S(2)}) %collective-permute-start.5) | collective-permute-done | bytes 196640 | tf_op jit(solution)/shard_map/ppermute | solution.py:159
  17.1 2.8 %collective-permute-done = bf16[384,256]{1,0:T(8,128)(2,1)S(1)} collective-permute-done((bf16[384,256]{1,0:T(8,128)(2,1)S(1)}, bf16[384,256]{1,0:T(8,128)(2,1)S(1)}, u32[]{:S(2)}, u32[]{:S(2)}) %collective-permute-start) | collective-permute-done | bytes 196640 | tf_op jit(solution)/shard_map/ppermute | solution.py:159
  20.0 3.3 %collective-permute-done.1 = bf16[384,256]{1,0:T(8,128)(2,1)S(1)} collective-permute-done((bf16[384,256]{1,0:T(8,128)(2,1)S(1)}, bf16[384,256]{1,0:T(8,128)(2,1)S(1)}, u32[]{:S(2)}, u32[]{:S(2)}) %collective-permute-start.1) | collective-permute-done | bytes 196640 | tf_op jit(solution)/shard_map/ppermute | solution.py:159
  24.5 1.2 %broadcast_in_dim.10.dq_in = bf16[384,1536]{1,0:T(8,128)(2,1)} broadcast(bf16[]{:T(256)} %constant.92.clone.1), dimensions={} | broadcast | bytes 1179650 | tf_op jit(solution)/shard_map/broadcast_in_dim | solution.py:145
  25.7 14.4 %shard_map.76 = (bf16[384,1536]{1,0:T(8,128)(2,1)}, f32[384,256]{1,0:T(8,128)}, bf16[1536,256]{1,0:T(8,128)(2,1)}, bf16[1536,256]{1,0:T(8,128)(2,1)}) custom-call(s32[96]{0:T(128)} %pad_add_fusion.tbl_ref, bf16[384,1536]{1,0:T(8,128)(2,1)} %q_ref.3, bf16[384,1536]{1,0:T(8,128)(2,1)} %do_ref.3, ...), custom_call_target="tpu_custom_call", output_to_operand_aliasing={{0}: (7, {})} | custom-call | tf_op jit(solution)/shard_map/pallas_call | solution.py:188
  40.6 0.9 copy-done.3
  41.5 14.4 %shard_map.77 = (bf16[384,1536]{1,0:T(8,128)(2,1)}, f32[384,256]{1,0:T(8,128)}, bf16[1536,256]{1,0:T(8,128)(2,1)}, bf16[1536,256]{1,0:T(8,128)(2,1)}) custom-call(s32[96]{0:T(128)} %pad_add_fusion.tbl_ref, bf16[384,1536]{1,0:T(8,128)(2,1)} %q_ref.3, bf16[384,1536]{1,0:T(8,128)(2,1)} %do_ref.3, ...), custom_call_target="tpu_custom_call", output_to_operand_aliasing={{0}: (7, {})} | custom-call | tf_op jit(solution)/shard_map/pallas_call | solution.py:188
  56.1 5.0 %all-to-all-start = ((bf16[4,96,1536]{2,1,0:T(8,128)(2,1)}), bf16[4,96,1536]{2,1,0:T(8,128)(2,1)S(1)}, u32[]{:S(2)}, u32[]{:S(2)}) async-start(bf16[4,96,1536]{2,1,0:T(8,128)(2,1)} %bitcast.22), calls=%async_computation | async-start | bytes 2359296 | tf_op jit(solution)/shard_map/all_to_all | solution.py:213
  61.1 1.3 %add_convert_fusion.1 = bf16[1536,256]{1,0:T(8,128)(2,1)S(1)} fusion(bf16[1536,256]{1,0:T(8,128)(2,1)} %collective-permute-done.8, bf16[1536,256]{1,0:T(8,128)(2,1)S(1)} %copy-done.5), kind=kLoop, calls=%fused_computation.1 | loop fusion | flops 1572864 | bytes 2359296 | tf_op jit(solution)/shard_map/convert_element_type | solution.py:201
  62.5 1.4 %collective-permute-start.10 = (bf16[384,256]{1,0:T(8,128)(2,1)S(1)}, bf16[384,256]{1,0:T(8,128)(2,1)S(1)}, u32[]{:S(2)}, u32[]{:S(2)}) collective-permute-start(bf16[384,256]{1,0:T(8,128)(2,1)S(1)} %get-tuple-element.28), channel_id=1, source_target_pairs={{0,16},{4,20},{8,24},{12,28},{16,0},{20,4},{24,8},{28,12},{1,17},{... | collective-permute-start | bytes 589832 | tf_op jit(solution)/shard_map/ppermute | solution.py:205
  63.9 0.8 collective-permute-start.11
  64.7 2.1 %collective-permute-start.9 = (bf16[384,256]{1,0:T(8,128)(2,1)S(1)}, bf16[384,256]{1,0:T(8,128)(2,1)S(1)}, u32[]{:S(2)}, u32[]{:S(2)}) collective-permute-start(bf16[384,256]{1,0:T(8,128)(2,1)S(1)} %get-tuple-element.26), channel_id=1, source_target_pairs={{0,24},{4,28},{8,0},{12,4},{16,8},{20,12},{24,16},{28,20},{1,25},{... | collective-permute-start | bytes 589832 | tf_op jit(solution)/shard_map/ppermute | solution.py:205
  67.1 0.8 fusion.11
  67.9 0.9 collective-permute-start.13
  69.2 5.3 %collective-permute-done.10 = bf16[384,256]{1,0:T(8,128)(2,1)S(1)} collective-permute-done((bf16[384,256]{1,0:T(8,128)(2,1)S(1)}, bf16[384,256]{1,0:T(8,128)(2,1)S(1)}, u32[]{:S(2)}, u32[]{:S(2)}) %collective-permute-start.10) | collective-permute-done | bytes 196640 | tf_op jit(solution)/shard_map/ppermute | solution.py:205
  74.5 1.5 %collective-permute-done.9 = bf16[384,256]{1,0:T(8,128)(2,1)S(1)} collective-permute-done((bf16[384,256]{1,0:T(8,128)(2,1)S(1)}, bf16[384,256]{1,0:T(8,128)(2,1)S(1)}, u32[]{:S(2)}, u32[]{:S(2)}) %collective-permute-start.9) | collective-permute-done | bytes 196640 | tf_op jit(solution)/shard_map/ppermute | solution.py:205
  76.0 1.2 %add_convert_fusion.3 = bf16[384,256]{1,0:T(8,128)(2,1)S(1)} fusion(f32[384,256]{1,0:T(8,128)S(1)} %copy-done.6, bf16[384,256]{1,0:T(8,128)(2,1)S(1)} %collective-permute-done.11, bf16[384,256]{1,0:T(8,128)(2,1)S(1)} %collective-permute-done.10, bf16[384,256]{1,0:T(8,128)(2,1)S(1)} %collective-permute-done.9, bf16[1536,256]{1,0:T(8,128)(2,1)} %collective-permute-done.8, ...), kind=kLoop, calls=%fused_computation.7 | loop fusion | flops 1081344 | bytes 1572864 | tf_op jit(solution)/shard_map/convert.8
  77.9 2.3 %collective-permute-done.13 = bf16[384,256]{1,0:T(8,128)(2,1)S(1)} collective-permute-done((bf16[384,256]{1,0:T(8,128)(2,1)}, bf16[384,256]{1,0:T(8,128)(2,1)S(1)}, u32[]{:S(2)}, u32[]{:S(2)}) %collective-permute-start.13) | collective-permute-done | bytes 196640 | tf_op jit(solution)/shard_map/ppermute | solution.py:205
  80.2 4.1 %collective-permute-done.15 = bf16[384,256]{1,0:T(8,128)(2,1)} collective-permute-done((bf16[384,256]{1,0:T(8,128)(2,1)}, bf16[384,256]{1,0:T(8,128)(2,1)}, u32[]{:S(2)}, u32[]{:S(2)}) %collective-permute-start.15) | collective-permute-done | bytes 196640 | tf_op jit(solution)/shard_map/ppermute | solution.py:205
  84.3 1.3 %add_convert_fusion.2 = bf16[384,256]{1,0:T(8,128)(2,1)S(1)} fusion(f32[384,256]{1,0:T(8,128)} %get-tuple-element.20, bf16[384,256]{1,0:T(8,128)(2,1)} %collective-permute-done.15, bf16[384,256]{1,0:T(8,128)(2,1)} %collective-permute-done.14, bf16[384,256]{1,0:T(8,128)(2,1)S(1)} %collective-permute-done.13, bf16[1536,256]{1,0:T(8,128)(2,1)S(1)} %collective-permute-done.12, ...), kind=kLoop, calls=%fused_computation.6 | loop fusion | flops 1081344 | bytes 1572864 | tf_op jit(solution)/shard_map/convert.7
  86.3 0.9 pad_maximum_fusion.2
  87.3 2.9 %all-to-all-done = bf16[4,96,1536]{2,1,0:T(8,128)(2,1)S(1)} async-done(((bf16[4,96,1536]{2,1,0:T(8,128)(2,1)}), bf16[4,96,1536]{2,1,0:T(8,128)(2,1)S(1)}, u32[]{:S(2)}, u32[]{:S(2)}) %all-to-all-start) | async-done | bytes 1179680 | tf_op jit(solution)/shard_map/all_to_all | solution.py:213
  90.2 1.1 %copy.39 = bf16[4,12,8,1536]{3,2,0,1:T(8,128)(2,1)} copy(bf16[4,12,8,1536]{3,2,1,0:T(8,128)(2,1)S(1)} %bitcast.23) | data formatting | bytes 2359296 | tf_op jit(solution)/shard_map/all_to_all | solution.py:213
  91.3 13.8 %all_to_all.35 = bf16[4,96,512]{2,1,0:T(8,128)(2,1)S(1)} all-to-all(bf16[4,96,512]{2,1,0:T(8,128)(2,1)S(1)} %bitcast.24), channel_id=1, replica_groups=mesh['ctx'=8,'uly'=4] {'uly'}, dimensions={0} | all-to-all | bytes 786432 | tf_op jit(solution)/shard_map/all_to_all | solution.py:215
  106.1 0.7 copy.41
  107.1 0.7 copy.42
  (63 shorter events, 7.9 us)
Async XLA Ops:
  0.6 8.3 %copy-start.7 = (s32[24,8]{0,1:T(8,128)S(1)}, s32[24,8]{0,1:T(8,128)}, u32[]{:S(2)}) copy-start(s32[24,8]{0,1:T(8,128)} %param.9) | copy-start | bytes 2308
  1.8 9.7 %collective-permute-start.4 = (bf16[384,256]{1,0:T(8,128)(2,1)S(1)}, bf16[384,256]{1,0:T(8,128)(2,1)S(1)}, u32[]{:S(2)}, u32[]{:S(2)}) collective-permute-start(bf16[384,256]{1,0:T(8,128)(2,1)S(1)} %pad_maximum_fusion.4), channel_id=1, source_target_pairs={{0,8},{4,12},{8,16},{12,20},{16,24},{20,28},{24,0},{28,4},{1,9},{5... | collective-permute-start | bytes 589832 | tf_op jit(solution)/shard_map/ppermute | solution.py:159
  4.8 11.0 %collective-permute-start.5 = (bf16[384,256]{1,0:T(8,128)(2,1)S(1)}, bf16[384,256]{1,0:T(8,128)(2,1)S(1)}, u32[]{:S(2)}, u32[]{:S(2)}) collective-permute-start(bf16[384,256]{1,0:T(8,128)(2,1)S(1)} %pad_maximum_fusion.4), channel_id=1, source_target_pairs={{0,16},{4,20},{8,24},{12,28},{16,0},{20,4},{24,8},{28,12},{1,17},{... | collective-permute-start | bytes 589832 | tf_op jit(solution)/shard_map/ppermute | solution.py:159
  6.3 10.0 %collective-permute-start.6 = (bf16[384,256]{1,0:T(8,128)(2,1)S(1)}, bf16[384,256]{1,0:T(8,128)(2,1)S(1)}, u32[]{:S(2)}, u32[]{:S(2)}) collective-permute-start(bf16[384,256]{1,0:T(8,128)(2,1)S(1)} %pad_maximum_fusion.4), channel_id=1, source_target_pairs={{0,24},{4,28},{8,0},{12,4},{16,8},{20,12},{24,16},{28,20},{1,25},{... | collective-permute-start | bytes 589832 | tf_op jit(solution)/shard_map/ppermute | solution.py:159
  7.8 12.2 %collective-permute-start = (bf16[384,256]{1,0:T(8,128)(2,1)S(1)}, bf16[384,256]{1,0:T(8,128)(2,1)S(1)}, u32[]{:S(2)}, u32[]{:S(2)}) collective-permute-start(bf16[384,256]{1,0:T(8,128)(2,1)S(1)} %pad_maximum_fusion.3), channel_id=1, source_target_pairs={{0,8},{4,12},{8,16},{12,20},{16,24},{20,28},{24,0},{28,4},{1,9},{5... | collective-permute-start | bytes 589832 | tf_op jit(solution)/shard_map/ppermute | solution.py:159
  8.4 14.9 %collective-permute-start.1 = (bf16[384,256]{1,0:T(8,128)(2,1)S(1)}, bf16[384,256]{1,0:T(8,128)(2,1)S(1)}, u32[]{:S(2)}, u32[]{:S(2)}) collective-permute-start(bf16[384,256]{1,0:T(8,128)(2,1)S(1)} %pad_maximum_fusion.3), channel_id=1, source_target_pairs={{0,16},{4,20},{8,24},{12,28},{16,0},{20,4},{24,8},{28,12},{1,17},{... | collective-permute-start | bytes 589832 | tf_op jit(solution)/shard_map/ppermute | solution.py:159
  11.5 12.1 %collective-permute-start.2 = (bf16[384,256]{1,0:T(8,128)(2,1)S(1)}, bf16[384,256]{1,0:T(8,128)(2,1)S(1)}, u32[]{:S(2)}, u32[]{:S(2)}) collective-permute-start(bf16[384,256]{1,0:T(8,128)(2,1)S(1)} %pad_maximum_fusion.3), channel_id=1, source_target_pairs={{0,24},{4,28},{8,0},{12,4},{16,8},{20,12},{24,16},{28,20},{1,25},{... | collective-permute-start | bytes 589832 | tf_op jit(solution)/shard_map/ppermute | solution.py:159
  16.4 9.3 %copy-start = (bf16[1536,256]{1,0:T(8,128)(2,1)}, bf16[1536,256]{1,0:T(8,128)(2,1)S(1)}, u32[]{:S(2)}) copy-start(bf16[1536,256]{1,0:T(8,128)(2,1)S(1)} %pad_maximum_fusion.1.k_ref.v_ref) | copy-start | bytes 2359300
  16.4 8.1 %collective-permute-start.7 = (bf16[1536,256]{1,0:T(8,128)(2,1)S(1)}, bf16[1536,256]{1,0:T(8,128)(2,1)S(1)}, u32[]{:S(2)}, u32[]{:S(2)}) collective-permute-start(bf16[1536,256]{1,0:T(8,128)(2,1)S(1)} %pad_maximum_fusion.1.k_ref.v_ref), channel_id=1, source_target_pairs={{0,4},{4,0},{8,12},{12,8},{16,20},{20,16},{24,28},{28,24},{1,5},{5... | collective-permute-start | bytes 2359304 | tf_op jit(solution)/shard_map/ppermute | solution.py:161
  23.7 16.5 %copy-start.1 = (bf16[1536,256]{1,0:T(8,128)(2,1)}, bf16[1536,256]{1,0:T(8,128)(2,1)S(1)}, u32[]{:S(2)}) copy-start(bf16[1536,256]{1,0:T(8,128)(2,1)S(1)} %pad_maximum_fusion.k_ref.v_ref) | copy-start | bytes 2359300
  23.7 16.9 %collective-permute-start.3 = (bf16[1536,256]{1,0:T(8,128)(2,1)S(1)}, bf16[1536,256]{1,0:T(8,128)(2,1)S(1)}, u32[]{:S(2)}, u32[]{:S(2)}) collective-permute-start(bf16[1536,256]{1,0:T(8,128)(2,1)S(1)} %pad_maximum_fusion.k_ref.v_ref), channel_id=1, source_target_pairs={{0,4},{4,0},{8,12},{12,8},{16,20},{20,16},{24,28},{28,24},{1,5},{5... | collective-permute-start | bytes 2359304 | tf_op jit(solution)/shard_map/ppermute | solution.py:161
  24.5 1.3 %copy-start.2 = (bf16[1536,256]{1,0:T(8,128)(2,1)}, bf16[1536,256]{1,0:T(8,128)(2,1)S(1)}, u32[]{:S(2)}) copy-start(bf16[1536,256]{1,0:T(8,128)(2,1)S(1)} %collective-permute-done.7.ko_ref.vo_ref) | copy-start | bytes 2359300
  40.2 20.9 %collective-permute-start.8 = (bf16[1536,256]{1,0:T(8,128)(2,1)}, bf16[1536,256]{1,0:T(8,128)(2,1)}, u32[]{:S(2)}, u32[]{:S(2)}) collective-permute-start(bf16[1536,256]{1,0:T(8,128)(2,1)} %get-tuple-element.16), channel_id=1, source_target_pairs={{0,4},{4,0},{8,12},{12,8},{16,20},{20,16},{24,28},{28,24},{1,5},{5... | collective-permute-start | bytes 2359304 | tf_op jit(solution)/shard_map/ppermute | solution.py:200
  40.6 0.9 copy-start.3
  56.0 10.9 %collective-permute-start.12 = (bf16[1536,256]{1,0:T(8,128)(2,1)}, bf16[1536,256]{1,0:T(8,128)(2,1)S(1)}, u32[]{:S(2)}, u32[]{:S(2)}) collective-permute-start(bf16[1536,256]{1,0:T(8,128)(2,1)} %get-tuple-element.19), channel_id=1, source_target_pairs={{0,4},{4,0},{8,12},{12,8},{16,20},{20,16},{24,28},{28,24},{1,5},{5... | collective-permute-start | bytes 2359304 | tf_op jit(solution)/shard_map/ppermute | solution.py:200
  56.1 5.0 %copy-start.5 = (bf16[1536,256]{1,0:T(8,128)(2,1)S(1)}, bf16[1536,256]{1,0:T(8,128)(2,1)}, u32[]{:S(2)}) copy-start(bf16[1536,256]{1,0:T(8,128)(2,1)} %get-tuple-element.15) | copy-start | bytes 2359300
  56.1 34.1 %all-to-all-start = ((bf16[4,96,1536]{2,1,0:T(8,128)(2,1)}), bf16[4,96,1536]{2,1,0:T(8,128)(2,1)S(1)}, u32[]{:S(2)}, u32[]{:S(2)}) async-start(bf16[4,96,1536]{2,1,0:T(8,128)(2,1)} %bitcast.22), calls=%async_computation | async-start | bytes 2359296 | tf_op jit(solution)/shard_map/all_to_all | solution.py:213
  62.4 4.4 %copy-start.4 = (bf16[1536,256]{1,0:T(8,128)(2,1)S(1)}, bf16[1536,256]{1,0:T(8,128)(2,1)}, u32[]{:S(2)}) copy-start(bf16[1536,256]{1,0:T(8,128)(2,1)} %get-tuple-element.18) | copy-start | bytes 2359300
  62.5 12.0 %collective-permute-start.10 = (bf16[384,256]{1,0:T(8,128)(2,1)S(1)}, bf16[384,256]{1,0:T(8,128)(2,1)S(1)}, u32[]{:S(2)}, u32[]{:S(2)}) collective-permute-start(bf16[384,256]{1,0:T(8,128)(2,1)S(1)} %get-tuple-element.28), channel_id=1, source_target_pairs={{0,16},{4,20},{8,24},{12,28},{16,0},{20,4},{24,8},{28,12},{1,17},{... | collective-permute-start | bytes 589832 | tf_op jit(solution)/shard_map/ppermute | solution.py:205
  63.9 10.6 %collective-permute-start.11 = (bf16[384,256]{1,0:T(8,128)(2,1)S(1)}, bf16[384,256]{1,0:T(8,128)(2,1)S(1)}, u32[]{:S(2)}, u32[]{:S(2)}) collective-permute-start(bf16[384,256]{1,0:T(8,128)(2,1)S(1)} %get-tuple-element.27), channel_id=1, source_target_pairs={{0,8},{4,12},{8,16},{12,20},{16,24},{20,28},{24,0},{28,4},{1,9},{5... | collective-permute-start | bytes 589832 | tf_op jit(solution)/shard_map/ppermute | solution.py:205
  64.7 11.3 %collective-permute-start.9 = (bf16[384,256]{1,0:T(8,128)(2,1)S(1)}, bf16[384,256]{1,0:T(8,128)(2,1)S(1)}, u32[]{:S(2)}, u32[]{:S(2)}) collective-permute-start(bf16[384,256]{1,0:T(8,128)(2,1)S(1)} %get-tuple-element.26), channel_id=1, source_target_pairs={{0,24},{4,28},{8,0},{12,4},{16,8},{20,12},{24,16},{28,20},{1,25},{... | collective-permute-start | bytes 589832 | tf_op jit(solution)/shard_map/ppermute | solution.py:205
  67.1 9.0 %copy-start.6 = (f32[384,256]{1,0:T(8,128)S(1)}, f32[384,256]{1,0:T(8,128)}, u32[]{:S(2)}) copy-start(f32[384,256]{1,0:T(8,128)} %get-tuple-element.17) | copy-start | bytes 1179652
  67.9 12.3 %collective-permute-start.13 = (bf16[384,256]{1,0:T(8,128)(2,1)}, bf16[384,256]{1,0:T(8,128)(2,1)S(1)}, u32[]{:S(2)}, u32[]{:S(2)}) collective-permute-start(bf16[384,256]{1,0:T(8,128)(2,1)} %get-tuple-element.29), channel_id=1, source_target_pairs={{0,24},{4,28},{8,0},{12,4},{16,8},{20,12},{24,16},{28,20},{1,25},{... | collective-permute-start | bytes 589832 | tf_op jit(solution)/shard_map/ppermute | solution.py:205
  68.7 11.5 %collective-permute-start.14 = (bf16[384,256]{1,0:T(8,128)(2,1)}, bf16[384,256]{1,0:T(8,128)(2,1)}, u32[]{:S(2)}, u32[]{:S(2)}) collective-permute-start(bf16[384,256]{1,0:T(8,128)(2,1)} %get-tuple-element.31), channel_id=1, source_target_pairs={{0,16},{4,20},{8,24},{12,28},{16,0},{20,4},{24,8},{28,12},{1,17},{... | collective-permute-start | bytes 589832 | tf_op jit(solution)/shard_map/ppermute | solution.py:205
  74.5 9.8 %collective-permute-start.15 = (bf16[384,256]{1,0:T(8,128)(2,1)}, bf16[384,256]{1,0:T(8,128)(2,1)}, u32[]{:S(2)}, u32[]{:S(2)}) collective-permute-start(bf16[384,256]{1,0:T(8,128)(2,1)} %get-tuple-element.30), channel_id=1, source_target_pairs={{0,8},{4,12},{8,16},{12,20},{16,24},{20,28},{24,0},{28,4},{1,9},{5... | collective-permute-start | bytes 589832 | tf_op jit(solution)/shard_map/ppermute | solution.py:205

commit v13 on v12

--- a/solution.py
+++ b/solution.py
@@ -195,6 +195,11 @@
                 jax.ShapeDtypeStruct((half, 2 * HD), jnp.bfloat16),
             ],
             input_output_aliases={7: 0},
+            cost_estimate=pl.CostEstimate(
+                flops=12 * nb * hpk * BLK * SLOTS * BLK * HD,
+                transcendentals=nb * hpk * BLK * SLOTS * BLK,
+                bytes_accessed=4 * nb * BLK * hpk * HD + 4 * half * HD * 2 + 12 * half * HD,
+            ),
             compiler_params=pltpu.CompilerParams(dimension_semantics=("arbitrary", "arbitrary")),
         )(table, query_rows, out_grad, kv_half, kv_half, kv_other, kv_other, dq)
         from_partner = lax.ppermute(far_other, "ctx", partner)

time: 108 us -> 107 us (level)
    unnamed x23 -> x21, local copies, waits for them, and re-layouts: 3.2 us -> 2.3 us
where the time goes in v13:
time: 107 us
  Pallas kernels  28.9 us (27%)
  waiting for transfers between devices  27.7 us (26%)
  starting transfers between devices  20.5 us (19%)
  blocking collectives  13.8 us (13%)
  local copies, waits for them, and re-layouts  9.02 us (8%)
  other arithmetic  6.02 us (6%)
    pallas_call x2, Pallas kernels, shards(): pl.pallas_call(kernel, grid_spec=grid_spec, out_shape=[jax.ShapeDtypeStru...  28.9 us
    all_to_all x1, blocking collectives, shards(): lax.all_to_all(kv_grad, 'uly', split_axis=0, concat_axis=1, tiled=True)  13.8 us
    ppermute x6, waiting for transfers between devices, shards(): lax.ppermute(mine[d * span:(d + 1) * span], 'ctx', pairs)  13.2 us
    ppermute x6, waiting for transfers between devices, shards(): gathered.append(lax.ppermute(kv_own, 'ctx', pairs))  11.6 us
    ppermute x6, starting transfers between devices, shards(): gathered.append(lax.ppermute(kv_own, 'ctx', pairs))  9.11 us
    ppermute x6, starting transfers between devices, shards(): lax.ppermute(mine[d * span:(d + 1) * span], 'ctx', pairs)  5.71 us
    all_to_all x1, starting transfers between devices, shards(): lax.all_to_all(dq, 'uly', split_axis=0, concat_axis=1, tiled=True)  5 us
    all_to_all x1, waiting for transfers between devices, shards(): lax.all_to_all(dq, 'uly', split_axis=0, concat_axis=1, tiled=True)  2.95 us
  transfers between devices with their start and end apart: 17, of which 11 were waited for; matrix products, arithmetic and copies ran while one was open for 9% of the time, Pallas kernels for 27%

profile of v13, /device:TPU:0, one launch (start us, length us, event | category | flops | bytes accessed | tf_op | source)
XLA Modules:
  0.0 106.9 jit_solution(3645953063567527217)
XLA Ops:
  0.7 1.1 %constant_dynamic-slice_fusion = (bf16[384,128]{1,0:T(8,128)(2,1)S(1)}, bf16[384,128]{1,0:T(8,128)(2,1)S(1)}, bf16[384,128]{1,0:T(8,128)(2,1)S(1)}, bf16[384,128]{1,0:T(8,128)(2,1)S(1)}) fusion(bf16[384,1024]{1,0:T(8,128)(2,1)} %param.7, s32[]{:T(128)S(6)} %select_n.71, s32[]{:T(128)S(6)} %select_n.70, bf16[384,1024]{1,0:T(8,128)(2,1)} %param.6), kind=kLoop, calls=%fused_computation.36 | loop fusion | bytes 786440 | tf_op jit(solution)/shard_map/dynamic_slice | solution.py:152
  1.8 3.0 %collective-permute-start.4 = (bf16[384,256]{1,0:T(8,128)(2,1)S(1)}, bf16[384,256]{1,0:T(8,128)(2,1)S(1)}, u32[]{:S(2)}, u32[]{:S(2)}) collective-permute-start(bf16[384,256]{1,0:T(8,128)(2,1)S(1)} %pad_maximum_fusion.4), channel_id=1, source_target_pairs={{0,8},{4,12},{8,16},{12,20},{16,24},{20,28},{24,0},{28,4},{1,9},{5... | collective-permute-start | bytes 589832 | tf_op jit(solution)/shard_map/ppermute | solution.py:159
  4.8 1.5 %collective-permute-start.5 = (bf16[384,256]{1,0:T(8,128)(2,1)S(1)}, bf16[384,256]{1,0:T(8,128)(2,1)S(1)}, u32[]{:S(2)}, u32[]{:S(2)}) collective-permute-start(bf16[384,256]{1,0:T(8,128)(2,1)S(1)} %pad_maximum_fusion.4), channel_id=1, source_target_pairs={{0,16},{4,20},{8,24},{12,28},{16,0},{20,4},{24,8},{28,12},{1,17},{... | collective-permute-start | bytes 589832 | tf_op jit(solution)/shard_map/ppermute | solution.py:159
  6.3 1.4 %collective-permute-start.6 = (bf16[384,256]{1,0:T(8,128)(2,1)S(1)}, bf16[384,256]{1,0:T(8,128)(2,1)S(1)}, u32[]{:S(2)}, u32[]{:S(2)}) collective-permute-start(bf16[384,256]{1,0:T(8,128)(2,1)S(1)} %pad_maximum_fusion.4), channel_id=1, source_target_pairs={{0,24},{4,28},{8,0},{12,4},{16,8},{20,12},{24,16},{28,20},{1,25},{... | collective-permute-start | bytes 589832 | tf_op jit(solution)/shard_map/ppermute | solution.py:159
  9.2 2.3 %collective-permute-done.4 = bf16[384,256]{1,0:T(8,128)(2,1)S(1)} collective-permute-done((bf16[384,256]{1,0:T(8,128)(2,1)S(1)}, bf16[384,256]{1,0:T(8,128)(2,1)S(1)}, u32[]{:S(2)}, u32[]{:S(2)}) %collective-permute-start.4) | collective-permute-done | bytes 196640 | tf_op jit(solution)/shard_map/ppermute | solution.py:159
  11.5 2.0 %collective-permute-start.2 = (bf16[384,256]{1,0:T(8,128)(2,1)S(1)}, bf16[384,256]{1,0:T(8,128)(2,1)S(1)}, u32[]{:S(2)}, u32[]{:S(2)}) collective-permute-start(bf16[384,256]{1,0:T(8,128)(2,1)S(1)} %pad_maximum_fusion.3), channel_id=1, source_target_pairs={{0,24},{4,28},{8,0},{12,4},{16,8},{20,12},{24,16},{28,20},{1,25},{... | collective-permute-start | bytes 589832 | tf_op jit(solution)/shard_map/ppermute | solution.py:159
  13.5 2.3 %collective-permute-done.5 = bf16[384,256]{1,0:T(8,128)(2,1)S(1)} collective-permute-done((bf16[384,256]{1,0:T(8,128)(2,1)S(1)}, bf16[384,256]{1,0:T(8,128)(2,1)S(1)}, u32[]{:S(2)}, u32[]{:S(2)}) %collective-permute-start.5) | collective-permute-done | bytes 196640 | tf_op jit(solution)/shard_map/ppermute | solution.py:159
  17.1 2.8 %collective-permute-done = bf16[384,256]{1,0:T(8,128)(2,1)S(1)} collective-permute-done((bf16[384,256]{1,0:T(8,128)(2,1)S(1)}, bf16[384,256]{1,0:T(8,128)(2,1)S(1)}, u32[]{:S(2)}, u32[]{:S(2)}) %collective-permute-start) | collective-permute-done | bytes 196640 | tf_op jit(solution)/shard_map/ppermute | solution.py:159
  20.0 3.3 %collective-permute-done.1 = bf16[384,256]{1,0:T(8,128)(2,1)S(1)} collective-permute-done((bf16[384,256]{1,0:T(8,128)(2,1)S(1)}, bf16[384,256]{1,0:T(8,128)(2,1)S(1)}, u32[]{:S(2)}, u32[]{:S(2)}) %collective-permute-start.1) | collective-permute-done | bytes 196640 | tf_op jit(solution)/shard_map/ppermute | solution.py:159
  23.8 0.7 pad_add_fusion.tbl_ref
  24.5 1.2 %broadcast_in_dim.10.dq_in = bf16[384,1536]{1,0:T(8,128)(2,1)} broadcast(bf16[]{:T(256)} %constant.92.clone.1), dimensions={} | broadcast | bytes 1179650 | tf_op jit(solution)/shard_map/broadcast_in_dim | solution.py:145
  25.7 14.4 %shard_map.76 = (bf16[384,1536]{1,0:T(8,128)(2,1)}, f32[384,256]{1,0:T(8,128)}, bf16[1536,256]{1,0:T(8,128)(2,1)}, bf16[1536,256]{1,0:T(8,128)(2,1)}) custom-call(s32[96]{0:T(128)} %pad_add_fusion.tbl_ref, bf16[384,1536]{1,0:T(8,128)(2,1)} %q_ref.3, bf16[384,1536]{1,0:T(8,128)(2,1)} %do_ref.3, ...), custom_call_target="tpu_custom_call", output_to_operand_aliasing={{0}: (7, {})} | custom-call | flops 3623878656 | bytes 5111808 | tf_op jit(solution)/shard_map/pallas_call | solution.py:188
  40.6 14.5 %shard_map.77 = (bf16[384,1536]{1,0:T(8,128)(2,1)}, f32[384,256]{1,0:T(8,128)}, bf16[1536,256]{1,0:T(8,128)(2,1)}, bf16[1536,256]{1,0:T(8,128)(2,1)}) custom-call(s32[96]{0:T(128)} %pad_add_fusion.tbl_ref, bf16[384,1536]{1,0:T(8,128)(2,1)} %q_ref.3, bf16[384,1536]{1,0:T(8,128)(2,1)} %do_ref.3, ...), custom_call_target="tpu_custom_call", output_to_operand_aliasing={{0}: (7, {})} | custom-call | flops 3623878656 | bytes 5111808 | tf_op jit(solution)/shard_map/pallas_call | solution.py:188
  55.2 5.0 %all-to-all-start = ((bf16[4,96,1536]{2,1,0:T(8,128)(2,1)}), bf16[4,96,1536]{2,1,0:T(8,128)(2,1)S(1)}, u32[]{:S(2)}, u32[]{:S(2)}) async-start(bf16[4,96,1536]{2,1,0:T(8,128)(2,1)} %bitcast.23), calls=%async_computation | async-start | bytes 2359296 | tf_op jit(solution)/shard_map/all_to_all | solution.py:218
  60.2 1.3 %add_convert_fusion.1 = bf16[1536,256]{1,0:T(8,128)(2,1)S(1)} fusion(bf16[1536,256]{1,0:T(8,128)(2,1)} %collective-permute-done.8, bf16[1536,256]{1,0:T(8,128)(2,1)S(1)} %copy-done.1), kind=kLoop, calls=%fused_computation.1 | loop fusion | flops 1572864 | bytes 2359296 | tf_op jit(solution)/shard_map/convert_element_type | solution.py:206
  61.6 1.4 %collective-permute-start.10 = (bf16[384,256]{1,0:T(8,128)(2,1)S(1)}, bf16[384,256]{1,0:T(8,128)(2,1)S(1)}, u32[]{:S(2)}, u32[]{:S(2)}) collective-permute-start(bf16[384,256]{1,0:T(8,128)(2,1)S(1)} %get-tuple-element.28), channel_id=1, source_target_pairs={{0,16},{4,20},{8,24},{12,28},{16,0},{20,4},{24,8},{28,12},{1,17},{... | collective-permute-start | bytes 589832 | tf_op jit(solution)/shard_map/ppermute | solution.py:210
  63.0 0.8 collective-permute-start.11
  63.8 2.1 %collective-permute-start.9 = (bf16[384,256]{1,0:T(8,128)(2,1)S(1)}, bf16[384,256]{1,0:T(8,128)(2,1)S(1)}, u32[]{:S(2)}, u32[]{:S(2)}) collective-permute-start(bf16[384,256]{1,0:T(8,128)(2,1)S(1)} %get-tuple-element.26), channel_id=1, source_target_pairs={{0,24},{4,28},{8,0},{12,4},{16,8},{20,12},{24,16},{28,20},{1,25},{... | collective-permute-start | bytes 589832 | tf_op jit(solution)/shard_map/ppermute | solution.py:210
  66.2 0.8 fusion.11
  67.0 0.9 collective-permute-start.13
  68.4 5.3 %collective-permute-done.10 = bf16[384,256]{1,0:T(8,128)(2,1)S(1)} collective-permute-done((bf16[384,256]{1,0:T(8,128)(2,1)S(1)}, bf16[384,256]{1,0:T(8,128)(2,1)S(1)}, u32[]{:S(2)}, u32[]{:S(2)}) %collective-permute-start.10) | collective-permute-done | bytes 196640 | tf_op jit(solution)/shard_map/ppermute | solution.py:210
  73.6 1.5 %collective-permute-done.9 = bf16[384,256]{1,0:T(8,128)(2,1)S(1)} collective-permute-done((bf16[384,256]{1,0:T(8,128)(2,1)S(1)}, bf16[384,256]{1,0:T(8,128)(2,1)S(1)}, u32[]{:S(2)}, u32[]{:S(2)}) %collective-permute-start.9) | collective-permute-done | bytes 196640 | tf_op jit(solution)/shard_map/ppermute | solution.py:210
  75.1 1.2 %add_convert_fusion.3 = bf16[384,256]{1,0:T(8,128)(2,1)S(1)} fusion(f32[384,256]{1,0:T(8,128)S(1)} %copy-done.4, bf16[384,256]{1,0:T(8,128)(2,1)S(1)} %collective-permute-done.11, bf16[384,256]{1,0:T(8,128)(2,1)S(1)} %collective-permute-done.10, bf16[384,256]{1,0:T(8,128)(2,1)S(1)} %collective-permute-done.9, bf16[1536,256]{1,0:T(8,128)(2,1)} %collective-permute-done.8, ...), kind=kLoop, calls=%fused_computation.7 | loop fusion | flops 1081344 | bytes 1572864 | tf_op jit(solution)/shard_map/convert.8
  77.0 2.3 %collective-permute-done.13 = bf16[384,256]{1,0:T(8,128)(2,1)S(1)} collective-permute-done((bf16[384,256]{1,0:T(8,128)(2,1)}, bf16[384,256]{1,0:T(8,128)(2,1)S(1)}, u32[]{:S(2)}, u32[]{:S(2)}) %collective-permute-start.13) | collective-permute-done | bytes 196640 | tf_op jit(solution)/shard_map/ppermute | solution.py:210
  79.4 4.1 %collective-permute-done.15 = bf16[384,256]{1,0:T(8,128)(2,1)} collective-permute-done((bf16[384,256]{1,0:T(8,128)(2,1)}, bf16[384,256]{1,0:T(8,128)(2,1)}, u32[]{:S(2)}, u32[]{:S(2)}) %collective-permute-start.15) | collective-permute-done | bytes 196640 | tf_op jit(solution)/shard_map/ppermute | solution.py:210
  83.4 1.3 %add_convert_fusion.2 = bf16[384,256]{1,0:T(8,128)(2,1)S(1)} fusion(f32[384,256]{1,0:T(8,128)} %get-tuple-element.20, bf16[384,256]{1,0:T(8,128)(2,1)} %collective-permute-done.15, bf16[384,256]{1,0:T(8,128)(2,1)} %collective-permute-done.14, bf16[384,256]{1,0:T(8,128)(2,1)S(1)} %collective-permute-done.13, bf16[1536,256]{1,0:T(8,128)(2,1)S(1)} %collective-permute-done.12, ...), kind=kLoop, calls=%fused_computation.6 | loop fusion | flops 1081344 | bytes 1572864 | tf_op jit(solution)/shard_map/convert.7
  85.4 0.9 pad_maximum_fusion.2
  86.4 2.9 %all-to-all-done = bf16[4,96,1536]{2,1,0:T(8,128)(2,1)S(1)} async-done(((bf16[4,96,1536]{2,1,0:T(8,128)(2,1)}), bf16[4,96,1536]{2,1,0:T(8,128)(2,1)S(1)}, u32[]{:S(2)}, u32[]{:S(2)}) %all-to-all-start) | async-done | bytes 1179680 | tf_op jit(solution)/shard_map/all_to_all | solution.py:218
  89.3 1.1 %copy.39 = bf16[4,12,8,1536]{3,2,0,1:T(8,128)(2,1)} copy(bf16[4,12,8,1536]{3,2,1,0:T(8,128)(2,1)S(1)} %bitcast.22) | data formatting | bytes 2359296 | tf_op jit(solution)/shard_map/all_to_all | solution.py:218
  90.5 13.8 %all_to_all.35 = bf16[4,96,512]{2,1,0:T(8,128)(2,1)S(1)} all-to-all(bf16[4,96,512]{2,1,0:T(8,128)(2,1)S(1)} %bitcast.24), channel_id=1, replica_groups=mesh['ctx'=8,'uly'=4] {'uly'}, dimensions={0} | all-to-all | bytes 786432 | tf_op jit(solution)/shard_map/all_to_all | solution.py:220
  105.2 0.7 copy.41
  106.2 0.7 copy.42
  (61 shorter events, 7.3 us)
Async XLA Ops:
  0.6 8.3 %copy-start.5 = (s32[24,8]{0,1:T(8,128)S(1)}, s32[24,8]{0,1:T(8,128)}, u32[]{:S(2)}) copy-start(s32[24,8]{0,1:T(8,128)} %param.9) | copy-start | bytes 2308
  1.8 9.7 %collective-permute-start.4 = (bf16[384,256]{1,0:T(8,128)(2,1)S(1)}, bf16[384,256]{1,0:T(8,128)(2,1)S(1)}, u32[]{:S(2)}, u32[]{:S(2)}) collective-permute-start(bf16[384,256]{1,0:T(8,128)(2,1)S(1)} %pad_maximum_fusion.4), channel_id=1, source_target_pairs={{0,8},{4,12},{8,16},{12,20},{16,24},{20,28},{24,0},{28,4},{1,9},{5... | collective-permute-start | bytes 589832 | tf_op jit(solution)/shard_map/ppermute | solution.py:159
  4.8 11.0 %collective-permute-start.5 = (bf16[384,256]{1,0:T(8,128)(2,1)S(1)}, bf16[384,256]{1,0:T(8,128)(2,1)S(1)}, u32[]{:S(2)}, u32[]{:S(2)}) collective-permute-start(bf16[384,256]{1,0:T(8,128)(2,1)S(1)} %pad_maximum_fusion.4), channel_id=1, source_target_pairs={{0,16},{4,20},{8,24},{12,28},{16,0},{20,4},{24,8},{28,12},{1,17},{... | collective-permute-start | bytes 589832 | tf_op jit(solution)/shard_map/ppermute | solution.py:159
  6.3 10.0 %collective-permute-start.6 = (bf16[384,256]{1,0:T(8,128)(2,1)S(1)}, bf16[384,256]{1,0:T(8,128)(2,1)S(1)}, u32[]{:S(2)}, u32[]{:S(2)}) collective-permute-start(bf16[384,256]{1,0:T(8,128)(2,1)S(1)} %pad_maximum_fusion.4), channel_id=1, source_target_pairs={{0,24},{4,28},{8,0},{12,4},{16,8},{20,12},{24,16},{28,20},{1,25},{... | collective-permute-start | bytes 589832 | tf_op jit(solution)/shard_map/ppermute | solution.py:159
  7.8 12.2 %collective-permute-start = (bf16[384,256]{1,0:T(8,128)(2,1)S(1)}, bf16[384,256]{1,0:T(8,128)(2,1)S(1)}, u32[]{:S(2)}, u32[]{:S(2)}) collective-permute-start(bf16[384,256]{1,0:T(8,128)(2,1)S(1)} %pad_maximum_fusion.3), channel_id=1, source_target_pairs={{0,8},{4,12},{8,16},{12,20},{16,24},{20,28},{24,0},{28,4},{1,9},{5... | collective-permute-start | bytes 589832 | tf_op jit(solution)/shard_map/ppermute | solution.py:159
  8.4 14.9 %collective-permute-start.1 = (bf16[384,256]{1,0:T(8,128)(2,1)S(1)}, bf16[384,256]{1,0:T(8,128)(2,1)S(1)}, u32[]{:S(2)}, u32[]{:S(2)}) collective-permute-start(bf16[384,256]{1,0:T(8,128)(2,1)S(1)} %pad_maximum_fusion.3), channel_id=1, source_target_pairs={{0,16},{4,20},{8,24},{12,28},{16,0},{20,4},{24,8},{28,12},{1,17},{... | collective-permute-start | bytes 589832 | tf_op jit(solution)/shard_map/ppermute | solution.py:159
  11.5 12.1 %collective-permute-start.2 = (bf16[384,256]{1,0:T(8,128)(2,1)S(1)}, bf16[384,256]{1,0:T(8,128)(2,1)S(1)}, u32[]{:S(2)}, u32[]{:S(2)}) collective-permute-start(bf16[384,256]{1,0:T(8,128)(2,1)S(1)} %pad_maximum_fusion.3), channel_id=1, source_target_pairs={{0,24},{4,28},{8,0},{12,4},{16,8},{20,12},{24,16},{28,20},{1,25},{... | collective-permute-start | bytes 589832 | tf_op jit(solution)/shard_map/ppermute | solution.py:159
  16.4 9.3 %copy-start.2 = (bf16[1536,256]{1,0:T(8,128)(2,1)}, bf16[1536,256]{1,0:T(8,128)(2,1)S(1)}, u32[]{:S(2)}) copy-start(bf16[1536,256]{1,0:T(8,128)(2,1)S(1)} %pad_maximum_fusion.1.k_ref.v_ref) | copy-start | bytes 2359300
  16.4 8.1 %collective-permute-start.7 = (bf16[1536,256]{1,0:T(8,128)(2,1)S(1)}, bf16[1536,256]{1,0:T(8,128)(2,1)S(1)}, u32[]{:S(2)}, u32[]{:S(2)}) collective-permute-start(bf16[1536,256]{1,0:T(8,128)(2,1)S(1)} %pad_maximum_fusion.1.k_ref.v_ref), channel_id=1, source_target_pairs={{0,4},{4,0},{8,12},{12,8},{16,20},{20,16},{24,28},{28,24},{1,5},{5... | collective-permute-start | bytes 2359304 | tf_op jit(solution)/shard_map/ppermute | solution.py:161
  23.7 16.5 %copy-start.3 = (bf16[1536,256]{1,0:T(8,128)(2,1)}, bf16[1536,256]{1,0:T(8,128)(2,1)S(1)}, u32[]{:S(2)}) copy-start(bf16[1536,256]{1,0:T(8,128)(2,1)S(1)} %pad_maximum_fusion.k_ref.v_ref) | copy-start | bytes 2359300
  23.7 16.9 %collective-permute-start.3 = (bf16[1536,256]{1,0:T(8,128)(2,1)S(1)}, bf16[1536,256]{1,0:T(8,128)(2,1)}, u32[]{:S(2)}, u32[]{:S(2)}) collective-permute-start(bf16[1536,256]{1,0:T(8,128)(2,1)S(1)} %pad_maximum_fusion.k_ref.v_ref), channel_id=1, source_target_pairs={{0,4},{4,0},{8,12},{12,8},{16,20},{20,16},{24,28},{28,24},{1,5},{5... | collective-permute-start | bytes 2359304 | tf_op jit(solution)/shard_map/ppermute | solution.py:161
  24.5 1.3 %copy-start.6 = (bf16[1536,256]{1,0:T(8,128)(2,1)}, bf16[1536,256]{1,0:T(8,128)(2,1)S(1)}, u32[]{:S(2)}) copy-start(bf16[1536,256]{1,0:T(8,128)(2,1)S(1)} %collective-permute-done.7.ko_ref.vo_ref) | copy-start | bytes 2359300
  40.2 20.0 %collective-permute-start.8 = (bf16[1536,256]{1,0:T(8,128)(2,1)}, bf16[1536,256]{1,0:T(8,128)(2,1)}, u32[]{:S(2)}, u32[]{:S(2)}) collective-permute-start(bf16[1536,256]{1,0:T(8,128)(2,1)} %get-tuple-element.16), channel_id=1, source_target_pairs={{0,4},{4,0},{8,12},{12,8},{16,20},{20,16},{24,28},{28,24},{1,5},{5... | collective-permute-start | bytes 2359304 | tf_op jit(solution)/shard_map/ppermute | solution.py:205
  55.1 10.9 %collective-permute-start.12 = (bf16[1536,256]{1,0:T(8,128)(2,1)}, bf16[1536,256]{1,0:T(8,128)(2,1)S(1)}, u32[]{:S(2)}, u32[]{:S(2)}) collective-permute-start(bf16[1536,256]{1,0:T(8,128)(2,1)} %get-tuple-element.19), channel_id=1, source_target_pairs={{0,4},{4,0},{8,12},{12,8},{16,20},{20,16},{24,28},{28,24},{1,5},{5... | collective-permute-start | bytes 2359304 | tf_op jit(solution)/shard_map/ppermute | solution.py:205
  55.2 5.0 %copy-start.1 = (bf16[1536,256]{1,0:T(8,128)(2,1)S(1)}, bf16[1536,256]{1,0:T(8,128)(2,1)}, u32[]{:S(2)}) copy-start(bf16[1536,256]{1,0:T(8,128)(2,1)} %get-tuple-element.15) | copy-start | bytes 2359300
  55.2 34.1 %all-to-all-start = ((bf16[4,96,1536]{2,1,0:T(8,128)(2,1)}), bf16[4,96,1536]{2,1,0:T(8,128)(2,1)S(1)}, u32[]{:S(2)}, u32[]{:S(2)}) async-start(bf16[4,96,1536]{2,1,0:T(8,128)(2,1)} %bitcast.23), calls=%async_computation | async-start | bytes 2359296 | tf_op jit(solution)/shard_map/all_to_all | solution.py:218
  61.6 4.4 %copy-start = (bf16[1536,256]{1,0:T(8,128)(2,1)S(1)}, bf16[1536,256]{1,0:T(8,128)(2,1)}, u32[]{:S(2)}) copy-start(bf16[1536,256]{1,0:T(8,128)(2,1)} %get-tuple-element.18) | copy-start | bytes 2359300
  61.6 12.0 %collective-permute-start.10 = (bf16[384,256]{1,0:T(8,128)(2,1)S(1)}, bf16[384,256]{1,0:T(8,128)(2,1)S(1)}, u32[]{:S(2)}, u32[]{:S(2)}) collective-permute-start(bf16[384,256]{1,0:T(8,128)(2,1)S(1)} %get-tuple-element.28), channel_id=1, source_target_pairs={{0,16},{4,20},{8,24},{12,28},{16,0},{20,4},{24,8},{28,12},{1,17},{... | collective-permute-start | bytes 589832 | tf_op jit(solution)/shard_map/ppermute | solution.py:210
  63.0 10.6 %collective-permute-start.11 = (bf16[384,256]{1,0:T(8,128)(2,1)S(1)}, bf16[384,256]{1,0:T(8,128)(2,1)S(1)}, u32[]{:S(2)}, u32[]{:S(2)}) collective-permute-start(bf16[384,256]{1,0:T(8,128)(2,1)S(1)} %get-tuple-element.27), channel_id=1, source_target_pairs={{0,8},{4,12},{8,16},{12,20},{16,24},{20,28},{24,0},{28,4},{1,9},{5... | collective-permute-start | bytes 589832 | tf_op jit(solution)/shard_map/ppermute | solution.py:210
  63.8 11.3 %collective-permute-start.9 = (bf16[384,256]{1,0:T(8,128)(2,1)S(1)}, bf16[384,256]{1,0:T(8,128)(2,1)S(1)}, u32[]{:S(2)}, u32[]{:S(2)}) collective-permute-start(bf16[384,256]{1,0:T(8,128)(2,1)S(1)} %get-tuple-element.26), channel_id=1, source_target_pairs={{0,24},{4,28},{8,0},{12,4},{16,8},{20,12},{24,16},{28,20},{1,25},{... | collective-permute-start | bytes 589832 | tf_op jit(solution)/shard_map/ppermute | solution.py:210
  66.2 9.0 %copy-start.4 = (f32[384,256]{1,0:T(8,128)S(1)}, f32[384,256]{1,0:T(8,128)}, u32[]{:S(2)}) copy-start(f32[384,256]{1,0:T(8,128)} %get-tuple-element.17) | copy-start | bytes 1179652
  67.0 12.3 %collective-permute-start.13 = (bf16[384,256]{1,0:T(8,128)(2,1)}, bf16[384,256]{1,0:T(8,128)(2,1)S(1)}, u32[]{:S(2)}, u32[]{:S(2)}) collective-permute-start(bf16[384,256]{1,0:T(8,128)(2,1)} %get-tuple-element.29), channel_id=1, source_target_pairs={{0,24},{4,28},{8,0},{12,4},{16,8},{20,12},{24,16},{28,20},{1,25},{... | collective-permute-start | bytes 589832 | tf_op jit(solution)/shard_map/ppermute | solution.py:210
  67.9 11.5 %collective-permute-start.14 = (bf16[384,256]{1,0:T(8,128)(2,1)}, bf16[384,256]{1,0:T(8,128)(2,1)}, u32[]{:S(2)}, u32[]{:S(2)}) collective-permute-start(bf16[384,256]{1,0:T(8,128)(2,1)} %get-tuple-element.31), channel_id=1, source_target_pairs={{0,16},{4,20},{8,24},{12,28},{16,0},{20,4},{24,8},{28,12},{1,17},{... | collective-permute-start | bytes 589832 | tf_op jit(solution)/shard_map/ppermute | solution.py:210
  73.6 9.8 %collective-permute-start.15 = (bf16[384,256]{1,0:T(8,128)(2,1)}, bf16[384,256]{1,0:T(8,128)(2,1)}, u32[]{:S(2)}, u32[]{:S(2)}) collective-permute-start(bf16[384,256]{1,0:T(8,128)(2,1)} %get-tuple-element.30), channel_id=1, source_target_pairs={{0,8},{4,12},{8,16},{12,20},{16,24},{20,28},{24,0},{28,4},{1,9},{5... | collective-permute-start | bytes 589832 | tf_op jit(solution)/shard_map/ppermute | solution.py:210

commit v14 on v13

--- a/solution.py
+++ b/solution.py
@@ -159,6 +159,8 @@
             gathered.append(lax.ppermute(kv_own, "ctx", pairs))
         kv_half = jnp.concatenate(gathered, axis=0)
         kv_other = lax.ppermute(kv_half, "ctx", partner)
+        if g > 0:
+            kv_half, kv_other, dq = lax.optimization_barrier((kv_half, kv_other, dq))
         grid_spec = pltpu.PrefetchScalarGridSpec(
             num_scalar_prefetch=1,
             grid=(1, nb),

time: 107 us -> 107 us (level)
  no operation moved by 1% of the time
where the time goes in v14:
time: 107 us
  Pallas kernels  28.9 us (27%)
  waiting for transfers between devices  27.7 us (26%)
  starting transfers between devices  20.5 us (19%)
  blocking collectives  13.8 us (13%)
  local copies, waits for them, and re-layouts  9.02 us (8%)
  other arithmetic  6.02 us (6%)
    pallas_call x2, Pallas kernels, shards(): pl.pallas_call(kernel, grid_spec=grid_spec, out_shape=[jax.ShapeDtypeStru...  28.9 us
    all_to_all x1, blocking collectives, shards(): lax.all_to_all(kv_grad, 'uly', split_axis=0, concat_axis=1, tiled=True)  13.8 us
    ppermute x6, waiting for transfers between devices, shards(): lax.ppermute(mine[d * span:(d + 1) * span], 'ctx', pairs)  13.2 us
    ppermute x6, waiting for transfers between devices, shards(): gathered.append(lax.ppermute(kv_own, 'ctx', pairs))  11.6 us
    ppermute x6, starting transfers between devices, shards(): gathered.append(lax.ppermute(kv_own, 'ctx', pairs))  9.11 us
    ppermute x6, starting transfers between devices, shards(): lax.ppermute(mine[d * span:(d + 1) * span], 'ctx', pairs)  5.71 us
    all_to_all x1, starting transfers between devices, shards(): lax.all_to_all(dq, 'uly', split_axis=0, concat_axis=1, tiled=True)  5 us
    all_to_all x1, waiting for transfers between devices, shards(): lax.all_to_all(dq, 'uly', split_axis=0, concat_axis=1, tiled=True)  2.95 us
  transfers between devices with their start and end apart: 17, of which 11 were waited for; matrix products, arithmetic and copies ran while one was open for 9% of the time, Pallas kernels for 27%

profile of v14, /device:TPU:0, one launch (start us, length us, event | category | flops | bytes accessed | tf_op | source)
XLA Modules:
  0.0 106.9 jit_solution(3645953063567527217)
XLA Ops:
  0.7 1.1 %constant_dynamic-slice_fusion = (bf16[384,128]{1,0:T(8,128)(2,1)S(1)}, bf16[384,128]{1,0:T(8,128)(2,1)S(1)}, bf16[384,128]{1,0:T(8,128)(2,1)S(1)}, bf16[384,128]{1,0:T(8,128)(2,1)S(1)}) fusion(bf16[384,1024]{1,0:T(8,128)(2,1)} %param.7, s32[]{:T(128)S(6)} %select_n.71, s32[]{:T(128)S(6)} %select_n.70, bf16[384,1024]{1,0:T(8,128)(2,1)} %param.6), kind=kLoop, calls=%fused_computation.36 | loop fusion | bytes 786440 | tf_op jit(solution)/shard_map/dynamic_slice | solution.py:152
  1.8 3.0 %collective-permute-start.4 = (bf16[384,256]{1,0:T(8,128)(2,1)S(1)}, bf16[384,256]{1,0:T(8,128)(2,1)S(1)}, u32[]{:S(2)}, u32[]{:S(2)}) collective-permute-start(bf16[384,256]{1,0:T(8,128)(2,1)S(1)} %pad_maximum_fusion.4), channel_id=1, source_target_pairs={{0,8},{4,12},{8,16},{12,20},{16,24},{20,28},{24,0},{28,4},{1,9},{5... | collective-permute-start | bytes 589832 | tf_op jit(solution)/shard_map/ppermute | solution.py:159
  4.8 1.5 %collective-permute-start.5 = (bf16[384,256]{1,0:T(8,128)(2,1)S(1)}, bf16[384,256]{1,0:T(8,128)(2,1)S(1)}, u32[]{:S(2)}, u32[]{:S(2)}) collective-permute-start(bf16[384,256]{1,0:T(8,128)(2,1)S(1)} %pad_maximum_fusion.4), channel_id=1, source_target_pairs={{0,16},{4,20},{8,24},{12,28},{16,0},{20,4},{24,8},{28,12},{1,17},{... | collective-permute-start | bytes 589832 | tf_op jit(solution)/shard_map/ppermute | solution.py:159
  6.3 1.4 %collective-permute-start.6 = (bf16[384,256]{1,0:T(8,128)(2,1)S(1)}, bf16[384,256]{1,0:T(8,128)(2,1)S(1)}, u32[]{:S(2)}, u32[]{:S(2)}) collective-permute-start(bf16[384,256]{1,0:T(8,128)(2,1)S(1)} %pad_maximum_fusion.4), channel_id=1, source_target_pairs={{0,24},{4,28},{8,0},{12,4},{16,8},{20,12},{24,16},{28,20},{1,25},{... | collective-permute-start | bytes 589832 | tf_op jit(solution)/shard_map/ppermute | solution.py:159
  9.2 2.3 %collective-permute-done.4 = bf16[384,256]{1,0:T(8,128)(2,1)S(1)} collective-permute-done((bf16[384,256]{1,0:T(8,128)(2,1)S(1)}, bf16[384,256]{1,0:T(8,128)(2,1)S(1)}, u32[]{:S(2)}, u32[]{:S(2)}) %collective-permute-start.4) | collective-permute-done | bytes 196640 | tf_op jit(solution)/shard_map/ppermute | solution.py:159
  11.5 2.0 %collective-permute-start.2 = (bf16[384,256]{1,0:T(8,128)(2,1)S(1)}, bf16[384,256]{1,0:T(8,128)(2,1)S(1)}, u32[]{:S(2)}, u32[]{:S(2)}) collective-permute-start(bf16[384,256]{1,0:T(8,128)(2,1)S(1)} %pad_maximum_fusion.3), channel_id=1, source_target_pairs={{0,24},{4,28},{8,0},{12,4},{16,8},{20,12},{24,16},{28,20},{1,25},{... | collective-permute-start | bytes 589832 | tf_op jit(solution)/shard_map/ppermute | solution.py:159
  13.5 2.3 %collective-permute-done.5 = bf16[384,256]{1,0:T(8,128)(2,1)S(1)} collective-permute-done((bf16[384,256]{1,0:T(8,128)(2,1)S(1)}, bf16[384,256]{1,0:T(8,128)(2,1)S(1)}, u32[]{:S(2)}, u32[]{:S(2)}) %collective-permute-start.5) | collective-permute-done | bytes 196640 | tf_op jit(solution)/shard_map/ppermute | solution.py:159
  17.1 2.8 %collective-permute-done = bf16[384,256]{1,0:T(8,128)(2,1)S(1)} collective-permute-done((bf16[384,256]{1,0:T(8,128)(2,1)S(1)}, bf16[384,256]{1,0:T(8,128)(2,1)S(1)}, u32[]{:S(2)}, u32[]{:S(2)}) %collective-permute-start) | collective-permute-done | bytes 196640 | tf_op jit(solution)/shard_map/ppermute | solution.py:159
  20.0 3.3 %collective-permute-done.1 = bf16[384,256]{1,0:T(8,128)(2,1)S(1)} collective-permute-done((bf16[384,256]{1,0:T(8,128)(2,1)S(1)}, bf16[384,256]{1,0:T(8,128)(2,1)S(1)}, u32[]{:S(2)}, u32[]{:S(2)}) %collective-permute-start.1) | collective-permute-done | bytes 196640 | tf_op jit(solution)/shard_map/ppermute | solution.py:159
  23.8 0.7 pad_add_fusion.tbl_ref
  24.5 1.2 %broadcast_in_dim.10.dq_in = bf16[384,1536]{1,0:T(8,128)(2,1)} broadcast(bf16[]{:T(256)} %constant.92.clone.1), dimensions={} | broadcast | bytes 1179650 | tf_op jit(solution)/shard_map/broadcast_in_dim | solution.py:145
  25.7 14.4 %shard_map.76 = (bf16[384,1536]{1,0:T(8,128)(2,1)}, f32[384,256]{1,0:T(8,128)}, bf16[1536,256]{1,0:T(8,128)(2,1)}, bf16[1536,256]{1,0:T(8,128)(2,1)}) custom-call(s32[96]{0:T(128)} %pad_add_fusion.tbl_ref, bf16[384,1536]{1,0:T(8,128)(2,1)} %q_ref.3, bf16[384,1536]{1,0:T(8,128)(2,1)} %do_ref.3, ...), custom_call_target="tpu_custom_call", output_to_operand_aliasing={{0}: (7, {})} | custom-call | flops 3623878656 | bytes 5111808 | tf_op jit(solution)/shard_map/pallas_call | solution.py:190
  40.6 14.5 %shard_map.77 = (bf16[384,1536]{1,0:T(8,128)(2,1)}, f32[384,256]{1,0:T(8,128)}, bf16[1536,256]{1,0:T(8,128)(2,1)}, bf16[1536,256]{1,0:T(8,128)(2,1)}) custom-call(s32[96]{0:T(128)} %pad_add_fusion.tbl_ref, bf16[384,1536]{1,0:T(8,128)(2,1)} %q_ref.3, bf16[384,1536]{1,0:T(8,128)(2,1)} %do_ref.3, ...), custom_call_target="tpu_custom_call", output_to_operand_aliasing={{0}: (7, {})} | custom-call | flops 3623878656 | bytes 5111808 | tf_op jit(solution)/shard_map/pallas_call | solution.py:190
  55.2 5.0 %all-to-all-start = ((bf16[4,96,1536]{2,1,0:T(8,128)(2,1)}), bf16[4,96,1536]{2,1,0:T(8,128)(2,1)S(1)}, u32[]{:S(2)}, u32[]{:S(2)}) async-start(bf16[4,96,1536]{2,1,0:T(8,128)(2,1)} %bitcast.23), calls=%async_computation | async-start | bytes 2359296 | tf_op jit(solution)/shard_map/all_to_all | solution.py:220
  60.2 1.3 %add_convert_fusion.1 = bf16[1536,256]{1,0:T(8,128)(2,1)S(1)} fusion(bf16[1536,256]{1,0:T(8,128)(2,1)} %collective-permute-done.8, bf16[1536,256]{1,0:T(8,128)(2,1)S(1)} %copy-done.1), kind=kLoop, calls=%fused_computation.1 | loop fusion | flops 1572864 | bytes 2359296 | tf_op jit(solution)/shard_map/convert_element_type | solution.py:208
  61.6 1.4 %collective-permute-start.10 = (bf16[384,256]{1,0:T(8,128)(2,1)S(1)}, bf16[384,256]{1,0:T(8,128)(2,1)S(1)}, u32[]{:S(2)}, u32[]{:S(2)}) collective-permute-start(bf16[384,256]{1,0:T(8,128)(2,1)S(1)} %get-tuple-element.34), channel_id=1, source_target_pairs={{0,16},{4,20},{8,24},{12,28},{16,0},{20,4},{24,8},{28,12},{1,17},{... | collective-permute-start | bytes 589832 | tf_op jit(solution)/shard_map/ppermute | solution.py:212
  63.0 0.8 collective-permute-start.11
  63.8 2.1 %collective-permute-start.9 = (bf16[384,256]{1,0:T(8,128)(2,1)S(1)}, bf16[384,256]{1,0:T(8,128)(2,1)S(1)}, u32[]{:S(2)}, u32[]{:S(2)}) collective-permute-start(bf16[384,256]{1,0:T(8,128)(2,1)S(1)} %get-tuple-element.32), channel_id=1, source_target_pairs={{0,24},{4,28},{8,0},{12,4},{16,8},{20,12},{24,16},{28,20},{1,25},{... | collective-permute-start | bytes 589832 | tf_op jit(solution)/shard_map/ppermute | solution.py:212
  66.2 0.8 fusion.11
  67.0 0.9 collective-permute-start.13
  68.4 5.3 %collective-permute-done.10 = bf16[384,256]{1,0:T(8,128)(2,1)S(1)} collective-permute-done((bf16[384,256]{1,0:T(8,128)(2,1)S(1)}, bf16[384,256]{1,0:T(8,128)(2,1)S(1)}, u32[]{:S(2)}, u32[]{:S(2)}) %collective-permute-start.10) | collective-permute-done | bytes 196640 | tf_op jit(solution)/shard_map/ppermute | solution.py:212
  73.6 1.5 %collective-permute-done.9 = bf16[384,256]{1,0:T(8,128)(2,1)S(1)} collective-permute-done((bf16[384,256]{1,0:T(8,128)(2,1)S(1)}, bf16[384,256]{1,0:T(8,128)(2,1)S(1)}, u32[]{:S(2)}, u32[]{:S(2)}) %collective-permute-start.9) | collective-permute-done | bytes 196640 | tf_op jit(solution)/shard_map/ppermute | solution.py:212
  75.1 1.2 %add_convert_fusion.3 = bf16[384,256]{1,0:T(8,128)(2,1)S(1)} fusion(f32[384,256]{1,0:T(8,128)S(1)} %copy-done.4, bf16[384,256]{1,0:T(8,128)(2,1)S(1)} %collective-permute-done.11, bf16[384,256]{1,0:T(8,128)(2,1)S(1)} %collective-permute-done.10, bf16[384,256]{1,0:T(8,128)(2,1)S(1)} %collective-permute-done.9, bf16[1536,256]{1,0:T(8,128)(2,1)} %collective-permute-done.8, ...), kind=kLoop, calls=%fused_computation.7 | loop fusion | flops 1081344 | bytes 1572864 | tf_op jit(solution)/shard_map/convert.8
  77.0 2.3 %collective-permute-done.13 = bf16[384,256]{1,0:T(8,128)(2,1)S(1)} collective-permute-done((bf16[384,256]{1,0:T(8,128)(2,1)}, bf16[384,256]{1,0:T(8,128)(2,1)S(1)}, u32[]{:S(2)}, u32[]{:S(2)}) %collective-permute-start.13) | collective-permute-done | bytes 196640 | tf_op jit(solution)/shard_map/ppermute | solution.py:212
  79.4 4.1 %collective-permute-done.15 = bf16[384,256]{1,0:T(8,128)(2,1)} collective-permute-done((bf16[384,256]{1,0:T(8,128)(2,1)}, bf16[384,256]{1,0:T(8,128)(2,1)}, u32[]{:S(2)}, u32[]{:S(2)}) %collective-permute-start.15) | collective-permute-done | bytes 196640 | tf_op jit(solution)/shard_map/ppermute | solution.py:212
  83.4 1.3 %add_convert_fusion.2 = bf16[384,256]{1,0:T(8,128)(2,1)S(1)} fusion(f32[384,256]{1,0:T(8,128)} %get-tuple-element.26, bf16[384,256]{1,0:T(8,128)(2,1)} %collective-permute-done.15, bf16[384,256]{1,0:T(8,128)(2,1)} %collective-permute-done.14, bf16[384,256]{1,0:T(8,128)(2,1)S(1)} %collective-permute-done.13, bf16[1536,256]{1,0:T(8,128)(2,1)S(1)} %collective-permute-done.12, ...), kind=kLoop, calls=%fused_computation.6 | loop fusion | flops 1081344 | bytes 1572864 | tf_op jit(solution)/shard_map/convert.7
  85.4 0.9 pad_maximum_fusion.2
  86.4 2.9 %all-to-all-done = bf16[4,96,1536]{2,1,0:T(8,128)(2,1)S(1)} async-done(((bf16[4,96,1536]{2,1,0:T(8,128)(2,1)}), bf16[4,96,1536]{2,1,0:T(8,128)(2,1)S(1)}, u32[]{:S(2)}, u32[]{:S(2)}) %all-to-all-start) | async-done | bytes 1179680 | tf_op jit(solution)/shard_map/all_to_all | solution.py:220
  89.3 1.1 %copy.39 = bf16[4,12,8,1536]{3,2,0,1:T(8,128)(2,1)} copy(bf16[4,12,8,1536]{3,2,1,0:T(8,128)(2,1)S(1)} %bitcast.22) | data formatting | bytes 2359296 | tf_op jit(solution)/shard_map/all_to_all | solution.py:220
  90.5 13.8 %all_to_all.35 = bf16[4,96,512]{2,1,0:T(8,128)(2,1)S(1)} all-to-all(bf16[4,96,512]{2,1,0:T(8,128)(2,1)S(1)} %bitcast.24), channel_id=1, replica_groups=mesh['ctx'=8,'uly'=4] {'uly'}, dimensions={0} | all-to-all | bytes 786432 | tf_op jit(solution)/shard_map/all_to_all | solution.py:222
  105.2 0.7 copy.41
  106.2 0.7 copy.42
  (61 shorter events, 7.3 us)
Async XLA Ops:
  0.6 8.3 %copy-start.5 = (s32[24,8]{0,1:T(8,128)S(1)}, s32[24,8]{0,1:T(8,128)}, u32[]{:S(2)}) copy-start(s32[24,8]{0,1:T(8,128)} %param.9) | copy-start | bytes 2308
  1.8 9.7 %collective-permute-start.4 = (bf16[384,256]{1,0:T(8,128)(2,1)S(1)}, bf16[384,256]{1,0:T(8,128)(2,1)S(1)}, u32[]{:S(2)}, u32[]{:S(2)}) collective-permute-start(bf16[384,256]{1,0:T(8,128)(2,1)S(1)} %pad_maximum_fusion.4), channel_id=1, source_target_pairs={{0,8},{4,12},{8,16},{12,20},{16,24},{20,28},{24,0},{28,4},{1,9},{5... | collective-permute-start | bytes 589832 | tf_op jit(solution)/shard_map/ppermute | solution.py:159
  4.8 11.0 %collective-permute-start.5 = (bf16[384,256]{1,0:T(8,128)(2,1)S(1)}, bf16[384,256]{1,0:T(8,128)(2,1)S(1)}, u32[]{:S(2)}, u32[]{:S(2)}) collective-permute-start(bf16[384,256]{1,0:T(8,128)(2,1)S(1)} %pad_maximum_fusion.4), channel_id=1, source_target_pairs={{0,16},{4,20},{8,24},{12,28},{16,0},{20,4},{24,8},{28,12},{1,17},{... | collective-permute-start | bytes 589832 | tf_op jit(solution)/shard_map/ppermute | solution.py:159
  6.3 10.0 %collective-permute-start.6 = (bf16[384,256]{1,0:T(8,128)(2,1)S(1)}, bf16[384,256]{1,0:T(8,128)(2,1)S(1)}, u32[]{:S(2)}, u32[]{:S(2)}) collective-permute-start(bf16[384,256]{1,0:T(8,128)(2,1)S(1)} %pad_maximum_fusion.4), channel_id=1, source_target_pairs={{0,24},{4,28},{8,0},{12,4},{16,8},{20,12},{24,16},{28,20},{1,25},{... | collective-permute-start | bytes 589832 | tf_op jit(solution)/shard_map/ppermute | solution.py:159
  7.8 12.2 %collective-permute-start = (bf16[384,256]{1,0:T(8,128)(2,1)S(1)}, bf16[384,256]{1,0:T(8,128)(2,1)S(1)}, u32[]{:S(2)}, u32[]{:S(2)}) collective-permute-start(bf16[384,256]{1,0:T(8,128)(2,1)S(1)} %pad_maximum_fusion.3), channel_id=1, source_target_pairs={{0,8},{4,12},{8,16},{12,20},{16,24},{20,28},{24,0},{28,4},{1,9},{5... | collective-permute-start | bytes 589832 | tf_op jit(solution)/shard_map/ppermute | solution.py:159
  8.4 14.9 %collective-permute-start.1 = (bf16[384,256]{1,0:T(8,128)(2,1)S(1)}, bf16[384,256]{1,0:T(8,128)(2,1)S(1)}, u32[]{:S(2)}, u32[]{:S(2)}) collective-permute-start(bf16[384,256]{1,0:T(8,128)(2,1)S(1)} %pad_maximum_fusion.3), channel_id=1, source_target_pairs={{0,16},{4,20},{8,24},{12,28},{16,0},{20,4},{24,8},{28,12},{1,17},{... | collective-permute-start | bytes 589832 | tf_op jit(solution)/shard_map/ppermute | solution.py:159
  11.5 12.1 %collective-permute-start.2 = (bf16[384,256]{1,0:T(8,128)(2,1)S(1)}, bf16[384,256]{1,0:T(8,128)(2,1)S(1)}, u32[]{:S(2)}, u32[]{:S(2)}) collective-permute-start(bf16[384,256]{1,0:T(8,128)(2,1)S(1)} %pad_maximum_fusion.3), channel_id=1, source_target_pairs={{0,24},{4,28},{8,0},{12,4},{16,8},{20,12},{24,16},{28,20},{1,25},{... | collective-permute-start | bytes 589832 | tf_op jit(solution)/shard_map/ppermute | solution.py:159
  16.4 9.3 %copy-start.2 = (bf16[1536,256]{1,0:T(8,128)(2,1)}, bf16[1536,256]{1,0:T(8,128)(2,1)S(1)}, u32[]{:S(2)}) copy-start(bf16[1536,256]{1,0:T(8,128)(2,1)S(1)} %pad_maximum_fusion.1.k_ref.v_ref) | copy-start | bytes 2359300
  16.4 8.1 %collective-permute-start.7 = (bf16[1536,256]{1,0:T(8,128)(2,1)S(1)}, bf16[1536,256]{1,0:T(8,128)(2,1)S(1)}, u32[]{:S(2)}, u32[]{:S(2)}) collective-permute-start(bf16[1536,256]{1,0:T(8,128)(2,1)S(1)} %pad_maximum_fusion.1.k_ref.v_ref), channel_id=1, source_target_pairs={{0,4},{4,0},{8,12},{12,8},{16,20},{20,16},{24,28},{28,24},{1,5},{5... | collective-permute-start | bytes 2359304 | tf_op jit(solution)/shard_map/ppermute | solution.py:161
  23.7 16.5 %copy-start.3 = (bf16[1536,256]{1,0:T(8,128)(2,1)}, bf16[1536,256]{1,0:T(8,128)(2,1)S(1)}, u32[]{:S(2)}) copy-start(bf16[1536,256]{1,0:T(8,128)(2,1)S(1)} %pad_maximum_fusion.k_ref.v_ref) | copy-start | bytes 2359300
  23.7 16.9 %collective-permute-start.3 = (bf16[1536,256]{1,0:T(8,128)(2,1)S(1)}, bf16[1536,256]{1,0:T(8,128)(2,1)}, u32[]{:S(2)}, u32[]{:S(2)}) collective-permute-start(bf16[1536,256]{1,0:T(8,128)(2,1)S(1)} %pad_maximum_fusion.k_ref.v_ref), channel_id=1, source_target_pairs={{0,4},{4,0},{8,12},{12,8},{16,20},{20,16},{24,28},{28,24},{1,5},{5... | collective-permute-start | bytes 2359304 | tf_op jit(solution)/shard_map/ppermute | solution.py:161
  24.5 1.3 %copy-start.6 = (bf16[1536,256]{1,0:T(8,128)(2,1)}, bf16[1536,256]{1,0:T(8,128)(2,1)S(1)}, u32[]{:S(2)}) copy-start(bf16[1536,256]{1,0:T(8,128)(2,1)S(1)} %collective-permute-done.7.ko_ref.vo_ref) | copy-start | bytes 2359300
  40.2 20.0 %collective-permute-start.8 = (bf16[1536,256]{1,0:T(8,128)(2,1)}, bf16[1536,256]{1,0:T(8,128)(2,1)}, u32[]{:S(2)}, u32[]{:S(2)}) collective-permute-start(bf16[1536,256]{1,0:T(8,128)(2,1)} %get-tuple-element.22), channel_id=1, source_target_pairs={{0,4},{4,0},{8,12},{12,8},{16,20},{20,16},{24,28},{28,24},{1,5},{5... | collective-permute-start | bytes 2359304 | tf_op jit(solution)/shard_map/ppermute | solution.py:207
  55.1 10.9 %collective-permute-start.12 = (bf16[1536,256]{1,0:T(8,128)(2,1)}, bf16[1536,256]{1,0:T(8,128)(2,1)S(1)}, u32[]{:S(2)}, u32[]{:S(2)}) collective-permute-start(bf16[1536,256]{1,0:T(8,128)(2,1)} %get-tuple-element.25), channel_id=1, source_target_pairs={{0,4},{4,0},{8,12},{12,8},{16,20},{20,16},{24,28},{28,24},{1,5},{5... | collective-permute-start | bytes 2359304 | tf_op jit(solution)/shard_map/ppermute | solution.py:207
  55.2 5.0 %copy-start.1 = (bf16[1536,256]{1,0:T(8,128)(2,1)S(1)}, bf16[1536,256]{1,0:T(8,128)(2,1)}, u32[]{:S(2)}) copy-start(bf16[1536,256]{1,0:T(8,128)(2,1)} %get-tuple-element.21) | copy-start | bytes 2359300
  55.2 34.1 %all-to-all-start = ((bf16[4,96,1536]{2,1,0:T(8,128)(2,1)}), bf16[4,96,1536]{2,1,0:T(8,128)(2,1)S(1)}, u32[]{:S(2)}, u32[]{:S(2)}) async-start(bf16[4,96,1536]{2,1,0:T(8,128)(2,1)} %bitcast.23), calls=%async_computation | async-start | bytes 2359296 | tf_op jit(solution)/shard_map/all_to_all | solution.py:220
  61.6 4.4 %copy-start = (bf16[1536,256]{1,0:T(8,128)(2,1)S(1)}, bf16[1536,256]{1,0:T(8,128)(2,1)}, u32[]{:S(2)}) copy-start(bf16[1536,256]{1,0:T(8,128)(2,1)} %get-tuple-element.24) | copy-start | bytes 2359300
  61.6 12.0 %collective-permute-start.10 = (bf16[384,256]{1,0:T(8,128)(2,1)S(1)}, bf16[384,256]{1,0:T(8,128)(2,1)S(1)}, u32[]{:S(2)}, u32[]{:S(2)}) collective-permute-start(bf16[384,256]{1,0:T(8,128)(2,1)S(1)} %get-tuple-element.34), channel_id=1, source_target_pairs={{0,16},{4,20},{8,24},{12,28},{16,0},{20,4},{24,8},{28,12},{1,17},{... | collective-permute-start | bytes 589832 | tf_op jit(solution)/shard_map/ppermute | solution.py:212
  63.0 10.6 %collective-permute-start.11 = (bf16[384,256]{1,0:T(8,128)(2,1)S(1)}, bf16[384,256]{1,0:T(8,128)(2,1)S(1)}, u32[]{:S(2)}, u32[]{:S(2)}) collective-permute-start(bf16[384,256]{1,0:T(8,128)(2,1)S(1)} %get-tuple-element.33), channel_id=1, source_target_pairs={{0,8},{4,12},{8,16},{12,20},{16,24},{20,28},{24,0},{28,4},{1,9},{5... | collective-permute-start | bytes 589832 | tf_op jit(solution)/shard_map/ppermute | solution.py:212
  63.8 11.3 %collective-permute-start.9 = (bf16[384,256]{1,0:T(8,128)(2,1)S(1)}, bf16[384,256]{1,0:T(8,128)(2,1)S(1)}, u32[]{:S(2)}, u32[]{:S(2)}) collective-permute-start(bf16[384,256]{1,0:T(8,128)(2,1)S(1)} %get-tuple-element.32), channel_id=1, source_target_pairs={{0,24},{4,28},{8,0},{12,4},{16,8},{20,12},{24,16},{28,20},{1,25},{... | collective-permute-start | bytes 589832 | tf_op jit(solution)/shard_map/ppermute | solution.py:212
  66.2 9.0 %copy-start.4 = (f32[384,256]{1,0:T(8,128)S(1)}, f32[384,256]{1,0:T(8,128)}, u32[]{:S(2)}) copy-start(f32[384,256]{1,0:T(8,128)} %get-tuple-element.23) | copy-start | bytes 1179652
  67.0 12.3 %collective-permute-start.13 = (bf16[384,256]{1,0:T(8,128)(2,1)}, bf16[384,256]{1,0:T(8,128)(2,1)S(1)}, u32[]{:S(2)}, u32[]{:S(2)}) collective-permute-start(bf16[384,256]{1,0:T(8,128)(2,1)} %get-tuple-element.35), channel_id=1, source_target_pairs={{0,24},{4,28},{8,0},{12,4},{16,8},{20,12},{24,16},{28,20},{1,25},{... | collective-permute-start | bytes 589832 | tf_op jit(solution)/shard_map/ppermute | solution.py:212
  67.9 11.5 %collective-permute-start.14 = (bf16[384,256]{1,0:T(8,128)(2,1)}, bf16[384,256]{1,0:T(8,128)(2,1)}, u32[]{:S(2)}, u32[]{:S(2)}) collective-permute-start(bf16[384,256]{1,0:T(8,128)(2,1)} %get-tuple-element.37), channel_id=1, source_target_pairs={{0,16},{4,20},{8,24},{12,28},{16,0},{20,4},{24,8},{28,12},{1,17},{... | collective-permute-start | bytes 589832 | tf_op jit(solution)/shard_map/ppermute | solution.py:212
  73.6 9.8 %collective-permute-start.15 = (bf16[384,256]{1,0:T(8,128)(2,1)}, bf16[384,256]{1,0:T(8,128)(2,1)}, u32[]{:S(2)}, u32[]{:S(2)}) collective-permute-start(bf16[384,256]{1,0:T(8,128)(2,1)} %get-tuple-element.36), channel_id=1, source_target_pairs={{0,8},{4,12},{8,16},{12,20},{16,24},{20,28},{24,0},{28,4},{1,9},{5... | collective-permute-start | bytes 589832 | tf_op jit(solution)/shard_map/ppermute | solution.py:212

commit v15 on v14

--- a/solution.py
+++ b/solution.py
@@ -19,7 +19,7 @@
     tbl_ref,
     q_ref, do_ref, k_ref, v_ref, ko_ref, vo_ref, dq_in,
     dq_ref, loc_ref, far_ref, fo_ref,
-    kc_ref, vc_ref, loc_acc, far_acc, fo_acc,
+    kc_ref, vc_ref, loc_acc, far_acc, fo_acc, s_ref, p_ref, pb_ref, ds_ref, dl_ref,
     *, hpk, kv_here, nb,
 ):
     g = pl.program_id(0)
@@ -60,15 +60,36 @@
     dos = jnp.concatenate([do_ref[:, h * HD:(h + 1) * HD] for h in range(hpk)], axis=0)
     nt = (((1,), (1,)), ((), ()))
     tn = (((0,), (0,)), ((), ()))
-    scores = lax.dot_general(qs, kc, nt, preferred_element_type=jnp.float32) * scale
-    peak = jnp.max(scores, axis=1, keepdims=True)
-    lifted = jnp.exp(scores - peak)
-    probs = lifted * (1.0 / jnp.sum(lifted, axis=1, keepdims=True))
-    probs_b = probs.astype(jnp.bfloat16)
+    rows = hpk * BLK
+    chunk = 16
+    s_ref[...] = lax.dot_general(qs, kc, nt, preferred_element_type=jnp.float32)
+
+    def softmax_rows(i, carry):
+        r0 = pl.multiple_of(i * chunk, chunk)
+        scores = s_ref[pl.ds(r0, chunk), :] * scale
+        peak = jnp.max(scores, axis=1, keepdims=True)
+        lifted = jnp.exp(scores - peak)
+        probs = lifted * (1.0 / jnp.sum(lifted, axis=1, keepdims=True))
+        p_ref[pl.ds(r0, chunk), :] = probs
+        pb_ref[pl.ds(r0, chunk), :] = probs.astype(jnp.bfloat16)
+        return carry
+
+    lax.fori_loop(0, rows // chunk, softmax_rows, 0, unroll=2)
+    probs_b = pb_ref[...]
     attended = jnp.dot(probs_b, vc, preferred_element_type=jnp.float32)
-    delta = jnp.sum(dos.astype(jnp.float32) * attended, axis=1, keepdims=True)
-    dprobs = lax.dot_general(dos, vc, nt, preferred_element_type=jnp.float32)
-    dscores = (probs * (dprobs - delta) * scale).astype(jnp.bfloat16)
+    dl_ref[...] = jnp.sum(dos.astype(jnp.float32) * attended, axis=1, keepdims=True)
+    s_ref[...] = lax.dot_general(dos, vc, nt, preferred_element_type=jnp.float32)
+
+    def score_grad_rows(i, carry):
+        r0 = pl.multiple_of(i * chunk, chunk)
+        probs = p_ref[pl.ds(r0, chunk), :]
+        dprobs = s_ref[pl.ds(r0, chunk), :]
+        delta = dl_ref[pl.ds(r0, chunk), :]
+        ds_ref[pl.ds(r0, chunk), :] = (probs * (dprobs - delta) * scale).astype(jnp.bfloat16)
+        return carry
+
+    lax.fori_loop(0, rows // chunk, score_grad_rows, 0, unroll=2)
+    dscores = ds_ref[...]
     dq = jnp.dot(dscores, kc, preferred_element_type=jnp.float32)
     for h in range(hpk):
         dq_ref[:, h * HD:(h + 1) * HD] = dq[h * BLK:(h + 1) * BLK].astype(jnp.bfloat16)
@@ -185,6 +206,11 @@
                 pltpu.VMEM((2, span, HD), jnp.float32),
                 pltpu.VMEM((2, half, HD), jnp.float32),
                 pltpu.VMEM((2, half, HD), jnp.float32),
+                pltpu.VMEM((hpk * BLK, SLOTS * BLK), jnp.float32),
+                pltpu.VMEM((hpk * BLK, SLOTS * BLK), jnp.float32),
+                pltpu.VMEM((hpk * BLK, SLOTS * BLK), jnp.bfloat16),
+                pltpu.VMEM((hpk * BLK, SLOTS * BLK), jnp.bfloat16),
+                pltpu.VMEM((hpk * BLK, 1), jnp.float32),
             ],
         )
         dq, loc, far, far_other = pl.pallas_call(

time: 107 us -> 146 us (1.36)
  Pallas kernels: 28.9 us -> 67.4 us
    pallas_call x2, Pallas kernels: 28.9 us -> 67.4 us  [shards(): pl.pallas_call(kernel, grid_spec=grid_spec, out_shape=[jax.ShapeDtypeStru...]
  transfers between devices with their start and end apart: 17 -> 17, of which waited for: 11 -> 11; matrix products, arithmetic and copies ran while one was open for 9% -> 7% of each run, Pallas kernels for 27% -> 46%
where the time goes in v15:
time: 146 us; the launch traced here: 145 us
  Pallas kernels  67.4 us (46%)
  waiting for transfers between devices  27.7 us (19%)
  starting transfers between devices  20.6 us (14%)
  blocking collectives  13.8 us (9%)
  local copies, waits for them, and re-layouts  9.02 us (6%)
  other arithmetic  6.02 us (4%)
    pallas_call x2, Pallas kernels, shards(): pl.pallas_call(kernel, grid_spec=grid_spec, out_shape=[jax.ShapeDtypeStru...  67.4 us
    all_to_all x1, blocking collectives, shards(): lax.all_to_all(kv_grad, 'uly', split_axis=0, concat_axis=1, tiled=True)  13.8 us
    ppermute x6, waiting for transfers between devices, shards(): lax.ppermute(mine[d * span:(d + 1) * span], 'ctx', pairs)  13.1 us
    ppermute x6, waiting for transfers between devices, shards(): gathered.append(lax.ppermute(kv_own, 'ctx', pairs))  11.6 us
    ppermute x6, starting transfers between devices, shards(): gathered.append(lax.ppermute(kv_own, 'ctx', pairs))  9.11 us
    ppermute x6, starting transfers between devices, shards(): lax.ppermute(mine[d * span:(d + 1) * span], 'ctx', pairs)  5.75 us
    all_to_all x1, starting transfers between devices, shards(): lax.all_to_all(dq, 'uly', split_axis=0, concat_axis=1, tiled=True)  5 us
    all_to_all x1, waiting for transfers between devices, shards(): lax.all_to_all(dq, 'uly', split_axis=0, concat_axis=1, tiled=True)  2.97 us
  transfers between devices with their start and end apart: 17, of which 11 were waited for; matrix products, arithmetic and copies ran while one was open for 7% of the time, Pallas kernels for 46%

profile of v15, /device:TPU:0, one launch (start us, length us, event | category | flops | bytes accessed | tf_op | source)
XLA Modules:
  0.0 145.4 jit_solution(5676299487138273868)
XLA Ops:
  0.7 1.1 constant_dynamic-slice_fusion
  1.8 3.0 %collective-permute-start.4 = (bf16[384,256]{1,0:T(8,128)(2,1)S(1)}, bf16[384,256]{1,0:T(8,128)(2,1)S(1)}, u32[]{:S(2)}, u32[]{:S(2)}) collective-permute-start(bf16[384,256]{1,0:T(8,128)(2,1)S(1)} %pad_maximum_fusion.4), channel_id=1, source_target_pairs={{0,8},{4,12},{8,16},{12,20},{16,24},{20,28},{24,0},{28,4},{1,9},{5... | collective-permute-start | bytes 589832 | tf_op jit(solution)/shard_map/ppermute | solution.py:180
  4.8 1.5 %collective-permute-start.5 = (bf16[384,256]{1,0:T(8,128)(2,1)S(1)}, bf16[384,256]{1,0:T(8,128)(2,1)S(1)}, u32[]{:S(2)}, u32[]{:S(2)}) collective-permute-start(bf16[384,256]{1,0:T(8,128)(2,1)S(1)} %pad_maximum_fusion.4), channel_id=1, source_target_pairs={{0,16},{4,20},{8,24},{12,28},{16,0},{20,4},{24,8},{28,12},{1,17},{... | collective-permute-start | bytes 589832 | tf_op jit(solution)/shard_map/ppermute | solution.py:180
  6.3 1.4 collective-permute-start.6
  9.2 2.3 %collective-permute-done.4 = bf16[384,256]{1,0:T(8,128)(2,1)S(1)} collective-permute-done((bf16[384,256]{1,0:T(8,128)(2,1)S(1)}, bf16[384,256]{1,0:T(8,128)(2,1)S(1)}, u32[]{:S(2)}, u32[]{:S(2)}) %collective-permute-start.4) | collective-permute-done | bytes 196640 | tf_op jit(solution)/shard_map/ppermute | solution.py:180
  11.5 2.0 %collective-permute-start.2 = (bf16[384,256]{1,0:T(8,128)(2,1)S(1)}, bf16[384,256]{1,0:T(8,128)(2,1)S(1)}, u32[]{:S(2)}, u32[]{:S(2)}) collective-permute-start(bf16[384,256]{1,0:T(8,128)(2,1)S(1)} %pad_maximum_fusion.3), channel_id=1, source_target_pairs={{0,24},{4,28},{8,0},{12,4},{16,8},{20,12},{24,16},{28,20},{1,25},{... | collective-permute-start | bytes 589832 | tf_op jit(solution)/shard_map/ppermute | solution.py:180
  13.5 2.3 %collective-permute-done.5 = bf16[384,256]{1,0:T(8,128)(2,1)S(1)} collective-permute-done((bf16[384,256]{1,0:T(8,128)(2,1)S(1)}, bf16[384,256]{1,0:T(8,128)(2,1)S(1)}, u32[]{:S(2)}, u32[]{:S(2)}) %collective-permute-start.5) | collective-permute-done | bytes 196640 | tf_op jit(solution)/shard_map/ppermute | solution.py:180
  17.1 2.8 %collective-permute-done = bf16[384,256]{1,0:T(8,128)(2,1)S(1)} collective-permute-done((bf16[384,256]{1,0:T(8,128)(2,1)S(1)}, bf16[384,256]{1,0:T(8,128)(2,1)S(1)}, u32[]{:S(2)}, u32[]{:S(2)}) %collective-permute-start) | collective-permute-done | bytes 196640 | tf_op jit(solution)/shard_map/ppermute | solution.py:180
  20.0 3.3 %collective-permute-done.1 = bf16[384,256]{1,0:T(8,128)(2,1)S(1)} collective-permute-done((bf16[384,256]{1,0:T(8,128)(2,1)S(1)}, bf16[384,256]{1,0:T(8,128)(2,1)S(1)}, u32[]{:S(2)}, u32[]{:S(2)}) %collective-permute-start.1) | collective-permute-done | bytes 196640 | tf_op jit(solution)/shard_map/ppermute | solution.py:180
  23.8 0.7 pad_add_fusion.tbl_ref
  24.5 1.2 broadcast_in_dim.10.dq_in
  25.7 33.7 %shard_map.76 = (bf16[384,1536]{1,0:T(8,128)(2,1)}, f32[384,256]{1,0:T(8,128)}, bf16[1536,256]{1,0:T(8,128)(2,1)}, bf16[1536,256]{1,0:T(8,128)(2,1)}) custom-call(s32[96]{0:T(128)} %pad_add_fusion.tbl_ref, bf16[384,1536]{1,0:T(8,128)(2,1)} %q_ref.3, bf16[384,1536]{1,0:T(8,128)(2,1)} %do_ref.3, ...), custom_call_target="tpu_custom_call", output_to_operand_aliasing={{0}: (7, {})} | custom-call | flops 3623878656 | bytes 5111808 | tf_op jit(solution)/shard_map/pallas_call | solution.py:216
  59.9 33.7 %shard_map.77 = (bf16[384,1536]{1,0:T(8,128)(2,1)}, f32[384,256]{1,0:T(8,128)}, bf16[1536,256]{1,0:T(8,128)(2,1)}, bf16[1536,256]{1,0:T(8,128)(2,1)}) custom-call(s32[96]{0:T(128)} %pad_add_fusion.tbl_ref, bf16[384,1536]{1,0:T(8,128)(2,1)} %q_ref.3, bf16[384,1536]{1,0:T(8,128)(2,1)} %do_ref.3, ...), custom_call_target="tpu_custom_call", output_to_operand_aliasing={{0}: (7, {})} | custom-call | flops 3623878656 | bytes 5111808 | tf_op jit(solution)/shard_map/pallas_call | solution.py:216
  93.7 5.0 %all-to-all-start = ((bf16[4,96,1536]{2,1,0:T(8,128)(2,1)}), bf16[4,96,1536]{2,1,0:T(8,128)(2,1)S(1)}, u32[]{:S(2)}, u32[]{:S(2)}) async-start(bf16[4,96,1536]{2,1,0:T(8,128)(2,1)} %bitcast.23), calls=%async_computation | async-start | bytes 2359296 | tf_op jit(solution)/shard_map/all_to_all | solution.py:246
  98.7 1.3 add_convert_fusion.1
  100.1 1.5 %collective-permute-start.10 = (bf16[384,256]{1,0:T(8,128)(2,1)S(1)}, bf16[384,256]{1,0:T(8,128)(2,1)S(1)}, u32[]{:S(2)}, u32[]{:S(2)}) collective-permute-start(bf16[384,256]{1,0:T(8,128)(2,1)S(1)} %get-tuple-element.34), channel_id=1, source_target_pairs={{0,16},{4,20},{8,24},{12,28},{16,0},{20,4},{24,8},{28,12},{1,17},{... | collective-permute-start | bytes 589832 | tf_op jit(solution)/shard_map/ppermute | solution.py:238
  101.6 0.8 collective-permute-start.11
  102.4 2.1 %collective-permute-start.9 = (bf16[384,256]{1,0:T(8,128)(2,1)S(1)}, bf16[384,256]{1,0:T(8,128)(2,1)S(1)}, u32[]{:S(2)}, u32[]{:S(2)}) collective-permute-start(bf16[384,256]{1,0:T(8,128)(2,1)S(1)} %get-tuple-element.32), channel_id=1, source_target_pairs={{0,24},{4,28},{8,0},{12,4},{16,8},{20,12},{24,16},{28,20},{1,25},{... | collective-permute-start | bytes 589832 | tf_op jit(solution)/shard_map/ppermute | solution.py:238
  104.7 0.8 fusion.11
  105.6 0.8 collective-permute-start.13
  106.9 5.2 %collective-permute-done.10 = bf16[384,256]{1,0:T(8,128)(2,1)S(1)} collective-permute-done((bf16[384,256]{1,0:T(8,128)(2,1)S(1)}, bf16[384,256]{1,0:T(8,128)(2,1)S(1)}, u32[]{:S(2)}, u32[]{:S(2)}) %collective-permute-start.10) | collective-permute-done | bytes 196640 | tf_op jit(solution)/shard_map/ppermute | solution.py:238
  112.2 1.5 %collective-permute-done.9 = bf16[384,256]{1,0:T(8,128)(2,1)S(1)} collective-permute-done((bf16[384,256]{1,0:T(8,128)(2,1)S(1)}, bf16[384,256]{1,0:T(8,128)(2,1)S(1)}, u32[]{:S(2)}, u32[]{:S(2)}) %collective-permute-start.9) | collective-permute-done | bytes 196640 | tf_op jit(solution)/shard_map/ppermute | solution.py:238
  113.7 1.2 add_convert_fusion.3
  115.5 2.3 %collective-permute-done.13 = bf16[384,256]{1,0:T(8,128)(2,1)S(1)} collective-permute-done((bf16[384,256]{1,0:T(8,128)(2,1)}, bf16[384,256]{1,0:T(8,128)(2,1)S(1)}, u32[]{:S(2)}, u32[]{:S(2)}) %collective-permute-start.13) | collective-permute-done | bytes 196640 | tf_op jit(solution)/shard_map/ppermute | solution.py:238
  117.9 4.0 %collective-permute-done.15 = bf16[384,256]{1,0:T(8,128)(2,1)} collective-permute-done((bf16[384,256]{1,0:T(8,128)(2,1)}, bf16[384,256]{1,0:T(8,128)(2,1)}, u32[]{:S(2)}, u32[]{:S(2)}) %collective-permute-start.15) | collective-permute-done | bytes 196640 | tf_op jit(solution)/shard_map/ppermute | solution.py:238
  121.9 1.3 add_convert_fusion.2
  123.9 0.9 pad_maximum_fusion.2
  124.9 3.0 %all-to-all-done = bf16[4,96,1536]{2,1,0:T(8,128)(2,1)S(1)} async-done(((bf16[4,96,1536]{2,1,0:T(8,128)(2,1)}), bf16[4,96,1536]{2,1,0:T(8,128)(2,1)S(1)}, u32[]{:S(2)}, u32[]{:S(2)}) %all-to-all-start) | async-done | bytes 1179680 | tf_op jit(solution)/shard_map/all_to_all | solution.py:246
  127.9 1.1 copy.39
  129.0 13.8 %all_to_all.35 = bf16[4,96,512]{2,1,0:T(8,128)(2,1)S(1)} all-to-all(bf16[4,96,512]{2,1,0:T(8,128)(2,1)S(1)} %bitcast.24), channel_id=1, replica_groups=mesh['ctx'=8,'uly'=4] {'uly'}, dimensions={0} | all-to-all | bytes 786432 | tf_op jit(solution)/shard_map/all_to_all | solution.py:248
  143.7 0.7 copy.41
  144.7 0.7 copy.42
  (61 shorter events, 7.3 us)
Async XLA Ops:
  0.6 8.3 %copy-start.5 = (s32[24,8]{0,1:T(8,128)S(1)}, s32[24,8]{0,1:T(8,128)}, u32[]{:S(2)}) copy-start(s32[24,8]{0,1:T(8,128)} %param.9) | copy-start | bytes 2308
  1.8 9.7 %collective-permute-start.4 = (bf16[384,256]{1,0:T(8,128)(2,1)S(1)}, bf16[384,256]{1,0:T(8,128)(2,1)S(1)}, u32[]{:S(2)}, u32[]{:S(2)}) collective-permute-start(bf16[384,256]{1,0:T(8,128)(2,1)S(1)} %pad_maximum_fusion.4), channel_id=1, source_target_pairs={{0,8},{4,12},{8,16},{12,20},{16,24},{20,28},{24,0},{28,4},{1,9},{5... | collective-permute-start | bytes 589832 | tf_op jit(solution)/shard_map/ppermute | solution.py:180
  4.8 11.0 %collective-permute-start.5 = (bf16[384,256]{1,0:T(8,128)(2,1)S(1)}, bf16[384,256]{1,0:T(8,128)(2,1)S(1)}, u32[]{:S(2)}, u32[]{:S(2)}) collective-permute-start(bf16[384,256]{1,0:T(8,128)(2,1)S(1)} %pad_maximum_fusion.4), channel_id=1, source_target_pairs={{0,16},{4,20},{8,24},{12,28},{16,0},{20,4},{24,8},{28,12},{1,17},{... | collective-permute-start | bytes 589832 | tf_op jit(solution)/shard_map/ppermute | solution.py:180
  6.3 10.0 %collective-permute-start.6 = (bf16[384,256]{1,0:T(8,128)(2,1)S(1)}, bf16[384,256]{1,0:T(8,128)(2,1)S(1)}, u32[]{:S(2)}, u32[]{:S(2)}) collective-permute-start(bf16[384,256]{1,0:T(8,128)(2,1)S(1)} %pad_maximum_fusion.4), channel_id=1, source_target_pairs={{0,24},{4,28},{8,0},{12,4},{16,8},{20,12},{24,16},{28,20},{1,25},{... | collective-permute-start | bytes 589832 | tf_op jit(solution)/shard_map/ppermute | solution.py:180
  7.8 12.2 %collective-permute-start = (bf16[384,256]{1,0:T(8,128)(2,1)S(1)}, bf16[384,256]{1,0:T(8,128)(2,1)S(1)}, u32[]{:S(2)}, u32[]{:S(2)}) collective-permute-start(bf16[384,256]{1,0:T(8,128)(2,1)S(1)} %pad_maximum_fusion.3), channel_id=1, source_target_pairs={{0,8},{4,12},{8,16},{12,20},{16,24},{20,28},{24,0},{28,4},{1,9},{5... | collective-permute-start | bytes 589832 | tf_op jit(solution)/shard_map/ppermute | solution.py:180
  8.4 14.9 %collective-permute-start.1 = (bf16[384,256]{1,0:T(8,128)(2,1)S(1)}, bf16[384,256]{1,0:T(8,128)(2,1)S(1)}, u32[]{:S(2)}, u32[]{:S(2)}) collective-permute-start(bf16[384,256]{1,0:T(8,128)(2,1)S(1)} %pad_maximum_fusion.3), channel_id=1, source_target_pairs={{0,16},{4,20},{8,24},{12,28},{16,0},{20,4},{24,8},{28,12},{1,17},{... | collective-permute-start | bytes 589832 | tf_op jit(solution)/shard_map/ppermute | solution.py:180
  11.5 12.1 %collective-permute-start.2 = (bf16[384,256]{1,0:T(8,128)(2,1)S(1)}, bf16[384,256]{1,0:T(8,128)(2,1)S(1)}, u32[]{:S(2)}, u32[]{:S(2)}) collective-permute-start(bf16[384,256]{1,0:T(8,128)(2,1)S(1)} %pad_maximum_fusion.3), channel_id=1, source_target_pairs={{0,24},{4,28},{8,0},{12,4},{16,8},{20,12},{24,16},{28,20},{1,25},{... | collective-permute-start | bytes 589832 | tf_op jit(solution)/shard_map/ppermute | solution.py:180
  16.4 9.3 %copy-start.2 = (bf16[1536,256]{1,0:T(8,128)(2,1)}, bf16[1536,256]{1,0:T(8,128)(2,1)S(1)}, u32[]{:S(2)}) copy-start(bf16[1536,256]{1,0:T(8,128)(2,1)S(1)} %pad_maximum_fusion.1.k_ref.v_ref) | copy-start | bytes 2359300
  16.4 8.1 %collective-permute-start.7 = (bf16[1536,256]{1,0:T(8,128)(2,1)S(1)}, bf16[1536,256]{1,0:T(8,128)(2,1)S(1)}, u32[]{:S(2)}, u32[]{:S(2)}) collective-permute-start(bf16[1536,256]{1,0:T(8,128)(2,1)S(1)} %pad_maximum_fusion.1.k_ref.v_ref), channel_id=1, source_target_pairs={{0,4},{4,0},{8,12},{12,8},{16,20},{20,16},{24,28},{28,24},{1,5},{5... | collective-permute-start | bytes 2359304 | tf_op jit(solution)/shard_map/ppermute | solution.py:182
  23.7 35.7 %copy-start.3 = (bf16[1536,256]{1,0:T(8,128)(2,1)}, bf16[1536,256]{1,0:T(8,128)(2,1)S(1)}, u32[]{:S(2)}) copy-start(bf16[1536,256]{1,0:T(8,128)(2,1)S(1)} %pad_maximum_fusion.k_ref.v_ref) | copy-start | bytes 2359300
  23.7 36.2 %collective-permute-start.3 = (bf16[1536,256]{1,0:T(8,128)(2,1)S(1)}, bf16[1536,256]{1,0:T(8,128)(2,1)}, u32[]{:S(2)}, u32[]{:S(2)}) collective-permute-start(bf16[1536,256]{1,0:T(8,128)(2,1)S(1)} %pad_maximum_fusion.k_ref.v_ref), channel_id=1, source_target_pairs={{0,4},{4,0},{8,12},{12,8},{16,20},{20,16},{24,28},{28,24},{1,5},{5... | collective-permute-start | bytes 2359304 | tf_op jit(solution)/shard_map/ppermute | solution.py:182
  24.5 1.3 copy-start.6
  59.4 39.3 %collective-permute-start.8 = (bf16[1536,256]{1,0:T(8,128)(2,1)}, bf16[1536,256]{1,0:T(8,128)(2,1)}, u32[]{:S(2)}, u32[]{:S(2)}) collective-permute-start(bf16[1536,256]{1,0:T(8,128)(2,1)} %get-tuple-element.22), channel_id=1, source_target_pairs={{0,4},{4,0},{8,12},{12,8},{16,20},{20,16},{24,28},{28,24},{1,5},{5... | collective-permute-start | bytes 2359304 | tf_op jit(solution)/shard_map/ppermute | solution.py:233
  93.6 10.9 %collective-permute-start.12 = (bf16[1536,256]{1,0:T(8,128)(2,1)}, bf16[1536,256]{1,0:T(8,128)(2,1)S(1)}, u32[]{:S(2)}, u32[]{:S(2)}) collective-permute-start(bf16[1536,256]{1,0:T(8,128)(2,1)} %get-tuple-element.25), channel_id=1, source_target_pairs={{0,4},{4,0},{8,12},{12,8},{16,20},{20,16},{24,28},{28,24},{1,5},{5... | collective-permute-start | bytes 2359304 | tf_op jit(solution)/shard_map/ppermute | solution.py:233
  93.7 5.0 %copy-start.1 = (bf16[1536,256]{1,0:T(8,128)(2,1)S(1)}, bf16[1536,256]{1,0:T(8,128)(2,1)}, u32[]{:S(2)}) copy-start(bf16[1536,256]{1,0:T(8,128)(2,1)} %get-tuple-element.21) | copy-start | bytes 2359300
  93.7 34.1 %all-to-all-start = ((bf16[4,96,1536]{2,1,0:T(8,128)(2,1)}), bf16[4,96,1536]{2,1,0:T(8,128)(2,1)S(1)}, u32[]{:S(2)}, u32[]{:S(2)}) async-start(bf16[4,96,1536]{2,1,0:T(8,128)(2,1)} %bitcast.23), calls=%async_computation | async-start | bytes 2359296 | tf_op jit(solution)/shard_map/all_to_all | solution.py:246
  100.1 4.5 %copy-start = (bf16[1536,256]{1,0:T(8,128)(2,1)S(1)}, bf16[1536,256]{1,0:T(8,128)(2,1)}, u32[]{:S(2)}) copy-start(bf16[1536,256]{1,0:T(8,128)(2,1)} %get-tuple-element.24) | copy-start | bytes 2359300
  100.1 12.0 %collective-permute-start.10 = (bf16[384,256]{1,0:T(8,128)(2,1)S(1)}, bf16[384,256]{1,0:T(8,128)(2,1)S(1)}, u32[]{:S(2)}, u32[]{:S(2)}) collective-permute-start(bf16[384,256]{1,0:T(8,128)(2,1)S(1)} %get-tuple-element.34), channel_id=1, source_target_pairs={{0,16},{4,20},{8,24},{12,28},{16,0},{20,4},{24,8},{28,12},{1,17},{... | collective-permute-start | bytes 589832 | tf_op jit(solution)/shard_map/ppermute | solution.py:238
  101.6 10.6 %collective-permute-start.11 = (bf16[384,256]{1,0:T(8,128)(2,1)S(1)}, bf16[384,256]{1,0:T(8,128)(2,1)S(1)}, u32[]{:S(2)}, u32[]{:S(2)}) collective-permute-start(bf16[384,256]{1,0:T(8,128)(2,1)S(1)} %get-tuple-element.33), channel_id=1, source_target_pairs={{0,8},{4,12},{8,16},{12,20},{16,24},{20,28},{24,0},{28,4},{1,9},{5... | collective-permute-start | bytes 589832 | tf_op jit(solution)/shard_map/ppermute | solution.py:238
  102.4 11.3 %collective-permute-start.9 = (bf16[384,256]{1,0:T(8,128)(2,1)S(1)}, bf16[384,256]{1,0:T(8,128)(2,1)S(1)}, u32[]{:S(2)}, u32[]{:S(2)}) collective-permute-start(bf16[384,256]{1,0:T(8,128)(2,1)S(1)} %get-tuple-element.32), channel_id=1, source_target_pairs={{0,24},{4,28},{8,0},{12,4},{16,8},{20,12},{24,16},{28,20},{1,25},{... | collective-permute-start | bytes 589832 | tf_op jit(solution)/shard_map/ppermute | solution.py:238
  104.7 8.9 %copy-start.4 = (f32[384,256]{1,0:T(8,128)S(1)}, f32[384,256]{1,0:T(8,128)}, u32[]{:S(2)}) copy-start(f32[384,256]{1,0:T(8,128)} %get-tuple-element.23) | copy-start | bytes 1179652
  105.6 12.3 %collective-permute-start.13 = (bf16[384,256]{1,0:T(8,128)(2,1)}, bf16[384,256]{1,0:T(8,128)(2,1)S(1)}, u32[]{:S(2)}, u32[]{:S(2)}) collective-permute-start(bf16[384,256]{1,0:T(8,128)(2,1)} %get-tuple-element.35), channel_id=1, source_target_pairs={{0,24},{4,28},{8,0},{12,4},{16,8},{20,12},{24,16},{28,20},{1,25},{... | collective-permute-start | bytes 589832 | tf_op jit(solution)/shard_map/ppermute | solution.py:238
  106.4 11.5 %collective-permute-start.14 = (bf16[384,256]{1,0:T(8,128)(2,1)}, bf16[384,256]{1,0:T(8,128)(2,1)}, u32[]{:S(2)}, u32[]{:S(2)}) collective-permute-start(bf16[384,256]{1,0:T(8,128)(2,1)} %get-tuple-element.37), channel_id=1, source_target_pairs={{0,16},{4,20},{8,24},{12,28},{16,0},{20,4},{24,8},{28,12},{1,17},{... | collective-permute-start | bytes 589832 | tf_op jit(solution)/shard_map/ppermute | solution.py:238
  112.2 9.7 %collective-permute-start.15 = (bf16[384,256]{1,0:T(8,128)(2,1)}, bf16[384,256]{1,0:T(8,128)(2,1)}, u32[]{:S(2)}, u32[]{:S(2)}) collective-permute-start(bf16[384,256]{1,0:T(8,128)(2,1)} %get-tuple-element.36), channel_id=1, source_target_pairs={{0,8},{4,12},{8,16},{12,20},{16,24},{20,28},{24,0},{28,4},{1,9},{5... | collective-permute-start | bytes 589832 | tf_op jit(solution)/shard_map/ppermute | solution.py:238

commit v16 on v15

--- a/solution.py
+++ b/solution.py
@@ -61,7 +61,7 @@
     nt = (((1,), (1,)), ((), ()))
     tn = (((0,), (0,)), ((), ()))
     rows = hpk * BLK
-    chunk = 16
+    chunk = BLK
     s_ref[...] = lax.dot_general(qs, kc, nt, preferred_element_type=jnp.float32)
 
     def softmax_rows(i, carry):
@@ -74,7 +74,7 @@
         pb_ref[pl.ds(r0, chunk), :] = probs.astype(jnp.bfloat16)
         return carry
 
-    lax.fori_loop(0, rows // chunk, softmax_rows, 0, unroll=2)
+    lax.fori_loop(0, rows // chunk, softmax_rows, 0, unroll=True)
     probs_b = pb_ref[...]
     attended = jnp.dot(probs_b, vc, preferred_element_type=jnp.float32)
     dl_ref[...] = jnp.sum(dos.astype(jnp.float32) * attended, axis=1, keepdims=True)
@@ -88,7 +88,7 @@
         ds_ref[pl.ds(r0, chunk), :] = (probs * (dprobs - delta) * scale).astype(jnp.bfloat16)
         return carry
 
-    lax.fori_loop(0, rows // chunk, score_grad_rows, 0, unroll=2)
+    lax.fori_loop(0, rows // chunk, score_grad_rows, 0, unroll=True)
     dscores = ds_ref[...]
     dq = jnp.dot(dscores, kc, preferred_element_type=jnp.float32)
     for h in range(hpk):

time: 146 us -> 112 us (0.77)
  Pallas kernels: 67.4 us -> 33.2 us
    pallas_call x2, Pallas kernels: 67.4 us -> 33.2 us  [shards(): pl.pallas_call(kernel, grid_spec=grid_spec, out_shape=[jax.ShapeDtypeStru...]
  transfers between devices with their start and end apart: 17 -> 17, of which waited for: 11 -> 11; matrix products, arithmetic and copies ran while one was open for 7% -> 9% of each run, Pallas kernels for 46% -> 30%
where the time goes in v16:
time: 112 us; the launch traced here: 111 us
  Pallas kernels  33.2 us (30%)
  waiting for transfers between devices  27.7 us (25%)
  starting transfers between devices  20.5 us (18%)
  blocking collectives  13.8 us (12%)
  local copies, waits for them, and re-layouts  9.02 us (8%)
  other arithmetic  6.02 us (5%)
    pallas_call x2, Pallas kernels, shards(): pl.pallas_call(kernel, grid_spec=grid_spec, out_shape=[jax.ShapeDtypeStru...  33.2 us
    all_to_all x1, blocking collectives, shards(): lax.all_to_all(kv_grad, 'uly', split_axis=0, concat_axis=1, tiled=True)  13.8 us
    ppermute x6, waiting for transfers between devices, shards(): lax.ppermute(mine[d * span:(d + 1) * span], 'ctx', pairs)  13.2 us
    ppermute x6, waiting for transfers between devices, shards(): gathered.append(lax.ppermute(kv_own, 'ctx', pairs))  11.6 us
    ppermute x6, starting transfers between devices, shards(): gathered.append(lax.ppermute(kv_own, 'ctx', pairs))  9.11 us
    ppermute x6, starting transfers between devices, shards(): lax.ppermute(mine[d * span:(d + 1) * span], 'ctx', pairs)  5.7 us
    all_to_all x1, starting transfers between devices, shards(): lax.all_to_all(dq, 'uly', split_axis=0, concat_axis=1, tiled=True)  5.01 us
    all_to_all x1, waiting for transfers between devices, shards(): lax.all_to_all(dq, 'uly', split_axis=0, concat_axis=1, tiled=True)  2.95 us
  transfers between devices with their start and end apart: 17, of which 11 were waited for; matrix products, arithmetic and copies ran while one was open for 9% of the time, Pallas kernels for 30%

profile of v16, /device:TPU:0, one launch (start us, length us, event | category | flops | bytes accessed | tf_op | source)
XLA Modules:
  0.0 111.2 jit_solution(6781747946518799641)
XLA Ops:
  0.7 1.1 constant_dynamic-slice_fusion
  1.8 3.0 %collective-permute-start.4 = (bf16[384,256]{1,0:T(8,128)(2,1)S(1)}, bf16[384,256]{1,0:T(8,128)(2,1)S(1)}, u32[]{:S(2)}, u32[]{:S(2)}) collective-permute-start(bf16[384,256]{1,0:T(8,128)(2,1)S(1)} %pad_maximum_fusion.4), channel_id=1, source_target_pairs={{0,8},{4,12},{8,16},{12,20},{16,24},{20,28},{24,0},{28,4},{1,9},{5... | collective-permute-start | bytes 589832 | tf_op jit(solution)/shard_map/ppermute | solution.py:180
  4.8 1.5 %collective-permute-start.5 = (bf16[384,256]{1,0:T(8,128)(2,1)S(1)}, bf16[384,256]{1,0:T(8,128)(2,1)S(1)}, u32[]{:S(2)}, u32[]{:S(2)}) collective-permute-start(bf16[384,256]{1,0:T(8,128)(2,1)S(1)} %pad_maximum_fusion.4), channel_id=1, source_target_pairs={{0,16},{4,20},{8,24},{12,28},{16,0},{20,4},{24,8},{28,12},{1,17},{... | collective-permute-start | bytes 589832 | tf_op jit(solution)/shard_map/ppermute | solution.py:180
  6.3 1.4 %collective-permute-start.6 = (bf16[384,256]{1,0:T(8,128)(2,1)S(1)}, bf16[384,256]{1,0:T(8,128)(2,1)S(1)}, u32[]{:S(2)}, u32[]{:S(2)}) collective-permute-start(bf16[384,256]{1,0:T(8,128)(2,1)S(1)} %pad_maximum_fusion.4), channel_id=1, source_target_pairs={{0,24},{4,28},{8,0},{12,4},{16,8},{20,12},{24,16},{28,20},{1,25},{... | collective-permute-start | bytes 589832 | tf_op jit(solution)/shard_map/ppermute | solution.py:180
  9.2 2.3 %collective-permute-done.4 = bf16[384,256]{1,0:T(8,128)(2,1)S(1)} collective-permute-done((bf16[384,256]{1,0:T(8,128)(2,1)S(1)}, bf16[384,256]{1,0:T(8,128)(2,1)S(1)}, u32[]{:S(2)}, u32[]{:S(2)}) %collective-permute-start.4) | collective-permute-done | bytes 196640 | tf_op jit(solution)/shard_map/ppermute | solution.py:180
  11.5 2.0 %collective-permute-start.2 = (bf16[384,256]{1,0:T(8,128)(2,1)S(1)}, bf16[384,256]{1,0:T(8,128)(2,1)S(1)}, u32[]{:S(2)}, u32[]{:S(2)}) collective-permute-start(bf16[384,256]{1,0:T(8,128)(2,1)S(1)} %pad_maximum_fusion.3), channel_id=1, source_target_pairs={{0,24},{4,28},{8,0},{12,4},{16,8},{20,12},{24,16},{28,20},{1,25},{... | collective-permute-start | bytes 589832 | tf_op jit(solution)/shard_map/ppermute | solution.py:180
  13.5 2.3 %collective-permute-done.5 = bf16[384,256]{1,0:T(8,128)(2,1)S(1)} collective-permute-done((bf16[384,256]{1,0:T(8,128)(2,1)S(1)}, bf16[384,256]{1,0:T(8,128)(2,1)S(1)}, u32[]{:S(2)}, u32[]{:S(2)}) %collective-permute-start.5) | collective-permute-done | bytes 196640 | tf_op jit(solution)/shard_map/ppermute | solution.py:180
  17.1 2.8 %collective-permute-done = bf16[384,256]{1,0:T(8,128)(2,1)S(1)} collective-permute-done((bf16[384,256]{1,0:T(8,128)(2,1)S(1)}, bf16[384,256]{1,0:T(8,128)(2,1)S(1)}, u32[]{:S(2)}, u32[]{:S(2)}) %collective-permute-start) | collective-permute-done | bytes 196640 | tf_op jit(solution)/shard_map/ppermute | solution.py:180
  20.0 3.3 %collective-permute-done.1 = bf16[384,256]{1,0:T(8,128)(2,1)S(1)} collective-permute-done((bf16[384,256]{1,0:T(8,128)(2,1)S(1)}, bf16[384,256]{1,0:T(8,128)(2,1)S(1)}, u32[]{:S(2)}, u32[]{:S(2)}) %collective-permute-start.1) | collective-permute-done | bytes 196640 | tf_op jit(solution)/shard_map/ppermute | solution.py:180
  23.8 0.7 pad_add_fusion.tbl_ref
  24.5 1.2 %broadcast_in_dim.10.dq_in = bf16[384,1536]{1,0:T(8,128)(2,1)} broadcast(bf16[]{:T(256)} %constant.92.clone.1), dimensions={} | broadcast | bytes 1179650 | tf_op jit(solution)/shard_map/broadcast_in_dim | solution.py:166
  25.7 16.6 %shard_map.76 = (bf16[384,1536]{1,0:T(8,128)(2,1)}, f32[384,256]{1,0:T(8,128)}, bf16[1536,256]{1,0:T(8,128)(2,1)}, bf16[1536,256]{1,0:T(8,128)(2,1)}) custom-call(s32[96]{0:T(128)} %pad_add_fusion.tbl_ref, bf16[384,1536]{1,0:T(8,128)(2,1)} %q_ref.3, bf16[384,1536]{1,0:T(8,128)(2,1)} %do_ref.3, ...), custom_call_target="tpu_custom_call", output_to_operand_aliasing={{0}: (7, {})} | custom-call | flops 3623878656 | bytes 5111808 | tf_op jit(solution)/shard_map/pallas_call | solution.py:216
  42.8 16.6 %shard_map.77 = (bf16[384,1536]{1,0:T(8,128)(2,1)}, f32[384,256]{1,0:T(8,128)}, bf16[1536,256]{1,0:T(8,128)(2,1)}, bf16[1536,256]{1,0:T(8,128)(2,1)}) custom-call(s32[96]{0:T(128)} %pad_add_fusion.tbl_ref, bf16[384,1536]{1,0:T(8,128)(2,1)} %q_ref.3, bf16[384,1536]{1,0:T(8,128)(2,1)} %do_ref.3, ...), custom_call_target="tpu_custom_call", output_to_operand_aliasing={{0}: (7, {})} | custom-call | flops 3623878656 | bytes 5111808 | tf_op jit(solution)/shard_map/pallas_call | solution.py:216
  59.5 5.0 %all-to-all-start = ((bf16[4,96,1536]{2,1,0:T(8,128)(2,1)}), bf16[4,96,1536]{2,1,0:T(8,128)(2,1)S(1)}, u32[]{:S(2)}, u32[]{:S(2)}) async-start(bf16[4,96,1536]{2,1,0:T(8,128)(2,1)} %bitcast.23), calls=%async_computation | async-start | bytes 2359296 | tf_op jit(solution)/shard_map/all_to_all | solution.py:246
  64.5 1.3 %add_convert_fusion.1 = bf16[1536,256]{1,0:T(8,128)(2,1)S(1)} fusion(bf16[1536,256]{1,0:T(8,128)(2,1)} %collective-permute-done.8, bf16[1536,256]{1,0:T(8,128)(2,1)S(1)} %copy-done.1), kind=kLoop, calls=%fused_computation.1 | loop fusion | flops 1572864 | bytes 2359296 | tf_op jit(solution)/shard_map/convert_element_type | solution.py:234
  65.9 1.4 %collective-permute-start.10 = (bf16[384,256]{1,0:T(8,128)(2,1)S(1)}, bf16[384,256]{1,0:T(8,128)(2,1)S(1)}, u32[]{:S(2)}, u32[]{:S(2)}) collective-permute-start(bf16[384,256]{1,0:T(8,128)(2,1)S(1)} %get-tuple-element.34), channel_id=1, source_target_pairs={{0,16},{4,20},{8,24},{12,28},{16,0},{20,4},{24,8},{28,12},{1,17},{... | collective-permute-start | bytes 589832 | tf_op jit(solution)/shard_map/ppermute | solution.py:238
  67.3 0.8 collective-permute-start.11
  68.1 2.1 %collective-permute-start.9 = (bf16[384,256]{1,0:T(8,128)(2,1)S(1)}, bf16[384,256]{1,0:T(8,128)(2,1)S(1)}, u32[]{:S(2)}, u32[]{:S(2)}) collective-permute-start(bf16[384,256]{1,0:T(8,128)(2,1)S(1)} %get-tuple-element.32), channel_id=1, source_target_pairs={{0,24},{4,28},{8,0},{12,4},{16,8},{20,12},{24,16},{28,20},{1,25},{... | collective-permute-start | bytes 589832 | tf_op jit(solution)/shard_map/ppermute | solution.py:238
  70.5 0.8 fusion.11
  71.3 0.8 collective-permute-start.13
  72.6 5.3 %collective-permute-done.10 = bf16[384,256]{1,0:T(8,128)(2,1)S(1)} collective-permute-done((bf16[384,256]{1,0:T(8,128)(2,1)S(1)}, bf16[384,256]{1,0:T(8,128)(2,1)S(1)}, u32[]{:S(2)}, u32[]{:S(2)}) %collective-permute-start.10) | collective-permute-done | bytes 196640 | tf_op jit(solution)/shard_map/ppermute | solution.py:238
  77.9 1.5 %collective-permute-done.9 = bf16[384,256]{1,0:T(8,128)(2,1)S(1)} collective-permute-done((bf16[384,256]{1,0:T(8,128)(2,1)S(1)}, bf16[384,256]{1,0:T(8,128)(2,1)S(1)}, u32[]{:S(2)}, u32[]{:S(2)}) %collective-permute-start.9) | collective-permute-done | bytes 196640 | tf_op jit(solution)/shard_map/ppermute | solution.py:238
  79.4 1.2 %add_convert_fusion.3 = bf16[384,256]{1,0:T(8,128)(2,1)S(1)} fusion(f32[384,256]{1,0:T(8,128)S(1)} %copy-done.4, bf16[384,256]{1,0:T(8,128)(2,1)S(1)} %collective-permute-done.11, bf16[384,256]{1,0:T(8,128)(2,1)S(1)} %collective-permute-done.10, bf16[384,256]{1,0:T(8,128)(2,1)S(1)} %collective-permute-done.9, bf16[1536,256]{1,0:T(8,128)(2,1)} %collective-permute-done.8, ...), kind=kLoop, calls=%fused_computation.7 | loop fusion | flops 1081344 | bytes 1572864 | tf_op jit(solution)/shard_map/convert.8
  81.3 2.3 %collective-permute-done.13 = bf16[384,256]{1,0:T(8,128)(2,1)S(1)} collective-permute-done((bf16[384,256]{1,0:T(8,128)(2,1)}, bf16[384,256]{1,0:T(8,128)(2,1)S(1)}, u32[]{:S(2)}, u32[]{:S(2)}) %collective-permute-start.13) | collective-permute-done | bytes 196640 | tf_op jit(solution)/shard_map/ppermute | solution.py:238
  83.6 4.0 %collective-permute-done.15 = bf16[384,256]{1,0:T(8,128)(2,1)} collective-permute-done((bf16[384,256]{1,0:T(8,128)(2,1)}, bf16[384,256]{1,0:T(8,128)(2,1)}, u32[]{:S(2)}, u32[]{:S(2)}) %collective-permute-start.15) | collective-permute-done | bytes 196640 | tf_op jit(solution)/shard_map/ppermute | solution.py:238
  87.7 1.3 %add_convert_fusion.2 = bf16[384,256]{1,0:T(8,128)(2,1)S(1)} fusion(f32[384,256]{1,0:T(8,128)} %get-tuple-element.26, bf16[384,256]{1,0:T(8,128)(2,1)} %collective-permute-done.15, bf16[384,256]{1,0:T(8,128)(2,1)} %collective-permute-done.14, bf16[384,256]{1,0:T(8,128)(2,1)S(1)} %collective-permute-done.13, bf16[1536,256]{1,0:T(8,128)(2,1)S(1)} %collective-permute-done.12, ...), kind=kLoop, calls=%fused_computation.6 | loop fusion | flops 1081344 | bytes 1572864 | tf_op jit(solution)/shard_map/convert.7
  89.7 0.9 pad_maximum_fusion.2
  90.7 3.0 %all-to-all-done = bf16[4,96,1536]{2,1,0:T(8,128)(2,1)S(1)} async-done(((bf16[4,96,1536]{2,1,0:T(8,128)(2,1)}), bf16[4,96,1536]{2,1,0:T(8,128)(2,1)S(1)}, u32[]{:S(2)}, u32[]{:S(2)}) %all-to-all-start) | async-done | bytes 1179680 | tf_op jit(solution)/shard_map/all_to_all | solution.py:246
  93.6 1.1 %copy.39 = bf16[4,12,8,1536]{3,2,0,1:T(8,128)(2,1)} copy(bf16[4,12,8,1536]{3,2,1,0:T(8,128)(2,1)S(1)} %bitcast.22) | data formatting | bytes 2359296 | tf_op jit(solution)/shard_map/all_to_all | solution.py:246
  94.8 13.8 %all_to_all.35 = bf16[4,96,512]{2,1,0:T(8,128)(2,1)S(1)} all-to-all(bf16[4,96,512]{2,1,0:T(8,128)(2,1)S(1)} %bitcast.24), channel_id=1, replica_groups=mesh['ctx'=8,'uly'=4] {'uly'}, dimensions={0} | all-to-all | bytes 786432 | tf_op jit(solution)/shard_map/all_to_all | solution.py:248
  109.5 0.7 copy.41
  110.5 0.7 copy.42
  (61 shorter events, 7.3 us)
Async XLA Ops:
  0.6 8.3 %copy-start.5 = (s32[24,8]{0,1:T(8,128)S(1)}, s32[24,8]{0,1:T(8,128)}, u32[]{:S(2)}) copy-start(s32[24,8]{0,1:T(8,128)} %param.9) | copy-start | bytes 2308
  1.8 9.7 %collective-permute-start.4 = (bf16[384,256]{1,0:T(8,128)(2,1)S(1)}, bf16[384,256]{1,0:T(8,128)(2,1)S(1)}, u32[]{:S(2)}, u32[]{:S(2)}) collective-permute-start(bf16[384,256]{1,0:T(8,128)(2,1)S(1)} %pad_maximum_fusion.4), channel_id=1, source_target_pairs={{0,8},{4,12},{8,16},{12,20},{16,24},{20,28},{24,0},{28,4},{1,9},{5... | collective-permute-start | bytes 589832 | tf_op jit(solution)/shard_map/ppermute | solution.py:180
  4.8 11.0 %collective-permute-start.5 = (bf16[384,256]{1,0:T(8,128)(2,1)S(1)}, bf16[384,256]{1,0:T(8,128)(2,1)S(1)}, u32[]{:S(2)}, u32[]{:S(2)}) collective-permute-start(bf16[384,256]{1,0:T(8,128)(2,1)S(1)} %pad_maximum_fusion.4), channel_id=1, source_target_pairs={{0,16},{4,20},{8,24},{12,28},{16,0},{20,4},{24,8},{28,12},{1,17},{... | collective-permute-start | bytes 589832 | tf_op jit(solution)/shard_map/ppermute | solution.py:180
  6.3 10.0 %collective-permute-start.6 = (bf16[384,256]{1,0:T(8,128)(2,1)S(1)}, bf16[384,256]{1,0:T(8,128)(2,1)S(1)}, u32[]{:S(2)}, u32[]{:S(2)}) collective-permute-start(bf16[384,256]{1,0:T(8,128)(2,1)S(1)} %pad_maximum_fusion.4), channel_id=1, source_target_pairs={{0,24},{4,28},{8,0},{12,4},{16,8},{20,12},{24,16},{28,20},{1,25},{... | collective-permute-start | bytes 589832 | tf_op jit(solution)/shard_map/ppermute | solution.py:180
  7.8 12.2 %collective-permute-start = (bf16[384,256]{1,0:T(8,128)(2,1)S(1)}, bf16[384,256]{1,0:T(8,128)(2,1)S(1)}, u32[]{:S(2)}, u32[]{:S(2)}) collective-permute-start(bf16[384,256]{1,0:T(8,128)(2,1)S(1)} %pad_maximum_fusion.3), channel_id=1, source_target_pairs={{0,8},{4,12},{8,16},{12,20},{16,24},{20,28},{24,0},{28,4},{1,9},{5... | collective-permute-start | bytes 589832 | tf_op jit(solution)/shard_map/ppermute | solution.py:180
  8.4 14.9 %collective-permute-start.1 = (bf16[384,256]{1,0:T(8,128)(2,1)S(1)}, bf16[384,256]{1,0:T(8,128)(2,1)S(1)}, u32[]{:S(2)}, u32[]{:S(2)}) collective-permute-start(bf16[384,256]{1,0:T(8,128)(2,1)S(1)} %pad_maximum_fusion.3), channel_id=1, source_target_pairs={{0,16},{4,20},{8,24},{12,28},{16,0},{20,4},{24,8},{28,12},{1,17},{... | collective-permute-start | bytes 589832 | tf_op jit(solution)/shard_map/ppermute | solution.py:180
  11.5 12.1 %collective-permute-start.2 = (bf16[384,256]{1,0:T(8,128)(2,1)S(1)}, bf16[384,256]{1,0:T(8,128)(2,1)S(1)}, u32[]{:S(2)}, u32[]{:S(2)}) collective-permute-start(bf16[384,256]{1,0:T(8,128)(2,1)S(1)} %pad_maximum_fusion.3), channel_id=1, source_target_pairs={{0,24},{4,28},{8,0},{12,4},{16,8},{20,12},{24,16},{28,20},{1,25},{... | collective-permute-start | bytes 589832 | tf_op jit(solution)/shard_map/ppermute | solution.py:180
  16.4 9.3 %copy-start.2 = (bf16[1536,256]{1,0:T(8,128)(2,1)}, bf16[1536,256]{1,0:T(8,128)(2,1)S(1)}, u32[]{:S(2)}) copy-start(bf16[1536,256]{1,0:T(8,128)(2,1)S(1)} %pad_maximum_fusion.1.k_ref.v_ref) | copy-start | bytes 2359300
  16.4 8.1 %collective-permute-start.7 = (bf16[1536,256]{1,0:T(8,128)(2,1)S(1)}, bf16[1536,256]{1,0:T(8,128)(2,1)S(1)}, u32[]{:S(2)}, u32[]{:S(2)}) collective-permute-start(bf16[1536,256]{1,0:T(8,128)(2,1)S(1)} %pad_maximum_fusion.1.k_ref.v_ref), channel_id=1, source_target_pairs={{0,4},{4,0},{8,12},{12,8},{16,20},{20,16},{24,28},{28,24},{1,5},{5... | collective-permute-start | bytes 2359304 | tf_op jit(solution)/shard_map/ppermute | solution.py:182
  23.7 18.6 %copy-start.3 = (bf16[1536,256]{1,0:T(8,128)(2,1)}, bf16[1536,256]{1,0:T(8,128)(2,1)S(1)}, u32[]{:S(2)}) copy-start(bf16[1536,256]{1,0:T(8,128)(2,1)S(1)} %pad_maximum_fusion.k_ref.v_ref) | copy-start | bytes 2359300
  23.7 19.1 %collective-permute-start.3 = (bf16[1536,256]{1,0:T(8,128)(2,1)S(1)}, bf16[1536,256]{1,0:T(8,128)(2,1)}, u32[]{:S(2)}, u32[]{:S(2)}) collective-permute-start(bf16[1536,256]{1,0:T(8,128)(2,1)S(1)} %pad_maximum_fusion.k_ref.v_ref), channel_id=1, source_target_pairs={{0,4},{4,0},{8,12},{12,8},{16,20},{20,16},{24,28},{28,24},{1,5},{5... | collective-permute-start | bytes 2359304 | tf_op jit(solution)/shard_map/ppermute | solution.py:182
  24.5 1.3 %copy-start.6 = (bf16[1536,256]{1,0:T(8,128)(2,1)}, bf16[1536,256]{1,0:T(8,128)(2,1)S(1)}, u32[]{:S(2)}) copy-start(bf16[1536,256]{1,0:T(8,128)(2,1)S(1)} %collective-permute-done.7.ko_ref.vo_ref) | copy-start | bytes 2359300
  42.3 22.2 %collective-permute-start.8 = (bf16[1536,256]{1,0:T(8,128)(2,1)}, bf16[1536,256]{1,0:T(8,128)(2,1)}, u32[]{:S(2)}, u32[]{:S(2)}) collective-permute-start(bf16[1536,256]{1,0:T(8,128)(2,1)} %get-tuple-element.22), channel_id=1, source_target_pairs={{0,4},{4,0},{8,12},{12,8},{16,20},{20,16},{24,28},{28,24},{1,5},{5... | collective-permute-start | bytes 2359304 | tf_op jit(solution)/shard_map/ppermute | solution.py:233
  59.4 10.9 %collective-permute-start.12 = (bf16[1536,256]{1,0:T(8,128)(2,1)}, bf16[1536,256]{1,0:T(8,128)(2,1)S(1)}, u32[]{:S(2)}, u32[]{:S(2)}) collective-permute-start(bf16[1536,256]{1,0:T(8,128)(2,1)} %get-tuple-element.25), channel_id=1, source_target_pairs={{0,4},{4,0},{8,12},{12,8},{16,20},{20,16},{24,28},{28,24},{1,5},{5... | collective-permute-start | bytes 2359304 | tf_op jit(solution)/shard_map/ppermute | solution.py:233
  59.5 5.0 %copy-start.1 = (bf16[1536,256]{1,0:T(8,128)(2,1)S(1)}, bf16[1536,256]{1,0:T(8,128)(2,1)}, u32[]{:S(2)}) copy-start(bf16[1536,256]{1,0:T(8,128)(2,1)} %get-tuple-element.21) | copy-start | bytes 2359300
  59.5 34.1 %all-to-all-start = ((bf16[4,96,1536]{2,1,0:T(8,128)(2,1)}), bf16[4,96,1536]{2,1,0:T(8,128)(2,1)S(1)}, u32[]{:S(2)}, u32[]{:S(2)}) async-start(bf16[4,96,1536]{2,1,0:T(8,128)(2,1)} %bitcast.23), calls=%async_computation | async-start | bytes 2359296 | tf_op jit(solution)/shard_map/all_to_all | solution.py:246
  65.8 4.4 %copy-start = (bf16[1536,256]{1,0:T(8,128)(2,1)S(1)}, bf16[1536,256]{1,0:T(8,128)(2,1)}, u32[]{:S(2)}) copy-start(bf16[1536,256]{1,0:T(8,128)(2,1)} %get-tuple-element.24) | copy-start | bytes 2359300
  65.9 12.0 %collective-permute-start.10 = (bf16[384,256]{1,0:T(8,128)(2,1)S(1)}, bf16[384,256]{1,0:T(8,128)(2,1)S(1)}, u32[]{:S(2)}, u32[]{:S(2)}) collective-permute-start(bf16[384,256]{1,0:T(8,128)(2,1)S(1)} %get-tuple-element.34), channel_id=1, source_target_pairs={{0,16},{4,20},{8,24},{12,28},{16,0},{20,4},{24,8},{28,12},{1,17},{... | collective-permute-start | bytes 589832 | tf_op jit(solution)/shard_map/ppermute | solution.py:238
  67.3 10.6 %collective-permute-start.11 = (bf16[384,256]{1,0:T(8,128)(2,1)S(1)}, bf16[384,256]{1,0:T(8,128)(2,1)S(1)}, u32[]{:S(2)}, u32[]{:S(2)}) collective-permute-start(bf16[384,256]{1,0:T(8,128)(2,1)S(1)} %get-tuple-element.33), channel_id=1, source_target_pairs={{0,8},{4,12},{8,16},{12,20},{16,24},{20,28},{24,0},{28,4},{1,9},{5... | collective-permute-start | bytes 589832 | tf_op jit(solution)/shard_map/ppermute | solution.py:238
  68.1 11.3 %collective-permute-start.9 = (bf16[384,256]{1,0:T(8,128)(2,1)S(1)}, bf16[384,256]{1,0:T(8,128)(2,1)S(1)}, u32[]{:S(2)}, u32[]{:S(2)}) collective-permute-start(bf16[384,256]{1,0:T(8,128)(2,1)S(1)} %get-tuple-element.32), channel_id=1, source_target_pairs={{0,24},{4,28},{8,0},{12,4},{16,8},{20,12},{24,16},{28,20},{1,25},{... | collective-permute-start | bytes 589832 | tf_op jit(solution)/shard_map/ppermute | solution.py:238
  70.5 9.0 %copy-start.4 = (f32[384,256]{1,0:T(8,128)S(1)}, f32[384,256]{1,0:T(8,128)}, u32[]{:S(2)}) copy-start(f32[384,256]{1,0:T(8,128)} %get-tuple-element.23) | copy-start | bytes 1179652
  71.3 12.3 %collective-permute-start.13 = (bf16[384,256]{1,0:T(8,128)(2,1)}, bf16[384,256]{1,0:T(8,128)(2,1)S(1)}, u32[]{:S(2)}, u32[]{:S(2)}) collective-permute-start(bf16[384,256]{1,0:T(8,128)(2,1)} %get-tuple-element.35), channel_id=1, source_target_pairs={{0,24},{4,28},{8,0},{12,4},{16,8},{20,12},{24,16},{28,20},{1,25},{... | collective-permute-start | bytes 589832 | tf_op jit(solution)/shard_map/ppermute | solution.py:238
  72.1 11.5 %collective-permute-start.14 = (bf16[384,256]{1,0:T(8,128)(2,1)}, bf16[384,256]{1,0:T(8,128)(2,1)}, u32[]{:S(2)}, u32[]{:S(2)}) collective-permute-start(bf16[384,256]{1,0:T(8,128)(2,1)} %get-tuple-element.37), channel_id=1, source_target_pairs={{0,16},{4,20},{8,24},{12,28},{16,0},{20,4},{24,8},{28,12},{1,17},{... | collective-permute-start | bytes 589832 | tf_op jit(solution)/shard_map/ppermute | solution.py:238
  77.9 9.8 %collective-permute-start.15 = (bf16[384,256]{1,0:T(8,128)(2,1)}, bf16[384,256]{1,0:T(8,128)(2,1)}, u32[]{:S(2)}, u32[]{:S(2)}) collective-permute-start(bf16[384,256]{1,0:T(8,128)(2,1)} %get-tuple-element.36), channel_id=1, source_target_pairs={{0,8},{4,12},{8,16},{12,20},{16,24},{20,28},{24,0},{28,4},{1,9},{5... | collective-permute-start | bytes 589832 | tf_op jit(solution)/shard_map/ppermute | solution.py:238

commit v17 on v14

--- a/solution.py
+++ b/solution.py
@@ -19,7 +19,7 @@
     tbl_ref,
     q_ref, do_ref, k_ref, v_ref, ko_ref, vo_ref, dq_in,
     dq_ref, loc_ref, far_ref, fo_ref,
-    kc_ref, vc_ref, loc_acc, far_acc, fo_acc,
+    kc_ref, vc_ref,
     *, hpk, kv_here, nb,
 ):
     g = pl.program_id(0)
@@ -39,11 +39,11 @@
     def kind_ref(i):
         return tbl_ref[3 * count + i]
 
-    @pl.when((g == 0) & (b == 0))
+    @pl.when(b == 0)
     def _():
-        loc_acc[...] = jnp.zeros_like(loc_acc)
-        far_acc[...] = jnp.zeros_like(far_acc)
-        fo_acc[...] = jnp.zeros_like(fo_acc)
+        loc_ref[...] = jnp.zeros_like(loc_ref)
+        far_ref[...] = jnp.zeros_like(far_ref)
+        fo_ref[...] = jnp.zeros_like(fo_ref)
 
     for s in range(SLOTS):
         row = pl.multiple_of(blk_ref(b * SLOTS + s) * BLK, BLK)
@@ -84,29 +84,20 @@
         kt = jnp.where(rounded, kt.astype(jnp.bfloat16).astype(jnp.float32), kt)
         vt = jnp.where(rounded, vt.astype(jnp.bfloat16).astype(jnp.float32), vt)
 
+        side = side_ref(b * SLOTS + s)
+
         @pl.when(kind == 2)
         def _():
-            loc_acc[g, pl.ds(row, BLK), :] += kt
-            loc_acc[kv_here + g, pl.ds(row, BLK), :] += vt
-
-        side = side_ref(b * SLOTS + s)
-
-        @pl.when((kind != 2) & (side == 0))
-        def _():
-            far_acc[g, pl.ds(row, BLK), :] += kt
-            far_acc[kv_here + g, pl.ds(row, BLK), :] += vt
-
-        @pl.when((kind != 2) & (side == 1))
-        def _():
-            fo_acc[g, pl.ds(row, BLK), :] += kt
-            fo_acc[kv_here + g, pl.ds(row, BLK), :] += vt
-
-    @pl.when((g == kv_here - 1) & (b == nb - 1))
-    def _():
-        for j in range(2 * kv_here):
-            loc_ref[:, j * HD:(j + 1) * HD] = loc_acc[j]
-            far_ref[:, j * HD:(j + 1) * HD] = far_acc[j].astype(jnp.bfloat16)
-            fo_ref[:, j * HD:(j + 1) * HD] = fo_acc[j].astype(jnp.bfloat16)
+            loc_ref[pl.ds(row, BLK), 0:HD] += kt
+            loc_ref[pl.ds(row, BLK), HD:2 * HD] += vt
+
+        for code, out in ((0, far_ref), (1, fo_ref)):
+            @pl.when((kind != 2) & (side == code))
+            def _():
+                kk = out[pl.ds(row, BLK), 0:HD].astype(jnp.float32) + kt
+                out[pl.ds(row, BLK), 0:HD] = kk.astype(jnp.bfloat16)
+                vv = out[pl.ds(row, BLK), HD:2 * HD].astype(jnp.float32) + vt
+                out[pl.ds(row, BLK), HD:2 * HD] = vv.astype(jnp.bfloat16)
 
 
 def shards(query_rows, key_rows, value_rows, out_grad, block_list):
@@ -182,9 +173,6 @@
             scratch_shapes=[
                 pltpu.VMEM((SLOTS * BLK, HD), jnp.bfloat16),
                 pltpu.VMEM((SLOTS * BLK, HD), jnp.bfloat16),
-                pltpu.VMEM((2, span, HD), jnp.float32),
-                pltpu.VMEM((2, half, HD), jnp.float32),
-                pltpu.VMEM((2, half, HD), jnp.float32),
             ],
         )
         dq, loc, far, far_other = pl.pallas_call(

time: 107 us -> 107 us (level)
  transfers between devices with their start and end apart: 17 -> 17, of which waited for: 11 -> 11; matrix products, arithmetic and copies ran while one was open for 9% -> 10% of each run, Pallas kernels for 27% -> 27%
where the time goes in v17:
time: 107 us; the launch traced here: 106 us
  Pallas kernels  28.2 us (26%)
  waiting for transfers between devices  27.7 us (26%)
  starting transfers between devices  20.6 us (19%)
  blocking collectives  13.8 us (13%)
  local copies, waits for them, and re-layouts  9.02 us (8%)
  other arithmetic  6.02 us (6%)
    pallas_call x2, Pallas kernels, shards(): pl.pallas_call(kernel, grid_spec=grid_spec, out_shape=[jax.ShapeDtypeStru...  28.2 us
    all_to_all x1, blocking collectives, shards(): lax.all_to_all(kv_grad, 'uly', split_axis=0, concat_axis=1, tiled=True)  13.8 us
    ppermute x6, waiting for transfers between devices, shards(): lax.ppermute(mine[d * span:(d + 1) * span], 'ctx', pairs)  13.2 us
    ppermute x6, waiting for transfers between devices, shards(): gathered.append(lax.ppermute(kv_own, 'ctx', pairs))  11.6 us
    ppermute x6, starting transfers between devices, shards(): gathered.append(lax.ppermute(kv_own, 'ctx', pairs))  9.11 us
    ppermute x6, starting transfers between devices, shards(): lax.ppermute(mine[d * span:(d + 1) * span], 'ctx', pairs)  5.74 us
    all_to_all x1, starting transfers between devices, shards(): lax.all_to_all(dq, 'uly', split_axis=0, concat_axis=1, tiled=True)  5.01 us
    all_to_all x1, waiting for transfers between devices, shards(): lax.all_to_all(dq, 'uly', split_axis=0, concat_axis=1, tiled=True)  2.91 us
  transfers between devices with their start and end apart: 17, of which 11 were waited for; matrix products, arithmetic and copies ran while one was open for 10% of the time, Pallas kernels for 27%

profile of v17, /device:TPU:0, one launch (start us, length us, event | category | flops | bytes accessed | tf_op | source)
XLA Modules:
  0.0 106.2 jit_solution(17454395613379543590)
XLA Ops:
  0.7 1.1 %constant_dynamic-slice_fusion = (bf16[384,128]{1,0:T(8,128)(2,1)S(1)}, bf16[384,128]{1,0:T(8,128)(2,1)S(1)}, bf16[384,128]{1,0:T(8,128)(2,1)S(1)}, bf16[384,128]{1,0:T(8,128)(2,1)S(1)}) fusion(bf16[384,1024]{1,0:T(8,128)(2,1)} %param.7, s32[]{:T(128)S(6)} %select_n.71, s32[]{:T(128)S(6)} %select_n.70, bf16[384,1024]{1,0:T(8,128)(2,1)} %param.6), kind=kLoop, calls=%fused_computation.36 | loop fusion | bytes 786440 | tf_op jit(solution)/shard_map/dynamic_slice | solution.py:143
  1.8 3.0 %collective-permute-start.4 = (bf16[384,256]{1,0:T(8,128)(2,1)S(1)}, bf16[384,256]{1,0:T(8,128)(2,1)S(1)}, u32[]{:S(2)}, u32[]{:S(2)}) collective-permute-start(bf16[384,256]{1,0:T(8,128)(2,1)S(1)} %pad_maximum_fusion.4), channel_id=1, source_target_pairs={{0,8},{4,12},{8,16},{12,20},{16,24},{20,28},{24,0},{28,4},{1,9},{5... | collective-permute-start | bytes 589832 | tf_op jit(solution)/shard_map/ppermute | solution.py:150
  4.8 1.5 %collective-permute-start.5 = (bf16[384,256]{1,0:T(8,128)(2,1)S(1)}, bf16[384,256]{1,0:T(8,128)(2,1)S(1)}, u32[]{:S(2)}, u32[]{:S(2)}) collective-permute-start(bf16[384,256]{1,0:T(8,128)(2,1)S(1)} %pad_maximum_fusion.4), channel_id=1, source_target_pairs={{0,16},{4,20},{8,24},{12,28},{16,0},{20,4},{24,8},{28,12},{1,17},{... | collective-permute-start | bytes 589832 | tf_op jit(solution)/shard_map/ppermute | solution.py:150
  6.3 1.4 %collective-permute-start.6 = (bf16[384,256]{1,0:T(8,128)(2,1)S(1)}, bf16[384,256]{1,0:T(8,128)(2,1)S(1)}, u32[]{:S(2)}, u32[]{:S(2)}) collective-permute-start(bf16[384,256]{1,0:T(8,128)(2,1)S(1)} %pad_maximum_fusion.4), channel_id=1, source_target_pairs={{0,24},{4,28},{8,0},{12,4},{16,8},{20,12},{24,16},{28,20},{1,25},{... | collective-permute-start | bytes 589832 | tf_op jit(solution)/shard_map/ppermute | solution.py:150
  9.2 2.3 %collective-permute-done.4 = bf16[384,256]{1,0:T(8,128)(2,1)S(1)} collective-permute-done((bf16[384,256]{1,0:T(8,128)(2,1)S(1)}, bf16[384,256]{1,0:T(8,128)(2,1)S(1)}, u32[]{:S(2)}, u32[]{:S(2)}) %collective-permute-start.4) | collective-permute-done | bytes 196640 | tf_op jit(solution)/shard_map/ppermute | solution.py:150
  11.5 2.0 %collective-permute-start.2 = (bf16[384,256]{1,0:T(8,128)(2,1)S(1)}, bf16[384,256]{1,0:T(8,128)(2,1)S(1)}, u32[]{:S(2)}, u32[]{:S(2)}) collective-permute-start(bf16[384,256]{1,0:T(8,128)(2,1)S(1)} %pad_maximum_fusion.3), channel_id=1, source_target_pairs={{0,24},{4,28},{8,0},{12,4},{16,8},{20,12},{24,16},{28,20},{1,25},{... | collective-permute-start | bytes 589832 | tf_op jit(solution)/shard_map/ppermute | solution.py:150
  13.5 2.3 %collective-permute-done.5 = bf16[384,256]{1,0:T(8,128)(2,1)S(1)} collective-permute-done((bf16[384,256]{1,0:T(8,128)(2,1)S(1)}, bf16[384,256]{1,0:T(8,128)(2,1)S(1)}, u32[]{:S(2)}, u32[]{:S(2)}) %collective-permute-start.5) | collective-permute-done | bytes 196640 | tf_op jit(solution)/shard_map/ppermute | solution.py:150
  17.1 2.8 %collective-permute-done = bf16[384,256]{1,0:T(8,128)(2,1)S(1)} collective-permute-done((bf16[384,256]{1,0:T(8,128)(2,1)S(1)}, bf16[384,256]{1,0:T(8,128)(2,1)S(1)}, u32[]{:S(2)}, u32[]{:S(2)}) %collective-permute-start) | collective-permute-done | bytes 196640 | tf_op jit(solution)/shard_map/ppermute | solution.py:150
  20.0 3.3 %collective-permute-done.1 = bf16[384,256]{1,0:T(8,128)(2,1)S(1)} collective-permute-done((bf16[384,256]{1,0:T(8,128)(2,1)S(1)}, bf16[384,256]{1,0:T(8,128)(2,1)S(1)}, u32[]{:S(2)}, u32[]{:S(2)}) %collective-permute-start.1) | collective-permute-done | bytes 196640 | tf_op jit(solution)/shard_map/ppermute | solution.py:150
  23.8 0.7 pad_add_fusion.tbl_ref
  24.5 1.2 %broadcast_in_dim.10.dq_in = bf16[384,1536]{1,0:T(8,128)(2,1)} broadcast(bf16[]{:T(256)} %constant.92.clone.1), dimensions={} | broadcast | bytes 1179650 | tf_op jit(solution)/shard_map/broadcast_in_dim | solution.py:136
  25.7 14.1 %shard_map.76 = (bf16[384,1536]{1,0:T(8,128)(2,1)}, f32[384,256]{1,0:T(8,128)}, bf16[1536,256]{1,0:T(8,128)(2,1)}, bf16[1536,256]{1,0:T(8,128)(2,1)}) custom-call(s32[96]{0:T(128)} %pad_add_fusion.tbl_ref, bf16[384,1536]{1,0:T(8,128)(2,1)} %q_ref.3, bf16[384,1536]{1,0:T(8,128)(2,1)} %do_ref.3, ...), custom_call_target="tpu_custom_call", output_to_operand_aliasing={{0}: (7, {})} | custom-call | flops 3623878656 | bytes 5111808 | tf_op jit(solution)/shard_map/pallas_call | solution.py:178
  40.3 14.1 %shard_map.77 = (bf16[384,1536]{1,0:T(8,128)(2,1)}, f32[384,256]{1,0:T(8,128)}, bf16[1536,256]{1,0:T(8,128)(2,1)}, bf16[1536,256]{1,0:T(8,128)(2,1)}) custom-call(s32[96]{0:T(128)} %pad_add_fusion.tbl_ref, bf16[384,1536]{1,0:T(8,128)(2,1)} %q_ref.3, bf16[384,1536]{1,0:T(8,128)(2,1)} %do_ref.3, ...), custom_call_target="tpu_custom_call", output_to_operand_aliasing={{0}: (7, {})} | custom-call | flops 3623878656 | bytes 5111808 | tf_op jit(solution)/shard_map/pallas_call | solution.py:178
  54.5 5.0 %all-to-all-start = ((bf16[4,96,1536]{2,1,0:T(8,128)(2,1)}), bf16[4,96,1536]{2,1,0:T(8,128)(2,1)S(1)}, u32[]{:S(2)}, u32[]{:S(2)}) async-start(bf16[4,96,1536]{2,1,0:T(8,128)(2,1)} %bitcast.23), calls=%async_computation | async-start | bytes 2359296 | tf_op jit(solution)/shard_map/all_to_all | solution.py:208
  59.5 1.3 %add_convert_fusion.1 = bf16[1536,256]{1,0:T(8,128)(2,1)S(1)} fusion(bf16[1536,256]{1,0:T(8,128)(2,1)} %collective-permute-done.8, bf16[1536,256]{1,0:T(8,128)(2,1)S(1)} %copy-done.1), kind=kLoop, calls=%fused_computation.1 | loop fusion | flops 1572864 | bytes 2359296 | tf_op jit(solution)/shard_map/convert_element_type | solution.py:196
  60.9 1.5 %collective-permute-start.10 = (bf16[384,256]{1,0:T(8,128)(2,1)S(1)}, bf16[384,256]{1,0:T(8,128)(2,1)S(1)}, u32[]{:S(2)}, u32[]{:S(2)}) collective-permute-start(bf16[384,256]{1,0:T(8,128)(2,1)S(1)} %get-tuple-element.34), channel_id=1, source_target_pairs={{0,16},{4,20},{8,24},{12,28},{16,0},{20,4},{24,8},{28,12},{1,17},{... | collective-permute-start | bytes 589832 | tf_op jit(solution)/shard_map/ppermute | solution.py:200
  62.4 0.8 collective-permute-start.11
  63.2 2.1 %collective-permute-start.9 = (bf16[384,256]{1,0:T(8,128)(2,1)S(1)}, bf16[384,256]{1,0:T(8,128)(2,1)S(1)}, u32[]{:S(2)}, u32[]{:S(2)}) collective-permute-start(bf16[384,256]{1,0:T(8,128)(2,1)S(1)} %get-tuple-element.32), channel_id=1, source_target_pairs={{0,24},{4,28},{8,0},{12,4},{16,8},{20,12},{24,16},{28,20},{1,25},{... | collective-permute-start | bytes 589832 | tf_op jit(solution)/shard_map/ppermute | solution.py:200
  65.5 0.8 fusion.11
  66.3 0.8 collective-permute-start.13
  67.7 5.2 %collective-permute-done.10 = bf16[384,256]{1,0:T(8,128)(2,1)S(1)} collective-permute-done((bf16[384,256]{1,0:T(8,128)(2,1)S(1)}, bf16[384,256]{1,0:T(8,128)(2,1)S(1)}, u32[]{:S(2)}, u32[]{:S(2)}) %collective-permute-start.10) | collective-permute-done | bytes 196640 | tf_op jit(solution)/shard_map/ppermute | solution.py:200
  73.0 1.5 %collective-permute-done.9 = bf16[384,256]{1,0:T(8,128)(2,1)S(1)} collective-permute-done((bf16[384,256]{1,0:T(8,128)(2,1)S(1)}, bf16[384,256]{1,0:T(8,128)(2,1)S(1)}, u32[]{:S(2)}, u32[]{:S(2)}) %collective-permute-start.9) | collective-permute-done | bytes 196640 | tf_op jit(solution)/shard_map/ppermute | solution.py:200
  74.5 1.2 %add_convert_fusion.3 = bf16[384,256]{1,0:T(8,128)(2,1)S(1)} fusion(f32[384,256]{1,0:T(8,128)S(1)} %copy-done.4, bf16[384,256]{1,0:T(8,128)(2,1)S(1)} %collective-permute-done.11, bf16[384,256]{1,0:T(8,128)(2,1)S(1)} %collective-permute-done.10, bf16[384,256]{1,0:T(8,128)(2,1)S(1)} %collective-permute-done.9, bf16[1536,256]{1,0:T(8,128)(2,1)} %collective-permute-done.8, ...), kind=kLoop, calls=%fused_computation.7 | loop fusion | flops 1081344 | bytes 1572864 | tf_op jit(solution)/shard_map/convert.8
  76.3 2.3 %collective-permute-done.13 = bf16[384,256]{1,0:T(8,128)(2,1)S(1)} collective-permute-done((bf16[384,256]{1,0:T(8,128)(2,1)}, bf16[384,256]{1,0:T(8,128)(2,1)S(1)}, u32[]{:S(2)}, u32[]{:S(2)}) %collective-permute-start.13) | collective-permute-done | bytes 196640 | tf_op jit(solution)/shard_map/ppermute | solution.py:200
  78.7 4.1 %collective-permute-done.15 = bf16[384,256]{1,0:T(8,128)(2,1)} collective-permute-done((bf16[384,256]{1,0:T(8,128)(2,1)}, bf16[384,256]{1,0:T(8,128)(2,1)}, u32[]{:S(2)}, u32[]{:S(2)}) %collective-permute-start.15) | collective-permute-done | bytes 196640 | tf_op jit(solution)/shard_map/ppermute | solution.py:200
  82.8 1.3 %add_convert_fusion.2 = bf16[384,256]{1,0:T(8,128)(2,1)S(1)} fusion(f32[384,256]{1,0:T(8,128)} %get-tuple-element.26, bf16[384,256]{1,0:T(8,128)(2,1)} %collective-permute-done.15, bf16[384,256]{1,0:T(8,128)(2,1)} %collective-permute-done.14, bf16[384,256]{1,0:T(8,128)(2,1)S(1)} %collective-permute-done.13, bf16[1536,256]{1,0:T(8,128)(2,1)S(1)} %collective-permute-done.12, ...), kind=kLoop, calls=%fused_computation.6 | loop fusion | flops 1081344 | bytes 1572864 | tf_op jit(solution)/shard_map/convert.7
  84.7 0.9 pad_maximum_fusion.2
  85.7 2.9 %all-to-all-done = bf16[4,96,1536]{2,1,0:T(8,128)(2,1)S(1)} async-done(((bf16[4,96,1536]{2,1,0:T(8,128)(2,1)}), bf16[4,96,1536]{2,1,0:T(8,128)(2,1)S(1)}, u32[]{:S(2)}, u32[]{:S(2)}) %all-to-all-start) | async-done | bytes 1179680 | tf_op jit(solution)/shard_map/all_to_all | solution.py:208
  88.6 1.1 %copy.39 = bf16[4,12,8,1536]{3,2,0,1:T(8,128)(2,1)} copy(bf16[4,12,8,1536]{3,2,1,0:T(8,128)(2,1)S(1)} %bitcast.22) | data formatting | bytes 2359296 | tf_op jit(solution)/shard_map/all_to_all | solution.py:208
  89.8 13.8 %all_to_all.35 = bf16[4,96,512]{2,1,0:T(8,128)(2,1)S(1)} all-to-all(bf16[4,96,512]{2,1,0:T(8,128)(2,1)S(1)} %bitcast.24), channel_id=1, replica_groups=mesh['ctx'=8,'uly'=4] {'uly'}, dimensions={0} | all-to-all | bytes 786432 | tf_op jit(solution)/shard_map/all_to_all | solution.py:210
  104.5 0.7 copy.41
  105.5 0.7 copy.42
  (61 shorter events, 7.3 us)
Async XLA Ops:
  0.6 8.3 %copy-start.5 = (s32[24,8]{0,1:T(8,128)S(1)}, s32[24,8]{0,1:T(8,128)}, u32[]{:S(2)}) copy-start(s32[24,8]{0,1:T(8,128)} %param.9) | copy-start | bytes 2308
  1.8 9.7 %collective-permute-start.4 = (bf16[384,256]{1,0:T(8,128)(2,1)S(1)}, bf16[384,256]{1,0:T(8,128)(2,1)S(1)}, u32[]{:S(2)}, u32[]{:S(2)}) collective-permute-start(bf16[384,256]{1,0:T(8,128)(2,1)S(1)} %pad_maximum_fusion.4), channel_id=1, source_target_pairs={{0,8},{4,12},{8,16},{12,20},{16,24},{20,28},{24,0},{28,4},{1,9},{5... | collective-permute-start | bytes 589832 | tf_op jit(solution)/shard_map/ppermute | solution.py:150
  4.8 11.0 %collective-permute-start.5 = (bf16[384,256]{1,0:T(8,128)(2,1)S(1)}, bf16[384,256]{1,0:T(8,128)(2,1)S(1)}, u32[]{:S(2)}, u32[]{:S(2)}) collective-permute-start(bf16[384,256]{1,0:T(8,128)(2,1)S(1)} %pad_maximum_fusion.4), channel_id=1, source_target_pairs={{0,16},{4,20},{8,24},{12,28},{16,0},{20,4},{24,8},{28,12},{1,17},{... | collective-permute-start | bytes 589832 | tf_op jit(solution)/shard_map/ppermute | solution.py:150
  6.3 10.0 %collective-permute-start.6 = (bf16[384,256]{1,0:T(8,128)(2,1)S(1)}, bf16[384,256]{1,0:T(8,128)(2,1)S(1)}, u32[]{:S(2)}, u32[]{:S(2)}) collective-permute-start(bf16[384,256]{1,0:T(8,128)(2,1)S(1)} %pad_maximum_fusion.4), channel_id=1, source_target_pairs={{0,24},{4,28},{8,0},{12,4},{16,8},{20,12},{24,16},{28,20},{1,25},{... | collective-permute-start | bytes 589832 | tf_op jit(solution)/shard_map/ppermute | solution.py:150
  7.8 12.2 %collective-permute-start = (bf16[384,256]{1,0:T(8,128)(2,1)S(1)}, bf16[384,256]{1,0:T(8,128)(2,1)S(1)}, u32[]{:S(2)}, u32[]{:S(2)}) collective-permute-start(bf16[384,256]{1,0:T(8,128)(2,1)S(1)} %pad_maximum_fusion.3), channel_id=1, source_target_pairs={{0,8},{4,12},{8,16},{12,20},{16,24},{20,28},{24,0},{28,4},{1,9},{5... | collective-permute-start | bytes 589832 | tf_op jit(solution)/shard_map/ppermute | solution.py:150
  8.4 14.9 %collective-permute-start.1 = (bf16[384,256]{1,0:T(8,128)(2,1)S(1)}, bf16[384,256]{1,0:T(8,128)(2,1)S(1)}, u32[]{:S(2)}, u32[]{:S(2)}) collective-permute-start(bf16[384,256]{1,0:T(8,128)(2,1)S(1)} %pad_maximum_fusion.3), channel_id=1, source_target_pairs={{0,16},{4,20},{8,24},{12,28},{16,0},{20,4},{24,8},{28,12},{1,17},{... | collective-permute-start | bytes 589832 | tf_op jit(solution)/shard_map/ppermute | solution.py:150
  11.5 12.1 %collective-permute-start.2 = (bf16[384,256]{1,0:T(8,128)(2,1)S(1)}, bf16[384,256]{1,0:T(8,128)(2,1)S(1)}, u32[]{:S(2)}, u32[]{:S(2)}) collective-permute-start(bf16[384,256]{1,0:T(8,128)(2,1)S(1)} %pad_maximum_fusion.3), channel_id=1, source_target_pairs={{0,24},{4,28},{8,0},{12,4},{16,8},{20,12},{24,16},{28,20},{1,25},{... | collective-permute-start | bytes 589832 | tf_op jit(solution)/shard_map/ppermute | solution.py:150
  16.4 9.3 %copy-start.2 = (bf16[1536,256]{1,0:T(8,128)(2,1)}, bf16[1536,256]{1,0:T(8,128)(2,1)S(1)}, u32[]{:S(2)}) copy-start(bf16[1536,256]{1,0:T(8,128)(2,1)S(1)} %pad_maximum_fusion.1.k_ref.v_ref) | copy-start | bytes 2359300
  16.4 8.1 %collective-permute-start.7 = (bf16[1536,256]{1,0:T(8,128)(2,1)S(1)}, bf16[1536,256]{1,0:T(8,128)(2,1)S(1)}, u32[]{:S(2)}, u32[]{:S(2)}) collective-permute-start(bf16[1536,256]{1,0:T(8,128)(2,1)S(1)} %pad_maximum_fusion.1.k_ref.v_ref), channel_id=1, source_target_pairs={{0,4},{4,0},{8,12},{12,8},{16,20},{20,16},{24,28},{28,24},{1,5},{5... | collective-permute-start | bytes 2359304 | tf_op jit(solution)/shard_map/ppermute | solution.py:152
  23.7 16.1 %copy-start.3 = (bf16[1536,256]{1,0:T(8,128)(2,1)}, bf16[1536,256]{1,0:T(8,128)(2,1)S(1)}, u32[]{:S(2)}) copy-start(bf16[1536,256]{1,0:T(8,128)(2,1)S(1)} %pad_maximum_fusion.k_ref.v_ref) | copy-start | bytes 2359300
  23.7 16.6 %collective-permute-start.3 = (bf16[1536,256]{1,0:T(8,128)(2,1)S(1)}, bf16[1536,256]{1,0:T(8,128)(2,1)}, u32[]{:S(2)}, u32[]{:S(2)}) collective-permute-start(bf16[1536,256]{1,0:T(8,128)(2,1)S(1)} %pad_maximum_fusion.k_ref.v_ref), channel_id=1, source_target_pairs={{0,4},{4,0},{8,12},{12,8},{16,20},{20,16},{24,28},{28,24},{1,5},{5... | collective-permute-start | bytes 2359304 | tf_op jit(solution)/shard_map/ppermute | solution.py:152
  24.5 1.3 %copy-start.6 = (bf16[1536,256]{1,0:T(8,128)(2,1)}, bf16[1536,256]{1,0:T(8,128)(2,1)S(1)}, u32[]{:S(2)}) copy-start(bf16[1536,256]{1,0:T(8,128)(2,1)S(1)} %collective-permute-done.7.ko_ref.vo_ref) | copy-start | bytes 2359300
  39.8 19.7 %collective-permute-start.8 = (bf16[1536,256]{1,0:T(8,128)(2,1)}, bf16[1536,256]{1,0:T(8,128)(2,1)}, u32[]{:S(2)}, u32[]{:S(2)}) collective-permute-start(bf16[1536,256]{1,0:T(8,128)(2,1)} %get-tuple-element.22), channel_id=1, source_target_pairs={{0,4},{4,0},{8,12},{12,8},{16,20},{20,16},{24,28},{28,24},{1,5},{5... | collective-permute-start | bytes 2359304 | tf_op jit(solution)/shard_map/ppermute | solution.py:195
  54.4 10.9 %collective-permute-start.12 = (bf16[1536,256]{1,0:T(8,128)(2,1)}, bf16[1536,256]{1,0:T(8,128)(2,1)S(1)}, u32[]{:S(2)}, u32[]{:S(2)}) collective-permute-start(bf16[1536,256]{1,0:T(8,128)(2,1)} %get-tuple-element.25), channel_id=1, source_target_pairs={{0,4},{4,0},{8,12},{12,8},{16,20},{20,16},{24,28},{28,24},{1,5},{5... | collective-permute-start | bytes 2359304 | tf_op jit(solution)/shard_map/ppermute | solution.py:195
  54.5 5.0 %copy-start.1 = (bf16[1536,256]{1,0:T(8,128)(2,1)S(1)}, bf16[1536,256]{1,0:T(8,128)(2,1)}, u32[]{:S(2)}) copy-start(bf16[1536,256]{1,0:T(8,128)(2,1)} %get-tuple-element.21) | copy-start | bytes 2359300
  54.5 34.1 %all-to-all-start = ((bf16[4,96,1536]{2,1,0:T(8,128)(2,1)}), bf16[4,96,1536]{2,1,0:T(8,128)(2,1)S(1)}, u32[]{:S(2)}, u32[]{:S(2)}) async-start(bf16[4,96,1536]{2,1,0:T(8,128)(2,1)} %bitcast.23), calls=%async_computation | async-start | bytes 2359296 | tf_op jit(solution)/shard_map/all_to_all | solution.py:208
  60.9 4.5 %copy-start = (bf16[1536,256]{1,0:T(8,128)(2,1)S(1)}, bf16[1536,256]{1,0:T(8,128)(2,1)}, u32[]{:S(2)}) copy-start(bf16[1536,256]{1,0:T(8,128)(2,1)} %get-tuple-element.24) | copy-start | bytes 2359300
  60.9 12.0 %collective-permute-start.10 = (bf16[384,256]{1,0:T(8,128)(2,1)S(1)}, bf16[384,256]{1,0:T(8,128)(2,1)S(1)}, u32[]{:S(2)}, u32[]{:S(2)}) collective-permute-start(bf16[384,256]{1,0:T(8,128)(2,1)S(1)} %get-tuple-element.34), channel_id=1, source_target_pairs={{0,16},{4,20},{8,24},{12,28},{16,0},{20,4},{24,8},{28,12},{1,17},{... | collective-permute-start | bytes 589832 | tf_op jit(solution)/shard_map/ppermute | solution.py:200
  62.4 10.6 %collective-permute-start.11 = (bf16[384,256]{1,0:T(8,128)(2,1)S(1)}, bf16[384,256]{1,0:T(8,128)(2,1)S(1)}, u32[]{:S(2)}, u32[]{:S(2)}) collective-permute-start(bf16[384,256]{1,0:T(8,128)(2,1)S(1)} %get-tuple-element.33), channel_id=1, source_target_pairs={{0,8},{4,12},{8,16},{12,20},{16,24},{20,28},{24,0},{28,4},{1,9},{5... | collective-permute-start | bytes 589832 | tf_op jit(solution)/shard_map/ppermute | solution.py:200
  63.2 11.3 %collective-permute-start.9 = (bf16[384,256]{1,0:T(8,128)(2,1)S(1)}, bf16[384,256]{1,0:T(8,128)(2,1)S(1)}, u32[]{:S(2)}, u32[]{:S(2)}) collective-permute-start(bf16[384,256]{1,0:T(8,128)(2,1)S(1)} %get-tuple-element.32), channel_id=1, source_target_pairs={{0,24},{4,28},{8,0},{12,4},{16,8},{20,12},{24,16},{28,20},{1,25},{... | collective-permute-start | bytes 589832 | tf_op jit(solution)/shard_map/ppermute | solution.py:200
  65.5 8.9 %copy-start.4 = (f32[384,256]{1,0:T(8,128)S(1)}, f32[384,256]{1,0:T(8,128)}, u32[]{:S(2)}) copy-start(f32[384,256]{1,0:T(8,128)} %get-tuple-element.23) | copy-start | bytes 1179652
  66.3 12.3 %collective-permute-start.13 = (bf16[384,256]{1,0:T(8,128)(2,1)}, bf16[384,256]{1,0:T(8,128)(2,1)S(1)}, u32[]{:S(2)}, u32[]{:S(2)}) collective-permute-start(bf16[384,256]{1,0:T(8,128)(2,1)} %get-tuple-element.35), channel_id=1, source_target_pairs={{0,24},{4,28},{8,0},{12,4},{16,8},{20,12},{24,16},{28,20},{1,25},{... | collective-permute-start | bytes 589832 | tf_op jit(solution)/shard_map/ppermute | solution.py:200
  67.2 11.5 %collective-permute-start.14 = (bf16[384,256]{1,0:T(8,128)(2,1)}, bf16[384,256]{1,0:T(8,128)(2,1)}, u32[]{:S(2)}, u32[]{:S(2)}) collective-permute-start(bf16[384,256]{1,0:T(8,128)(2,1)} %get-tuple-element.37), channel_id=1, source_target_pairs={{0,16},{4,20},{8,24},{12,28},{16,0},{20,4},{24,8},{28,12},{1,17},{... | collective-permute-start | bytes 589832 | tf_op jit(solution)/shard_map/ppermute | solution.py:200
  72.9 9.8 %collective-permute-start.15 = (bf16[384,256]{1,0:T(8,128)(2,1)}, bf16[384,256]{1,0:T(8,128)(2,1)}, u32[]{:S(2)}, u32[]{:S(2)}) collective-permute-start(bf16[384,256]{1,0:T(8,128)(2,1)} %get-tuple-element.36), channel_id=1, source_target_pairs={{0,8},{4,12},{8,16},{12,20},{16,24},{20,28},{24,0},{28,4},{1,9},{5... | collective-permute-start | bytes 589832 | tf_op jit(solution)/shard_map/ppermute | solution.py:200

commit v18 on v17

--- a/solution.py
+++ b/solution.py
@@ -17,11 +17,10 @@
 
 def attention_kernel(
     tbl_ref,
-    q_ref, do_ref, k_ref, v_ref, ko_ref, vo_ref, dq_in,
-    dq_ref, loc_ref, far_ref, fo_ref,
-    kc_ref, vc_ref,
-    *, hpk, kv_here, nb,
+    q_ref, do_ref, k_ref, v_ref, ko_ref, vo_ref, *refs,
+    hpk, kv_here, nb,
 ):
+    dq_ref, loc_ref, far_ref, fo_ref, kc_ref, vc_ref = refs[-6:]
     g = pl.program_id(0)
     b = pl.program_id(1)
     scale = 1.0 / math.sqrt(HD)
@@ -133,7 +132,7 @@
     table = jnp.concatenate([blk, side, dst, kind]).astype(jnp.int32)
 
     kernel = functools.partial(attention_kernel, hpk=hpk, kv_here=1, nb=nb)
-    dq = jnp.zeros((nb * BLK, heads_here * HD), jnp.bfloat16)
+    dq = None
     sums = []
     for g in range(kv_here):
         col = (first_kv + g) * HD
@@ -162,8 +161,7 @@
                 pl.BlockSpec((half, HD), lambda z, b, *_: (0, 1)),
                 pl.BlockSpec((half, HD), lambda z, b, *_: (0, 0)),
                 pl.BlockSpec((half, HD), lambda z, b, *_: (0, 1)),
-                pl.BlockSpec(memory_space=pl.ANY),
-            ],
+            ] + ([] if dq is None else [pl.BlockSpec(memory_space=pl.ANY)]),
             out_specs=[
                 pl.BlockSpec((BLK, hpk * HD), lambda z, b, *_, g=g: (b, g)),
                 pl.BlockSpec((span, 2 * HD), lambda z, b, *_: (0, 0)),
@@ -184,14 +182,14 @@
                 jax.ShapeDtypeStruct((half, 2 * HD), jnp.bfloat16),
                 jax.ShapeDtypeStruct((half, 2 * HD), jnp.bfloat16),
             ],
-            input_output_aliases={7: 0},
+            input_output_aliases={} if dq is None else {7: 0},
             cost_estimate=pl.CostEstimate(
                 flops=12 * nb * hpk * BLK * SLOTS * BLK * HD,
                 transcendentals=nb * hpk * BLK * SLOTS * BLK,
                 bytes_accessed=4 * nb * BLK * hpk * HD + 4 * half * HD * 2 + 12 * half * HD,
             ),
             compiler_params=pltpu.CompilerParams(dimension_semantics=("arbitrary", "arbitrary")),
-        )(table, query_rows, out_grad, kv_half, kv_half, kv_other, kv_other, dq)
+        )(table, query_rows, out_grad, kv_half, kv_half, kv_other, kv_other, *([] if dq is None else [dq]))
         from_partner = lax.ppermute(far_other, "ctx", partner)
         mine = (far.astype(jnp.float32) + from_partner.astype(jnp.float32)).astype(jnp.bfloat16)
         total = far[0:span].astype(jnp.float32) + from_partner[0:span].astype(jnp.float32)

time: 107 us -> 106 us (level)
    broadcast_in_dim x1 -> x0, local copies, waits for them, and re-layouts: 1.16 us -> none  [shards(): dq = jnp.zeros((nb * BLK, heads_here * HD), jnp.bfloat16)]
  transfers between devices with their start and end apart: 17 -> 17, of which waited for: 11 -> 11; matrix products, arithmetic and copies ran while one was open for 10% -> 8% of each run, Pallas kernels for 27% -> 27%
where the time goes in v18:
time: 106 us
  Pallas kernels  28.2 us (27%)
  waiting for transfers between devices  27.7 us (26%)
  starting transfers between devices  20.6 us (19%)
  blocking collectives  13.8 us (13%)
  local copies, waits for them, and re-layouts  8.63 us (8%)
  other arithmetic  6.02 us (6%)
    pallas_call x2, Pallas kernels, shards(): pl.pallas_call(kernel, grid_spec=grid_spec, out_shape=[jax.ShapeDtypeStru...  28.2 us
    all_to_all x1, blocking collectives, shards(): lax.all_to_all(kv_grad, 'uly', split_axis=0, concat_axis=1, tiled=True)  13.8 us
    ppermute x6, waiting for transfers between devices, shards(): lax.ppermute(mine[d * span:(d + 1) * span], 'ctx', pairs)  13.2 us
    ppermute x6, waiting for transfers between devices, shards(): gathered.append(lax.ppermute(kv_own, 'ctx', pairs))  11.6 us
    ppermute x6, starting transfers between devices, shards(): gathered.append(lax.ppermute(kv_own, 'ctx', pairs))  9.11 us
    ppermute x6, starting transfers between devices, shards(): lax.ppermute(mine[d * span:(d + 1) * span], 'ctx', pairs)  5.74 us
    all_to_all x1, starting transfers between devices, shards(): lax.all_to_all(dq, 'uly', split_axis=0, concat_axis=1, tiled=True)  5.01 us
    unnamed x21, local copies, waits for them, and re-layouts  3.08 us
  transfers between devices with their start and end apart: 17, of which 11 were waited for; matrix products, arithmetic and copies ran while one was open for 8% of the time, Pallas kernels for 27%

profile of v18, /device:TPU:0, one launch (start us, length us, event | category | flops | bytes accessed | tf_op | source)
XLA Modules:
  0.0 105.8 jit_solution(1227381422048922404)
XLA Ops:
  0.7 1.1 %constant_dynamic-slice_fusion = (bf16[384,128]{1,0:T(8,128)(2,1)S(1)}, bf16[384,128]{1,0:T(8,128)(2,1)S(1)}, bf16[384,128]{1,0:T(8,128)(2,1)S(1)}, bf16[384,128]{1,0:T(8,128)(2,1)S(1)}) fusion(bf16[384,1024]{1,0:T(8,128)(2,1)} %param.7, s32[]{:T(128)S(6)} %select_n.71, s32[]{:T(128)S(6)} %select_n.70, bf16[384,1024]{1,0:T(8,128)(2,1)} %param.6), kind=kLoop, calls=%fused_computation.36 | loop fusion | bytes 786440 | tf_op jit(solution)/shard_map/dynamic_slice | solution.py:142
  1.8 3.0 %collective-permute-start.4 = (bf16[384,256]{1,0:T(8,128)(2,1)S(1)}, bf16[384,256]{1,0:T(8,128)(2,1)S(1)}, u32[]{:S(2)}, u32[]{:S(2)}) collective-permute-start(bf16[384,256]{1,0:T(8,128)(2,1)S(1)} %pad_maximum_fusion.4), channel_id=1, source_target_pairs={{0,8},{4,12},{8,16},{12,20},{16,24},{20,28},{24,0},{28,4},{1,9},{5... | collective-permute-start | bytes 589832 | tf_op jit(solution)/shard_map/ppermute | solution.py:149
  4.8 1.5 %collective-permute-start.5 = (bf16[384,256]{1,0:T(8,128)(2,1)S(1)}, bf16[384,256]{1,0:T(8,128)(2,1)S(1)}, u32[]{:S(2)}, u32[]{:S(2)}) collective-permute-start(bf16[384,256]{1,0:T(8,128)(2,1)S(1)} %pad_maximum_fusion.4), channel_id=1, source_target_pairs={{0,16},{4,20},{8,24},{12,28},{16,0},{20,4},{24,8},{28,12},{1,17},{... | collective-permute-start | bytes 589832 | tf_op jit(solution)/shard_map/ppermute | solution.py:149
  6.3 1.4 %collective-permute-start.6 = (bf16[384,256]{1,0:T(8,128)(2,1)S(1)}, bf16[384,256]{1,0:T(8,128)(2,1)S(1)}, u32[]{:S(2)}, u32[]{:S(2)}) collective-permute-start(bf16[384,256]{1,0:T(8,128)(2,1)S(1)} %pad_maximum_fusion.4), channel_id=1, source_target_pairs={{0,24},{4,28},{8,0},{12,4},{16,8},{20,12},{24,16},{28,20},{1,25},{... | collective-permute-start | bytes 589832 | tf_op jit(solution)/shard_map/ppermute | solution.py:149
  9.2 2.3 %collective-permute-done.4 = bf16[384,256]{1,0:T(8,128)(2,1)S(1)} collective-permute-done((bf16[384,256]{1,0:T(8,128)(2,1)S(1)}, bf16[384,256]{1,0:T(8,128)(2,1)S(1)}, u32[]{:S(2)}, u32[]{:S(2)}) %collective-permute-start.4) | collective-permute-done | bytes 196640 | tf_op jit(solution)/shard_map/ppermute | solution.py:149
  11.5 2.0 %collective-permute-start.2 = (bf16[384,256]{1,0:T(8,128)(2,1)S(1)}, bf16[384,256]{1,0:T(8,128)(2,1)S(1)}, u32[]{:S(2)}, u32[]{:S(2)}) collective-permute-start(bf16[384,256]{1,0:T(8,128)(2,1)S(1)} %pad_maximum_fusion.3), channel_id=1, source_target_pairs={{0,24},{4,28},{8,0},{12,4},{16,8},{20,12},{24,16},{28,20},{1,25},{... | collective-permute-start | bytes 589832 | tf_op jit(solution)/shard_map/ppermute | solution.py:149
  13.5 2.3 %collective-permute-done.5 = bf16[384,256]{1,0:T(8,128)(2,1)S(1)} collective-permute-done((bf16[384,256]{1,0:T(8,128)(2,1)S(1)}, bf16[384,256]{1,0:T(8,128)(2,1)S(1)}, u32[]{:S(2)}, u32[]{:S(2)}) %collective-permute-start.5) | collective-permute-done | bytes 196640 | tf_op jit(solution)/shard_map/ppermute | solution.py:149
  17.1 2.8 %collective-permute-done = bf16[384,256]{1,0:T(8,128)(2,1)S(1)} collective-permute-done((bf16[384,256]{1,0:T(8,128)(2,1)S(1)}, bf16[384,256]{1,0:T(8,128)(2,1)S(1)}, u32[]{:S(2)}, u32[]{:S(2)}) %collective-permute-start) | collective-permute-done | bytes 196640 | tf_op jit(solution)/shard_map/ppermute | solution.py:149
  20.0 3.3 %collective-permute-done.1 = bf16[384,256]{1,0:T(8,128)(2,1)S(1)} collective-permute-done((bf16[384,256]{1,0:T(8,128)(2,1)S(1)}, bf16[384,256]{1,0:T(8,128)(2,1)S(1)}, u32[]{:S(2)}, u32[]{:S(2)}) %collective-permute-start.1) | collective-permute-done | bytes 196640 | tf_op jit(solution)/shard_map/ppermute | solution.py:149
  23.8 0.7 pad_add_fusion.tbl_ref
  24.5 0.9 copy-done.6
  25.3 14.1 %shard_map.76 = (bf16[384,1536]{1,0:T(8,128)(2,1)}, f32[384,256]{1,0:T(8,128)}, bf16[1536,256]{1,0:T(8,128)(2,1)}, bf16[1536,256]{1,0:T(8,128)(2,1)}) custom-call(s32[96]{0:T(128)} %pad_add_fusion.tbl_ref, bf16[384,1536]{1,0:T(8,128)(2,1)} %q_ref.3, bf16[384,1536]{1,0:T(8,128)(2,1)} %do_ref.3, bf16[1536,256]{1,0:T(8,128)(2,1)} %copy-done.2, ...), custom_call_target="tpu_custom_call" | custom-call | flops 3623878656 | bytes 5111808 | tf_op jit(solution)/shard_map/pallas_call | solution.py:176
  39.9 14.1 %shard_map.77 = (bf16[384,1536]{1,0:T(8,128)(2,1)}, f32[384,256]{1,0:T(8,128)}, bf16[1536,256]{1,0:T(8,128)(2,1)}, bf16[1536,256]{1,0:T(8,128)(2,1)}) custom-call(s32[96]{0:T(128)} %pad_add_fusion.tbl_ref, bf16[384,1536]{1,0:T(8,128)(2,1)} %q_ref.3, bf16[384,1536]{1,0:T(8,128)(2,1)} %do_ref.3, ...), custom_call_target="tpu_custom_call", output_to_operand_aliasing={{0}: (7, {})} | custom-call | flops 3623878656 | bytes 5111808 | tf_op jit(solution)/shard_map/pallas_call | solution.py:176
  54.1 5.0 %all-to-all-start = ((bf16[4,96,1536]{2,1,0:T(8,128)(2,1)}), bf16[4,96,1536]{2,1,0:T(8,128)(2,1)S(1)}, u32[]{:S(2)}, u32[]{:S(2)}) async-start(bf16[4,96,1536]{2,1,0:T(8,128)(2,1)} %bitcast.27), calls=%async_computation | async-start | bytes 2359296 | tf_op jit(solution)/shard_map/all_to_all | solution.py:206
  59.1 1.3 %add_convert_fusion.1 = bf16[1536,256]{1,0:T(8,128)(2,1)S(1)} fusion(bf16[1536,256]{1,0:T(8,128)(2,1)} %collective-permute-done.8, bf16[1536,256]{1,0:T(8,128)(2,1)S(1)} %copy-done.1), kind=kLoop, calls=%fused_computation.1 | loop fusion | flops 1572864 | bytes 2359296 | tf_op jit(solution)/shard_map/convert_element_type | solution.py:194
  60.5 1.5 %collective-permute-start.10 = (bf16[384,256]{1,0:T(8,128)(2,1)S(1)}, bf16[384,256]{1,0:T(8,128)(2,1)S(1)}, u32[]{:S(2)}, u32[]{:S(2)}) collective-permute-start(bf16[384,256]{1,0:T(8,128)(2,1)S(1)} %get-tuple-element.34), channel_id=1, source_target_pairs={{0,16},{4,20},{8,24},{12,28},{16,0},{20,4},{24,8},{28,12},{1,17},{... | collective-permute-start | bytes 589832 | tf_op jit(solution)/shard_map/ppermute | solution.py:198
  62.0 0.8 collective-permute-start.11
  62.8 2.1 %collective-permute-start.9 = (bf16[384,256]{1,0:T(8,128)(2,1)S(1)}, bf16[384,256]{1,0:T(8,128)(2,1)S(1)}, u32[]{:S(2)}, u32[]{:S(2)}) collective-permute-start(bf16[384,256]{1,0:T(8,128)(2,1)S(1)} %get-tuple-element.32), channel_id=1, source_target_pairs={{0,24},{4,28},{8,0},{12,4},{16,8},{20,12},{24,16},{28,20},{1,25},{... | collective-permute-start | bytes 589832 | tf_op jit(solution)/shard_map/ppermute | solution.py:198
  65.1 0.8 fusion.11
  66.0 0.8 collective-permute-start.13
  67.3 5.2 %collective-permute-done.10 = bf16[384,256]{1,0:T(8,128)(2,1)S(1)} collective-permute-done((bf16[384,256]{1,0:T(8,128)(2,1)S(1)}, bf16[384,256]{1,0:T(8,128)(2,1)S(1)}, u32[]{:S(2)}, u32[]{:S(2)}) %collective-permute-start.10) | collective-permute-done | bytes 196640 | tf_op jit(solution)/shard_map/ppermute | solution.py:198
  72.6 1.5 %collective-permute-done.9 = bf16[384,256]{1,0:T(8,128)(2,1)S(1)} collective-permute-done((bf16[384,256]{1,0:T(8,128)(2,1)S(1)}, bf16[384,256]{1,0:T(8,128)(2,1)S(1)}, u32[]{:S(2)}, u32[]{:S(2)}) %collective-permute-start.9) | collective-permute-done | bytes 196640 | tf_op jit(solution)/shard_map/ppermute | solution.py:198
  74.1 1.2 %add_convert_fusion.3 = bf16[384,256]{1,0:T(8,128)(2,1)S(1)} fusion(f32[384,256]{1,0:T(8,128)S(1)} %copy-done.4, bf16[384,256]{1,0:T(8,128)(2,1)S(1)} %collective-permute-done.11, bf16[384,256]{1,0:T(8,128)(2,1)S(1)} %collective-permute-done.10, bf16[384,256]{1,0:T(8,128)(2,1)S(1)} %collective-permute-done.9, bf16[1536,256]{1,0:T(8,128)(2,1)} %collective-permute-done.8, ...), kind=kLoop, calls=%fused_computation.7 | loop fusion | flops 1081344 | bytes 1572864 | tf_op jit(solution)/shard_map/convert.8
  75.9 2.3 %collective-permute-done.13 = bf16[384,256]{1,0:T(8,128)(2,1)S(1)} collective-permute-done((bf16[384,256]{1,0:T(8,128)(2,1)}, bf16[384,256]{1,0:T(8,128)(2,1)S(1)}, u32[]{:S(2)}, u32[]{:S(2)}) %collective-permute-start.13) | collective-permute-done | bytes 196640 | tf_op jit(solution)/shard_map/ppermute | solution.py:198
  78.3 4.1 %collective-permute-done.15 = bf16[384,256]{1,0:T(8,128)(2,1)} collective-permute-done((bf16[384,256]{1,0:T(8,128)(2,1)}, bf16[384,256]{1,0:T(8,128)(2,1)}, u32[]{:S(2)}, u32[]{:S(2)}) %collective-permute-start.15) | collective-permute-done | bytes 196640 | tf_op jit(solution)/shard_map/ppermute | solution.py:198
  82.4 1.3 %add_convert_fusion.2 = bf16[384,256]{1,0:T(8,128)(2,1)S(1)} fusion(f32[384,256]{1,0:T(8,128)} %get-tuple-element.26, bf16[384,256]{1,0:T(8,128)(2,1)} %collective-permute-done.15, bf16[384,256]{1,0:T(8,128)(2,1)} %collective-permute-done.14, bf16[384,256]{1,0:T(8,128)(2,1)S(1)} %collective-permute-done.13, bf16[1536,256]{1,0:T(8,128)(2,1)S(1)} %collective-permute-done.12, ...), kind=kLoop, calls=%fused_computation.6 | loop fusion | flops 1081344 | bytes 1572864 | tf_op jit(solution)/shard_map/convert.7
  84.4 0.9 pad_maximum_fusion.2
  85.3 2.9 %all-to-all-done = bf16[4,96,1536]{2,1,0:T(8,128)(2,1)S(1)} async-done(((bf16[4,96,1536]{2,1,0:T(8,128)(2,1)}), bf16[4,96,1536]{2,1,0:T(8,128)(2,1)S(1)}, u32[]{:S(2)}, u32[]{:S(2)}) %all-to-all-start) | async-done | bytes 1179680 | tf_op jit(solution)/shard_map/all_to_all | solution.py:206
  88.3 1.1 %copy.38 = bf16[4,12,8,1536]{3,2,0,1:T(8,128)(2,1)} copy(bf16[4,12,8,1536]{3,2,1,0:T(8,128)(2,1)S(1)} %bitcast.22) | data formatting | bytes 2359296 | tf_op jit(solution)/shard_map/all_to_all | solution.py:206
  89.4 13.8 %all_to_all.35 = bf16[4,96,512]{2,1,0:T(8,128)(2,1)S(1)} all-to-all(bf16[4,96,512]{2,1,0:T(8,128)(2,1)S(1)} %bitcast.23), channel_id=1, replica_groups=mesh['ctx'=8,'uly'=4] {'uly'}, dimensions={0} | all-to-all | bytes 786432 | tf_op jit(solution)/shard_map/all_to_all | solution.py:208
  104.1 0.7 copy.40
  105.1 0.7 copy.41
  (60 shorter events, 7.2 us)
Async XLA Ops:
  0.6 8.3 %copy-start.5 = (s32[24,8]{0,1:T(8,128)S(1)}, s32[24,8]{0,1:T(8,128)}, u32[]{:S(2)}) copy-start(s32[24,8]{0,1:T(8,128)} %param.9) | copy-start | bytes 2308
  1.8 9.7 %collective-permute-start.4 = (bf16[384,256]{1,0:T(8,128)(2,1)S(1)}, bf16[384,256]{1,0:T(8,128)(2,1)S(1)}, u32[]{:S(2)}, u32[]{:S(2)}) collective-permute-start(bf16[384,256]{1,0:T(8,128)(2,1)S(1)} %pad_maximum_fusion.4), channel_id=1, source_target_pairs={{0,8},{4,12},{8,16},{12,20},{16,24},{20,28},{24,0},{28,4},{1,9},{5... | collective-permute-start | bytes 589832 | tf_op jit(solution)/shard_map/ppermute | solution.py:149
  4.8 11.0 %collective-permute-start.5 = (bf16[384,256]{1,0:T(8,128)(2,1)S(1)}, bf16[384,256]{1,0:T(8,128)(2,1)S(1)}, u32[]{:S(2)}, u32[]{:S(2)}) collective-permute-start(bf16[384,256]{1,0:T(8,128)(2,1)S(1)} %pad_maximum_fusion.4), channel_id=1, source_target_pairs={{0,16},{4,20},{8,24},{12,28},{16,0},{20,4},{24,8},{28,12},{1,17},{... | collective-permute-start | bytes 589832 | tf_op jit(solution)/shard_map/ppermute | solution.py:149
  6.3 10.0 %collective-permute-start.6 = (bf16[384,256]{1,0:T(8,128)(2,1)S(1)}, bf16[384,256]{1,0:T(8,128)(2,1)S(1)}, u32[]{:S(2)}, u32[]{:S(2)}) collective-permute-start(bf16[384,256]{1,0:T(8,128)(2,1)S(1)} %pad_maximum_fusion.4), channel_id=1, source_target_pairs={{0,24},{4,28},{8,0},{12,4},{16,8},{20,12},{24,16},{28,20},{1,25},{... | collective-permute-start | bytes 589832 | tf_op jit(solution)/shard_map/ppermute | solution.py:149
  7.8 12.2 %collective-permute-start = (bf16[384,256]{1,0:T(8,128)(2,1)S(1)}, bf16[384,256]{1,0:T(8,128)(2,1)S(1)}, u32[]{:S(2)}, u32[]{:S(2)}) collective-permute-start(bf16[384,256]{1,0:T(8,128)(2,1)S(1)} %pad_maximum_fusion.3), channel_id=1, source_target_pairs={{0,8},{4,12},{8,16},{12,20},{16,24},{20,28},{24,0},{28,4},{1,9},{5... | collective-permute-start | bytes 589832 | tf_op jit(solution)/shard_map/ppermute | solution.py:149
  8.4 14.9 %collective-permute-start.1 = (bf16[384,256]{1,0:T(8,128)(2,1)S(1)}, bf16[384,256]{1,0:T(8,128)(2,1)S(1)}, u32[]{:S(2)}, u32[]{:S(2)}) collective-permute-start(bf16[384,256]{1,0:T(8,128)(2,1)S(1)} %pad_maximum_fusion.3), channel_id=1, source_target_pairs={{0,16},{4,20},{8,24},{12,28},{16,0},{20,4},{24,8},{28,12},{1,17},{... | collective-permute-start | bytes 589832 | tf_op jit(solution)/shard_map/ppermute | solution.py:149
  11.5 12.1 %collective-permute-start.2 = (bf16[384,256]{1,0:T(8,128)(2,1)S(1)}, bf16[384,256]{1,0:T(8,128)(2,1)S(1)}, u32[]{:S(2)}, u32[]{:S(2)}) collective-permute-start(bf16[384,256]{1,0:T(8,128)(2,1)S(1)} %pad_maximum_fusion.3), channel_id=1, source_target_pairs={{0,24},{4,28},{8,0},{12,4},{16,8},{20,12},{24,16},{28,20},{1,25},{... | collective-permute-start | bytes 589832 | tf_op jit(solution)/shard_map/ppermute | solution.py:149
  16.4 8.1 %copy-start.2 = (bf16[1536,256]{1,0:T(8,128)(2,1)}, bf16[1536,256]{1,0:T(8,128)(2,1)S(1)}, u32[]{:S(2)}) copy-start(bf16[1536,256]{1,0:T(8,128)(2,1)S(1)} %pad_maximum_fusion.1.k_ref.v_ref) | copy-start | bytes 2359300
  16.4 8.1 %collective-permute-start.7 = (bf16[1536,256]{1,0:T(8,128)(2,1)S(1)}, bf16[1536,256]{1,0:T(8,128)(2,1)S(1)}, u32[]{:S(2)}, u32[]{:S(2)}) collective-permute-start(bf16[1536,256]{1,0:T(8,128)(2,1)S(1)} %pad_maximum_fusion.1.k_ref.v_ref), channel_id=1, source_target_pairs={{0,4},{4,0},{8,12},{12,8},{16,20},{20,16},{24,28},{28,24},{1,5},{5... | collective-permute-start | bytes 2359304 | tf_op jit(solution)/shard_map/ppermute | solution.py:151
  23.7 15.7 %copy-start.3 = (bf16[1536,256]{1,0:T(8,128)(2,1)}, bf16[1536,256]{1,0:T(8,128)(2,1)S(1)}, u32[]{:S(2)}) copy-start(bf16[1536,256]{1,0:T(8,128)(2,1)S(1)} %pad_maximum_fusion.k_ref.v_ref) | copy-start | bytes 2359300
  23.7 16.2 %collective-permute-start.3 = (bf16[1536,256]{1,0:T(8,128)(2,1)S(1)}, bf16[1536,256]{1,0:T(8,128)(2,1)}, u32[]{:S(2)}, u32[]{:S(2)}) collective-permute-start(bf16[1536,256]{1,0:T(8,128)(2,1)S(1)} %pad_maximum_fusion.k_ref.v_ref), channel_id=1, source_target_pairs={{0,4},{4,0},{8,12},{12,8},{16,20},{20,16},{24,28},{28,24},{1,5},{5... | collective-permute-start | bytes 2359304 | tf_op jit(solution)/shard_map/ppermute | solution.py:151
  24.5 0.9 copy-start.6
  39.4 19.7 %collective-permute-start.8 = (bf16[1536,256]{1,0:T(8,128)(2,1)}, bf16[1536,256]{1,0:T(8,128)(2,1)}, u32[]{:S(2)}, u32[]{:S(2)}) collective-permute-start(bf16[1536,256]{1,0:T(8,128)(2,1)} %get-tuple-element.22), channel_id=1, source_target_pairs={{0,4},{4,0},{8,12},{12,8},{16,20},{20,16},{24,28},{28,24},{1,5},{5... | collective-permute-start | bytes 2359304 | tf_op jit(solution)/shard_map/ppermute | solution.py:193
  54.0 10.9 %collective-permute-start.12 = (bf16[1536,256]{1,0:T(8,128)(2,1)}, bf16[1536,256]{1,0:T(8,128)(2,1)S(1)}, u32[]{:S(2)}, u32[]{:S(2)}) collective-permute-start(bf16[1536,256]{1,0:T(8,128)(2,1)} %get-tuple-element.25), channel_id=1, source_target_pairs={{0,4},{4,0},{8,12},{12,8},{16,20},{20,16},{24,28},{28,24},{1,5},{5... | collective-permute-start | bytes 2359304 | tf_op jit(solution)/shard_map/ppermute | solution.py:193
  54.1 5.0 %copy-start.1 = (bf16[1536,256]{1,0:T(8,128)(2,1)S(1)}, bf16[1536,256]{1,0:T(8,128)(2,1)}, u32[]{:S(2)}) copy-start(bf16[1536,256]{1,0:T(8,128)(2,1)} %get-tuple-element.21) | copy-start | bytes 2359300
  54.1 34.1 %all-to-all-start = ((bf16[4,96,1536]{2,1,0:T(8,128)(2,1)}), bf16[4,96,1536]{2,1,0:T(8,128)(2,1)S(1)}, u32[]{:S(2)}, u32[]{:S(2)}) async-start(bf16[4,96,1536]{2,1,0:T(8,128)(2,1)} %bitcast.27), calls=%async_computation | async-start | bytes 2359296 | tf_op jit(solution)/shard_map/all_to_all | solution.py:206
  60.5 4.4 %copy-start = (bf16[1536,256]{1,0:T(8,128)(2,1)S(1)}, bf16[1536,256]{1,0:T(8,128)(2,1)}, u32[]{:S(2)}) copy-start(bf16[1536,256]{1,0:T(8,128)(2,1)} %get-tuple-element.24) | copy-start | bytes 2359300
  60.5 12.0 %collective-permute-start.10 = (bf16[384,256]{1,0:T(8,128)(2,1)S(1)}, bf16[384,256]{1,0:T(8,128)(2,1)S(1)}, u32[]{:S(2)}, u32[]{:S(2)}) collective-permute-start(bf16[384,256]{1,0:T(8,128)(2,1)S(1)} %get-tuple-element.34), channel_id=1, source_target_pairs={{0,16},{4,20},{8,24},{12,28},{16,0},{20,4},{24,8},{28,12},{1,17},{... | collective-permute-start | bytes 589832 | tf_op jit(solution)/shard_map/ppermute | solution.py:198
  62.0 10.6 %collective-permute-start.11 = (bf16[384,256]{1,0:T(8,128)(2,1)S(1)}, bf16[384,256]{1,0:T(8,128)(2,1)S(1)}, u32[]{:S(2)}, u32[]{:S(2)}) collective-permute-start(bf16[384,256]{1,0:T(8,128)(2,1)S(1)} %get-tuple-element.33), channel_id=1, source_target_pairs={{0,8},{4,12},{8,16},{12,20},{16,24},{20,28},{24,0},{28,4},{1,9},{5... | collective-permute-start | bytes 589832 | tf_op jit(solution)/shard_map/ppermute | solution.py:198
  62.8 11.3 %collective-permute-start.9 = (bf16[384,256]{1,0:T(8,128)(2,1)S(1)}, bf16[384,256]{1,0:T(8,128)(2,1)S(1)}, u32[]{:S(2)}, u32[]{:S(2)}) collective-permute-start(bf16[384,256]{1,0:T(8,128)(2,1)S(1)} %get-tuple-element.32), channel_id=1, source_target_pairs={{0,24},{4,28},{8,0},{12,4},{16,8},{20,12},{24,16},{28,20},{1,25},{... | collective-permute-start | bytes 589832 | tf_op jit(solution)/shard_map/ppermute | solution.py:198
  65.1 8.9 %copy-start.4 = (f32[384,256]{1,0:T(8,128)S(1)}, f32[384,256]{1,0:T(8,128)}, u32[]{:S(2)}) copy-start(f32[384,256]{1,0:T(8,128)} %get-tuple-element.23) | copy-start | bytes 1179652
  66.0 12.3 %collective-permute-start.13 = (bf16[384,256]{1,0:T(8,128)(2,1)}, bf16[384,256]{1,0:T(8,128)(2,1)S(1)}, u32[]{:S(2)}, u32[]{:S(2)}) collective-permute-start(bf16[384,256]{1,0:T(8,128)(2,1)} %get-tuple-element.35), channel_id=1, source_target_pairs={{0,24},{4,28},{8,0},{12,4},{16,8},{20,12},{24,16},{28,20},{1,25},{... | collective-permute-start | bytes 589832 | tf_op jit(solution)/shard_map/ppermute | solution.py:198
  66.8 11.5 %collective-permute-start.14 = (bf16[384,256]{1,0:T(8,128)(2,1)}, bf16[384,256]{1,0:T(8,128)(2,1)}, u32[]{:S(2)}, u32[]{:S(2)}) collective-permute-start(bf16[384,256]{1,0:T(8,128)(2,1)} %get-tuple-element.37), channel_id=1, source_target_pairs={{0,16},{4,20},{8,24},{12,28},{16,0},{20,4},{24,8},{28,12},{1,17},{... | collective-permute-start | bytes 589832 | tf_op jit(solution)/shard_map/ppermute | solution.py:198
  72.6 9.8 %collective-permute-start.15 = (bf16[384,256]{1,0:T(8,128)(2,1)}, bf16[384,256]{1,0:T(8,128)(2,1)}, u32[]{:S(2)}, u32[]{:S(2)}) collective-permute-start(bf16[384,256]{1,0:T(8,128)(2,1)} %get-tuple-element.36), channel_id=1, source_target_pairs={{0,8},{4,12},{8,16},{12,20},{16,24},{20,28},{24,0},{28,4},{1,9},{5... | collective-permute-start | bytes 589832 | tf_op jit(solution)/shard_map/ppermute | solution.py:198

commit v19 on v18

--- a/solution.py
+++ b/solution.py
@@ -191,6 +191,8 @@
             compiler_params=pltpu.CompilerParams(dimension_semantics=("arbitrary", "arbitrary")),
         )(table, query_rows, out_grad, kv_half, kv_half, kv_other, kv_other, *([] if dq is None else [dq]))
         from_partner = lax.ppermute(far_other, "ctx", partner)
+        if g == kv_here - 1:
+            dq, from_partner = lax.optimization_barrier((dq, from_partner))
         mine = (far.astype(jnp.float32) + from_partner.astype(jnp.float32)).astype(jnp.bfloat16)
         total = far[0:span].astype(jnp.float32) + from_partner[0:span].astype(jnp.float32)
         for d in range(1, members):

time: 106 us -> 109 us (1.028)
  waiting for transfers between devices: 27.7 us -> 30.7 us
    all_to_all x1, waiting for transfers between devices: 2.92 us -> 11.3 us  [shards(): lax.all_to_all(dq, 'uly', split_axis=0, concat_axis=1, tiled=True)]
    ppermute x6, waiting for transfers between devices: 13.2 us -> 7.83 us  [shards(): lax.ppermute(mine[d * span:(d + 1) * span], 'ctx', pairs)]
    convert_element_type x2, other arithmetic: 1.53 us -> 0.39 us  [shards(): (far.astype(jnp.float32) + from_partner.astype(jnp.float32)).astype(jnp.b...]
  transfers between devices with their start and end apart: 17 -> 17, of which waited for: 11 -> 10; matrix products, arithmetic and copies ran while one was open for 8% -> 8% of each run, Pallas kernels for 27% -> 26%
where the time goes in v19:
time: 109 us
  waiting for transfers between devices  30.7 us (28%)
  Pallas kernels  28.3 us (26%)
  starting transfers between devices  21.5 us (20%)
  blocking collectives  13.6 us (12%)
  local copies, waits for them, and re-layouts  9.23 us (8%)
  other arithmetic  4.98 us (5%)
    pallas_call x2, Pallas kernels, shards(): pl.pallas_call(kernel, grid_spec=grid_spec, out_shape=[jax.ShapeDtypeStru...  28.3 us
    all_to_all x1, blocking collectives, shards(): lax.all_to_all(kv_grad, 'uly', split_axis=0, concat_axis=1, tiled=True)  13.6 us
    ppermute x6, waiting for transfers between devices, shards(): gathered.append(lax.ppermute(kv_own, 'ctx', pairs))  11.6 us
    all_to_all x1, waiting for transfers between devices, shards(): lax.all_to_all(dq, 'uly', split_axis=0, concat_axis=1, tiled=True)  11.3 us
    ppermute x6, starting transfers between devices, shards(): gathered.append(lax.ppermute(kv_own, 'ctx', pairs))  9.11 us
    ppermute x6, waiting for transfers between devices, shards(): lax.ppermute(mine[d * span:(d + 1) * span], 'ctx', pairs)  7.83 us
    ppermute x6, starting transfers between devices, shards(): lax.ppermute(mine[d * span:(d + 1) * span], 'ctx', pairs)  6.63 us
    all_to_all x1, starting transfers between devices, shards(): lax.all_to_all(dq, 'uly', split_axis=0, concat_axis=1, tiled=True)  5 us
  transfers between devices with their start and end apart: 17, of which 10 were waited for; matrix products, arithmetic and copies ran while one was open for 8% of the time, Pallas kernels for 26%

profile of v19, /device:TPU:0, one launch (start us, length us, event | category | flops | bytes accessed | tf_op | source)
XLA Modules:
  0.0 109.1 jit_solution(9976895039577395884)
XLA Ops:
  0.7 1.1 constant_dynamic-slice_fusion
  1.8 3.0 %collective-permute-start.4 = (bf16[384,256]{1,0:T(8,128)(2,1)S(1)}, bf16[384,256]{1,0:T(8,128)(2,1)S(1)}, u32[]{:S(2)}, u32[]{:S(2)}) collective-permute-start(bf16[384,256]{1,0:T(8,128)(2,1)S(1)} %pad_maximum_fusion.4), channel_id=1, source_target_pairs={{0,8},{4,12},{8,16},{12,20},{16,24},{20,28},{24,0},{28,4},{1,9},{5... | collective-permute-start | bytes 589832 | tf_op jit(solution)/shard_map/ppermute | solution.py:149
  4.8 1.5 %collective-permute-start.5 = (bf16[384,256]{1,0:T(8,128)(2,1)S(1)}, bf16[384,256]{1,0:T(8,128)(2,1)S(1)}, u32[]{:S(2)}, u32[]{:S(2)}) collective-permute-start(bf16[384,256]{1,0:T(8,128)(2,1)S(1)} %pad_maximum_fusion.4), channel_id=1, source_target_pairs={{0,16},{4,20},{8,24},{12,28},{16,0},{20,4},{24,8},{28,12},{1,17},{... | collective-permute-start | bytes 589832 | tf_op jit(solution)/shard_map/ppermute | solution.py:149
  6.3 1.4 %collective-permute-start.6 = (bf16[384,256]{1,0:T(8,128)(2,1)S(1)}, bf16[384,256]{1,0:T(8,128)(2,1)S(1)}, u32[]{:S(2)}, u32[]{:S(2)}) collective-permute-start(bf16[384,256]{1,0:T(8,128)(2,1)S(1)} %pad_maximum_fusion.4), channel_id=1, source_target_pairs={{0,24},{4,28},{8,0},{12,4},{16,8},{20,12},{24,16},{28,20},{1,25},{... | collective-permute-start | bytes 589832 | tf_op jit(solution)/shard_map/ppermute | solution.py:149
  7.8 0.6 collective-permute-start
  9.2 2.3 %collective-permute-done.4 = bf16[384,256]{1,0:T(8,128)(2,1)S(1)} collective-permute-done((bf16[384,256]{1,0:T(8,128)(2,1)S(1)}, bf16[384,256]{1,0:T(8,128)(2,1)S(1)}, u32[]{:S(2)}, u32[]{:S(2)}) %collective-permute-start.4) | collective-permute-done | bytes 196640 | tf_op jit(solution)/shard_map/ppermute | solution.py:149
  11.5 2.0 %collective-permute-start.2 = (bf16[384,256]{1,0:T(8,128)(2,1)S(1)}, bf16[384,256]{1,0:T(8,128)(2,1)S(1)}, u32[]{:S(2)}, u32[]{:S(2)}) collective-permute-start(bf16[384,256]{1,0:T(8,128)(2,1)S(1)} %pad_maximum_fusion.3), channel_id=1, source_target_pairs={{0,24},{4,28},{8,0},{12,4},{16,8},{20,12},{24,16},{28,20},{1,25},{... | collective-permute-start | bytes 589832 | tf_op jit(solution)/shard_map/ppermute | solution.py:149
  13.5 2.3 %collective-permute-done.5 = bf16[384,256]{1,0:T(8,128)(2,1)S(1)} collective-permute-done((bf16[384,256]{1,0:T(8,128)(2,1)S(1)}, bf16[384,256]{1,0:T(8,128)(2,1)S(1)}, u32[]{:S(2)}, u32[]{:S(2)}) %collective-permute-start.5) | collective-permute-done | bytes 196640 | tf_op jit(solution)/shard_map/ppermute | solution.py:149
  17.1 2.8 %collective-permute-done = bf16[384,256]{1,0:T(8,128)(2,1)S(1)} collective-permute-done((bf16[384,256]{1,0:T(8,128)(2,1)S(1)}, bf16[384,256]{1,0:T(8,128)(2,1)S(1)}, u32[]{:S(2)}, u32[]{:S(2)}) %collective-permute-start) | collective-permute-done | bytes 196640 | tf_op jit(solution)/shard_map/ppermute | solution.py:149
  20.0 3.3 %collective-permute-done.1 = bf16[384,256]{1,0:T(8,128)(2,1)S(1)} collective-permute-done((bf16[384,256]{1,0:T(8,128)(2,1)S(1)}, bf16[384,256]{1,0:T(8,128)(2,1)S(1)}, u32[]{:S(2)}, u32[]{:S(2)}) %collective-permute-start.1) | collective-permute-done | bytes 196640 | tf_op jit(solution)/shard_map/ppermute | solution.py:149
  23.8 0.7 pad_add_fusion.tbl_ref
  24.5 14.1 %shard_map.76 = (bf16[384,1536]{1,0:T(8,128)(2,1)}, f32[384,256]{1,0:T(8,128)}, bf16[1536,256]{1,0:T(8,128)(2,1)}, bf16[1536,256]{1,0:T(8,128)(2,1)}) custom-call(s32[96]{0:T(128)} %pad_add_fusion.tbl_ref, bf16[384,1536]{1,0:T(8,128)(2,1)} %q_ref.3, bf16[384,1536]{1,0:T(8,128)(2,1)} %do_ref.3, bf16[1536,256]{1,0:T(8,128)(2,1)} %copy-done.3, ...), custom_call_target="tpu_custom_call" | custom-call | flops 3623878656 | bytes 5111808 | tf_op jit(solution)/shard_map/pallas_call | solution.py:176
  39.0 14.2 %shard_map.77 = (bf16[384,1536]{1,0:T(8,128)(2,1)}, f32[384,256]{1,0:T(8,128)}, bf16[1536,256]{1,0:T(8,128)(2,1)}, bf16[1536,256]{1,0:T(8,128)(2,1)}) custom-call(s32[96]{0:T(128)} %pad_add_fusion.tbl_ref, bf16[384,1536]{1,0:T(8,128)(2,1)} %q_ref.3, bf16[384,1536]{1,0:T(8,128)(2,1)} %do_ref.3, ...), custom_call_target="tpu_custom_call", output_to_operand_aliasing={{0}: (7, {})} | custom-call | flops 3623878656 | bytes 5111808 | tf_op jit(solution)/shard_map/pallas_call | solution.py:176
  53.5 0.7 copy-done.2
  54.3 0.8 fusion.10
  55.1 1.5 %collective-permute-start.10 = (bf16[384,256]{1,0:T(8,128)(2,1)}, bf16[384,256]{1,0:T(8,128)(2,1)S(1)}, u32[]{:S(2)}, u32[]{:S(2)}) collective-permute-start(bf16[384,256]{1,0:T(8,128)(2,1)} %get-tuple-element.36), channel_id=1, source_target_pairs={{0,24},{4,28},{8,0},{12,4},{16,8},{20,12},{24,16},{28,20},{1,25},{... | collective-permute-start | bytes 589832 | tf_op jit(solution)/shard_map/ppermute | solution.py:200
  56.6 1.6 %collective-permute-start.11 = (bf16[384,256]{1,0:T(8,128)(2,1)}, bf16[384,256]{1,0:T(8,128)(2,1)S(1)}, u32[]{:S(2)}, u32[]{:S(2)}) collective-permute-start(bf16[384,256]{1,0:T(8,128)(2,1)} %get-tuple-element.38), channel_id=1, source_target_pairs={{0,16},{4,20},{8,24},{12,28},{16,0},{20,4},{24,8},{28,12},{1,17},{... | collective-permute-start | bytes 589832 | tf_op jit(solution)/shard_map/ppermute | solution.py:200
  58.5 5.0 %all-to-all-start = ((bf16[4,96,1536]{2,1,0:T(8,128)(2,1)}), bf16[4,96,1536]{2,1,0:T(8,128)(2,1)S(1)}, u32[]{:S(2)}, u32[]{:S(2)}) async-start(bf16[4,96,1536]{2,1,0:T(8,128)(2,1)} %bitcast.27), calls=%async_computation | async-start | bytes 2359296 | tf_op jit(solution)/shard_map/all_to_all | solution.py:208
  63.7 0.8 fusion.11
  64.5 2.6 %collective-permute-start.13 = (bf16[384,256]{1,0:T(8,128)(2,1)}, bf16[384,256]{1,0:T(8,128)(2,1)S(1)}, u32[]{:S(2)}, u32[]{:S(2)}) collective-permute-start(bf16[384,256]{1,0:T(8,128)(2,1)} %get-tuple-element.39), channel_id=1, source_target_pairs={{0,24},{4,28},{8,0},{12,4},{16,8},{20,12},{24,16},{28,20},{1,25},{... | collective-permute-start | bytes 589832 | tf_op jit(solution)/shard_map/ppermute | solution.py:200
  67.2 0.5 collective-permute-start.14
  67.9 1.3 %add_convert_fusion.3 = bf16[384,256]{1,0:T(8,128)(2,1)S(1)} fusion(f32[384,256]{1,0:T(8,128)S(1)} %copy-done.5, bf16[384,256]{1,0:T(8,128)(2,1)} %collective-permute-done.12, bf16[384,256]{1,0:T(8,128)(2,1)S(1)} %collective-permute-done.11, bf16[384,256]{1,0:T(8,128)(2,1)S(1)} %collective-permute-done.10, bf16[1536,256]{1,0:T(8,128)(2,1)} %copy-done.2, ...), kind=kLoop, calls=%fused_computation.7 | loop fusion | flops 1081344 | bytes 1572864 | tf_op jit(solution)/shard_map/convert.8
  69.9 2.9 %collective-permute-done.13 = bf16[384,256]{1,0:T(8,128)(2,1)S(1)} collective-permute-done((bf16[384,256]{1,0:T(8,128)(2,1)}, bf16[384,256]{1,0:T(8,128)(2,1)S(1)}, u32[]{:S(2)}, u32[]{:S(2)}) %collective-permute-start.13) | collective-permute-done | bytes 196640 | tf_op jit(solution)/shard_map/ppermute | solution.py:200
  72.8 4.7 %collective-permute-done.14 = bf16[384,256]{1,0:T(8,128)(2,1)} collective-permute-done((bf16[384,256]{1,0:T(8,128)(2,1)}, bf16[384,256]{1,0:T(8,128)(2,1)}, u32[]{:S(2)}, u32[]{:S(2)}) %collective-permute-start.14) | collective-permute-done | bytes 196640 | tf_op jit(solution)/shard_map/ppermute | solution.py:200
  77.5 1.3 %add_convert_fusion.2 = bf16[384,256]{1,0:T(8,128)(2,1)S(1)} fusion(f32[384,256]{1,0:T(8,128)} %get-tuple-element.30, bf16[384,256]{1,0:T(8,128)(2,1)} %collective-permute-done.15, bf16[384,256]{1,0:T(8,128)(2,1)} %collective-permute-done.14, bf16[384,256]{1,0:T(8,128)(2,1)S(1)} %collective-permute-done.13, bf16[1536,256]{1,0:T(8,128)(2,1)S(1)} %collective-permute-done.8, ...), kind=kLoop, calls=%fused_computation.6 | loop fusion | flops 1081344 | bytes 1572864 | tf_op jit(solution)/shard_map/convert.7
  79.5 0.9 pad_maximum_fusion.2
  80.5 11.3 %all-to-all-done = bf16[4,96,1536]{2,1,0:T(8,128)(2,1)S(1)} async-done(((bf16[4,96,1536]{2,1,0:T(8,128)(2,1)}), bf16[4,96,1536]{2,1,0:T(8,128)(2,1)S(1)}, u32[]{:S(2)}, u32[]{:S(2)}) %all-to-all-start) | async-done | bytes 1179680 | tf_op jit(solution)/shard_map/all_to_all | solution.py:208
  91.8 1.1 %copy.38 = bf16[4,12,8,1536]{3,2,0,1:T(8,128)(2,1)} copy(bf16[4,12,8,1536]{3,2,1,0:T(8,128)(2,1)S(1)} %bitcast.22) | data formatting | bytes 2359296 | tf_op jit(solution)/shard_map/all_to_all | solution.py:208
  92.9 13.6 %all_to_all.35 = bf16[4,96,512]{2,1,0:T(8,128)(2,1)S(1)} all-to-all(bf16[4,96,512]{2,1,0:T(8,128)(2,1)S(1)} %bitcast.23), channel_id=1, replica_groups=mesh['ctx'=8,'uly'=4] {'uly'}, dimensions={0} | all-to-all | bytes 786432 | tf_op jit(solution)/shard_map/all_to_all | solution.py:210
  106.6 0.5 fusion.12
  107.4 0.7 copy.40
  108.4 0.7 copy.41
  (60 shorter events, 6.2 us)
Async XLA Ops:
  0.6 8.3 %copy-start.6 = (s32[24,8]{0,1:T(8,128)S(1)}, s32[24,8]{0,1:T(8,128)}, u32[]{:S(2)}) copy-start(s32[24,8]{0,1:T(8,128)} %param.9) | copy-start | bytes 2308
  1.8 9.7 %collective-permute-start.4 = (bf16[384,256]{1,0:T(8,128)(2,1)S(1)}, bf16[384,256]{1,0:T(8,128)(2,1)S(1)}, u32[]{:S(2)}, u32[]{:S(2)}) collective-permute-start(bf16[384,256]{1,0:T(8,128)(2,1)S(1)} %pad_maximum_fusion.4), channel_id=1, source_target_pairs={{0,8},{4,12},{8,16},{12,20},{16,24},{20,28},{24,0},{28,4},{1,9},{5... | collective-permute-start | bytes 589832 | tf_op jit(solution)/shard_map/ppermute | solution.py:149
  4.8 11.0 %collective-permute-start.5 = (bf16[384,256]{1,0:T(8,128)(2,1)S(1)}, bf16[384,256]{1,0:T(8,128)(2,1)S(1)}, u32[]{:S(2)}, u32[]{:S(2)}) collective-permute-start(bf16[384,256]{1,0:T(8,128)(2,1)S(1)} %pad_maximum_fusion.4), channel_id=1, source_target_pairs={{0,16},{4,20},{8,24},{12,28},{16,0},{20,4},{24,8},{28,12},{1,17},{... | collective-permute-start | bytes 589832 | tf_op jit(solution)/shard_map/ppermute | solution.py:149
  6.3 10.0 %collective-permute-start.6 = (bf16[384,256]{1,0:T(8,128)(2,1)S(1)}, bf16[384,256]{1,0:T(8,128)(2,1)S(1)}, u32[]{:S(2)}, u32[]{:S(2)}) collective-permute-start(bf16[384,256]{1,0:T(8,128)(2,1)S(1)} %pad_maximum_fusion.4), channel_id=1, source_target_pairs={{0,24},{4,28},{8,0},{12,4},{16,8},{20,12},{24,16},{28,20},{1,25},{... | collective-permute-start | bytes 589832 | tf_op jit(solution)/shard_map/ppermute | solution.py:149
  7.8 12.2 %collective-permute-start = (bf16[384,256]{1,0:T(8,128)(2,1)S(1)}, bf16[384,256]{1,0:T(8,128)(2,1)S(1)}, u32[]{:S(2)}, u32[]{:S(2)}) collective-permute-start(bf16[384,256]{1,0:T(8,128)(2,1)S(1)} %pad_maximum_fusion.3), channel_id=1, source_target_pairs={{0,8},{4,12},{8,16},{12,20},{16,24},{20,28},{24,0},{28,4},{1,9},{5... | collective-permute-start | bytes 589832 | tf_op jit(solution)/shard_map/ppermute | solution.py:149
  8.4 14.9 %collective-permute-start.1 = (bf16[384,256]{1,0:T(8,128)(2,1)S(1)}, bf16[384,256]{1,0:T(8,128)(2,1)S(1)}, u32[]{:S(2)}, u32[]{:S(2)}) collective-permute-start(bf16[384,256]{1,0:T(8,128)(2,1)S(1)} %pad_maximum_fusion.3), channel_id=1, source_target_pairs={{0,16},{4,20},{8,24},{12,28},{16,0},{20,4},{24,8},{28,12},{1,17},{... | collective-permute-start | bytes 589832 | tf_op jit(solution)/shard_map/ppermute | solution.py:149
  11.5 12.1 %collective-permute-start.2 = (bf16[384,256]{1,0:T(8,128)(2,1)S(1)}, bf16[384,256]{1,0:T(8,128)(2,1)S(1)}, u32[]{:S(2)}, u32[]{:S(2)}) collective-permute-start(bf16[384,256]{1,0:T(8,128)(2,1)S(1)} %pad_maximum_fusion.3), channel_id=1, source_target_pairs={{0,24},{4,28},{8,0},{12,4},{16,8},{20,12},{24,16},{28,20},{1,25},{... | collective-permute-start | bytes 589832 | tf_op jit(solution)/shard_map/ppermute | solution.py:149
  16.4 8.1 %copy-start.3 = (bf16[1536,256]{1,0:T(8,128)(2,1)}, bf16[1536,256]{1,0:T(8,128)(2,1)S(1)}, u32[]{:S(2)}) copy-start(bf16[1536,256]{1,0:T(8,128)(2,1)S(1)} %pad_maximum_fusion.1.k_ref.v_ref) | copy-start | bytes 2359300
  16.4 8.1 %collective-permute-start.7 = (bf16[1536,256]{1,0:T(8,128)(2,1)S(1)}, bf16[1536,256]{1,0:T(8,128)(2,1)}, u32[]{:S(2)}, u32[]{:S(2)}) collective-permute-start(bf16[1536,256]{1,0:T(8,128)(2,1)S(1)} %pad_maximum_fusion.1.k_ref.v_ref), channel_id=1, source_target_pairs={{0,4},{4,0},{8,12},{12,8},{16,20},{20,16},{24,28},{28,24},{1,5},{5... | collective-permute-start | bytes 2359304 | tf_op jit(solution)/shard_map/ppermute | solution.py:151
  23.7 14.8 %copy-start.4 = (bf16[1536,256]{1,0:T(8,128)(2,1)}, bf16[1536,256]{1,0:T(8,128)(2,1)S(1)}, u32[]{:S(2)}) copy-start(bf16[1536,256]{1,0:T(8,128)(2,1)S(1)} %pad_maximum_fusion.k_ref.v_ref) | copy-start | bytes 2359300
  23.7 15.3 %collective-permute-start.3 = (bf16[1536,256]{1,0:T(8,128)(2,1)S(1)}, bf16[1536,256]{1,0:T(8,128)(2,1)}, u32[]{:S(2)}, u32[]{:S(2)}) collective-permute-start(bf16[1536,256]{1,0:T(8,128)(2,1)S(1)} %pad_maximum_fusion.k_ref.v_ref), channel_id=1, source_target_pairs={{0,4},{4,0},{8,12},{12,8},{16,20},{20,16},{24,28},{28,24},{1,5},{5... | collective-permute-start | bytes 2359304 | tf_op jit(solution)/shard_map/ppermute | solution.py:151
  38.5 14.8 %collective-permute-start.9 = (bf16[1536,256]{1,0:T(8,128)(2,1)}, bf16[1536,256]{1,0:T(8,128)(2,1)S(1)}, u32[]{:S(2)}, u32[]{:S(2)}) collective-permute-start(bf16[1536,256]{1,0:T(8,128)(2,1)} %get-tuple-element.26), channel_id=1, source_target_pairs={{0,4},{4,0},{8,12},{12,8},{16,20},{20,16},{24,28},{28,24},{1,5},{5... | collective-permute-start | bytes 2359304 | tf_op jit(solution)/shard_map/ppermute | solution.py:193
  39.0 14.3 %copy-start.1 = (bf16[1536,256]{1,0:T(8,128)(2,1)S(1)}, bf16[1536,256]{1,0:T(8,128)(2,1)}, u32[]{:S(2)}) copy-start(bf16[1536,256]{1,0:T(8,128)(2,1)} %get-tuple-element.25) | copy-start | bytes 2359300
  53.2 5.3 %collective-permute-start.8 = (bf16[1536,256]{1,0:T(8,128)(2,1)}, bf16[1536,256]{1,0:T(8,128)(2,1)S(1)}, u32[]{:S(2)}, u32[]{:S(2)}) collective-permute-start(bf16[1536,256]{1,0:T(8,128)(2,1)} %get-tuple-element.23), channel_id=1, source_target_pairs={{0,4},{4,0},{8,12},{12,8},{16,20},{20,16},{24,28},{28,24},{1,5},{5... | collective-permute-start | bytes 2359304 | tf_op jit(solution)/shard_map/ppermute | solution.py:193
  53.3 0.9 copy-start.2
  55.1 12.6 %collective-permute-start.10 = (bf16[384,256]{1,0:T(8,128)(2,1)}, bf16[384,256]{1,0:T(8,128)(2,1)S(1)}, u32[]{:S(2)}, u32[]{:S(2)}) collective-permute-start(bf16[384,256]{1,0:T(8,128)(2,1)} %get-tuple-element.36), channel_id=1, source_target_pairs={{0,24},{4,28},{8,0},{12,4},{16,8},{20,12},{24,16},{28,20},{1,25},{... | collective-permute-start | bytes 589832 | tf_op jit(solution)/shard_map/ppermute | solution.py:200
  56.6 11.4 %collective-permute-start.11 = (bf16[384,256]{1,0:T(8,128)(2,1)}, bf16[384,256]{1,0:T(8,128)(2,1)S(1)}, u32[]{:S(2)}, u32[]{:S(2)}) collective-permute-start(bf16[384,256]{1,0:T(8,128)(2,1)} %get-tuple-element.38), channel_id=1, source_target_pairs={{0,16},{4,20},{8,24},{12,28},{16,0},{20,4},{24,8},{28,12},{1,17},{... | collective-permute-start | bytes 589832 | tf_op jit(solution)/shard_map/ppermute | solution.py:200
  58.2 9.7 %collective-permute-start.12 = (bf16[384,256]{1,0:T(8,128)(2,1)S(1)}, bf16[384,256]{1,0:T(8,128)(2,1)}, u32[]{:S(2)}, u32[]{:S(2)}) collective-permute-start(bf16[384,256]{1,0:T(8,128)(2,1)S(1)} %get-tuple-element.37), channel_id=1, source_target_pairs={{0,8},{4,12},{8,16},{12,20},{16,24},{20,28},{24,0},{28,4},{1,9},{5... | collective-permute-start | bytes 589832 | tf_op jit(solution)/shard_map/ppermute | solution.py:200
  58.5 5.0 %copy-start = (bf16[1536,256]{1,0:T(8,128)(2,1)S(1)}, bf16[1536,256]{1,0:T(8,128)(2,1)}, u32[]{:S(2)}) copy-start(bf16[1536,256]{1,0:T(8,128)(2,1)} %get-tuple-element.28) | copy-start | bytes 2359300
  58.5 33.3 %all-to-all-start = ((bf16[4,96,1536]{2,1,0:T(8,128)(2,1)}), bf16[4,96,1536]{2,1,0:T(8,128)(2,1)S(1)}, u32[]{:S(2)}, u32[]{:S(2)}) async-start(bf16[4,96,1536]{2,1,0:T(8,128)(2,1)} %bitcast.27), calls=%async_computation | async-start | bytes 2359296 | tf_op jit(solution)/shard_map/all_to_all | solution.py:208
  63.7 4.2 %copy-start.5 = (f32[384,256]{1,0:T(8,128)S(1)}, f32[384,256]{1,0:T(8,128)}, u32[]{:S(2)}) copy-start(f32[384,256]{1,0:T(8,128)} %get-tuple-element.27) | copy-start | bytes 1179652
  64.5 8.3 %collective-permute-start.13 = (bf16[384,256]{1,0:T(8,128)(2,1)}, bf16[384,256]{1,0:T(8,128)(2,1)S(1)}, u32[]{:S(2)}, u32[]{:S(2)}) collective-permute-start(bf16[384,256]{1,0:T(8,128)(2,1)} %get-tuple-element.39), channel_id=1, source_target_pairs={{0,24},{4,28},{8,0},{12,4},{16,8},{20,12},{24,16},{28,20},{1,25},{... | collective-permute-start | bytes 589832 | tf_op jit(solution)/shard_map/ppermute | solution.py:200
  67.2 10.4 %collective-permute-start.14 = (bf16[384,256]{1,0:T(8,128)(2,1)}, bf16[384,256]{1,0:T(8,128)(2,1)}, u32[]{:S(2)}, u32[]{:S(2)}) collective-permute-start(bf16[384,256]{1,0:T(8,128)(2,1)} %get-tuple-element.41), channel_id=1, source_target_pairs={{0,16},{4,20},{8,24},{12,28},{16,0},{20,4},{24,8},{28,12},{1,17},{... | collective-permute-start | bytes 589832 | tf_op jit(solution)/shard_map/ppermute | solution.py:200
  67.7 9.9 %collective-permute-start.15 = (bf16[384,256]{1,0:T(8,128)(2,1)}, bf16[384,256]{1,0:T(8,128)(2,1)}, u32[]{:S(2)}, u32[]{:S(2)}) collective-permute-start(bf16[384,256]{1,0:T(8,128)(2,1)} %get-tuple-element.40), channel_id=1, source_target_pairs={{0,8},{4,12},{8,16},{12,20},{16,24},{20,28},{24,0},{28,4},{1,9},{5... | collective-permute-start | bytes 589832 | tf_op jit(solution)/shard_map/ppermute | solution.py:200

commit v20 on v17

--- a/solution.py
+++ b/solution.py
@@ -126,7 +126,7 @@
     remote = jnp.logical_not(local) & jnp.logical_not(is_global)
     kind = jnp.where(local, 2, jnp.where(remote, 0, 1)).astype(jnp.int32).reshape(-1)
     owner_side = (owner % 2 != core).astype(jnp.int32)
-    half_row = ((member - owner // 2) % members) * nb + rows % nb
+    half_row = jnp.bitwise_xor(member, owner // 2) * nb + rows % nb
     dst = jnp.where(local, rows - shard_index * nb, half_row).astype(jnp.int32).reshape(-1)
     blk = half_row.astype(jnp.int32).reshape(-1)
     side = owner_side.reshape(-1)
@@ -146,7 +146,7 @@
         )
         gathered = [kv_own]
         for d in range(1, members):
-            pairs = [(i, (i + 2 * d) % shard_count) for i in range(shard_count)]
+            pairs = [(i, i ^ (2 * d)) for i in range(shard_count)]
             gathered.append(lax.ppermute(kv_own, "ctx", pairs))
         kv_half = jnp.concatenate(gathered, axis=0)
         kv_other = lax.ppermute(kv_half, "ctx", partner)
@@ -196,7 +196,7 @@
         mine = (far.astype(jnp.float32) + from_partner.astype(jnp.float32)).astype(jnp.bfloat16)
         total = far[0:span].astype(jnp.float32) + from_partner[0:span].astype(jnp.float32)
         for d in range(1, members):
-            pairs = [(i, (i - 2 * d) % shard_count) for i in range(shard_count)]
+            pairs = [(i, i ^ (2 * d)) for i in range(shard_count)]
             total = total + lax.ppermute(
                 mine[d * span:(d + 1) * span], "ctx", pairs
             ).astype(jnp.float32)

time: 107 us -> 107 us (level)
  starting transfers between devices: 20.6 us -> 24 us
  waiting for transfers between devices: 27.7 us -> 24.5 us
    ppermute x6, starting transfers between devices: 9.11 us -> 11.1 us  [shards(): gathered.append(lax.ppermute(kv_own, 'ctx', pairs))]
    ppermute x6, waiting for transfers between devices: 11.6 us -> 9.78 us  [shards(): gathered.append(lax.ppermute(kv_own, 'ctx', pairs))]
    ppermute x6, starting transfers between devices: 5.74 us -> 7.12 us  [shards(): lax.ppermute(mine[d * span:(d + 1) * span], 'ctx', pairs)]
    ppermute x6, waiting for transfers between devices: 13.2 us -> 11.9 us  [shards(): lax.ppermute(mine[d * span:(d + 1) * span], 'ctx', pairs)]
  transfers between devices with their start and end apart: 17 -> 17, of which waited for: 11 -> 8; matrix products, arithmetic and copies ran while one was open for 10% -> 9% of each run, Pallas kernels for 27% -> 26%
where the time goes in v20:
time: 107 us; the launch traced here: 106 us
  Pallas kernels  28.2 us (26%)
  waiting for transfers between devices  24.5 us (23%)
  starting transfers between devices  24 us (22%)
  blocking collectives  13.8 us (13%)
  local copies, waits for them, and re-layouts  9.02 us (8%)
  other arithmetic  6.01 us (6%)
    pallas_call x2, Pallas kernels, shards(): pl.pallas_call(kernel, grid_spec=grid_spec, out_shape=[jax.ShapeDtypeStru...  28.2 us
    all_to_all x1, blocking collectives, shards(): lax.all_to_all(kv_grad, 'uly', split_axis=0, concat_axis=1, tiled=True)  13.8 us
    ppermute x6, waiting for transfers between devices, shards(): lax.ppermute(mine[d * span:(d + 1) * span], 'ctx', pairs)  11.9 us
    ppermute x6, starting transfers between devices, shards(): gathered.append(lax.ppermute(kv_own, 'ctx', pairs))  11.1 us
    ppermute x6, waiting for transfers between devices, shards(): gathered.append(lax.ppermute(kv_own, 'ctx', pairs))  9.78 us
    ppermute x6, starting transfers between devices, shards(): lax.ppermute(mine[d * span:(d + 1) * span], 'ctx', pairs)  7.12 us
    all_to_all x1, starting transfers between devices, shards(): lax.all_to_all(dq, 'uly', split_axis=0, concat_axis=1, tiled=True)  5.01 us
    all_to_all x1, waiting for transfers between devices, shards(): lax.all_to_all(dq, 'uly', split_axis=0, concat_axis=1, tiled=True)  2.78 us
  transfers between devices with their start and end apart: 17, of which 8 were waited for; matrix products, arithmetic and copies ran while one was open for 9% of the time, Pallas kernels for 26%

profile of v20, /device:TPU:0, one launch (start us, length us, event | category | flops | bytes accessed | tf_op | source)
XLA Modules:
  0.0 106.4 jit_solution(15607249232247553288)
XLA Ops:
  0.7 1.1 %constant_dynamic-slice_fusion = (bf16[384,128]{1,0:T(8,128)(2,1)S(1)}, bf16[384,128]{1,0:T(8,128)(2,1)S(1)}, bf16[384,128]{1,0:T(8,128)(2,1)S(1)}, bf16[384,128]{1,0:T(8,128)(2,1)S(1)}) fusion(bf16[384,1024]{1,0:T(8,128)(2,1)} %param.7, s32[]{:T(128)S(6)} %select_n.66, s32[]{:T(128)S(6)} %select_n.65, bf16[384,1024]{1,0:T(8,128)(2,1)} %param.6), kind=kLoop, calls=%fused_computation.32 | loop fusion | bytes 786440 | tf_op jit(solution)/shard_map/dynamic_slice | solution.py:143
  1.8 3.0 %collective-permute-start.4 = (bf16[384,256]{1,0:T(8,128)(2,1)S(1)}, bf16[384,256]{1,0:T(8,128)(2,1)S(1)}, u32[]{:S(2)}, u32[]{:S(2)}) collective-permute-start(bf16[384,256]{1,0:T(8,128)(2,1)S(1)} %pad_maximum_fusion.4), channel_id=1, source_target_pairs={{0,8},{4,12},{8,0},{12,4},{16,24},{20,28},{24,16},{28,20},{1,9},{5... | collective-permute-start | bytes 589832 | tf_op jit(solution)/shard_map/ppermute | solution.py:150
  4.8 1.5 %collective-permute-start.5 = (bf16[384,256]{1,0:T(8,128)(2,1)S(1)}, bf16[384,256]{1,0:T(8,128)(2,1)S(1)}, u32[]{:S(2)}, u32[]{:S(2)}) collective-permute-start(bf16[384,256]{1,0:T(8,128)(2,1)S(1)} %pad_maximum_fusion.4), channel_id=1, source_target_pairs={{0,16},{4,20},{8,24},{12,28},{16,0},{20,4},{24,8},{28,12},{1,17},{... | collective-permute-start | bytes 589832 | tf_op jit(solution)/shard_map/ppermute | solution.py:150
  6.4 2.0 %collective-permute-start = (bf16[384,256]{1,0:T(8,128)(2,1)S(1)}, bf16[384,256]{1,0:T(8,128)(2,1)S(1)}, u32[]{:S(2)}, u32[]{:S(2)}) collective-permute-start(bf16[384,256]{1,0:T(8,128)(2,1)S(1)} %pad_maximum_fusion.3), channel_id=1, source_target_pairs={{0,8},{4,12},{8,0},{12,4},{16,24},{20,28},{24,16},{28,20},{1,9},{5... | collective-permute-start | bytes 589832 | tf_op jit(solution)/shard_map/ppermute | solution.py:150
  8.4 1.5 %collective-permute-start.1 = (bf16[384,256]{1,0:T(8,128)(2,1)S(1)}, bf16[384,256]{1,0:T(8,128)(2,1)S(1)}, u32[]{:S(2)}, u32[]{:S(2)}) collective-permute-start(bf16[384,256]{1,0:T(8,128)(2,1)S(1)} %pad_maximum_fusion.3), channel_id=1, source_target_pairs={{0,16},{4,20},{8,24},{12,28},{16,0},{20,4},{24,8},{28,12},{1,17},{... | collective-permute-start | bytes 589832 | tf_op jit(solution)/shard_map/ppermute | solution.py:150
  10.5 3.0 %collective-permute-start.2 = (bf16[384,256]{1,0:T(8,128)(2,1)S(1)}, bf16[384,256]{1,0:T(8,128)(2,1)S(1)}, u32[]{:S(2)}, u32[]{:S(2)}) collective-permute-start(bf16[384,256]{1,0:T(8,128)(2,1)S(1)} %pad_maximum_fusion.3), channel_id=1, source_target_pairs={{0,24},{4,28},{8,16},{12,20},{16,8},{20,12},{24,0},{28,4},{1,25},{... | collective-permute-start | bytes 589832 | tf_op jit(solution)/shard_map/ppermute | solution.py:150
  13.5 3.3 %collective-permute-done.5 = bf16[384,256]{1,0:T(8,128)(2,1)S(1)} collective-permute-done((bf16[384,256]{1,0:T(8,128)(2,1)S(1)}, bf16[384,256]{1,0:T(8,128)(2,1)S(1)}, u32[]{:S(2)}, u32[]{:S(2)}) %collective-permute-start.5) | collective-permute-done | bytes 196640 | tf_op jit(solution)/shard_map/ppermute | solution.py:150
  17.7 1.3 %collective-permute-done = bf16[384,256]{1,0:T(8,128)(2,1)S(1)} collective-permute-done((bf16[384,256]{1,0:T(8,128)(2,1)S(1)}, bf16[384,256]{1,0:T(8,128)(2,1)S(1)}, u32[]{:S(2)}, u32[]{:S(2)}) %collective-permute-start) | collective-permute-done | bytes 196640 | tf_op jit(solution)/shard_map/ppermute | solution.py:150
  19.0 4.8 %collective-permute-done.1 = bf16[384,256]{1,0:T(8,128)(2,1)S(1)} collective-permute-done((bf16[384,256]{1,0:T(8,128)(2,1)S(1)}, bf16[384,256]{1,0:T(8,128)(2,1)S(1)}, u32[]{:S(2)}, u32[]{:S(2)}) %collective-permute-start.1) | collective-permute-done | bytes 196640 | tf_op jit(solution)/shard_map/ppermute | solution.py:150
  24.6 1.2 %broadcast_in_dim.10.dq_in = bf16[384,1536]{1,0:T(8,128)(2,1)} broadcast(bf16[]{:T(256)} %constant.83.clone.1), dimensions={} | broadcast | bytes 1179650 | tf_op jit(solution)/shard_map/broadcast_in_dim | solution.py:136
  25.9 14.1 %shard_map.76 = (bf16[384,1536]{1,0:T(8,128)(2,1)}, f32[384,256]{1,0:T(8,128)}, bf16[1536,256]{1,0:T(8,128)(2,1)}, bf16[1536,256]{1,0:T(8,128)(2,1)}) custom-call(s32[96]{0:T(128)} %pad_add_fusion.tbl_ref, bf16[384,1536]{1,0:T(8,128)(2,1)} %q_ref.3, bf16[384,1536]{1,0:T(8,128)(2,1)} %do_ref.3, ...), custom_call_target="tpu_custom_call", output_to_operand_aliasing={{0}: (7, {})} | custom-call | flops 3623878656 | bytes 5111808 | tf_op jit(solution)/shard_map/pallas_call | solution.py:178
  40.5 14.1 %shard_map.77 = (bf16[384,1536]{1,0:T(8,128)(2,1)}, f32[384,256]{1,0:T(8,128)}, bf16[1536,256]{1,0:T(8,128)(2,1)}, bf16[1536,256]{1,0:T(8,128)(2,1)}) custom-call(s32[96]{0:T(128)} %pad_add_fusion.tbl_ref, bf16[384,1536]{1,0:T(8,128)(2,1)} %q_ref.3, bf16[384,1536]{1,0:T(8,128)(2,1)} %do_ref.3, ...), custom_call_target="tpu_custom_call", output_to_operand_aliasing={{0}: (7, {})} | custom-call | flops 3623878656 | bytes 5111808 | tf_op jit(solution)/shard_map/pallas_call | solution.py:178
  54.7 5.0 %all-to-all-start = ((bf16[4,96,1536]{2,1,0:T(8,128)(2,1)}), bf16[4,96,1536]{2,1,0:T(8,128)(2,1)S(1)}, u32[]{:S(2)}, u32[]{:S(2)}) async-start(bf16[4,96,1536]{2,1,0:T(8,128)(2,1)} %bitcast.23), calls=%async_computation | async-start | bytes 2359296 | tf_op jit(solution)/shard_map/all_to_all | solution.py:208
  59.7 1.3 %add_convert_fusion.1 = bf16[1536,256]{1,0:T(8,128)(2,1)S(1)} fusion(bf16[1536,256]{1,0:T(8,128)(2,1)} %collective-permute-done.8, bf16[1536,256]{1,0:T(8,128)(2,1)S(1)} %copy-done.1), kind=kLoop, calls=%fused_computation.1 | loop fusion | flops 1572864 | bytes 2359296 | tf_op jit(solution)/shard_map/convert_element_type | solution.py:196
  61.1 1.6 %collective-permute-start.10 = (bf16[384,256]{1,0:T(8,128)(2,1)S(1)}, bf16[384,256]{1,0:T(8,128)(2,1)S(1)}, u32[]{:S(2)}, u32[]{:S(2)}) collective-permute-start(bf16[384,256]{1,0:T(8,128)(2,1)S(1)} %get-tuple-element.34), channel_id=1, source_target_pairs={{0,16},{4,20},{8,24},{12,28},{16,0},{20,4},{24,8},{28,12},{1,17},{... | collective-permute-start | bytes 589832 | tf_op jit(solution)/shard_map/ppermute | solution.py:200
  62.7 1.2 %collective-permute-start.11 = (bf16[384,256]{1,0:T(8,128)(2,1)S(1)}, bf16[384,256]{1,0:T(8,128)(2,1)S(1)}, u32[]{:S(2)}, u32[]{:S(2)}) collective-permute-start(bf16[384,256]{1,0:T(8,128)(2,1)S(1)} %get-tuple-element.33), channel_id=1, source_target_pairs={{0,24},{4,28},{8,16},{12,20},{16,8},{20,12},{24,0},{28,4},{1,25},{... | collective-permute-start | bytes 589832 | tf_op jit(solution)/shard_map/ppermute | solution.py:200
  63.9 0.7 collective-permute-start.9
  64.9 0.8 fusion.10
  65.7 1.3 %collective-permute-start.13 = (bf16[384,256]{1,0:T(8,128)(2,1)}, bf16[384,256]{1,0:T(8,128)(2,1)S(1)}, u32[]{:S(2)}, u32[]{:S(2)}) collective-permute-start(bf16[384,256]{1,0:T(8,128)(2,1)} %get-tuple-element.35), channel_id=1, source_target_pairs={{0,8},{4,12},{8,0},{12,4},{16,24},{20,28},{24,16},{28,20},{1,9},{5... | collective-permute-start | bytes 589832 | tf_op jit(solution)/shard_map/ppermute | solution.py:200
  67.0 0.8 collective-permute-start.14
  67.8 5.4 %collective-permute-done.10 = bf16[384,256]{1,0:T(8,128)(2,1)S(1)} collective-permute-done((bf16[384,256]{1,0:T(8,128)(2,1)S(1)}, bf16[384,256]{1,0:T(8,128)(2,1)S(1)}, u32[]{:S(2)}, u32[]{:S(2)}) %collective-permute-start.10) | collective-permute-done | bytes 196640 | tf_op jit(solution)/shard_map/ppermute | solution.py:200
  73.1 1.5 %collective-permute-start.15 = (bf16[384,256]{1,0:T(8,128)(2,1)}, bf16[384,256]{1,0:T(8,128)(2,1)}, u32[]{:S(2)}, u32[]{:S(2)}) collective-permute-start(bf16[384,256]{1,0:T(8,128)(2,1)} %get-tuple-element.36), channel_id=1, source_target_pairs={{0,24},{4,28},{8,16},{12,20},{16,8},{20,12},{24,0},{28,4},{1,25},{... | collective-permute-start | bytes 589832 | tf_op jit(solution)/shard_map/ppermute | solution.py:200
  74.6 1.2 %add_convert_fusion.3 = bf16[384,256]{1,0:T(8,128)(2,1)S(1)} fusion(f32[384,256]{1,0:T(8,128)S(1)} %copy-done.4, bf16[384,256]{1,0:T(8,128)(2,1)S(1)} %collective-permute-done.11, bf16[384,256]{1,0:T(8,128)(2,1)S(1)} %collective-permute-done.10, bf16[384,256]{1,0:T(8,128)(2,1)S(1)} %collective-permute-done.9, bf16[1536,256]{1,0:T(8,128)(2,1)} %collective-permute-done.8, ...), kind=kLoop, calls=%fused_computation.7 | loop fusion | flops 1081344 | bytes 1572864 | tf_op jit(solution)/shard_map/convert.8
  76.5 2.3 %collective-permute-done.13 = bf16[384,256]{1,0:T(8,128)(2,1)S(1)} collective-permute-done((bf16[384,256]{1,0:T(8,128)(2,1)}, bf16[384,256]{1,0:T(8,128)(2,1)S(1)}, u32[]{:S(2)}, u32[]{:S(2)}) %collective-permute-start.13) | collective-permute-done | bytes 196640 | tf_op jit(solution)/shard_map/ppermute | solution.py:200
  78.9 4.2 %collective-permute-done.15 = bf16[384,256]{1,0:T(8,128)(2,1)} collective-permute-done((bf16[384,256]{1,0:T(8,128)(2,1)}, bf16[384,256]{1,0:T(8,128)(2,1)}, u32[]{:S(2)}, u32[]{:S(2)}) %collective-permute-start.15) | collective-permute-done | bytes 196640 | tf_op jit(solution)/shard_map/ppermute | solution.py:200
  83.1 1.3 %add_convert_fusion.2 = bf16[384,256]{1,0:T(8,128)(2,1)S(1)} fusion(f32[384,256]{1,0:T(8,128)} %get-tuple-element.26, bf16[384,256]{1,0:T(8,128)(2,1)} %collective-permute-done.15, bf16[384,256]{1,0:T(8,128)(2,1)} %collective-permute-done.14, bf16[384,256]{1,0:T(8,128)(2,1)S(1)} %collective-permute-done.13, bf16[1536,256]{1,0:T(8,128)(2,1)S(1)} %collective-permute-done.12, ...), kind=kLoop, calls=%fused_computation.6 | loop fusion | flops 1081344 | bytes 1572864 | tf_op jit(solution)/shard_map/convert.7
  85.1 0.9 pad_maximum_fusion.2
  86.1 2.8 %all-to-all-done = bf16[4,96,1536]{2,1,0:T(8,128)(2,1)S(1)} async-done(((bf16[4,96,1536]{2,1,0:T(8,128)(2,1)}), bf16[4,96,1536]{2,1,0:T(8,128)(2,1)S(1)}, u32[]{:S(2)}, u32[]{:S(2)}) %all-to-all-start) | async-done | bytes 1179680 | tf_op jit(solution)/shard_map/all_to_all | solution.py:208
  88.8 1.1 %copy.39 = bf16[4,12,8,1536]{3,2,0,1:T(8,128)(2,1)} copy(bf16[4,12,8,1536]{3,2,1,0:T(8,128)(2,1)S(1)} %bitcast.22) | data formatting | bytes 2359296 | tf_op jit(solution)/shard_map/all_to_all | solution.py:208
  90.0 13.8 %all_to_all.35 = bf16[4,96,512]{2,1,0:T(8,128)(2,1)S(1)} all-to-all(bf16[4,96,512]{2,1,0:T(8,128)(2,1)S(1)} %bitcast.24), channel_id=1, replica_groups=mesh['ctx'=8,'uly'=4] {'uly'}, dimensions={0} | all-to-all | bytes 786432 | tf_op jit(solution)/shard_map/all_to_all | solution.py:210
  104.7 0.7 copy.41
  105.7 0.7 copy.42
  (61 shorter events, 5.9 us)
Async XLA Ops:
  0.6 9.3 %copy-start.5 = (s32[24,8]{0,1:T(8,128)S(1)}, s32[24,8]{0,1:T(8,128)}, u32[]{:S(2)}) copy-start(s32[24,8]{0,1:T(8,128)} %param.9) | copy-start | bytes 2308
  1.8 8.7 %collective-permute-start.4 = (bf16[384,256]{1,0:T(8,128)(2,1)S(1)}, bf16[384,256]{1,0:T(8,128)(2,1)S(1)}, u32[]{:S(2)}, u32[]{:S(2)}) collective-permute-start(bf16[384,256]{1,0:T(8,128)(2,1)S(1)} %pad_maximum_fusion.4), channel_id=1, source_target_pairs={{0,8},{4,12},{8,0},{12,4},{16,24},{20,28},{24,16},{28,20},{1,9},{5... | collective-permute-start | bytes 589832 | tf_op jit(solution)/shard_map/ppermute | solution.py:150
  4.8 12.0 %collective-permute-start.5 = (bf16[384,256]{1,0:T(8,128)(2,1)S(1)}, bf16[384,256]{1,0:T(8,128)(2,1)S(1)}, u32[]{:S(2)}, u32[]{:S(2)}) collective-permute-start(bf16[384,256]{1,0:T(8,128)(2,1)S(1)} %pad_maximum_fusion.4), channel_id=1, source_target_pairs={{0,16},{4,20},{8,24},{12,28},{16,0},{20,4},{24,8},{28,12},{1,17},{... | collective-permute-start | bytes 589832 | tf_op jit(solution)/shard_map/ppermute | solution.py:150
  6.3 10.5 %collective-permute-start.6 = (bf16[384,256]{1,0:T(8,128)(2,1)S(1)}, bf16[384,256]{1,0:T(8,128)(2,1)S(1)}, u32[]{:S(2)}, u32[]{:S(2)}) collective-permute-start(bf16[384,256]{1,0:T(8,128)(2,1)S(1)} %pad_maximum_fusion.4), channel_id=1, source_target_pairs={{0,24},{4,28},{8,16},{12,20},{16,8},{20,12},{24,0},{28,4},{1,25},{... | collective-permute-start | bytes 589832 | tf_op jit(solution)/shard_map/ppermute | solution.py:150
  6.4 12.6 %collective-permute-start = (bf16[384,256]{1,0:T(8,128)(2,1)S(1)}, bf16[384,256]{1,0:T(8,128)(2,1)S(1)}, u32[]{:S(2)}, u32[]{:S(2)}) collective-permute-start(bf16[384,256]{1,0:T(8,128)(2,1)S(1)} %pad_maximum_fusion.3), channel_id=1, source_target_pairs={{0,8},{4,12},{8,0},{12,4},{16,24},{20,28},{24,16},{28,20},{1,9},{5... | collective-permute-start | bytes 589832 | tf_op jit(solution)/shard_map/ppermute | solution.py:150
  8.4 15.4 %collective-permute-start.1 = (bf16[384,256]{1,0:T(8,128)(2,1)S(1)}, bf16[384,256]{1,0:T(8,128)(2,1)S(1)}, u32[]{:S(2)}, u32[]{:S(2)}) collective-permute-start(bf16[384,256]{1,0:T(8,128)(2,1)S(1)} %pad_maximum_fusion.3), channel_id=1, source_target_pairs={{0,16},{4,20},{8,24},{12,28},{16,0},{20,4},{24,8},{28,12},{1,17},{... | collective-permute-start | bytes 589832 | tf_op jit(solution)/shard_map/ppermute | solution.py:150
  10.5 13.3 %collective-permute-start.2 = (bf16[384,256]{1,0:T(8,128)(2,1)S(1)}, bf16[384,256]{1,0:T(8,128)(2,1)S(1)}, u32[]{:S(2)}, u32[]{:S(2)}) collective-permute-start(bf16[384,256]{1,0:T(8,128)(2,1)S(1)} %pad_maximum_fusion.3), channel_id=1, source_target_pairs={{0,24},{4,28},{8,16},{12,20},{16,8},{20,12},{24,0},{28,4},{1,25},{... | collective-permute-start | bytes 589832 | tf_op jit(solution)/shard_map/ppermute | solution.py:150
  16.9 8.9 %copy-start.2 = (bf16[1536,256]{1,0:T(8,128)(2,1)}, bf16[1536,256]{1,0:T(8,128)(2,1)S(1)}, u32[]{:S(2)}) copy-start(bf16[1536,256]{1,0:T(8,128)(2,1)S(1)} %pad_maximum_fusion.1.k_ref.v_ref) | copy-start | bytes 2359300
  16.9 7.7 %collective-permute-start.7 = (bf16[1536,256]{1,0:T(8,128)(2,1)S(1)}, bf16[1536,256]{1,0:T(8,128)(2,1)S(1)}, u32[]{:S(2)}, u32[]{:S(2)}) collective-permute-start(bf16[1536,256]{1,0:T(8,128)(2,1)S(1)} %pad_maximum_fusion.1.k_ref.v_ref), channel_id=1, source_target_pairs={{0,4},{4,0},{8,12},{12,8},{16,20},{20,16},{24,28},{28,24},{1,5},{5... | collective-permute-start | bytes 2359304 | tf_op jit(solution)/shard_map/ppermute | solution.py:152
  23.9 16.1 %copy-start.3 = (bf16[1536,256]{1,0:T(8,128)(2,1)}, bf16[1536,256]{1,0:T(8,128)(2,1)S(1)}, u32[]{:S(2)}) copy-start(bf16[1536,256]{1,0:T(8,128)(2,1)S(1)} %pad_maximum_fusion.k_ref.v_ref) | copy-start | bytes 2359300
  23.9 16.6 %collective-permute-start.3 = (bf16[1536,256]{1,0:T(8,128)(2,1)S(1)}, bf16[1536,256]{1,0:T(8,128)(2,1)}, u32[]{:S(2)}, u32[]{:S(2)}) collective-permute-start(bf16[1536,256]{1,0:T(8,128)(2,1)S(1)} %pad_maximum_fusion.k_ref.v_ref), channel_id=1, source_target_pairs={{0,4},{4,0},{8,12},{12,8},{16,20},{20,16},{24,28},{28,24},{1,5},{5... | collective-permute-start | bytes 2359304 | tf_op jit(solution)/shard_map/ppermute | solution.py:152
  24.6 1.3 %copy-start.6 = (bf16[1536,256]{1,0:T(8,128)(2,1)}, bf16[1536,256]{1,0:T(8,128)(2,1)S(1)}, u32[]{:S(2)}) copy-start(bf16[1536,256]{1,0:T(8,128)(2,1)S(1)} %collective-permute-done.7.ko_ref.vo_ref) | copy-start | bytes 2359300
  40.0 19.7 %collective-permute-start.8 = (bf16[1536,256]{1,0:T(8,128)(2,1)}, bf16[1536,256]{1,0:T(8,128)(2,1)}, u32[]{:S(2)}, u32[]{:S(2)}) collective-permute-start(bf16[1536,256]{1,0:T(8,128)(2,1)} %get-tuple-element.22), channel_id=1, source_target_pairs={{0,4},{4,0},{8,12},{12,8},{16,20},{20,16},{24,28},{28,24},{1,5},{5... | collective-permute-start | bytes 2359304 | tf_op jit(solution)/shard_map/ppermute | solution.py:195
  54.6 10.1 %collective-permute-start.12 = (bf16[1536,256]{1,0:T(8,128)(2,1)}, bf16[1536,256]{1,0:T(8,128)(2,1)S(1)}, u32[]{:S(2)}, u32[]{:S(2)}) collective-permute-start(bf16[1536,256]{1,0:T(8,128)(2,1)} %get-tuple-element.25), channel_id=1, source_target_pairs={{0,4},{4,0},{8,12},{12,8},{16,20},{20,16},{24,28},{28,24},{1,5},{5... | collective-permute-start | bytes 2359304 | tf_op jit(solution)/shard_map/ppermute | solution.py:195
  54.7 5.0 %copy-start.1 = (bf16[1536,256]{1,0:T(8,128)(2,1)S(1)}, bf16[1536,256]{1,0:T(8,128)(2,1)}, u32[]{:S(2)}) copy-start(bf16[1536,256]{1,0:T(8,128)(2,1)} %get-tuple-element.21) | copy-start | bytes 2359300
  54.7 34.1 %all-to-all-start = ((bf16[4,96,1536]{2,1,0:T(8,128)(2,1)}), bf16[4,96,1536]{2,1,0:T(8,128)(2,1)S(1)}, u32[]{:S(2)}, u32[]{:S(2)}) async-start(bf16[4,96,1536]{2,1,0:T(8,128)(2,1)} %bitcast.23), calls=%async_computation | async-start | bytes 2359296 | tf_op jit(solution)/shard_map/all_to_all | solution.py:208
  61.0 3.6 %copy-start = (bf16[1536,256]{1,0:T(8,128)(2,1)S(1)}, bf16[1536,256]{1,0:T(8,128)(2,1)}, u32[]{:S(2)}) copy-start(bf16[1536,256]{1,0:T(8,128)(2,1)} %get-tuple-element.24) | copy-start | bytes 2359300
  61.1 12.0 %collective-permute-start.10 = (bf16[384,256]{1,0:T(8,128)(2,1)S(1)}, bf16[384,256]{1,0:T(8,128)(2,1)S(1)}, u32[]{:S(2)}, u32[]{:S(2)}) collective-permute-start(bf16[384,256]{1,0:T(8,128)(2,1)S(1)} %get-tuple-element.34), channel_id=1, source_target_pairs={{0,16},{4,20},{8,24},{12,28},{16,0},{20,4},{24,8},{28,12},{1,17},{... | collective-permute-start | bytes 589832 | tf_op jit(solution)/shard_map/ppermute | solution.py:200
  62.7 11.9 %collective-permute-start.11 = (bf16[384,256]{1,0:T(8,128)(2,1)S(1)}, bf16[384,256]{1,0:T(8,128)(2,1)S(1)}, u32[]{:S(2)}, u32[]{:S(2)}) collective-permute-start(bf16[384,256]{1,0:T(8,128)(2,1)S(1)} %get-tuple-element.33), channel_id=1, source_target_pairs={{0,24},{4,28},{8,16},{12,20},{16,8},{20,12},{24,0},{28,4},{1,25},{... | collective-permute-start | bytes 589832 | tf_op jit(solution)/shard_map/ppermute | solution.py:200
  63.9 10.7 %collective-permute-start.9 = (bf16[384,256]{1,0:T(8,128)(2,1)S(1)}, bf16[384,256]{1,0:T(8,128)(2,1)S(1)}, u32[]{:S(2)}, u32[]{:S(2)}) collective-permute-start(bf16[384,256]{1,0:T(8,128)(2,1)S(1)} %get-tuple-element.32), channel_id=1, source_target_pairs={{0,8},{4,12},{8,0},{12,4},{16,24},{20,28},{24,16},{28,20},{1,9},{5... | collective-permute-start | bytes 589832 | tf_op jit(solution)/shard_map/ppermute | solution.py:200
  64.9 9.8 %copy-start.4 = (f32[384,256]{1,0:T(8,128)S(1)}, f32[384,256]{1,0:T(8,128)}, u32[]{:S(2)}) copy-start(f32[384,256]{1,0:T(8,128)} %get-tuple-element.23) | copy-start | bytes 1179652
  65.7 13.1 %collective-permute-start.13 = (bf16[384,256]{1,0:T(8,128)(2,1)}, bf16[384,256]{1,0:T(8,128)(2,1)S(1)}, u32[]{:S(2)}, u32[]{:S(2)}) collective-permute-start(bf16[384,256]{1,0:T(8,128)(2,1)} %get-tuple-element.35), channel_id=1, source_target_pairs={{0,8},{4,12},{8,0},{12,4},{16,24},{20,28},{24,16},{28,20},{1,9},{5... | collective-permute-start | bytes 589832 | tf_op jit(solution)/shard_map/ppermute | solution.py:200
  67.0 11.9 %collective-permute-start.14 = (bf16[384,256]{1,0:T(8,128)(2,1)}, bf16[384,256]{1,0:T(8,128)(2,1)}, u32[]{:S(2)}, u32[]{:S(2)}) collective-permute-start(bf16[384,256]{1,0:T(8,128)(2,1)} %get-tuple-element.37), channel_id=1, source_target_pairs={{0,16},{4,20},{8,24},{12,28},{16,0},{20,4},{24,8},{28,12},{1,17},{... | collective-permute-start | bytes 589832 | tf_op jit(solution)/shard_map/ppermute | solution.py:200
  73.1 9.9 %collective-permute-start.15 = (bf16[384,256]{1,0:T(8,128)(2,1)}, bf16[384,256]{1,0:T(8,128)(2,1)}, u32[]{:S(2)}, u32[]{:S(2)}) collective-permute-start(bf16[384,256]{1,0:T(8,128)(2,1)} %get-tuple-element.36), channel_id=1, source_target_pairs={{0,24},{4,28},{8,16},{12,20},{16,8},{20,12},{24,0},{28,4},{1,25},{... | collective-permute-start | bytes 589832 | tf_op jit(solution)/shard_map/ppermute | solution.py:200

commit v21 on v17

--- a/solution.py
+++ b/solution.py
@@ -135,33 +135,30 @@
     kernel = functools.partial(attention_kernel, hpk=hpk, kv_here=1, nb=nb)
     dq = jnp.zeros((nb * BLK, heads_here * HD), jnp.bfloat16)
     sums = []
+    kv_own = jnp.concatenate(
+        [
+            lax.dynamic_slice_in_dim(key_rows, first_kv * HD, kv_here * HD, axis=1),
+            lax.dynamic_slice_in_dim(value_rows, first_kv * HD, kv_here * HD, axis=1),
+        ],
+        axis=1,
+    )
+    gathered = [kv_own]
+    for d in range(1, members):
+        pairs = [(i, (i + 2 * d) % shard_count) for i in range(shard_count)]
+        gathered.append(lax.ppermute(kv_own, "ctx", pairs))
+    kv_half = jnp.concatenate(gathered, axis=0)
+    kv_other = lax.ppermute(kv_half, "ctx", partner)
     for g in range(kv_here):
-        col = (first_kv + g) * HD
-        kv_own = jnp.concatenate(
-            [
-                lax.dynamic_slice_in_dim(key_rows, col, HD, axis=1),
-                lax.dynamic_slice_in_dim(value_rows, col, HD, axis=1),
-            ],
-            axis=1,
-        )
-        gathered = [kv_own]
-        for d in range(1, members):
-            pairs = [(i, (i + 2 * d) % shard_count) for i in range(shard_count)]
-            gathered.append(lax.ppermute(kv_own, "ctx", pairs))
-        kv_half = jnp.concatenate(gathered, axis=0)
-        kv_other = lax.ppermute(kv_half, "ctx", partner)
-        if g > 0:
-            kv_half, kv_other, dq = lax.optimization_barrier((kv_half, kv_other, dq))
         grid_spec = pltpu.PrefetchScalarGridSpec(
             num_scalar_prefetch=1,
             grid=(1, nb),
             in_specs=[
                 pl.BlockSpec((BLK, hpk * HD), lambda z, b, *_, g=g: (b, g)),
                 pl.BlockSpec((BLK, hpk * HD), lambda z, b, *_, g=g: (b, g)),
-                pl.BlockSpec((half, HD), lambda z, b, *_: (0, 0)),
-                pl.BlockSpec((half, HD), lambda z, b, *_: (0, 1)),
-                pl.BlockSpec((half, HD), lambda z, b, *_: (0, 0)),
-                pl.BlockSpec((half, HD), lambda z, b, *_: (0, 1)),
+                pl.BlockSpec((half, HD), lambda z, b, *_, g=g: (0, g)),
+                pl.BlockSpec((half, HD), lambda z, b, *_, g=g: (0, kv_here + g)),
+                pl.BlockSpec((half, HD), lambda z, b, *_, g=g: (0, g)),
+                pl.BlockSpec((half, HD), lambda z, b, *_, g=g: (0, kv_here + g)),
                 pl.BlockSpec(memory_space=pl.ANY),
             ],
             out_specs=[

time: 107 us -> 109 us (1.019)
  local copies, waits for them, and re-layouts: 9.02 us -> 11 us
    ppermute x6, waiting for transfers between devices: 13.2 us -> 7.59 us  [shards(): lax.ppermute(mine[d * span:(d + 1) * span], 'ctx', pairs)]
    ppermute x6 -> x3, waiting for transfers between devices: 11.6 us -> 15.8 us  [shards(): gathered.append(lax.ppermute(kv_own, 'ctx', pairs))]
    ppermute x6, starting transfers between devices: 5.74 us -> 9.34 us  [shards(): lax.ppermute(mine[d * span:(d + 1) * span], 'ctx', pairs)]
    ppermute x6 -> x3, starting transfers between devices: 9.11 us -> 5.94 us  [shards(): gathered.append(lax.ppermute(kv_own, 'ctx', pairs))]
    ppermute x2 -> x1, waiting for transfers between devices: 0.01 us -> 1.82 us  [shards(): kv_other = lax.ppermute(kv_half, 'ctx', partner)]
  transfers between devices with their start and end apart: 17 -> 13, of which waited for: 11 -> 7; matrix products, arithmetic and copies ran while one was open for 10% -> 10% of each run, Pallas kernels for 27% -> 13%
where the time goes in v21:
time: 109 us
  Pallas kernels  28.2 us (26%)
  waiting for transfers between devices  27.4 us (25%)
  starting transfers between devices  20.8 us (19%)
  blocking collectives  13.7 us (13%)
  local copies, waits for them, and re-layouts  11 us (10%)
  other arithmetic  6.62 us (6%)
    pallas_call x2, Pallas kernels, shards(): pl.pallas_call(kernel, grid_spec=grid_spec, out_shape=[jax.ShapeDtypeStru...  28.2 us
    ppermute x3, waiting for transfers between devices, shards(): gathered.append(lax.ppermute(kv_own, 'ctx', pairs))  15.8 us
    all_to_all x1, blocking collectives, shards(): lax.all_to_all(kv_grad, 'uly', split_axis=0, concat_axis=1, tiled=True)  13.7 us
    ppermute x6, starting transfers between devices, shards(): lax.ppermute(mine[d * span:(d + 1) * span], 'ctx', pairs)  9.34 us
    ppermute x6, waiting for transfers between devices, shards(): lax.ppermute(mine[d * span:(d + 1) * span], 'ctx', pairs)  7.59 us
    ppermute x3, starting transfers between devices, shards(): gathered.append(lax.ppermute(kv_own, 'ctx', pairs))  5.94 us
    all_to_all x1, starting transfers between devices, shards(): lax.all_to_all(dq, 'uly', split_axis=0, concat_axis=1, tiled=True)  4.87 us
    unnamed x21, local copies, waits for them, and re-layouts  3.37 us
  transfers between devices with their start and end apart: 13, of which 7 were waited for; matrix products, arithmetic and copies ran while one was open for 10% of the time, Pallas kernels for 13%

profile of v21, /device:TPU:0, one launch (start us, length us, event | category | flops | bytes accessed | tf_op | source)
XLA Modules:
  0.0 108.7 jit_solution(17226612635957611741)
XLA Ops:
  0.7 1.1 constant_dynamic-slice_fusion
  1.8 3.0 %collective-permute-start = (bf16[384,512]{1,0:T(8,128)(2,1)S(1)}, bf16[384,512]{1,0:T(8,128)(2,1)S(1)}, u32[]{:S(2)}, u32[]{:S(2)}) collective-permute-start(bf16[384,512]{1,0:T(8,128)(2,1)S(1)} %pad_maximum_fusion.1), channel_id=1, source_target_pairs={{0,8},{4,12},{8,16},{12,20},{16,24},{20,28},{24,0},{28,4},{1,9},{5... | collective-permute-start | bytes 1179656 | tf_op jit(solution)/shard_map/ppermute | solution.py:148
  4.8 1.5 %collective-permute-start.1 = (bf16[384,512]{1,0:T(8,128)(2,1)S(1)}, bf16[384,512]{1,0:T(8,128)(2,1)S(1)}, u32[]{:S(2)}, u32[]{:S(2)}) collective-permute-start(bf16[384,512]{1,0:T(8,128)(2,1)S(1)} %pad_maximum_fusion.1), channel_id=1, source_target_pairs={{0,16},{4,20},{8,24},{12,28},{16,0},{20,4},{24,8},{28,12},{1,17},{... | collective-permute-start | bytes 1179656 | tf_op jit(solution)/shard_map/ppermute | solution.py:148
  6.3 1.4 %collective-permute-start.2 = (bf16[384,512]{1,0:T(8,128)(2,1)S(1)}, bf16[384,512]{1,0:T(8,128)(2,1)S(1)}, u32[]{:S(2)}, u32[]{:S(2)}) collective-permute-start(bf16[384,512]{1,0:T(8,128)(2,1)S(1)} %pad_maximum_fusion.1), channel_id=1, source_target_pairs={{0,24},{4,28},{8,0},{12,4},{16,8},{20,12},{24,16},{28,20},{1,25},{... | collective-permute-start | bytes 1179656 | tf_op jit(solution)/shard_map/ppermute | solution.py:148
  7.7 8.0 %collective-permute-done = bf16[384,512]{1,0:T(8,128)(2,1)S(1)} collective-permute-done((bf16[384,512]{1,0:T(8,128)(2,1)S(1)}, bf16[384,512]{1,0:T(8,128)(2,1)S(1)}, u32[]{:S(2)}, u32[]{:S(2)}) %collective-permute-start) | collective-permute-done | bytes 393248 | tf_op jit(solution)/shard_map/ppermute | solution.py:148
  15.7 7.6 %collective-permute-done.1 = bf16[384,512]{1,0:T(8,128)(2,1)S(1)} collective-permute-done((bf16[384,512]{1,0:T(8,128)(2,1)S(1)}, bf16[384,512]{1,0:T(8,128)(2,1)S(1)}, u32[]{:S(2)}, u32[]{:S(2)}) %collective-permute-start.1) | collective-permute-done | bytes 393248 | tf_op jit(solution)/shard_map/ppermute | solution.py:148
  24.7 0.6 pad_add_fusion.tbl_ref
  25.3 1.8 %collective-permute-done.3.ko_ref.vo_ref = bf16[1536,512]{1,0:T(8,128)(2,1)S(1)} collective-permute-done((bf16[1536,512]{1,0:T(8,128)(2,1)S(1)}, bf16[1536,512]{1,0:T(8,128)(2,1)S(1)}, u32[]{:S(2)}, u32[]{:S(2)}) %collective-permute-start.3) | collective-permute-done | bytes 1572896 | tf_op jit(solution)/shard_map/ppermute | solution.py:150
  27.1 1.2 %broadcast_in_dim.10.dq_in = bf16[384,1536]{1,0:T(8,128)(2,1)} broadcast(bf16[]{:T(256)} %constant.92.clone.1), dimensions={} | broadcast | bytes 1179650 | tf_op jit(solution)/shard_map/broadcast_in_dim | solution.py:136
  28.6 14.1 %shard_map.76 = (bf16[384,1536]{1,0:T(8,128)(2,1)}, f32[384,256]{1,0:T(8,128)}, bf16[1536,256]{1,0:T(8,128)(2,1)}, bf16[1536,256]{1,0:T(8,128)(2,1)}) custom-call(s32[96]{0:T(128)} %pad_add_fusion.tbl_ref, bf16[384,1536]{1,0:T(8,128)(2,1)} %q_ref.3, bf16[384,1536]{1,0:T(8,128)(2,1)} %do_ref.3, ...), custom_call_target="tpu_custom_call", output_to_operand_aliasing={{0}: (7, {})} | custom-call | flops 3623878656 | bytes 5111808 | tf_op jit(solution)/shard_map/pallas_call | solution.py:175
  42.9 14.1 %shard_map.77 = (bf16[384,1536]{1,0:T(8,128)(2,1)}, f32[384,256]{1,0:T(8,128)}, bf16[1536,256]{1,0:T(8,128)(2,1)}, bf16[1536,256]{1,0:T(8,128)(2,1)}) custom-call(s32[96]{0:T(128)} %pad_add_fusion.tbl_ref, bf16[384,1536]{1,0:T(8,128)(2,1)} %q_ref.3, bf16[384,1536]{1,0:T(8,128)(2,1)} %do_ref.3, ...), custom_call_target="tpu_custom_call", output_to_operand_aliasing={{0}: (7, {})} | custom-call | flops 3623878656 | bytes 5111808 | tf_op jit(solution)/shard_map/pallas_call | solution.py:175
  57.0 0.4 collective-permute-start.8
  57.5 4.9 %all-to-all-start = ((bf16[4,96,1536]{2,1,0:T(8,128)(2,1)}), bf16[4,96,1536]{2,1,0:T(8,128)(2,1)S(1)}, u32[]{:S(2)}, u32[]{:S(2)}) async-start(bf16[4,96,1536]{2,1,0:T(8,128)(2,1)} %bitcast.23), calls=%async_computation | async-start | bytes 2359296 | tf_op jit(solution)/shard_map/all_to_all | solution.py:205
  62.4 0.9 copy-done.3
  63.2 1.4 %add_convert_fusion.1 = bf16[1536,256]{1,0:T(8,128)(2,1)S(1)} fusion(bf16[1536,256]{1,0:T(8,128)(2,1)} %copy-done.3, bf16[1536,256]{1,0:T(8,128)(2,1)S(1)} %copy-done.2), kind=kLoop, calls=%fused_computation.2 | loop fusion | flops 1572864 | bytes 2359296 | tf_op jit(solution)/shard_map/convert_element_type | solution.py:193
  64.7 1.7 %collective-permute-start.5 = (bf16[384,256]{1,0:T(8,128)(2,1)S(1)}, bf16[384,256]{1,0:T(8,128)(2,1)S(1)}, u32[]{:S(2)}, u32[]{:S(2)}) collective-permute-start(bf16[384,256]{1,0:T(8,128)(2,1)S(1)} %get-tuple-element.26), channel_id=1, source_target_pairs={{0,24},{4,28},{8,0},{12,4},{16,8},{20,12},{24,16},{28,20},{1,25},{... | collective-permute-start | bytes 589832 | tf_op jit(solution)/shard_map/ppermute | solution.py:197
  66.4 1.5 %collective-permute-start.6 = (bf16[384,256]{1,0:T(8,128)(2,1)S(1)}, bf16[384,256]{1,0:T(8,128)(2,1)S(1)}, u32[]{:S(2)}, u32[]{:S(2)}) collective-permute-start(bf16[384,256]{1,0:T(8,128)(2,1)S(1)} %get-tuple-element.28), channel_id=1, source_target_pairs={{0,16},{4,20},{8,24},{12,28},{16,0},{20,4},{24,8},{28,12},{1,17},{... | collective-permute-start | bytes 589832 | tf_op jit(solution)/shard_map/ppermute | solution.py:197
  68.4 0.8 fusion.11
  69.3 0.6 collective-permute-start.10
  69.8 2.6 %collective-permute-start.11 = (bf16[384,256]{1,0:T(8,128)(2,1)}, bf16[384,256]{1,0:T(8,128)(2,1)}, u32[]{:S(2)}, u32[]{:S(2)}) collective-permute-start(bf16[384,256]{1,0:T(8,128)(2,1)} %get-tuple-element.30), channel_id=1, source_target_pairs={{0,8},{4,12},{8,16},{12,20},{16,24},{20,28},{24,0},{28,4},{1,9},{5... | collective-permute-start | bytes 589832 | tf_op jit(solution)/shard_map/ppermute | solution.py:197
  72.5 2.6 %collective-permute-start.9 = (bf16[384,256]{1,0:T(8,128)(2,1)}, bf16[384,256]{1,0:T(8,128)(2,1)}, u32[]{:S(2)}, u32[]{:S(2)}) collective-permute-start(bf16[384,256]{1,0:T(8,128)(2,1)} %get-tuple-element.29), channel_id=1, source_target_pairs={{0,24},{4,28},{8,0},{12,4},{16,8},{20,12},{24,16},{28,20},{1,25},{... | collective-permute-start | bytes 589832 | tf_op jit(solution)/shard_map/ppermute | solution.py:197
  75.1 7.5 %collective-permute-done.6 = bf16[384,256]{1,0:T(8,128)(2,1)S(1)} collective-permute-done((bf16[384,256]{1,0:T(8,128)(2,1)S(1)}, bf16[384,256]{1,0:T(8,128)(2,1)S(1)}, u32[]{:S(2)}, u32[]{:S(2)}) %collective-permute-start.6) | collective-permute-done | bytes 196640 | tf_op jit(solution)/shard_map/ppermute | solution.py:197
  82.7 1.8 %add_convert_fusion.3 = bf16[384,256]{1,0:T(8,128)(2,1)} fusion(f32[384,256]{1,0:T(8,128)S(1)} %copy-done.4, bf16[384,256]{1,0:T(8,128)(2,1)S(1)} %collective-permute-done.7, bf16[384,256]{1,0:T(8,128)(2,1)S(1)} %collective-permute-done.6, bf16[384,256]{1,0:T(8,128)(2,1)S(1)} %collective-permute-done.5, bf16[1536,256]{1,0:T(8,128)(2,1)} %copy-done.3, ...), kind=kLoop, calls=%fused_computation.7 | loop fusion | flops 1081344 | bytes 1572864 | tf_op jit(solution)/shard_map/convert.8
  84.4 1.0 reshape.62
  86.1 1.3 %add_convert_fusion.2 = bf16[384,256]{1,0:T(8,128)(2,1)S(1)} fusion(f32[384,256]{1,0:T(8,128)} %get-tuple-element.20, bf16[384,256]{1,0:T(8,128)(2,1)} %collective-permute-done.11, bf16[384,256]{1,0:T(8,128)(2,1)} %collective-permute-done.10, bf16[384,256]{1,0:T(8,128)(2,1)} %collective-permute-done.9, bf16[1536,256]{1,0:T(8,128)(2,1)S(1)} %collective-permute-done.8, ...), kind=kLoop, calls=%fused_computation.6 | loop fusion | flops 1081344 | bytes 1572864 | tf_op jit(solution)/shard_map/convert.7
  88.1 0.9 pad_maximum_fusion.2
  89.1 2.2 %all-to-all-done = bf16[4,96,1536]{2,1,0:T(8,128)(2,1)S(1)} async-done(((bf16[4,96,1536]{2,1,0:T(8,128)(2,1)}), bf16[4,96,1536]{2,1,0:T(8,128)(2,1)S(1)}, u32[]{:S(2)}, u32[]{:S(2)}) %all-to-all-start) | async-done | bytes 1179680 | tf_op jit(solution)/shard_map/all_to_all | solution.py:205
  91.3 1.1 %copy.39 = bf16[4,12,8,1536]{3,2,0,1:T(8,128)(2,1)} copy(bf16[4,12,8,1536]{3,2,1,0:T(8,128)(2,1)S(1)} %bitcast.22) | data formatting | bytes 2359296 | tf_op jit(solution)/shard_map/all_to_all | solution.py:205
  92.4 13.7 %all_to_all.35 = bf16[4,96,512]{2,1,0:T(8,128)(2,1)S(1)} all-to-all(bf16[4,96,512]{2,1,0:T(8,128)(2,1)S(1)} %bitcast.24), channel_id=1, replica_groups=mesh['ctx'=8,'uly'=4] {'uly'}, dimensions={0} | all-to-all | bytes 786432 | tf_op jit(solution)/shard_map/all_to_all | solution.py:207
  106.2 0.5 fusion.12
  107.0 0.7 copy.41
  108.0 0.7 copy.42
  (51 shorter events, 4.5 us)
Async XLA Ops:
  1.8 22.0 %copy-start.5 = (s32[24,8]{0,1:T(8,128)S(1)}, s32[24,8]{0,1:T(8,128)}, u32[]{:S(2)}) copy-start(s32[24,8]{0,1:T(8,128)} %param.9) | copy-start | bytes 2308
  1.8 13.9 %collective-permute-start = (bf16[384,512]{1,0:T(8,128)(2,1)S(1)}, bf16[384,512]{1,0:T(8,128)(2,1)S(1)}, u32[]{:S(2)}, u32[]{:S(2)}) collective-permute-start(bf16[384,512]{1,0:T(8,128)(2,1)S(1)} %pad_maximum_fusion.1), channel_id=1, source_target_pairs={{0,8},{4,12},{8,16},{12,20},{16,24},{20,28},{24,0},{28,4},{1,9},{5... | collective-permute-start | bytes 1179656 | tf_op jit(solution)/shard_map/ppermute | solution.py:148
  4.8 18.5 %collective-permute-start.1 = (bf16[384,512]{1,0:T(8,128)(2,1)S(1)}, bf16[384,512]{1,0:T(8,128)(2,1)S(1)}, u32[]{:S(2)}, u32[]{:S(2)}) collective-permute-start(bf16[384,512]{1,0:T(8,128)(2,1)S(1)} %pad_maximum_fusion.1), channel_id=1, source_target_pairs={{0,16},{4,20},{8,24},{12,28},{16,0},{20,4},{24,8},{28,12},{1,17},{... | collective-permute-start | bytes 1179656 | tf_op jit(solution)/shard_map/ppermute | solution.py:148
  6.3 17.3 %collective-permute-start.2 = (bf16[384,512]{1,0:T(8,128)(2,1)S(1)}, bf16[384,512]{1,0:T(8,128)(2,1)S(1)}, u32[]{:S(2)}, u32[]{:S(2)}) collective-permute-start(bf16[384,512]{1,0:T(8,128)(2,1)S(1)} %pad_maximum_fusion.1), channel_id=1, source_target_pairs={{0,24},{4,28},{8,0},{12,4},{16,8},{20,12},{24,16},{28,20},{1,25},{... | collective-permute-start | bytes 1179656 | tf_op jit(solution)/shard_map/ppermute | solution.py:148
  23.7 4.7 %copy-start = (bf16[1536,512]{1,0:T(8,128)(2,1)}, bf16[1536,512]{1,0:T(8,128)(2,1)S(1)}, u32[]{:S(2)}) copy-start(bf16[1536,512]{1,0:T(8,128)(2,1)S(1)} %pad_maximum_fusion.k_ref.v_ref) | copy-start | bytes 4718596
  23.7 3.5 %collective-permute-start.3 = (bf16[1536,512]{1,0:T(8,128)(2,1)S(1)}, bf16[1536,512]{1,0:T(8,128)(2,1)S(1)}, u32[]{:S(2)}, u32[]{:S(2)}) collective-permute-start(bf16[1536,512]{1,0:T(8,128)(2,1)S(1)} %pad_maximum_fusion.k_ref.v_ref), channel_id=1, source_target_pairs={{0,4},{4,0},{8,12},{12,8},{16,20},{20,16},{24,28},{28,24},{1,5},{5... | collective-permute-start | bytes 4718600 | tf_op jit(solution)/shard_map/ppermute | solution.py:150
  27.1 1.5 %copy-start.6 = (bf16[1536,512]{1,0:T(8,128)(2,1)}, bf16[1536,512]{1,0:T(8,128)(2,1)S(1)}, u32[]{:S(2)}) copy-start(bf16[1536,512]{1,0:T(8,128)(2,1)S(1)} %collective-permute-done.3.ko_ref.vo_ref) | copy-start | bytes 4718596
  42.8 19.6 %collective-permute-start.4 = (bf16[1536,256]{1,0:T(8,128)(2,1)}, bf16[1536,256]{1,0:T(8,128)(2,1)S(1)}, u32[]{:S(2)}, u32[]{:S(2)}) collective-permute-start(bf16[1536,256]{1,0:T(8,128)(2,1)} %get-tuple-element.16), channel_id=1, source_target_pairs={{0,4},{4,0},{8,12},{12,8},{16,20},{20,16},{24,28},{28,24},{1,5},{5... | collective-permute-start | bytes 2359304 | tf_op jit(solution)/shard_map/ppermute | solution.py:192
  57.0 6.2 %copy-start.2 = (bf16[1536,256]{1,0:T(8,128)(2,1)S(1)}, bf16[1536,256]{1,0:T(8,128)(2,1)}, u32[]{:S(2)}) copy-start(bf16[1536,256]{1,0:T(8,128)(2,1)} %get-tuple-element.15) | copy-start | bytes 2359300
  57.0 11.2 %collective-permute-start.8 = (bf16[1536,256]{1,0:T(8,128)(2,1)}, bf16[1536,256]{1,0:T(8,128)(2,1)S(1)}, u32[]{:S(2)}, u32[]{:S(2)}) collective-permute-start(bf16[1536,256]{1,0:T(8,128)(2,1)} %get-tuple-element.19), channel_id=1, source_target_pairs={{0,4},{4,0},{8,12},{12,8},{16,20},{20,16},{24,28},{28,24},{1,5},{5... | collective-permute-start | bytes 2359304 | tf_op jit(solution)/shard_map/ppermute | solution.py:192
  57.5 33.8 %all-to-all-start = ((bf16[4,96,1536]{2,1,0:T(8,128)(2,1)}), bf16[4,96,1536]{2,1,0:T(8,128)(2,1)S(1)}, u32[]{:S(2)}, u32[]{:S(2)}) async-start(bf16[4,96,1536]{2,1,0:T(8,128)(2,1)} %bitcast.23), calls=%async_computation | async-start | bytes 2359296 | tf_op jit(solution)/shard_map/all_to_all | solution.py:205
  62.4 0.9 copy-start.3
  63.2 5.0 %copy-start.1 = (bf16[1536,256]{1,0:T(8,128)(2,1)S(1)}, bf16[1536,256]{1,0:T(8,128)(2,1)}, u32[]{:S(2)}) copy-start(bf16[1536,256]{1,0:T(8,128)(2,1)} %get-tuple-element.18) | copy-start | bytes 2359300
  64.7 7.8 %collective-permute-start.5 = (bf16[384,256]{1,0:T(8,128)(2,1)S(1)}, bf16[384,256]{1,0:T(8,128)(2,1)S(1)}, u32[]{:S(2)}, u32[]{:S(2)}) collective-permute-start(bf16[384,256]{1,0:T(8,128)(2,1)S(1)} %get-tuple-element.26), channel_id=1, source_target_pairs={{0,24},{4,28},{8,0},{12,4},{16,8},{20,12},{24,16},{28,20},{1,25},{... | collective-permute-start | bytes 589832 | tf_op jit(solution)/shard_map/ppermute | solution.py:197
  66.4 16.2 %collective-permute-start.6 = (bf16[384,256]{1,0:T(8,128)(2,1)S(1)}, bf16[384,256]{1,0:T(8,128)(2,1)S(1)}, u32[]{:S(2)}, u32[]{:S(2)}) collective-permute-start(bf16[384,256]{1,0:T(8,128)(2,1)S(1)} %get-tuple-element.28), channel_id=1, source_target_pairs={{0,16},{4,20},{8,24},{12,28},{16,0},{20,4},{24,8},{28,12},{1,17},{... | collective-permute-start | bytes 589832 | tf_op jit(solution)/shard_map/ppermute | solution.py:197
  67.9 14.7 %collective-permute-start.7 = (bf16[384,256]{1,0:T(8,128)(2,1)S(1)}, bf16[384,256]{1,0:T(8,128)(2,1)S(1)}, u32[]{:S(2)}, u32[]{:S(2)}) collective-permute-start(bf16[384,256]{1,0:T(8,128)(2,1)S(1)} %get-tuple-element.27), channel_id=1, source_target_pairs={{0,8},{4,12},{8,16},{12,20},{16,24},{20,28},{24,0},{28,4},{1,9},{5... | collective-permute-start | bytes 589832 | tf_op jit(solution)/shard_map/ppermute | solution.py:197
  68.2 14.4 %copy-start.4 = (f32[384,256]{1,0:T(8,128)S(1)}, f32[384,256]{1,0:T(8,128)}, u32[]{:S(2)}) copy-start(f32[384,256]{1,0:T(8,128)} %get-tuple-element.17) | copy-start | bytes 1179652
  69.3 16.8 %collective-permute-start.10 = (bf16[384,256]{1,0:T(8,128)(2,1)}, bf16[384,256]{1,0:T(8,128)(2,1)}, u32[]{:S(2)}, u32[]{:S(2)}) collective-permute-start(bf16[384,256]{1,0:T(8,128)(2,1)} %get-tuple-element.31), channel_id=1, source_target_pairs={{0,16},{4,20},{8,24},{12,28},{16,0},{20,4},{24,8},{28,12},{1,17},{... | collective-permute-start | bytes 589832 | tf_op jit(solution)/shard_map/ppermute | solution.py:197
  69.8 16.2 %collective-permute-start.11 = (bf16[384,256]{1,0:T(8,128)(2,1)}, bf16[384,256]{1,0:T(8,128)(2,1)}, u32[]{:S(2)}, u32[]{:S(2)}) collective-permute-start(bf16[384,256]{1,0:T(8,128)(2,1)} %get-tuple-element.30), channel_id=1, source_target_pairs={{0,8},{4,12},{8,16},{12,20},{16,24},{20,28},{24,0},{28,4},{1,9},{5... | collective-permute-start | bytes 589832 | tf_op jit(solution)/shard_map/ppermute | solution.py:197
  72.5 13.5 %collective-permute-start.9 = (bf16[384,256]{1,0:T(8,128)(2,1)}, bf16[384,256]{1,0:T(8,128)(2,1)}, u32[]{:S(2)}, u32[]{:S(2)}) collective-permute-start(bf16[384,256]{1,0:T(8,128)(2,1)} %get-tuple-element.29), channel_id=1, source_target_pairs={{0,24},{4,28},{8,0},{12,4},{16,8},{20,12},{24,16},{28,20},{1,25},{... | collective-permute-start | bytes 589832 | tf_op jit(solution)/shard_map/ppermute | solution.py:197

commit v22 on v17

--- a/solution.py
+++ b/solution.py
@@ -80,9 +80,6 @@
         row = pl.multiple_of(dst_ref(b * SLOTS + s) * BLK, BLK)
         kt = kterm[:, s * BLK:(s + 1) * BLK]
         vt = vterm[:, s * BLK:(s + 1) * BLK]
-        rounded = kind == 0
-        kt = jnp.where(rounded, kt.astype(jnp.bfloat16).astype(jnp.float32), kt)
-        vt = jnp.where(rounded, vt.astype(jnp.bfloat16).astype(jnp.float32), vt)
 
         side = side_ref(b * SLOTS + s)
 
@@ -92,12 +89,17 @@
             loc_ref[pl.ds(row, BLK), HD:2 * HD] += vt
 
         for code, out in ((0, far_ref), (1, fo_ref)):
-            @pl.when((kind != 2) & (side == code))
-            def _():
-                kk = out[pl.ds(row, BLK), 0:HD].astype(jnp.float32) + kt
-                out[pl.ds(row, BLK), 0:HD] = kk.astype(jnp.bfloat16)
-                vv = out[pl.ds(row, BLK), HD:2 * HD].astype(jnp.float32) + vt
-                out[pl.ds(row, BLK), HD:2 * HD] = vv.astype(jnp.bfloat16)
+            for round_it in (True, False):
+                @pl.when((kind == (0 if round_it else 1)) & (side == code))
+                def _():
+                    ka, va = kt, vt
+                    if round_it:
+                        ka = ka.astype(jnp.bfloat16).astype(jnp.float32)
+                        va = va.astype(jnp.bfloat16).astype(jnp.float32)
+                    kk = out[pl.ds(row, BLK), 0:HD].astype(jnp.float32) + ka
+                    out[pl.ds(row, BLK), 0:HD] = kk.astype(jnp.bfloat16)
+                    vv = out[pl.ds(row, BLK), HD:2 * HD].astype(jnp.float32) + va
+                    out[pl.ds(row, BLK), HD:2 * HD] = vv.astype(jnp.bfloat16)
 
 
 def shards(query_rows, key_rows, value_rows, out_grad, block_list):

time: 107 us -> 107 us (level)
  transfers between devices with their start and end apart: 17 -> 17, of which waited for: 11 -> 11; matrix products, arithmetic and copies ran while one was open for 10% -> 9% of each run, Pallas kernels for 27% -> 27%
where the time goes in v22:
time: 107 us
  Pallas kernels  28.7 us (27%)
  waiting for transfers between devices  27.7 us (26%)
  starting transfers between devices  20.6 us (19%)
  blocking collectives  13.8 us (13%)
  local copies, waits for them, and re-layouts  9.02 us (8%)
  other arithmetic  6.02 us (6%)
    pallas_call x2, Pallas kernels, shards(): pl.pallas_call(kernel, grid_spec=grid_spec, out_shape=[jax.ShapeDtypeStru...  28.7 us
    all_to_all x1, blocking collectives, shards(): lax.all_to_all(kv_grad, 'uly', split_axis=0, concat_axis=1, tiled=True)  13.8 us
    ppermute x6, waiting for transfers between devices, shards(): lax.ppermute(mine[d * span:(d + 1) * span], 'ctx', pairs)  13.2 us
    ppermute x6, waiting for transfers between devices, shards(): gathered.append(lax.ppermute(kv_own, 'ctx', pairs))  11.6 us
    ppermute x6, starting transfers between devices, shards(): gathered.append(lax.ppermute(kv_own, 'ctx', pairs))  9.11 us
    ppermute x6, starting transfers between devices, shards(): lax.ppermute(mine[d * span:(d + 1) * span], 'ctx', pairs)  5.75 us
    all_to_all x1, starting transfers between devices, shards(): lax.all_to_all(dq, 'uly', split_axis=0, concat_axis=1, tiled=True)  5.01 us
    all_to_all x1, waiting for transfers between devices, shards(): lax.all_to_all(dq, 'uly', split_axis=0, concat_axis=1, tiled=True)  2.91 us
  transfers between devices with their start and end apart: 17, of which 11 were waited for; matrix products, arithmetic and copies ran while one was open for 9% of the time, Pallas kernels for 27%

profile of v22, /device:TPU:0, one launch (start us, length us, event | category | flops | bytes accessed | tf_op | source)
XLA Modules:
  0.0 106.8 jit_solution(1564269229165853580)
XLA Ops:
  0.7 1.1 %constant_dynamic-slice_fusion = (bf16[384,128]{1,0:T(8,128)(2,1)S(1)}, bf16[384,128]{1,0:T(8,128)(2,1)S(1)}, bf16[384,128]{1,0:T(8,128)(2,1)S(1)}, bf16[384,128]{1,0:T(8,128)(2,1)S(1)}) fusion(bf16[384,1024]{1,0:T(8,128)(2,1)} %param.7, s32[]{:T(128)S(6)} %select_n.71, s32[]{:T(128)S(6)} %select_n.70, bf16[384,1024]{1,0:T(8,128)(2,1)} %param.6), kind=kLoop, calls=%fused_computation.36 | loop fusion | bytes 786440 | tf_op jit(solution)/shard_map/dynamic_slice | solution.py:145
  1.8 3.0 %collective-permute-start.4 = (bf16[384,256]{1,0:T(8,128)(2,1)S(1)}, bf16[384,256]{1,0:T(8,128)(2,1)S(1)}, u32[]{:S(2)}, u32[]{:S(2)}) collective-permute-start(bf16[384,256]{1,0:T(8,128)(2,1)S(1)} %pad_maximum_fusion.4), channel_id=1, source_target_pairs={{0,8},{4,12},{8,16},{12,20},{16,24},{20,28},{24,0},{28,4},{1,9},{5... | collective-permute-start | bytes 589832 | tf_op jit(solution)/shard_map/ppermute | solution.py:152
  4.8 1.5 %collective-permute-start.5 = (bf16[384,256]{1,0:T(8,128)(2,1)S(1)}, bf16[384,256]{1,0:T(8,128)(2,1)S(1)}, u32[]{:S(2)}, u32[]{:S(2)}) collective-permute-start(bf16[384,256]{1,0:T(8,128)(2,1)S(1)} %pad_maximum_fusion.4), channel_id=1, source_target_pairs={{0,16},{4,20},{8,24},{12,28},{16,0},{20,4},{24,8},{28,12},{1,17},{... | collective-permute-start | bytes 589832 | tf_op jit(solution)/shard_map/ppermute | solution.py:152
  6.3 1.4 %collective-permute-start.6 = (bf16[384,256]{1,0:T(8,128)(2,1)S(1)}, bf16[384,256]{1,0:T(8,128)(2,1)S(1)}, u32[]{:S(2)}, u32[]{:S(2)}) collective-permute-start(bf16[384,256]{1,0:T(8,128)(2,1)S(1)} %pad_maximum_fusion.4), channel_id=1, source_target_pairs={{0,24},{4,28},{8,0},{12,4},{16,8},{20,12},{24,16},{28,20},{1,25},{... | collective-permute-start | bytes 589832 | tf_op jit(solution)/shard_map/ppermute | solution.py:152
  9.2 2.3 %collective-permute-done.4 = bf16[384,256]{1,0:T(8,128)(2,1)S(1)} collective-permute-done((bf16[384,256]{1,0:T(8,128)(2,1)S(1)}, bf16[384,256]{1,0:T(8,128)(2,1)S(1)}, u32[]{:S(2)}, u32[]{:S(2)}) %collective-permute-start.4) | collective-permute-done | bytes 196640 | tf_op jit(solution)/shard_map/ppermute | solution.py:152
  11.5 2.0 %collective-permute-start.2 = (bf16[384,256]{1,0:T(8,128)(2,1)S(1)}, bf16[384,256]{1,0:T(8,128)(2,1)S(1)}, u32[]{:S(2)}, u32[]{:S(2)}) collective-permute-start(bf16[384,256]{1,0:T(8,128)(2,1)S(1)} %pad_maximum_fusion.3), channel_id=1, source_target_pairs={{0,24},{4,28},{8,0},{12,4},{16,8},{20,12},{24,16},{28,20},{1,25},{... | collective-permute-start | bytes 589832 | tf_op jit(solution)/shard_map/ppermute | solution.py:152
  13.5 2.3 %collective-permute-done.5 = bf16[384,256]{1,0:T(8,128)(2,1)S(1)} collective-permute-done((bf16[384,256]{1,0:T(8,128)(2,1)S(1)}, bf16[384,256]{1,0:T(8,128)(2,1)S(1)}, u32[]{:S(2)}, u32[]{:S(2)}) %collective-permute-start.5) | collective-permute-done | bytes 196640 | tf_op jit(solution)/shard_map/ppermute | solution.py:152
  17.1 2.8 %collective-permute-done = bf16[384,256]{1,0:T(8,128)(2,1)S(1)} collective-permute-done((bf16[384,256]{1,0:T(8,128)(2,1)S(1)}, bf16[384,256]{1,0:T(8,128)(2,1)S(1)}, u32[]{:S(2)}, u32[]{:S(2)}) %collective-permute-start) | collective-permute-done | bytes 196640 | tf_op jit(solution)/shard_map/ppermute | solution.py:152
  20.0 3.3 %collective-permute-done.1 = bf16[384,256]{1,0:T(8,128)(2,1)S(1)} collective-permute-done((bf16[384,256]{1,0:T(8,128)(2,1)S(1)}, bf16[384,256]{1,0:T(8,128)(2,1)S(1)}, u32[]{:S(2)}, u32[]{:S(2)}) %collective-permute-start.1) | collective-permute-done | bytes 196640 | tf_op jit(solution)/shard_map/ppermute | solution.py:152
  23.8 0.7 pad_add_fusion.tbl_ref
  24.5 1.2 %broadcast_in_dim.10.dq_in = bf16[384,1536]{1,0:T(8,128)(2,1)} broadcast(bf16[]{:T(256)} %constant.92.clone.1), dimensions={} | broadcast | bytes 1179650 | tf_op jit(solution)/shard_map/broadcast_in_dim | solution.py:138
  25.7 14.3 %shard_map.76 = (bf16[384,1536]{1,0:T(8,128)(2,1)}, f32[384,256]{1,0:T(8,128)}, bf16[1536,256]{1,0:T(8,128)(2,1)}, bf16[1536,256]{1,0:T(8,128)(2,1)}) custom-call(s32[96]{0:T(128)} %pad_add_fusion.tbl_ref, bf16[384,1536]{1,0:T(8,128)(2,1)} %q_ref.3, bf16[384,1536]{1,0:T(8,128)(2,1)} %do_ref.3, ...), custom_call_target="tpu_custom_call", output_to_operand_aliasing={{0}: (7, {})} | custom-call | flops 3623878656 | bytes 5111808 | tf_op jit(solution)/shard_map/pallas_call | solution.py:180
  40.6 14.4 %shard_map.77 = (bf16[384,1536]{1,0:T(8,128)(2,1)}, f32[384,256]{1,0:T(8,128)}, bf16[1536,256]{1,0:T(8,128)(2,1)}, bf16[1536,256]{1,0:T(8,128)(2,1)}) custom-call(s32[96]{0:T(128)} %pad_add_fusion.tbl_ref, bf16[384,1536]{1,0:T(8,128)(2,1)} %q_ref.3, bf16[384,1536]{1,0:T(8,128)(2,1)} %do_ref.3, ...), custom_call_target="tpu_custom_call", output_to_operand_aliasing={{0}: (7, {})} | custom-call | flops 3623878656 | bytes 5111808 | tf_op jit(solution)/shard_map/pallas_call | solution.py:180
  55.1 5.0 %all-to-all-start = ((bf16[4,96,1536]{2,1,0:T(8,128)(2,1)}), bf16[4,96,1536]{2,1,0:T(8,128)(2,1)S(1)}, u32[]{:S(2)}, u32[]{:S(2)}) async-start(bf16[4,96,1536]{2,1,0:T(8,128)(2,1)} %bitcast.23), calls=%async_computation | async-start | bytes 2359296 | tf_op jit(solution)/shard_map/all_to_all | solution.py:210
  60.1 1.3 %add_convert_fusion.1 = bf16[1536,256]{1,0:T(8,128)(2,1)S(1)} fusion(bf16[1536,256]{1,0:T(8,128)(2,1)} %collective-permute-done.8, bf16[1536,256]{1,0:T(8,128)(2,1)S(1)} %copy-done.1), kind=kLoop, calls=%fused_computation.1 | loop fusion | flops 1572864 | bytes 2359296 | tf_op jit(solution)/shard_map/convert_element_type | solution.py:198
  61.5 1.5 %collective-permute-start.10 = (bf16[384,256]{1,0:T(8,128)(2,1)S(1)}, bf16[384,256]{1,0:T(8,128)(2,1)S(1)}, u32[]{:S(2)}, u32[]{:S(2)}) collective-permute-start(bf16[384,256]{1,0:T(8,128)(2,1)S(1)} %get-tuple-element.34), channel_id=1, source_target_pairs={{0,16},{4,20},{8,24},{12,28},{16,0},{20,4},{24,8},{28,12},{1,17},{... | collective-permute-start | bytes 589832 | tf_op jit(solution)/shard_map/ppermute | solution.py:202
  63.0 0.8 collective-permute-start.11
  63.7 2.1 %collective-permute-start.9 = (bf16[384,256]{1,0:T(8,128)(2,1)S(1)}, bf16[384,256]{1,0:T(8,128)(2,1)S(1)}, u32[]{:S(2)}, u32[]{:S(2)}) collective-permute-start(bf16[384,256]{1,0:T(8,128)(2,1)S(1)} %get-tuple-element.32), channel_id=1, source_target_pairs={{0,24},{4,28},{8,0},{12,4},{16,8},{20,12},{24,16},{28,20},{1,25},{... | collective-permute-start | bytes 589832 | tf_op jit(solution)/shard_map/ppermute | solution.py:202
  66.1 0.8 fusion.11
  66.9 0.8 collective-permute-start.13
  68.3 5.2 %collective-permute-done.10 = bf16[384,256]{1,0:T(8,128)(2,1)S(1)} collective-permute-done((bf16[384,256]{1,0:T(8,128)(2,1)S(1)}, bf16[384,256]{1,0:T(8,128)(2,1)S(1)}, u32[]{:S(2)}, u32[]{:S(2)}) %collective-permute-start.10) | collective-permute-done | bytes 196640 | tf_op jit(solution)/shard_map/ppermute | solution.py:202
  73.5 1.5 %collective-permute-done.9 = bf16[384,256]{1,0:T(8,128)(2,1)S(1)} collective-permute-done((bf16[384,256]{1,0:T(8,128)(2,1)S(1)}, bf16[384,256]{1,0:T(8,128)(2,1)S(1)}, u32[]{:S(2)}, u32[]{:S(2)}) %collective-permute-start.9) | collective-permute-done | bytes 196640 | tf_op jit(solution)/shard_map/ppermute | solution.py:202
  75.0 1.2 %add_convert_fusion.3 = bf16[384,256]{1,0:T(8,128)(2,1)S(1)} fusion(f32[384,256]{1,0:T(8,128)S(1)} %copy-done.4, bf16[384,256]{1,0:T(8,128)(2,1)S(1)} %collective-permute-done.11, bf16[384,256]{1,0:T(8,128)(2,1)S(1)} %collective-permute-done.10, bf16[384,256]{1,0:T(8,128)(2,1)S(1)} %collective-permute-done.9, bf16[1536,256]{1,0:T(8,128)(2,1)} %collective-permute-done.8, ...), kind=kLoop, calls=%fused_computation.7 | loop fusion | flops 1081344 | bytes 1572864 | tf_op jit(solution)/shard_map/convert.8
  76.9 2.3 %collective-permute-done.13 = bf16[384,256]{1,0:T(8,128)(2,1)S(1)} collective-permute-done((bf16[384,256]{1,0:T(8,128)(2,1)}, bf16[384,256]{1,0:T(8,128)(2,1)S(1)}, u32[]{:S(2)}, u32[]{:S(2)}) %collective-permute-start.13) | collective-permute-done | bytes 196640 | tf_op jit(solution)/shard_map/ppermute | solution.py:202
  79.2 4.1 %collective-permute-done.15 = bf16[384,256]{1,0:T(8,128)(2,1)} collective-permute-done((bf16[384,256]{1,0:T(8,128)(2,1)}, bf16[384,256]{1,0:T(8,128)(2,1)}, u32[]{:S(2)}, u32[]{:S(2)}) %collective-permute-start.15) | collective-permute-done | bytes 196640 | tf_op jit(solution)/shard_map/ppermute | solution.py:202
  83.3 1.3 %add_convert_fusion.2 = bf16[384,256]{1,0:T(8,128)(2,1)S(1)} fusion(f32[384,256]{1,0:T(8,128)} %get-tuple-element.26, bf16[384,256]{1,0:T(8,128)(2,1)} %collective-permute-done.15, bf16[384,256]{1,0:T(8,128)(2,1)} %collective-permute-done.14, bf16[384,256]{1,0:T(8,128)(2,1)S(1)} %collective-permute-done.13, bf16[1536,256]{1,0:T(8,128)(2,1)S(1)} %collective-permute-done.12, ...), kind=kLoop, calls=%fused_computation.6 | loop fusion | flops 1081344 | bytes 1572864 | tf_op jit(solution)/shard_map/convert.7
  85.3 0.9 pad_maximum_fusion.2
  86.3 2.9 %all-to-all-done = bf16[4,96,1536]{2,1,0:T(8,128)(2,1)S(1)} async-done(((bf16[4,96,1536]{2,1,0:T(8,128)(2,1)}), bf16[4,96,1536]{2,1,0:T(8,128)(2,1)S(1)}, u32[]{:S(2)}, u32[]{:S(2)}) %all-to-all-start) | async-done | bytes 1179680 | tf_op jit(solution)/shard_map/all_to_all | solution.py:210
  89.2 1.1 %copy.39 = bf16[4,12,8,1536]{3,2,0,1:T(8,128)(2,1)} copy(bf16[4,12,8,1536]{3,2,1,0:T(8,128)(2,1)S(1)} %bitcast.22) | data formatting | bytes 2359296 | tf_op jit(solution)/shard_map/all_to_all | solution.py:210
  90.3 13.8 %all_to_all.35 = bf16[4,96,512]{2,1,0:T(8,128)(2,1)S(1)} all-to-all(bf16[4,96,512]{2,1,0:T(8,128)(2,1)S(1)} %bitcast.24), channel_id=1, replica_groups=mesh['ctx'=8,'uly'=4] {'uly'}, dimensions={0} | all-to-all | bytes 786432 | tf_op jit(solution)/shard_map/all_to_all | solution.py:212
  105.1 0.7 copy.41
  106.1 0.7 copy.42
  (61 shorter events, 7.3 us)
Async XLA Ops:
  0.6 8.3 %copy-start.5 = (s32[24,8]{0,1:T(8,128)S(1)}, s32[24,8]{0,1:T(8,128)}, u32[]{:S(2)}) copy-start(s32[24,8]{0,1:T(8,128)} %param.9) | copy-start | bytes 2308
  1.8 9.7 %collective-permute-start.4 = (bf16[384,256]{1,0:T(8,128)(2,1)S(1)}, bf16[384,256]{1,0:T(8,128)(2,1)S(1)}, u32[]{:S(2)}, u32[]{:S(2)}) collective-permute-start(bf16[384,256]{1,0:T(8,128)(2,1)S(1)} %pad_maximum_fusion.4), channel_id=1, source_target_pairs={{0,8},{4,12},{8,16},{12,20},{16,24},{20,28},{24,0},{28,4},{1,9},{5... | collective-permute-start | bytes 589832 | tf_op jit(solution)/shard_map/ppermute | solution.py:152
  4.8 11.0 %collective-permute-start.5 = (bf16[384,256]{1,0:T(8,128)(2,1)S(1)}, bf16[384,256]{1,0:T(8,128)(2,1)S(1)}, u32[]{:S(2)}, u32[]{:S(2)}) collective-permute-start(bf16[384,256]{1,0:T(8,128)(2,1)S(1)} %pad_maximum_fusion.4), channel_id=1, source_target_pairs={{0,16},{4,20},{8,24},{12,28},{16,0},{20,4},{24,8},{28,12},{1,17},{... | collective-permute-start | bytes 589832 | tf_op jit(solution)/shard_map/ppermute | solution.py:152
  6.3 10.0 %collective-permute-start.6 = (bf16[384,256]{1,0:T(8,128)(2,1)S(1)}, bf16[384,256]{1,0:T(8,128)(2,1)S(1)}, u32[]{:S(2)}, u32[]{:S(2)}) collective-permute-start(bf16[384,256]{1,0:T(8,128)(2,1)S(1)} %pad_maximum_fusion.4), channel_id=1, source_target_pairs={{0,24},{4,28},{8,0},{12,4},{16,8},{20,12},{24,16},{28,20},{1,25},{... | collective-permute-start | bytes 589832 | tf_op jit(solution)/shard_map/ppermute | solution.py:152
  7.8 12.2 %collective-permute-start = (bf16[384,256]{1,0:T(8,128)(2,1)S(1)}, bf16[384,256]{1,0:T(8,128)(2,1)S(1)}, u32[]{:S(2)}, u32[]{:S(2)}) collective-permute-start(bf16[384,256]{1,0:T(8,128)(2,1)S(1)} %pad_maximum_fusion.3), channel_id=1, source_target_pairs={{0,8},{4,12},{8,16},{12,20},{16,24},{20,28},{24,0},{28,4},{1,9},{5... | collective-permute-start | bytes 589832 | tf_op jit(solution)/shard_map/ppermute | solution.py:152
  8.4 14.9 %collective-permute-start.1 = (bf16[384,256]{1,0:T(8,128)(2,1)S(1)}, bf16[384,256]{1,0:T(8,128)(2,1)S(1)}, u32[]{:S(2)}, u32[]{:S(2)}) collective-permute-start(bf16[384,256]{1,0:T(8,128)(2,1)S(1)} %pad_maximum_fusion.3), channel_id=1, source_target_pairs={{0,16},{4,20},{8,24},{12,28},{16,0},{20,4},{24,8},{28,12},{1,17},{... | collective-permute-start | bytes 589832 | tf_op jit(solution)/shard_map/ppermute | solution.py:152
  11.5 12.1 %collective-permute-start.2 = (bf16[384,256]{1,0:T(8,128)(2,1)S(1)}, bf16[384,256]{1,0:T(8,128)(2,1)S(1)}, u32[]{:S(2)}, u32[]{:S(2)}) collective-permute-start(bf16[384,256]{1,0:T(8,128)(2,1)S(1)} %pad_maximum_fusion.3), channel_id=1, source_target_pairs={{0,24},{4,28},{8,0},{12,4},{16,8},{20,12},{24,16},{28,20},{1,25},{... | collective-permute-start | bytes 589832 | tf_op jit(solution)/shard_map/ppermute | solution.py:152
  16.4 9.3 %copy-start.2 = (bf16[1536,256]{1,0:T(8,128)(2,1)}, bf16[1536,256]{1,0:T(8,128)(2,1)S(1)}, u32[]{:S(2)}) copy-start(bf16[1536,256]{1,0:T(8,128)(2,1)S(1)} %pad_maximum_fusion.1.k_ref.v_ref) | copy-start | bytes 2359300
  16.4 8.1 %collective-permute-start.7 = (bf16[1536,256]{1,0:T(8,128)(2,1)S(1)}, bf16[1536,256]{1,0:T(8,128)(2,1)S(1)}, u32[]{:S(2)}, u32[]{:S(2)}) collective-permute-start(bf16[1536,256]{1,0:T(8,128)(2,1)S(1)} %pad_maximum_fusion.1.k_ref.v_ref), channel_id=1, source_target_pairs={{0,4},{4,0},{8,12},{12,8},{16,20},{20,16},{24,28},{28,24},{1,5},{5... | collective-permute-start | bytes 2359304 | tf_op jit(solution)/shard_map/ppermute | solution.py:154
  23.7 16.4 %copy-start.3 = (bf16[1536,256]{1,0:T(8,128)(2,1)}, bf16[1536,256]{1,0:T(8,128)(2,1)S(1)}, u32[]{:S(2)}) copy-start(bf16[1536,256]{1,0:T(8,128)(2,1)S(1)} %pad_maximum_fusion.k_ref.v_ref) | copy-start | bytes 2359300
  23.7 16.9 %collective-permute-start.3 = (bf16[1536,256]{1,0:T(8,128)(2,1)S(1)}, bf16[1536,256]{1,0:T(8,128)(2,1)}, u32[]{:S(2)}, u32[]{:S(2)}) collective-permute-start(bf16[1536,256]{1,0:T(8,128)(2,1)S(1)} %pad_maximum_fusion.k_ref.v_ref), channel_id=1, source_target_pairs={{0,4},{4,0},{8,12},{12,8},{16,20},{20,16},{24,28},{28,24},{1,5},{5... | collective-permute-start | bytes 2359304 | tf_op jit(solution)/shard_map/ppermute | solution.py:154
  24.5 1.3 %copy-start.6 = (bf16[1536,256]{1,0:T(8,128)(2,1)}, bf16[1536,256]{1,0:T(8,128)(2,1)S(1)}, u32[]{:S(2)}) copy-start(bf16[1536,256]{1,0:T(8,128)(2,1)S(1)} %collective-permute-done.7.ko_ref.vo_ref) | copy-start | bytes 2359300
  40.1 20.0 %collective-permute-start.8 = (bf16[1536,256]{1,0:T(8,128)(2,1)}, bf16[1536,256]{1,0:T(8,128)(2,1)}, u32[]{:S(2)}, u32[]{:S(2)}) collective-permute-start(bf16[1536,256]{1,0:T(8,128)(2,1)} %get-tuple-element.22), channel_id=1, source_target_pairs={{0,4},{4,0},{8,12},{12,8},{16,20},{20,16},{24,28},{28,24},{1,5},{5... | collective-permute-start | bytes 2359304 | tf_op jit(solution)/shard_map/ppermute | solution.py:197
  55.0 10.9 %collective-permute-start.12 = (bf16[1536,256]{1,0:T(8,128)(2,1)}, bf16[1536,256]{1,0:T(8,128)(2,1)S(1)}, u32[]{:S(2)}, u32[]{:S(2)}) collective-permute-start(bf16[1536,256]{1,0:T(8,128)(2,1)} %get-tuple-element.25), channel_id=1, source_target_pairs={{0,4},{4,0},{8,12},{12,8},{16,20},{20,16},{24,28},{28,24},{1,5},{5... | collective-permute-start | bytes 2359304 | tf_op jit(solution)/shard_map/ppermute | solution.py:197
  55.1 5.0 %copy-start.1 = (bf16[1536,256]{1,0:T(8,128)(2,1)S(1)}, bf16[1536,256]{1,0:T(8,128)(2,1)}, u32[]{:S(2)}) copy-start(bf16[1536,256]{1,0:T(8,128)(2,1)} %get-tuple-element.21) | copy-start | bytes 2359300
  55.1 34.1 %all-to-all-start = ((bf16[4,96,1536]{2,1,0:T(8,128)(2,1)}), bf16[4,96,1536]{2,1,0:T(8,128)(2,1)S(1)}, u32[]{:S(2)}, u32[]{:S(2)}) async-start(bf16[4,96,1536]{2,1,0:T(8,128)(2,1)} %bitcast.23), calls=%async_computation | async-start | bytes 2359296 | tf_op jit(solution)/shard_map/all_to_all | solution.py:210
  61.4 4.5 %copy-start = (bf16[1536,256]{1,0:T(8,128)(2,1)S(1)}, bf16[1536,256]{1,0:T(8,128)(2,1)}, u32[]{:S(2)}) copy-start(bf16[1536,256]{1,0:T(8,128)(2,1)} %get-tuple-element.24) | copy-start | bytes 2359300
  61.5 12.0 %collective-permute-start.10 = (bf16[384,256]{1,0:T(8,128)(2,1)S(1)}, bf16[384,256]{1,0:T(8,128)(2,1)S(1)}, u32[]{:S(2)}, u32[]{:S(2)}) collective-permute-start(bf16[384,256]{1,0:T(8,128)(2,1)S(1)} %get-tuple-element.34), channel_id=1, source_target_pairs={{0,16},{4,20},{8,24},{12,28},{16,0},{20,4},{24,8},{28,12},{1,17},{... | collective-permute-start | bytes 589832 | tf_op jit(solution)/shard_map/ppermute | solution.py:202
  63.0 10.6 %collective-permute-start.11 = (bf16[384,256]{1,0:T(8,128)(2,1)S(1)}, bf16[384,256]{1,0:T(8,128)(2,1)S(1)}, u32[]{:S(2)}, u32[]{:S(2)}) collective-permute-start(bf16[384,256]{1,0:T(8,128)(2,1)S(1)} %get-tuple-element.33), channel_id=1, source_target_pairs={{0,8},{4,12},{8,16},{12,20},{16,24},{20,28},{24,0},{28,4},{1,9},{5... | collective-permute-start | bytes 589832 | tf_op jit(solution)/shard_map/ppermute | solution.py:202
  63.7 11.3 %collective-permute-start.9 = (bf16[384,256]{1,0:T(8,128)(2,1)S(1)}, bf16[384,256]{1,0:T(8,128)(2,1)S(1)}, u32[]{:S(2)}, u32[]{:S(2)}) collective-permute-start(bf16[384,256]{1,0:T(8,128)(2,1)S(1)} %get-tuple-element.32), channel_id=1, source_target_pairs={{0,24},{4,28},{8,0},{12,4},{16,8},{20,12},{24,16},{28,20},{1,25},{... | collective-permute-start | bytes 589832 | tf_op jit(solution)/shard_map/ppermute | solution.py:202
  66.1 8.9 %copy-start.4 = (f32[384,256]{1,0:T(8,128)S(1)}, f32[384,256]{1,0:T(8,128)}, u32[]{:S(2)}) copy-start(f32[384,256]{1,0:T(8,128)} %get-tuple-element.23) | copy-start | bytes 1179652
  66.9 12.3 %collective-permute-start.13 = (bf16[384,256]{1,0:T(8,128)(2,1)}, bf16[384,256]{1,0:T(8,128)(2,1)S(1)}, u32[]{:S(2)}, u32[]{:S(2)}) collective-permute-start(bf16[384,256]{1,0:T(8,128)(2,1)} %get-tuple-element.35), channel_id=1, source_target_pairs={{0,24},{4,28},{8,0},{12,4},{16,8},{20,12},{24,16},{28,20},{1,25},{... | collective-permute-start | bytes 589832 | tf_op jit(solution)/shard_map/ppermute | solution.py:202
  67.8 11.5 %collective-permute-start.14 = (bf16[384,256]{1,0:T(8,128)(2,1)}, bf16[384,256]{1,0:T(8,128)(2,1)}, u32[]{:S(2)}, u32[]{:S(2)}) collective-permute-start(bf16[384,256]{1,0:T(8,128)(2,1)} %get-tuple-element.37), channel_id=1, source_target_pairs={{0,16},{4,20},{8,24},{12,28},{16,0},{20,4},{24,8},{28,12},{1,17},{... | collective-permute-start | bytes 589832 | tf_op jit(solution)/shard_map/ppermute | solution.py:202
  73.5 9.8 %collective-permute-start.15 = (bf16[384,256]{1,0:T(8,128)(2,1)}, bf16[384,256]{1,0:T(8,128)(2,1)}, u32[]{:S(2)}, u32[]{:S(2)}) collective-permute-start(bf16[384,256]{1,0:T(8,128)(2,1)} %get-tuple-element.36), channel_id=1, source_target_pairs={{0,8},{4,12},{8,16},{12,20},{16,24},{20,28},{24,0},{28,4},{1,9},{5... | collective-permute-start | bytes 589832 | tf_op jit(solution)/shard_map/ppermute | solution.py:202
